TPU v7x, 128 devices: a whole 4x4x4 slice. The times are simulated.
128 devices in a mesh: rows: 8 (over x, z_hi), cols: 8 (over y, core), rep: 2 (over z_lo).
Axes of the slice: x: 4, y: 4, z: 4 (z_hi: 2, z_lo: 2; z = z_hi * 2 + z_lo), core: 2. Of those that a mesh axis runs over, the one named last changes fastest.
Arguments:
- inputs: bfloat16 [8, 128, 256, 256], P('rep', 'rows', 'cols'), may hold values from -6 to 6
- upstream: bfloat16 [8, 128, 256, 256], P('rep', 'rows', 'cols'), may hold values from -6 to 6
- kernel: bfloat16 [3, 3, 256, 256], replicated, may hold values from -0.125 to 0.125
- probe_init: float32 [128, 256, 256], P('rows', 'cols'), may hold values from -18 to 18
Outputs:
- outputs: bfloat16 [8, 128, 256, 256], P('rep', 'rows', 'cols')
- input_grad: bfloat16 [8, 128, 256, 256], P('rep', 'rows', 'cols')
- kernel_grad: float32 [256, 2304], P(('rows', 'cols'))
- probe_out: float32 [128, 256, 256], P('rows', 'cols')
- lipschitz: float32 [], replicated
- norm_trace: float32 [3], replicated
All inputs are finite; a program needn't handle non-finite values.
Results may differ from a plain program's by a relative error of at most 0.011.
Values may be sent and summed in bfloat16 or wider, within the bound.
No kernel may reach another device: no remote copies, remote signals or barrier semaphores. Data moves between devices by JAX's collectives and lax.ppermute only.
A program may use at most 128 MiB of HBM per device.

v0:
```python
import math

import jax
import jax.numpy as jnp
from jax import lax
from jax.sharding import PartitionSpec as P

ITERS = 4


def extended(cells, sides, width, closed):
    for axis, dim in sides:
        count = lax.axis_size(axis)
        ends = count if closed else count - 1
        head = lax.slice_in_dim(cells, 0, width, axis=dim)
        tail = lax.slice_in_dim(cells, cells.shape[dim] - width, cells.shape[dim], axis=dim)
        cells = jnp.concatenate(
            [
                lax.ppermute(tail, axis, [(i, (i + 1) % count) for i in range(ends)]),
                cells,
                lax.ppermute(head, axis, [((i + 1) % count, i) for i in range(ends)]),
            ],
            axis=dim,
        )
    return cells


def butterfly_sum(value, axes):
    for axis in axes:
        count = lax.axis_size(axis)
        step = 1
        while step < count:
            value = value + lax.ppermute(value, axis, [(i, i ^ step) for i in range(count)])
            step *= 2
    return value


def halving_scatter(value, axes):
    for axis in axes:
        count = lax.axis_size(axis)
        index = lax.axis_index(axis)
        step = count // 2
        while step >= 1:
            half = value.shape[0] // 2
            upper = (index // step) % 2
            keep = lax.dynamic_slice_in_dim(value, upper * half, half, axis=0)
            send = lax.dynamic_slice_in_dim(value, (1 - upper) * half, half, axis=0)
            value = keep + lax.ppermute(send, axis, [(i, i ^ step) for i in range(count)])
            step //= 2
    return value


def conv(padded, weights, adjoint):
    if adjoint:
        weights = weights[::-1, ::-1]
    return lax.conv_general_dilated(
        padded,
        weights,
        window_strides=(1, 1),
        padding="VALID",
        dimension_numbers=("NHWC", "HWOI" if adjoint else "HWIO", "NHWC"),
        preferred_element_type=jnp.float32,
    )


def per_device(inputs, upstream, kernel, probe_init):
    batch = inputs.shape[0]
    height = inputs.shape[1]
    breadth = inputs.shape[2]
    channels = kernel.shape[2]
    rows_count = lax.axis_size("rows")
    cols_count = lax.axis_size("cols")
    count = float(height * rows_count * breadth * cols_count * channels)
    field = (("rows", 0), ("cols", 1))
    iterate = probe_init.astype(jnp.bfloat16)
    padded_probe = extended(iterate, field, 2, True)

    def power_step(carry, _):
        padded_probe, iterate = carry
        image = conv(padded_probe[None], kernel, False).astype(jnp.bfloat16)
        back = conv(image, kernel, True)[0]
        padded_back = extended(back, field, 2, True)
        squared = butterfly_sum(jnp.sum(back * back), ("rows", "cols"))
        scale_now = jnp.sqrt(squared / count + 1e-06)
        iterate = (back / scale_now).astype(jnp.bfloat16)
        padded_probe = (padded_back / scale_now).astype(jnp.bfloat16)
        return (padded_probe, iterate), scale_now

    (padded_probe, iterate), norm_trace = lax.scan(
        power_step, (padded_probe, iterate), None, length=ITERS - 1
    )
    image = conv(padded_probe[None], kernel, False).astype(jnp.bfloat16)
    back = conv(image, kernel, True)[0]
    wide_iter = iterate.astype(jnp.float32)
    totals = butterfly_sum(
        jnp.stack([jnp.sum(back * back), jnp.sum(wide_iter * wide_iter)]),
        ("rows", "cols"),
    )
    sum_back = totals[0]
    sum_probe = totals[1]
    lipschitz = jnp.sqrt(jnp.sqrt(sum_back / sum_probe))
    probe_out = back / jnp.sqrt(sum_back / count + 1e-06)
    padded_both = extended(
        jnp.concatenate([inputs, upstream], axis=0), (("rows", 1), ("cols", 2)), 1, False
    )
    padded_in = padded_both[:batch]
    padded_up = padded_both[batch:]
    outputs = conv(padded_in, kernel, False).astype(jnp.bfloat16)
    input_grad = conv(padded_up, kernel, True).astype(jnp.bfloat16)
    local_grad = lax.conv_general_dilated(
        padded_in,
        upstream,
        window_strides=(1, 1),
        padding="VALID",
        dimension_numbers=("CHWN", "IHWO", "CHWN"),
        preferred_element_type=jnp.float32,
    ).reshape(channels, 9 * channels)
    owned = halving_scatter(local_grad, ("rows", "cols"))
    owned = butterfly_sum(owned, ("rep",))
    total_cells = batch * lax.axis_size("rep") * height * rows_count * breadth * cols_count
    kernel_grad = owned * (1.0 / math.sqrt(total_cells))
    return (outputs, input_grad, kernel_grad, probe_out, lipschitz, norm_trace)


def solution(mesh):
    placed = (
        P("rep", "rows", "cols", None),
        P("rep", "rows", "cols", None),
        P(),
        P("rows", "cols", None),
    )
    return jax.shard_map(
        per_device,
        mesh=mesh,
        in_specs=placed,
        out_specs=(
            P("rep", "rows", "cols", None),
            P("rep", "rows", "cols", None),
            P(("rows", "cols"), None),
            P("rows", "cols", None),
            P(),
            P(),
        ),
        check_vma=False,
    )
```

profile of v0, /device:TPU:0, one launch (start us, length us, event | category | flops | bytes accessed | tf_op | source)
XLA Modules:
  0.0 255.7 jit_solution(9949802938415824358)
XLA Ops:
  2.1 6.2 %collective-permute-start.22 = (bf16[2,32,256]{2,0,1:T(2,128)(2,1)S(1)}, bf16[2,32,256]{2,0,1:T(2,128)(2,1)S(1)}, u32[]{:S(2)}, u32[]{:S(2)}) collective-permute-start(bf16[2,32,256]{2,0,1:T(2,128)(2,1)S(1)} %get-tuple-element.68), channel_id=1, source_target_pairs={{16,0},{32,16},{48,32},{64,48},{80,64},{96,80},{112,96},{0,112},{1... | collective-permute-start | bytes 98312 | tf_op jit(solution)/shard_map/ppermute | solution.py:21
  8.4 2.1 copy.25
  11.4 4.5 %collective-permute-done.21 = bf16[2,32,256]{2,0,1:T(2,128)(2,1)S(1)} collective-permute-done((bf16[2,32,256]{2,0,1:T(2,128)(2,1)S(1)}, bf16[2,32,256]{2,0,1:T(2,128)(2,1)S(1)}, u32[]{:S(2)}, u32[]{:S(2)}) %collective-permute-start.21) | collective-permute-done | bytes 32800 | tf_op jit(solution)/shard_map/ppermute | solution.py:19
  18.4 6.1 %collective-permute-start.10 = (bf16[8,1,32,256]{3,0,2,1:T(8,128)(2,1)S(1)}, bf16[8,1,32,256]{3,0,2,1:T(8,128)(2,1)S(1)}, u32[]{:S(2)}, u32[]{:S(2)}) collective-permute-start(bf16[8,1,32,256]{3,0,2,1:T(8,128)(2,1)S(1)} %get-tuple-element.63), channel_id=1, source_target_pairs={{0,16},{16,32},{32,48},{48,64},{64,80},{80,96},{96,112},{1,17},{17... | collective-permute-start | bytes 393224 | tf_op jit(solution)/shard_map/ppermute | solution.py:19
  25.0 1.6 collective-permute-done.11
  29.2 3.2 %collective-permute-start.12 = (bf16[8,18,1,256]{3,0,2,1:T(8,128)(2,1)S(1)}, bf16[8,18,1,256]{3,0,2,1:T(8,128)(2,1)S(1)}, u32[]{:S(2)}, u32[]{:S(2)}) collective-permute-start(bf16[8,18,1,256]{3,0,2,1:T(8,128)(2,1)S(1)} %get-tuple-element.61), channel_id=1, source_target_pairs={{0,2},{2,4},{4,6},{6,8},{8,10},{10,12},{12,14},{1,3},{3,5},{5,7},{... | collective-permute-start | bytes 221192 | tf_op jit(solution)/shard_map/ppermute | solution.py:19
  32.4 127.7 %while.14 = (s32[]{:T(128)}, bf16[20,36,256]{2,0,1:T(8,128)(2,1)S(1)}, bf16[16,32,256]{2,0,1:T(8,128)(2,1)}, f32[3]{0:T(128)S(1)}, bf16[3,3,256,256]{3,2,1,0:T(8...) while((s32[]{:T(128)}, bf16[20,36,256]{2,0,1:T(8,128)(2,1)S(1)}, ...), condition=%wide.region_2.3_spmd, body=%wide.region_0.2_spmd.sunk | while | flops 1609814016 | bytes 18578212 | solution.py:89
  35.8 3.1 %collective-permute-start = (f32[2,32,256]{2,0,1:T(2,128)S(1)}, f32[2,32,256]{2,0,1:T(2,128)S(1)}, u32[]{:S(2)}, u32[]{:S(2)}) collective-permute-start(f32[2,32,256]{2,0,1:T(2,128)S(1)} %slice_bitcast_fusion.11), channel_id=1, source_target_pairs={{16,0},{32,16},{48,32},{64,48},{80,64},{96,80},{112,96},{0,112},{1... | collective-permute-start | bytes 196616 | tf_op jit(solution)/shard_map/while/body/eval_jaxpr/ppermute | solution.py:21
  41.0 4.4 %collective-permute-start.4 = (f32[]{:T(128)}, f32[]{:T(128)}, u32[]{:S(2)}, u32[]{:S(2)}) collective-permute-start(f32[]{:T(128)} %multiply_reduce_fusion.3), channel_id=1, source_target_pairs={{0,16},{16,0},{32,48},{48,32},{64,80},{80,64},{96,112},{112,96},{1... | collective-permute-start | bytes 20 | tf_op jit(solution)/shard_map/while/body/eval_jaxpr/ppermute | solution.py:33
  45.4 1.6 collective-permute-done.4
  48.3 2.2 collective-permute-start.5
  52.5 2.1 collective-permute-start.6
  54.6 3.0 %collective-permute-done.6 = f32[]{:T(128)} collective-permute-done((f32[]{:T(128)}, f32[]{:T(128)}, u32[]{:S(2)}, u32[]{:S(2)}) %collective-permute-start.6) | collective-permute-done | bytes 36 | tf_op jit(solution)/shard_map/while/body/eval_jaxpr/ppermute | solution.py:33
  60.0 2.9 %collective-permute-start.8 = (f32[]{:T(128)}, f32[]{:T(128)}, u32[]{:S(2)}, u32[]{:S(2)}) collective-permute-start(f32[]{:T(128)} %add.182), channel_id=1, source_target_pairs={{0,4},{2,6},{4,0},{6,2},{8,12},{10,14},{12,8},{14,10},{1,5},{3,7},... | collective-permute-start | bytes 20 | tf_op jit(solution)/shard_map/while/body/eval_jaxpr/ppermute | solution.py:33
  64.2 4.2 %collective-permute-start.9 = (f32[]{:T(128)}, f32[]{:T(128)}, u32[]{:S(2)}, u32[]{:S(2)}) collective-permute-start(f32[]{:T(128)} %add.183), channel_id=1, source_target_pairs={{0,8},{2,10},{4,12},{6,14},{8,0},{10,2},{12,4},{14,6},{1,9},{3,11}... | collective-permute-start | bytes 20 | tf_op jit(solution)/shard_map/while/body/eval_jaxpr/ppermute | solution.py:33
  72.2 3.0 %collective-permute-done.3 = f32[20,2,256]{2,0,1:T(8,128)S(1)} collective-permute-done((f32[20,2,256]{2,0,1:T(8,128)S(1)}, f32[20,2,256]{2,0,1:T(8,128)S(1)}, u32[]{:S(2)}, u32[]{:S(2)}) %collective-permute-start.3) | collective-permute-done | bytes 40992 | tf_op jit(solution)/shard_map/while/body/eval_jaxpr/ppermute | solution.py:19
  78.8 3.9 %collective-permute-start = (f32[2,32,256]{2,0,1:T(2,128)S(1)}, f32[2,32,256]{2,0,1:T(2,128)S(1)}, u32[]{:S(2)}, u32[]{:S(2)}) collective-permute-start(f32[2,32,256]{2,0,1:T(2,128)S(1)} %slice_bitcast_fusion.11), channel_id=1, source_target_pairs={{16,0},{32,16},{48,32},{64,48},{80,64},{96,80},{112,96},{0,112},{1... | collective-permute-start | bytes 196616 | tf_op jit(solution)/shard_map/while/body/eval_jaxpr/ppermute | solution.py:21
  83.8 4.2 %collective-permute-start.4 = (f32[]{:T(128)}, f32[]{:T(128)}, u32[]{:S(2)}, u32[]{:S(2)}) collective-permute-start(f32[]{:T(128)} %multiply_reduce_fusion.3), channel_id=1, source_target_pairs={{0,16},{16,0},{32,48},{48,32},{64,80},{80,64},{96,112},{112,96},{1... | collective-permute-start | bytes 20 | tf_op jit(solution)/shard_map/while/body/eval_jaxpr/ppermute | solution.py:33
  90.8 2.0 collective-permute-start.5
  95.0 2.8 %collective-permute-start.6 = (f32[]{:T(128)}, f32[]{:T(128)}, u32[]{:S(2)}, u32[]{:S(2)}) collective-permute-start(f32[]{:T(128)} %add.180), channel_id=1, source_target_pairs={{0,64},{16,80},{32,96},{48,112},{64,0},{80,16},{96,32},{112,48},{1... | collective-permute-start | bytes 20 | tf_op jit(solution)/shard_map/while/body/eval_jaxpr/ppermute | solution.py:33
  97.9 2.2 collective-permute-done.6
  103.9 2.2 collective-permute-done.8
  106.7 2.6 %collective-permute-start.9 = (f32[]{:T(128)}, f32[]{:T(128)}, u32[]{:S(2)}, u32[]{:S(2)}) collective-permute-start(f32[]{:T(128)} %add.183), channel_id=1, source_target_pairs={{0,8},{2,10},{4,12},{6,14},{8,0},{10,2},{12,4},{14,6},{1,9},{3,11}... | collective-permute-start | bytes 20 | tf_op jit(solution)/shard_map/while/body/eval_jaxpr/ppermute | solution.py:33
  109.3 2.5 collective-permute-done.9
  114.3 3.0 %collective-permute-done.3 = f32[20,2,256]{2,0,1:T(8,128)S(1)} collective-permute-done((f32[20,2,256]{2,0,1:T(8,128)S(1)}, f32[20,2,256]{2,0,1:T(8,128)S(1)}, u32[]{:S(2)}, u32[]{:S(2)}) %collective-permute-start.3) | collective-permute-done | bytes 40992 | tf_op jit(solution)/shard_map/while/body/eval_jaxpr/ppermute | solution.py:19
  120.9 5.1 %collective-permute-start = (f32[2,32,256]{2,0,1:T(2,128)S(1)}, f32[2,32,256]{2,0,1:T(2,128)S(1)}, u32[]{:S(2)}, u32[]{:S(2)}) collective-permute-start(f32[2,32,256]{2,0,1:T(2,128)S(1)} %slice_bitcast_fusion.11), channel_id=1, source_target_pairs={{16,0},{32,16},{48,32},{64,48},{80,64},{96,80},{112,96},{0,112},{1... | collective-permute-start | bytes 196616 | tf_op jit(solution)/shard_map/while/body/eval_jaxpr/ppermute | solution.py:21
  127.0 2.9 %collective-permute-start.4 = (f32[]{:T(128)}, f32[]{:T(128)}, u32[]{:S(2)}, u32[]{:S(2)}) collective-permute-start(f32[]{:T(128)} %multiply_reduce_fusion.3), channel_id=1, source_target_pairs={{0,16},{16,0},{32,48},{48,32},{64,80},{80,64},{96,112},{112,96},{1... | collective-permute-start | bytes 20 | tf_op jit(solution)/shard_map/while/body/eval_jaxpr/ppermute | solution.py:33
  130.0 2.1 collective-permute-done.4
  134.9 2.1 collective-permute-done.5
  137.7 3.5 %collective-permute-start.6 = (f32[]{:T(128)}, f32[]{:T(128)}, u32[]{:S(2)}, u32[]{:S(2)}) collective-permute-start(f32[]{:T(128)} %add.180), channel_id=1, source_target_pairs={{0,64},{16,80},{32,96},{48,112},{64,0},{80,16},{96,32},{112,48},{1... | collective-permute-start | bytes 20 | tf_op jit(solution)/shard_map/while/body/eval_jaxpr/ppermute | solution.py:33
  146.5 2.2 collective-permute-done.8
  150.8 3.6 %collective-permute-done.9 = f32[]{:T(128)} collective-permute-done((f32[]{:T(128)}, f32[]{:T(128)}, u32[]{:S(2)}, u32[]{:S(2)}) %collective-permute-start.9) | collective-permute-done | bytes 36 | tf_op jit(solution)/shard_map/while/body/eval_jaxpr/ppermute | solution.py:33
  156.9 3.0 %collective-permute-done.3 = f32[20,2,256]{2,0,1:T(8,128)S(1)} collective-permute-done((f32[20,2,256]{2,0,1:T(8,128)S(1)}, f32[20,2,256]{2,0,1:T(8,128)S(1)}, u32[]{:S(2)}, u32[]{:S(2)}) %collective-permute-start.3) | collective-permute-done | bytes 40992 | tf_op jit(solution)/shard_map/while/body/eval_jaxpr/ppermute | solution.py:19
  161.0 1.6 slice.95
  163.9 5.6 %fusion.54 = f32[256,3,3,256]{0,3,2,1:T(8,128)S(1)} fusion(bf16[8,18,34,256]{3,0,2,1:T(8,128)(2,1)S(1)} %pad_maximum_fusion.3, bf16[4,16,32,256]{3,2,1,0:T(8,128)(2,1)S(1)} %copy-done.7), kind=kOutput, calls=%fused_computation.68 | convolution fusion | flops 2415919104 | bytes 4661248 | tf_op jit(solution)/shard_map/conv_general_dilated | solution.py:110
  171.1 2.1 collective-permute-start.14
  173.2 2.5 fusion.49
  176.5 2.4 select_reduce_fusion
  180.3 3.6 %collective-permute-start.25 = (f32[2]{0:T(128)S(1)}, f32[2]{0:T(128)S(1)}, u32[]{:S(2)}, u32[]{:S(2)}) collective-permute-start(f32[2]{0:T(128)S(1)} %pad_maximum_fusion.14), channel_id=1, source_target_pairs={{0,16},{16,0},{32,48},{48,32},{64,80},{80,64},{96,112},{112,96},{1... | collective-permute-start | bytes 32 | tf_op jit(solution)/shard_map/ppermute | solution.py:33
  188.2 9.7 %collective-permute-done.26 = f32[2]{0:T(128)S(1)} collective-permute-done((f32[2]{0:T(128)S(1)}, f32[2]{0:T(128)S(1)}, u32[]{:S(2)}, u32[]{:S(2)}) %collective-permute-start.26) | collective-permute-done | bytes 40 | tf_op jit(solution)/shard_map/ppermute | solution.py:33
  200.1 4.2 %collective-permute-done.27 = f32[2]{0:T(128)S(1)} collective-permute-done((f32[2]{0:T(128)S(1)}, f32[2]{0:T(128)S(1)}, u32[]{:S(2)}, u32[]{:S(2)}) %collective-permute-start.27) | collective-permute-done | bytes 40 | tf_op jit(solution)/shard_map/ppermute | solution.py:33
  205.5 3.4 %collective-permute-done.29 = f32[2]{0:T(128)S(1)} collective-permute-done((f32[2]{0:T(128)S(1)}, f32[2]{0:T(128)S(1)}, u32[]{:S(2)}, u32[]{:S(2)}) %collective-permute-start.29) | collective-permute-done | bytes 40 | tf_op jit(solution)/shard_map/ppermute | solution.py:33
  210.2 3.8 %collective-permute-done.30 = f32[2]{0:T(128)S(1)} collective-permute-done((f32[2]{0:T(128)S(1)}, f32[2]{0:T(128)S(1)}, u32[]{:S(2)}, u32[]{:S(2)}) %collective-permute-start.30) | collective-permute-done | bytes 40 | tf_op jit(solution)/shard_map/ppermute | solution.py:33
  219.4 8.4 %collective-permute-done.15 = f32[64,2304]{1,0:T(8,128)S(1)} collective-permute-done((f32[64,2304]{1,0:T(8,128)S(1)}, f32[64,2304]{1,0:T(8,128)S(1)}, u32[]{:S(2)}, u32[]{:S(2)}) %collective-permute-start.15) | collective-permute-done | bytes 589856 | tf_op jit(solution)/shard_map/ppermute | solution.py:48
  227.9 3.6 %collective-permute-start.16 = (f32[32,2304]{1,0:T(8,128)S(1)}, f32[32,2304]{1,0:T(8,128)S(1)}, u32[]{:S(2)}, u32[]{:S(2)}) collective-permute-start(f32[32,2304]{1,0:T(8,128)S(1)} %constant_dynamic-slice_fusion.3), channel_id=1, source_target_pairs={{0,16},{16,0},{32,48},{48,32},{64,80},{80,64},{96,112},{112,96},{1... | collective-permute-start | bytes 884744 | tf_op jit(solution)/shard_map/ppermute | solution.py:48
  233.5 2.7 %collective-permute-done.16 = f32[32,2304]{1,0:T(8,128)S(1)} collective-permute-done((f32[32,2304]{1,0:T(8,128)S(1)}, f32[32,2304]{1,0:T(8,128)S(1)}, u32[]{:S(2)}, u32[]{:S(2)}) %collective-permute-start.16) | collective-permute-done | bytes 294944 | tf_op jit(solution)/shard_map/ppermute | solution.py:48
  237.9 3.5 %select_convert_fusion.1 = bf16[16,32,5,256]{3,1,2,0:T(8,128)(2,1)S(1)} fusion(bf16[3,3,256,256]{3,2,1,0:T(8,128)(2,1)S(1)} %copy-done.11, bf16[18,4,7,2,256]{4,2,1,3,0:T(8,128)(2,1)S(1)} %slice.88, bf16[18,4,8,5,256]{4,2,1,3,0:T(8,128)(2,1)S(1)} %copy.27, pred[32,5]{0,1:T(8,128)(4,1)S(1)} %copy-done.13), kind=kOutput, calls=%fused_computation.41 | convolution fusion | flops 3027402752 | bytes 4481184 | tf_op jit(solution)/shard_map/conv_general_dilated | solution.py:56
  244.4 3.4 %select_convert_fusion = bf16[16,32,5,256]{3,1,2,0:T(8,128)(2,1)S(1)} fusion(bf16[3,3,256,256]{3,2,1,0:T(8,128)(2,1)S(1)} %copy-done.11, bf16[18,4,7,2,256]{4,2,1,3,0:T(8,128)(2,1)S(1)} %slice.91, bf16[18,4,8,5,256]{4,2,1,3,0:T(8,128)(2,1)S(1)} %copy.30, pred[32,5]{0,1:T(8,128)(4,1)S(1)} %copy-done.13), kind=kOutput, calls=%fused_computation.40 | convolution fusion | flops 3027402752 | bytes 4481184 | tf_op jit(solution)/shard_map/conv_general_dilated | solution.py:56
  (207 shorter events, 76.7 us)
Async XLA Ops:
  2.1 9.3 %collective-permute-start.22 = (bf16[2,32,256]{2,0,1:T(2,128)(2,1)S(1)}, bf16[2,32,256]{2,0,1:T(2,128)(2,1)S(1)}, u32[]{:S(2)}, u32[]{:S(2)}) collective-permute-start(bf16[2,32,256]{2,0,1:T(2,128)(2,1)S(1)} %get-tuple-element.68), channel_id=1, source_target_pairs={{16,0},{32,16},{48,32},{64,48},{80,64},{96,80},{112,96},{0,112},{1... | collective-permute-start | bytes 98312 | tf_op jit(solution)/shard_map/ppermute | solution.py:21
  8.4 7.5 %collective-permute-start.21 = (bf16[2,32,256]{2,0,1:T(2,128)(2,1)S(1)}, bf16[2,32,256]{2,0,1:T(2,128)(2,1)S(1)}, u32[]{:S(2)}, u32[]{:S(2)}) collective-permute-start(bf16[2,32,256]{2,0,1:T(2,128)(2,1)S(1)} %get-tuple-element.67), channel_id=1, source_target_pairs={{0,16},{16,32},{32,48},{48,64},{64,80},{80,96},{96,112},{112,0},{1... | collective-permute-start | bytes 98312 | tf_op jit(solution)/shard_map/ppermute | solution.py:19
  15.9 8.8 %collective-permute-start.24 = (bf16[20,2,256]{2,0,1:T(8,128)(2,1)S(1)}, bf16[20,2,256]{2,0,1:T(8,128)(2,1)S(1)}, u32[]{:S(2)}, u32[]{:S(2)}) collective-permute-start(bf16[20,2,256]{2,0,1:T(8,128)(2,1)S(1)} %get-tuple-element.66), channel_id=1, source_target_pairs={{2,0},{4,2},{6,4},{8,6},{10,8},{12,10},{14,12},{0,14},{3,1},{5,3},... | collective-permute-start | bytes 61448 | tf_op jit(solution)/shard_map/ppermute | solution.py:21
  16.9 7.8 %collective-permute-start.23 = (bf16[20,2,256]{2,0,1:T(8,128)(2,1)S(1)}, bf16[20,2,256]{2,0,1:T(8,128)(2,1)S(1)}, u32[]{:S(2)}, u32[]{:S(2)}) collective-permute-start(bf16[20,2,256]{2,0,1:T(8,128)(2,1)S(1)} %get-tuple-element.65), channel_id=1, source_target_pairs={{0,2},{2,4},{4,6},{6,8},{8,10},{10,12},{12,14},{14,0},{1,3},{3,5},... | collective-permute-start | bytes 61448 | tf_op jit(solution)/shard_map/ppermute | solution.py:19
  17.1 9.5 %collective-permute-start.11 = (bf16[8,1,32,256]{3,0,2,1:T(8,128)(2,1)S(1)}, bf16[8,1,32,256]{3,0,2,1:T(8,128)(2,1)S(1)}, u32[]{:S(2)}, u32[]{:S(2)}) collective-permute-start(bf16[8,1,32,256]{3,0,2,1:T(8,128)(2,1)S(1)} %get-tuple-element.64), channel_id=1, source_target_pairs={{16,0},{32,16},{48,32},{64,48},{80,64},{96,80},{112,96},{17,1},{33... | collective-permute-start | bytes 393224 | tf_op jit(solution)/shard_map/ppermute | solution.py:21
  18.4 9.4 %collective-permute-start.10 = (bf16[8,1,32,256]{3,0,2,1:T(8,128)(2,1)S(1)}, bf16[8,1,32,256]{3,0,2,1:T(8,128)(2,1)S(1)}, u32[]{:S(2)}, u32[]{:S(2)}) collective-permute-start(bf16[8,1,32,256]{3,0,2,1:T(8,128)(2,1)S(1)} %get-tuple-element.63), channel_id=1, source_target_pairs={{0,16},{16,32},{32,48},{48,64},{64,80},{80,96},{96,112},{1,17},{17... | collective-permute-start | bytes 393224 | tf_op jit(solution)/shard_map/ppermute | solution.py:19
  27.9 134.8 %collective-permute-start.13 = (bf16[8,18,1,256]{3,0,2,1:T(8,128)(2,1)S(1)}, bf16[8,18,1,256]{3,0,2,1:T(8,128)(2,1)S(1)}, u32[]{:S(2)}, u32[]{:S(2)}) collective-permute-start(bf16[8,18,1,256]{3,0,2,1:T(8,128)(2,1)S(1)} %get-tuple-element.62), channel_id=1, source_target_pairs={{2,0},{4,2},{6,4},{8,6},{10,8},{12,10},{14,12},{3,1},{5,3},{7,5},{... | collective-permute-start | bytes 221192 | tf_op jit(solution)/shard_map/ppermute | solution.py:21
  29.2 133.5 %collective-permute-start.12 = (bf16[8,18,1,256]{3,0,2,1:T(8,128)(2,1)S(1)}, bf16[8,18,1,256]{3,0,2,1:T(8,128)(2,1)S(1)}, u32[]{:S(2)}, u32[]{:S(2)}) collective-permute-start(bf16[8,18,1,256]{3,0,2,1:T(8,128)(2,1)S(1)} %get-tuple-element.61), channel_id=1, source_target_pairs={{0,2},{2,4},{4,6},{6,8},{8,10},{10,12},{12,14},{1,3},{3,5},{5,7},{... | collective-permute-start | bytes 221192 | tf_op jit(solution)/shard_map/ppermute | solution.py:19
  35.8 34.1 %collective-permute-start = (f32[2,32,256]{2,0,1:T(2,128)S(1)}, f32[2,32,256]{2,0,1:T(2,128)S(1)}, u32[]{:S(2)}, u32[]{:S(2)}) collective-permute-start(f32[2,32,256]{2,0,1:T(2,128)S(1)} %slice_bitcast_fusion.11), channel_id=1, source_target_pairs={{16,0},{32,16},{48,32},{64,48},{80,64},{96,80},{112,96},{0,112},{1... | collective-permute-start | bytes 196616 | tf_op jit(solution)/shard_map/while/body/eval_jaxpr/ppermute | solution.py:21
  39.0 31.0 %collective-permute-start.1 = (f32[2,32,256]{2,0,1:T(2,128)S(1)}, f32[2,32,256]{2,0,1:T(2,128)S(1)}, u32[]{:S(2)}, u32[]{:S(2)}) collective-permute-start(f32[2,32,256]{2,0,1:T(2,128)S(1)} %slice_bitcast_fusion.13), channel_id=1, source_target_pairs={{0,16},{16,32},{32,48},{48,64},{64,80},{80,96},{96,112},{112,0},{1... | collective-permute-start | bytes 196616 | tf_op jit(solution)/shard_map/while/body/eval_jaxpr/ppermute | solution.py:19
  41.0 6.1 %collective-permute-start.4 = (f32[]{:T(128)}, f32[]{:T(128)}, u32[]{:S(2)}, u32[]{:S(2)}) collective-permute-start(f32[]{:T(128)} %multiply_reduce_fusion.3), channel_id=1, source_target_pairs={{0,16},{16,0},{32,48},{48,32},{64,80},{80,64},{96,112},{112,96},{1... | collective-permute-start | bytes 20 | tf_op jit(solution)/shard_map/while/body/eval_jaxpr/ppermute | solution.py:33
  48.3 3.6 %collective-permute-start.5 = (f32[]{:T(128)}, f32[]{:T(128)}, u32[]{:S(2)}, u32[]{:S(2)}) collective-permute-start(f32[]{:T(128)} %add.179), channel_id=1, source_target_pairs={{0,32},{16,48},{32,0},{48,16},{64,96},{80,112},{96,64},{112,80},{1... | collective-permute-start | bytes 20 | tf_op jit(solution)/shard_map/while/body/eval_jaxpr/ppermute | solution.py:33
  52.5 5.1 %collective-permute-start.6 = (f32[]{:T(128)}, f32[]{:T(128)}, u32[]{:S(2)}, u32[]{:S(2)}) collective-permute-start(f32[]{:T(128)} %add.180), channel_id=1, source_target_pairs={{0,64},{16,80},{32,96},{48,112},{64,0},{80,16},{96,32},{112,48},{1... | collective-permute-start | bytes 20 | tf_op jit(solution)/shard_map/while/body/eval_jaxpr/ppermute | solution.py:33
  60.0 3.6 %collective-permute-start.8 = (f32[]{:T(128)}, f32[]{:T(128)}, u32[]{:S(2)}, u32[]{:S(2)}) collective-permute-start(f32[]{:T(128)} %add.182), channel_id=1, source_target_pairs={{0,4},{2,6},{4,0},{6,2},{8,12},{10,14},{12,8},{14,10},{1,5},{3,7},... | collective-permute-start | bytes 20 | tf_op jit(solution)/shard_map/while/body/eval_jaxpr/ppermute | solution.py:33
  64.2 5.1 %collective-permute-start.9 = (f32[]{:T(128)}, f32[]{:T(128)}, u32[]{:S(2)}, u32[]{:S(2)}) collective-permute-start(f32[]{:T(128)} %add.183), channel_id=1, source_target_pairs={{0,8},{2,10},{4,12},{6,14},{8,0},{10,2},{12,4},{14,6},{1,9},{3,11}... | collective-permute-start | bytes 20 | tf_op jit(solution)/shard_map/while/body/eval_jaxpr/ppermute | solution.py:33
  70.0 2.2 collective-permute-start.2
  70.5 4.7 %collective-permute-start.3 = (f32[20,2,256]{2,0,1:T(8,128)S(1)}, f32[20,2,256]{2,0,1:T(8,128)S(1)}, u32[]{:S(2)}, u32[]{:S(2)}) collective-permute-start(f32[20,2,256]{2,0,1:T(8,128)S(1)} %get-tuple-element.109), channel_id=1, source_target_pairs={{0,2},{2,4},{4,6},{6,8},{8,10},{10,12},{12,14},{14,0},{1,3},{3,5},... | collective-permute-start | bytes 122888 | tf_op jit(solution)/shard_map/while/body/eval_jaxpr/ppermute | solution.py:19
  78.8 33.7 %collective-permute-start = (f32[2,32,256]{2,0,1:T(2,128)S(1)}, f32[2,32,256]{2,0,1:T(2,128)S(1)}, u32[]{:S(2)}, u32[]{:S(2)}) collective-permute-start(f32[2,32,256]{2,0,1:T(2,128)S(1)} %slice_bitcast_fusion.11), channel_id=1, source_target_pairs={{16,0},{32,16},{48,32},{64,48},{80,64},{96,80},{112,96},{0,112},{1... | collective-permute-start | bytes 196616 | tf_op jit(solution)/shard_map/while/body/eval_jaxpr/ppermute | solution.py:21
  82.7 29.7 %collective-permute-start.1 = (f32[2,32,256]{2,0,1:T(2,128)S(1)}, f32[2,32,256]{2,0,1:T(2,128)S(1)}, u32[]{:S(2)}, u32[]{:S(2)}) collective-permute-start(f32[2,32,256]{2,0,1:T(2,128)S(1)} %slice_bitcast_fusion.13), channel_id=1, source_target_pairs={{0,16},{16,32},{32,48},{48,64},{64,80},{80,96},{96,112},{112,0},{1... | collective-permute-start | bytes 196616 | tf_op jit(solution)/shard_map/while/body/eval_jaxpr/ppermute | solution.py:19
  83.8 5.8 %collective-permute-start.4 = (f32[]{:T(128)}, f32[]{:T(128)}, u32[]{:S(2)}, u32[]{:S(2)}) collective-permute-start(f32[]{:T(128)} %multiply_reduce_fusion.3), channel_id=1, source_target_pairs={{0,16},{16,0},{32,48},{48,32},{64,80},{80,64},{96,112},{112,96},{1... | collective-permute-start | bytes 20 | tf_op jit(solution)/shard_map/while/body/eval_jaxpr/ppermute | solution.py:33
  90.8 3.6 %collective-permute-start.5 = (f32[]{:T(128)}, f32[]{:T(128)}, u32[]{:S(2)}, u32[]{:S(2)}) collective-permute-start(f32[]{:T(128)} %add.179), channel_id=1, source_target_pairs={{0,32},{16,48},{32,0},{48,16},{64,96},{80,112},{96,64},{112,80},{1... | collective-permute-start | bytes 20 | tf_op jit(solution)/shard_map/while/body/eval_jaxpr/ppermute | solution.py:33
  95.0 5.1 %collective-permute-start.6 = (f32[]{:T(128)}, f32[]{:T(128)}, u32[]{:S(2)}, u32[]{:S(2)}) collective-permute-start(f32[]{:T(128)} %add.180), channel_id=1, source_target_pairs={{0,64},{16,80},{32,96},{48,112},{64,0},{80,16},{96,32},{112,48},{1... | collective-permute-start | bytes 20 | tf_op jit(solution)/shard_map/while/body/eval_jaxpr/ppermute | solution.py:33
  100.7 1.2 collective-permute-start.7
  102.5 3.6 %collective-permute-start.8 = (f32[]{:T(128)}, f32[]{:T(128)}, u32[]{:S(2)}, u32[]{:S(2)}) collective-permute-start(f32[]{:T(128)} %add.182), channel_id=1, source_target_pairs={{0,4},{2,6},{4,0},{6,2},{8,12},{10,14},{12,8},{14,10},{1,5},{3,7},... | collective-permute-start | bytes 20 | tf_op jit(solution)/shard_map/while/body/eval_jaxpr/ppermute | solution.py:33
  106.7 5.1 %collective-permute-start.9 = (f32[]{:T(128)}, f32[]{:T(128)}, u32[]{:S(2)}, u32[]{:S(2)}) collective-permute-start(f32[]{:T(128)} %add.183), channel_id=1, source_target_pairs={{0,8},{2,10},{4,12},{6,14},{8,0},{10,2},{12,4},{14,6},{1,9},{3,11}... | collective-permute-start | bytes 20 | tf_op jit(solution)/shard_map/while/body/eval_jaxpr/ppermute | solution.py:33
  112.5 1.8 collective-permute-start.2
  112.5 4.7 %collective-permute-start.3 = (f32[20,2,256]{2,0,1:T(8,128)S(1)}, f32[20,2,256]{2,0,1:T(8,128)S(1)}, u32[]{:S(2)}, u32[]{:S(2)}) collective-permute-start(f32[20,2,256]{2,0,1:T(8,128)S(1)} %get-tuple-element.109), channel_id=1, source_target_pairs={{0,2},{2,4},{4,6},{6,8},{8,10},{10,12},{12,14},{14,0},{1,3},{3,5},... | collective-permute-start | bytes 122888 | tf_op jit(solution)/shard_map/while/body/eval_jaxpr/ppermute | solution.py:19
  120.9 34.2 %collective-permute-start = (f32[2,32,256]{2,0,1:T(2,128)S(1)}, f32[2,32,256]{2,0,1:T(2,128)S(1)}, u32[]{:S(2)}, u32[]{:S(2)}) collective-permute-start(f32[2,32,256]{2,0,1:T(2,128)S(1)} %slice_bitcast_fusion.11), channel_id=1, source_target_pairs={{16,0},{32,16},{48,32},{64,48},{80,64},{96,80},{112,96},{0,112},{1... | collective-permute-start | bytes 196616 | tf_op jit(solution)/shard_map/while/body/eval_jaxpr/ppermute | solution.py:21
  126.0 29.1 %collective-permute-start.1 = (f32[2,32,256]{2,0,1:T(2,128)S(1)}, f32[2,32,256]{2,0,1:T(2,128)S(1)}, u32[]{:S(2)}, u32[]{:S(2)}) collective-permute-start(f32[2,32,256]{2,0,1:T(2,128)S(1)} %slice_bitcast_fusion.13), channel_id=1, source_target_pairs={{0,16},{16,32},{32,48},{48,64},{64,80},{80,96},{96,112},{112,0},{1... | collective-permute-start | bytes 196616 | tf_op jit(solution)/shard_map/while/body/eval_jaxpr/ppermute | solution.py:19
  127.0 5.1 %collective-permute-start.4 = (f32[]{:T(128)}, f32[]{:T(128)}, u32[]{:S(2)}, u32[]{:S(2)}) collective-permute-start(f32[]{:T(128)} %multiply_reduce_fusion.3), channel_id=1, source_target_pairs={{0,16},{16,0},{32,48},{48,32},{64,80},{80,64},{96,112},{112,96},{1... | collective-permute-start | bytes 20 | tf_op jit(solution)/shard_map/while/body/eval_jaxpr/ppermute | solution.py:33
  133.5 3.6 %collective-permute-start.5 = (f32[]{:T(128)}, f32[]{:T(128)}, u32[]{:S(2)}, u32[]{:S(2)}) collective-permute-start(f32[]{:T(128)} %add.179), channel_id=1, source_target_pairs={{0,32},{16,48},{32,0},{48,16},{64,96},{80,112},{96,64},{112,80},{1... | collective-permute-start | bytes 20 | tf_op jit(solution)/shard_map/while/body/eval_jaxpr/ppermute | solution.py:33
  137.7 5.1 %collective-permute-start.6 = (f32[]{:T(128)}, f32[]{:T(128)}, u32[]{:S(2)}, u32[]{:S(2)}) collective-permute-start(f32[]{:T(128)} %add.180), channel_id=1, source_target_pairs={{0,64},{16,80},{32,96},{48,112},{64,0},{80,16},{96,32},{112,48},{1... | collective-permute-start | bytes 20 | tf_op jit(solution)/shard_map/while/body/eval_jaxpr/ppermute | solution.py:33
  145.2 3.6 %collective-permute-start.8 = (f32[]{:T(128)}, f32[]{:T(128)}, u32[]{:S(2)}, u32[]{:S(2)}) collective-permute-start(f32[]{:T(128)} %add.182), channel_id=1, source_target_pairs={{0,4},{2,6},{4,0},{6,2},{8,12},{10,14},{12,8},{14,10},{1,5},{3,7},... | collective-permute-start | bytes 20 | tf_op jit(solution)/shard_map/while/body/eval_jaxpr/ppermute | solution.py:33
  149.4 5.1 %collective-permute-start.9 = (f32[]{:T(128)}, f32[]{:T(128)}, u32[]{:S(2)}, u32[]{:S(2)}) collective-permute-start(f32[]{:T(128)} %add.183), channel_id=1, source_target_pairs={{0,8},{2,10},{4,12},{6,14},{8,0},{10,2},{12,4},{14,6},{1,9},{3,11}... | collective-permute-start | bytes 20 | tf_op jit(solution)/shard_map/while/body/eval_jaxpr/ppermute | solution.py:33
  155.2 1.8 collective-permute-start.2
  155.2 4.7 %collective-permute-start.3 = (f32[20,2,256]{2,0,1:T(8,128)S(1)}, f32[20,2,256]{2,0,1:T(8,128)S(1)}, u32[]{:S(2)}, u32[]{:S(2)}) collective-permute-start(f32[20,2,256]{2,0,1:T(8,128)S(1)} %get-tuple-element.109), channel_id=1, source_target_pairs={{0,2},{2,4},{4,6},{6,8},{8,10},{10,12},{12,14},{14,0},{1,3},{3,5},... | collective-permute-start | bytes 122888 | tf_op jit(solution)/shard_map/while/body/eval_jaxpr/ppermute | solution.py:19
  171.1 43.2 %collective-permute-start.14 = (f32[128,2304]{1,0:T(8,128)}, f32[128,2304]{1,0:T(8,128)S(1)}, u32[]{:S(2)}, u32[]{:S(2)}) collective-permute-start(f32[128,2304]{1,0:T(8,128)} %copy.43), channel_id=1, source_target_pairs={{0,64},{16,80},{32,96},{48,112},{64,0},{80,16},{96,32},{112,48},{1... | collective-permute-start | bytes 3538952 | tf_op jit(solution)/shard_map/ppermute | solution.py:48
  180.3 5.1 %collective-permute-start.25 = (f32[2]{0:T(128)S(1)}, f32[2]{0:T(128)S(1)}, u32[]{:S(2)}, u32[]{:S(2)}) collective-permute-start(f32[2]{0:T(128)S(1)} %pad_maximum_fusion.14), channel_id=1, source_target_pairs={{0,16},{16,0},{32,48},{48,32},{64,80},{80,64},{96,112},{112,96},{1... | collective-permute-start | bytes 32 | tf_op jit(solution)/shard_map/ppermute | solution.py:33
  186.7 11.1 %collective-permute-start.26 = (f32[2]{0:T(128)S(1)}, f32[2]{0:T(128)S(1)}, u32[]{:S(2)}, u32[]{:S(2)}) collective-permute-start(f32[2]{0:T(128)S(1)} %fusion.93), channel_id=1, source_target_pairs={{0,32},{16,48},{32,0},{48,16},{64,96},{80,112},{96,64},{112,80},{1... | collective-permute-start | bytes 32 | tf_op jit(solution)/shard_map/ppermute | solution.py:33
  199.2 5.1 %collective-permute-start.27 = (f32[2]{0:T(128)S(1)}, f32[2]{0:T(128)S(1)}, u32[]{:S(2)}, u32[]{:S(2)}) collective-permute-start(f32[2]{0:T(128)S(1)} %fusion.94), channel_id=1, source_target_pairs={{0,64},{16,80},{32,96},{48,112},{64,0},{80,16},{96,32},{112,48},{1... | collective-permute-start | bytes 32 | tf_op jit(solution)/shard_map/ppermute | solution.py:33
  205.4 3.5 %collective-permute-start.29 = (f32[2]{0:T(128)S(1)}, f32[2]{0:T(128)S(1)}, u32[]{:S(2)}, u32[]{:S(2)}) collective-permute-start(f32[2]{0:T(128)S(1)} %add.156), channel_id=1, source_target_pairs={{0,4},{2,6},{4,0},{6,2},{8,12},{10,14},{12,8},{14,10},{1,5},{3,7},... | collective-permute-start | bytes 32 | tf_op jit(solution)/shard_map/ppermute | solution.py:33
  208.9 5.0 %collective-permute-start.30 = (f32[2]{0:T(128)S(1)}, f32[2]{0:T(128)S(1)}, u32[]{:S(2)}, u32[]{:S(2)}) collective-permute-start(f32[2]{0:T(128)S(1)} %add.157), channel_id=1, source_target_pairs={{0,8},{2,10},{4,12},{6,14},{8,0},{10,2},{12,4},{14,6},{1,9},{3,11}... | collective-permute-start | bytes 32 | tf_op jit(solution)/shard_map/ppermute | solution.py:33
  214.6 13.2 %collective-permute-start.15 = (f32[64,2304]{1,0:T(8,128)S(1)}, f32[64,2304]{1,0:T(8,128)S(1)}, u32[]{:S(2)}, u32[]{:S(2)}) collective-permute-start(f32[64,2304]{1,0:T(8,128)S(1)} %constant_dynamic-slice_fusion.4), channel_id=1, source_target_pairs={{0,32},{16,48},{32,0},{48,16},{64,96},{80,112},{96,64},{112,80},{1... | collective-permute-start | bytes 1769480 | tf_op jit(solution)/shard_map/ppermute | solution.py:48
  227.9 8.3 %collective-permute-start.16 = (f32[32,2304]{1,0:T(8,128)S(1)}, f32[32,2304]{1,0:T(8,128)S(1)}, u32[]{:S(2)}, u32[]{:S(2)}) collective-permute-start(f32[32,2304]{1,0:T(8,128)S(1)} %constant_dynamic-slice_fusion.3), channel_id=1, source_target_pairs={{0,16},{16,0},{32,48},{48,32},{64,80},{80,64},{96,112},{112,96},{1... | collective-permute-start | bytes 884744 | tf_op jit(solution)/shard_map/ppermute | solution.py:48
  236.3 7.8 %collective-permute-start.17 = (f32[16,2304]{1,0:T(8,128)S(1)}, f32[16,2304]{1,0:T(8,128)S(1)}, u32[]{:S(2)}, u32[]{:S(2)}) collective-permute-start(f32[16,2304]{1,0:T(8,128)S(1)} %constant_dynamic-slice_fusion.2), channel_id=1, source_target_pairs={{0,8},{2,10},{4,12},{6,14},{8,0},{10,2},{12,4},{14,6},{1,9},{3,11}... | collective-permute-start | bytes 442376 | tf_op jit(solution)/shard_map/ppermute | solution.py:48
  244.1 4.5 %collective-permute-start.18 = (f32[8,2304]{1,0:T(8,128)S(1)}, f32[8,2304]{1,0:T(8,128)S(1)}, u32[]{:S(2)}, u32[]{:S(2)}) collective-permute-start(f32[8,2304]{1,0:T(8,128)S(1)} %constant_dynamic-slice_fusion.1), channel_id=1, source_target_pairs={{0,4},{2,6},{4,0},{6,2},{8,12},{10,14},{12,8},{14,10},{1,5},{3,7},... | collective-permute-start | bytes 221192 | tf_op jit(solution)/shard_map/ppermute | solution.py:48
  248.6 1.3 collective-permute-start.19
  249.9 4.0 %collective-permute-start.20 = (f32[4,2304]{1,0:T(4,128)S(1)}, f32[4,2304]{1,0:T(4,128)S(1)}, u32[]{:S(2)}, u32[]{:S(2)}) collective-permute-start(f32[4,2304]{1,0:T(4,128)S(1)} %dynamic-slice_add_fusion.4), channel_id=1, source_target_pairs={{0,1},{1,0},{2,3},{3,2},{4,5},{5,4},{6,7},{7,6},{8,9},{9,8},{10,11... | collective-permute-start | bytes 110600 | tf_op jit(solution)/shard_map/ppermute | solution.py:33
  (22 other events, 121.8 us)
where the time goes:
time: 257 us; the launch traced here: 256 us
  starting transfers between devices  92.8 us (36%)
  waiting for transfers between devices  84.8 us (33%)
  local copies, waits for them, and re-layouts  23.7 us (9%)
  matrix products  23.5 us (9%)
  loops' own time  13.9 us (5%)
  other arithmetic  12.4 us (5%)
  between operations  4.65 us (2%)
    ppermute x25, waiting for transfers between devices, butterfly_sum(): lax.ppermute(value, axis, [(i, i ^ step) for i in range(count)])  53.9 us
    ppermute x25, starting transfers between devices, butterfly_sum(): lax.ppermute(value, axis, [(i, i ^ step) for i in range(count)])  50.6 us
    ppermute x10, starting transfers between devices, extended(): lax.ppermute(head, axis, [((i + 1) % count, i) for i in range(ends)])  22.4 us
    conv_general_dilated x10, matrix products, conv(): lax.conv_general_dilated(padded, weights, window_strides=(1, 1), padding=...  17.8 us
    ppermute x10, waiting for transfers between devices, extended(): lax.ppermute(tail, axis, [(i, (i + 1) % count) for i in range(ends)])  14.7 us
    another operation x1, loops' own time, per_device(): lax.scan(power_step, (padded_probe, iterate), None, length=ITERS - 1)  13.9 us
    ppermute x6, waiting for transfers between devices, halving_scatter(): lax.ppermute(send, axis, [(i, i ^ step) for i in range(count)])  12.9 us
    ppermute x10, starting transfers between devices, extended(): lax.ppermute(tail, axis, [(i, (i + 1) % count) for i in range(ends)])  11.5 us
  transfers between devices with their start and end apart: 51, of which 38 were waited for; matrix products, arithmetic and copies ran while one was open for 18% of the time, Pallas kernels for 0%

commit v1 on v0

--- a/solution.py
+++ b/solution.py
@@ -35,18 +35,25 @@
     return value
 
 
-def halving_scatter(value, axes):
+def halving_order(axes):
+    order = []
     for axis in axes:
+        step = 1
+        while step < lax.axis_size(axis):
+            order.append((axis, step))
+            step *= 2
+    return order
+
+
+def halving_scatter(value, order):
+    for axis, step in order:
         count = lax.axis_size(axis)
         index = lax.axis_index(axis)
-        step = count // 2
-        while step >= 1:
-            half = value.shape[0] // 2
-            upper = (index // step) % 2
-            keep = lax.dynamic_slice_in_dim(value, upper * half, half, axis=0)
-            send = lax.dynamic_slice_in_dim(value, (1 - upper) * half, half, axis=0)
-            value = keep + lax.ppermute(send, axis, [(i, i ^ step) for i in range(count)])
-            step //= 2
+        half = value.shape[0] // 2
+        upper = (index // step) % 2
+        keep = lax.dynamic_slice_in_dim(value, upper * half, half, axis=0)
+        send = lax.dynamic_slice_in_dim(value, (1 - upper) * half, half, axis=0)
+        value = keep + lax.ppermute(send, axis, [(i, i ^ step) for i in range(count)])
     return value
 
 
@@ -115,7 +122,11 @@
         dimension_numbers=("CHWN", "IHWO", "CHWN"),
         preferred_element_type=jnp.float32,
     ).reshape(channels, 9 * channels)
-    owned = halving_scatter(local_grad, ("rows", "cols"))
+    order = halving_order(("cols", "rows"))
+    bits = len(order)
+    local_grad = local_grad.reshape((2,) * bits + (channels >> bits, 9 * channels))
+    local_grad = local_grad.transpose(tuple(reversed(range(bits))) + (bits, bits + 1))
+    owned = halving_scatter(local_grad.reshape(channels, 9 * channels), order)
     owned = butterfly_sum(owned, ("rep",))
     total_cells = batch * lax.axis_size("rep") * height * rows_count * breadth * cols_count
     kernel_grad = owned * (1.0 / math.sqrt(total_cells))

time: 257 us -> 265 us (1.031)
  local copies, waits for them, and re-layouts: 23.7 us -> 35.9 us
    ppermute x25, waiting for transfers between devices: 53.9 us -> 48.4 us  [butterfly_sum(): lax.ppermute(value, axis, [(i, i ^ step) for i in range(count)])]
    ppermute x6, waiting for transfers between devices: 12.9 us -> 17.3 us  [halving_scatter(): lax.ppermute(send, axis, [(i, i ^ step) for i in range(count)])]
    another operation x0 -> x1, local copies, waits for them, and re-layouts: none -> 3.41 us  [per_device(): local_grad.reshape((2,) * bits + (channels >> bits, 9 * channels))]
    transpose x0 -> x1, local copies, waits for them, and re-layouts: none -> 3.3 us  [per_device(): local_grad.transpose(tuple(reversed(range(bits))) + (bits, bits + 1))]
    conv_general_dilated x0 -> x1, local copies, waits for them, and re-layouts: none -> 3.09 us  [per_device(): lax.conv_general_dilated(padded_in, upstream, window_strides=(1, 1), padd...]
  transfers between devices with their start and end apart: 51 -> 51, of which waited for: 38 -> 37; matrix products, arithmetic and copies ran while one was open for 18% -> 16% of each run, Pallas kernels for 0% -> 0%
where the time goes in v1:
time: 265 us; the launch traced here: 264 us
  starting transfers between devices  90.8 us (34%)
  waiting for transfers between devices  83.7 us (32%)
  local copies, waits for them, and re-layouts  35.9 us (14%)
  matrix products  22.5 us (8%)
  loops' own time  13.9 us (5%)
  other arithmetic  12.4 us (5%)
  between operations  4.68 us (2%)
    ppermute x25, starting transfers between devices, butterfly_sum(): lax.ppermute(value, axis, [(i, i ^ step) for i in range(count)])  48.5 us
    ppermute x25, waiting for transfers between devices, butterfly_sum(): lax.ppermute(value, axis, [(i, i ^ step) for i in range(count)])  48.4 us
    ppermute x10, starting transfers between devices, extended(): lax.ppermute(head, axis, [((i + 1) % count, i) for i in range(ends)])  22.4 us
    ppermute x6, waiting for transfers between devices, halving_scatter(): lax.ppermute(send, axis, [(i, i ^ step) for i in range(count)])  17.3 us
    conv_general_dilated x10, matrix products, conv(): lax.conv_general_dilated(padded, weights, window_strides=(1, 1), padding=...  15.5 us
    ppermute x10, waiting for transfers between devices, extended(): lax.ppermute(tail, axis, [(i, (i + 1) % count) for i in range(ends)])  14.7 us
    another operation x1, loops' own time, per_device(): lax.scan(power_step, (padded_probe, iterate), None, length=ITERS - 1)  13.9 us
    ppermute x10, starting transfers between devices, extended(): lax.ppermute(tail, axis, [(i, (i + 1) % count) for i in range(ends)])  11.5 us
  transfers between devices with their start and end apart: 51, of which 37 were waited for; matrix products, arithmetic and copies ran while one was open for 16% of the time, Pallas kernels for 0%

profile of v1, /device:TPU:0, one launch (start us, length us, event | category | flops | bytes accessed | tf_op | source)
XLA Modules:
  0.0 263.8 jit_solution(11106984061976796562)
XLA Ops:
  2.1 6.2 %collective-permute-start.22 = (bf16[2,32,256]{2,0,1:T(2,128)(2,1)S(1)}, bf16[2,32,256]{2,0,1:T(2,128)(2,1)S(1)}, u32[]{:S(2)}, u32[]{:S(2)}) collective-permute-start(bf16[2,32,256]{2,0,1:T(2,128)(2,1)S(1)} %get-tuple-element.72), channel_id=1, source_target_pairs={{16,0},{32,16},{48,32},{64,48},{80,64},{96,80},{112,96},{0,112},{1... | collective-permute-start | bytes 98312 | tf_op jit(solution)/shard_map/ppermute | solution.py:21
  8.4 2.1 copy.46
  11.4 4.5 %collective-permute-done.21 = bf16[2,32,256]{2,0,1:T(2,128)(2,1)S(1)} collective-permute-done((bf16[2,32,256]{2,0,1:T(2,128)(2,1)S(1)}, bf16[2,32,256]{2,0,1:T(2,128)(2,1)S(1)}, u32[]{:S(2)}, u32[]{:S(2)}) %collective-permute-start.21) | collective-permute-done | bytes 32800 | tf_op jit(solution)/shard_map/ppermute | solution.py:19
  18.4 6.1 %collective-permute-start.10 = (bf16[8,1,32,256]{3,0,2,1:T(8,128)(2,1)S(1)}, bf16[8,1,32,256]{3,0,2,1:T(8,128)(2,1)S(1)}, u32[]{:S(2)}, u32[]{:S(2)}) collective-permute-start(bf16[8,1,32,256]{3,0,2,1:T(8,128)(2,1)S(1)} %get-tuple-element.67), channel_id=1, source_target_pairs={{0,16},{16,32},{32,48},{48,64},{64,80},{80,96},{96,112},{1,17},{17... | collective-permute-start | bytes 393224 | tf_op jit(solution)/shard_map/ppermute | solution.py:19
  29.2 3.2 %collective-permute-start.12 = (bf16[8,18,1,256]{3,0,2,1:T(8,128)(2,1)S(1)}, bf16[8,18,1,256]{3,0,2,1:T(8,128)(2,1)S(1)}, u32[]{:S(2)}, u32[]{:S(2)}) collective-permute-start(bf16[8,18,1,256]{3,0,2,1:T(8,128)(2,1)S(1)} %get-tuple-element.65), channel_id=1, source_target_pairs={{0,2},{2,4},{4,6},{6,8},{8,10},{10,12},{12,14},{1,3},{3,5},{5,7},{... | collective-permute-start | bytes 221192 | tf_op jit(solution)/shard_map/ppermute | solution.py:19
  32.4 127.7 %while.14 = (s32[]{:T(128)}, bf16[20,36,256]{2,0,1:T(8,128)(2,1)S(1)}, bf16[16,32,256]{2,0,1:T(8,128)(2,1)}, f32[3]{0:T(128)S(1)}, bf16[3,3,256,256]{3,2,1,0:T(8...) while((s32[]{:T(128)}, bf16[20,36,256]{2,0,1:T(8,128)(2,1)S(1)}, ...), condition=%wide.region_2.3_spmd, body=%wide.region_0.2_spmd.sunk | while | flops 1609814016 | bytes 18578212 | solution.py:96
  35.8 3.1 %collective-permute-start = (f32[2,32,256]{2,0,1:T(2,128)S(1)}, f32[2,32,256]{2,0,1:T(2,128)S(1)}, u32[]{:S(2)}, u32[]{:S(2)}) collective-permute-start(f32[2,32,256]{2,0,1:T(2,128)S(1)} %slice_bitcast_fusion.11), channel_id=1, source_target_pairs={{16,0},{32,16},{48,32},{64,48},{80,64},{96,80},{112,96},{0,112},{1... | collective-permute-start | bytes 196616 | tf_op jit(solution)/shard_map/while/body/eval_jaxpr/ppermute | solution.py:21
  41.0 4.4 %collective-permute-start.4 = (f32[]{:T(128)}, f32[]{:T(128)}, u32[]{:S(2)}, u32[]{:S(2)}) collective-permute-start(f32[]{:T(128)} %multiply_reduce_fusion.3), channel_id=1, source_target_pairs={{0,16},{16,0},{32,48},{48,32},{64,80},{80,64},{96,112},{112,96},{1... | collective-permute-start | bytes 20 | tf_op jit(solution)/shard_map/while/body/eval_jaxpr/ppermute | solution.py:33
  48.3 2.2 collective-permute-start.5
  52.5 2.1 collective-permute-start.6
  54.6 3.0 %collective-permute-done.6 = f32[]{:T(128)} collective-permute-done((f32[]{:T(128)}, f32[]{:T(128)}, u32[]{:S(2)}, u32[]{:S(2)}) %collective-permute-start.6) | collective-permute-done | bytes 36 | tf_op jit(solution)/shard_map/while/body/eval_jaxpr/ppermute | solution.py:33
  60.0 2.9 %collective-permute-start.8 = (f32[]{:T(128)}, f32[]{:T(128)}, u32[]{:S(2)}, u32[]{:S(2)}) collective-permute-start(f32[]{:T(128)} %add.183), channel_id=1, source_target_pairs={{0,4},{2,6},{4,0},{6,2},{8,12},{10,14},{12,8},{14,10},{1,5},{3,7},... | collective-permute-start | bytes 20 | tf_op jit(solution)/shard_map/while/body/eval_jaxpr/ppermute | solution.py:33
  64.2 4.2 %collective-permute-start.9 = (f32[]{:T(128)}, f32[]{:T(128)}, u32[]{:S(2)}, u32[]{:S(2)}) collective-permute-start(f32[]{:T(128)} %add.184), channel_id=1, source_target_pairs={{0,8},{2,10},{4,12},{6,14},{8,0},{10,2},{12,4},{14,6},{1,9},{3,11}... | collective-permute-start | bytes 20 | tf_op jit(solution)/shard_map/while/body/eval_jaxpr/ppermute | solution.py:33
  72.2 3.0 %collective-permute-done.3 = f32[20,2,256]{2,0,1:T(8,128)S(1)} collective-permute-done((f32[20,2,256]{2,0,1:T(8,128)S(1)}, f32[20,2,256]{2,0,1:T(8,128)S(1)}, u32[]{:S(2)}, u32[]{:S(2)}) %collective-permute-start.3) | collective-permute-done | bytes 40992 | tf_op jit(solution)/shard_map/while/body/eval_jaxpr/ppermute | solution.py:19
  78.8 3.9 %collective-permute-start = (f32[2,32,256]{2,0,1:T(2,128)S(1)}, f32[2,32,256]{2,0,1:T(2,128)S(1)}, u32[]{:S(2)}, u32[]{:S(2)}) collective-permute-start(f32[2,32,256]{2,0,1:T(2,128)S(1)} %slice_bitcast_fusion.11), channel_id=1, source_target_pairs={{16,0},{32,16},{48,32},{64,48},{80,64},{96,80},{112,96},{0,112},{1... | collective-permute-start | bytes 196616 | tf_op jit(solution)/shard_map/while/body/eval_jaxpr/ppermute | solution.py:21
  83.8 4.2 %collective-permute-start.4 = (f32[]{:T(128)}, f32[]{:T(128)}, u32[]{:S(2)}, u32[]{:S(2)}) collective-permute-start(f32[]{:T(128)} %multiply_reduce_fusion.3), channel_id=1, source_target_pairs={{0,16},{16,0},{32,48},{48,32},{64,80},{80,64},{96,112},{112,96},{1... | collective-permute-start | bytes 20 | tf_op jit(solution)/shard_map/while/body/eval_jaxpr/ppermute | solution.py:33
  95.0 2.8 %collective-permute-start.6 = (f32[]{:T(128)}, f32[]{:T(128)}, u32[]{:S(2)}, u32[]{:S(2)}) collective-permute-start(f32[]{:T(128)} %add.181), channel_id=1, source_target_pairs={{0,64},{16,80},{32,96},{48,112},{64,0},{80,16},{96,32},{112,48},{1... | collective-permute-start | bytes 20 | tf_op jit(solution)/shard_map/while/body/eval_jaxpr/ppermute | solution.py:33
  97.9 2.2 collective-permute-done.6
  103.9 2.2 collective-permute-done.8
  106.7 2.6 collective-permute-start.9
  109.3 2.5 collective-permute-done.9
  114.3 3.0 %collective-permute-done.3 = f32[20,2,256]{2,0,1:T(8,128)S(1)} collective-permute-done((f32[20,2,256]{2,0,1:T(8,128)S(1)}, f32[20,2,256]{2,0,1:T(8,128)S(1)}, u32[]{:S(2)}, u32[]{:S(2)}) %collective-permute-start.3) | collective-permute-done | bytes 40992 | tf_op jit(solution)/shard_map/while/body/eval_jaxpr/ppermute | solution.py:19
  120.9 5.1 %collective-permute-start = (f32[2,32,256]{2,0,1:T(2,128)S(1)}, f32[2,32,256]{2,0,1:T(2,128)S(1)}, u32[]{:S(2)}, u32[]{:S(2)}) collective-permute-start(f32[2,32,256]{2,0,1:T(2,128)S(1)} %slice_bitcast_fusion.11), channel_id=1, source_target_pairs={{16,0},{32,16},{48,32},{64,48},{80,64},{96,80},{112,96},{0,112},{1... | collective-permute-start | bytes 196616 | tf_op jit(solution)/shard_map/while/body/eval_jaxpr/ppermute | solution.py:21
  127.0 2.9 %collective-permute-start.4 = (f32[]{:T(128)}, f32[]{:T(128)}, u32[]{:S(2)}, u32[]{:S(2)}) collective-permute-start(f32[]{:T(128)} %multiply_reduce_fusion.3), channel_id=1, source_target_pairs={{0,16},{16,0},{32,48},{48,32},{64,80},{80,64},{96,112},{112,96},{1... | collective-permute-start | bytes 20 | tf_op jit(solution)/shard_map/while/body/eval_jaxpr/ppermute | solution.py:33
  130.0 2.1 collective-permute-done.4
  134.9 2.1 collective-permute-done.5
  137.7 3.5 %collective-permute-start.6 = (f32[]{:T(128)}, f32[]{:T(128)}, u32[]{:S(2)}, u32[]{:S(2)}) collective-permute-start(f32[]{:T(128)} %add.181), channel_id=1, source_target_pairs={{0,64},{16,80},{32,96},{48,112},{64,0},{80,16},{96,32},{112,48},{1... | collective-permute-start | bytes 20 | tf_op jit(solution)/shard_map/while/body/eval_jaxpr/ppermute | solution.py:33
  146.5 2.2 collective-permute-done.8
  150.8 3.6 %collective-permute-done.9 = f32[]{:T(128)} collective-permute-done((f32[]{:T(128)}, f32[]{:T(128)}, u32[]{:S(2)}, u32[]{:S(2)}) %collective-permute-start.9) | collective-permute-done | bytes 36 | tf_op jit(solution)/shard_map/while/body/eval_jaxpr/ppermute | solution.py:33
  156.9 3.0 %collective-permute-done.3 = f32[20,2,256]{2,0,1:T(8,128)S(1)} collective-permute-done((f32[20,2,256]{2,0,1:T(8,128)S(1)}, f32[20,2,256]{2,0,1:T(8,128)S(1)}, u32[]{:S(2)}, u32[]{:S(2)}) %collective-permute-start.3) | collective-permute-done | bytes 40992 | tf_op jit(solution)/shard_map/while/body/eval_jaxpr/ppermute | solution.py:19
  164.2 6.9 %fusion.54 = f32[256,3,3,256]{0,3,2,1:T(8,128)} fusion(bf16[8,18,34,256]{3,0,2,1:T(8,128)(2,1)S(1)} %pad_maximum_fusion.3, bf16[4,16,32,256]{3,2,1,0:T(8,128)(2,1)S(1)} %copy-done.7), kind=kOutput, calls=%fused_computation.69 | convolution fusion | flops 2415919104 | bytes 4661248 | tf_op jit(solution)/shard_map/conv_general_dilated | solution.py:117
  171.1 3.1 %copy.54 = f32[256,3,3,256]{3,2,1,0:T(4,128)S(1)} copy(f32[256,3,3,256]{0,3,2,1:T(8,128)} %fusion.54) | data formatting | bytes 4718592 | tf_op jit(solution)/shard_map/conv_general_dilated | solution.py:117
  174.2 3.4 %reshape_reshape.3 = f32[2,2,2,2,2,2,4,2304]{7,6,5,4,3,2,1,0:T(4,128)} reshape(f32[256,3,3,256]{3,2,1,0:T(4,128)S(1)} %copy.54) | data formatting | bytes 4718592 | tf_op jit(solution)/shard_map/reshape;reshape | solution.py:127
  177.6 3.3 %copy.55 = f32[2,2,2,2,2,2,4,2304]{7,6,5,4,3,2,1,0:T(4,128)} copy(f32[2,2,2,2,2,2,4,2304]{7,6,0,1,2,3,4,5:T(4,128)} %bitcast.110) | data formatting | bytes 4718592 | tf_op jit(solution)/shard_map/transpose | solution.py:128
  180.9 2.6 reshape.28
  189.8 3.0 %collective-permute-start.25 = (f32[2]{0:T(128)S(1)}, f32[2]{0:T(128)S(1)}, u32[]{:S(2)}, u32[]{:S(2)}) collective-permute-start(f32[2]{0:T(128)S(1)} %pad_maximum_fusion.14), channel_id=1, source_target_pairs={{0,16},{16,0},{32,48},{48,32},{64,80},{80,64},{96,112},{112,96},{1... | collective-permute-start | bytes 32 | tf_op jit(solution)/shard_map/ppermute | solution.py:33
  192.8 2.1 collective-permute-done.25
  196.3 3.5 %collective-permute-done.26 = f32[2]{0:T(128)S(1)} collective-permute-done((f32[2]{0:T(128)S(1)}, f32[2]{0:T(128)S(1)}, u32[]{:S(2)}, u32[]{:S(2)}) %collective-permute-start.26) | collective-permute-done | bytes 40 | tf_op jit(solution)/shard_map/ppermute | solution.py:33
  201.2 2.1 collective-permute-start.27
  203.3 2.9 %collective-permute-done.27 = f32[2]{0:T(128)S(1)} collective-permute-done((f32[2]{0:T(128)S(1)}, f32[2]{0:T(128)S(1)}, u32[]{:S(2)}, u32[]{:S(2)}) %collective-permute-start.27) | collective-permute-done | bytes 40 | tf_op jit(solution)/shard_map/ppermute | solution.py:33
  207.4 3.5 %collective-permute-done.29 = f32[2]{0:T(128)S(1)} collective-permute-done((f32[2]{0:T(128)S(1)}, f32[2]{0:T(128)S(1)}, u32[]{:S(2)}, u32[]{:S(2)}) %collective-permute-start.29) | collective-permute-done | bytes 40 | tf_op jit(solution)/shard_map/ppermute | solution.py:33
  210.9 5.0 %collective-permute-done.30 = f32[2]{0:T(128)S(1)} collective-permute-done((f32[2]{0:T(128)S(1)}, f32[2]{0:T(128)S(1)}, u32[]{:S(2)}, u32[]{:S(2)}) %collective-permute-start.30) | collective-permute-done | bytes 40 | tf_op jit(solution)/shard_map/ppermute | solution.py:33
  220.4 10.0 %collective-permute-done.15 = f32[64,2304]{1,0:T(8,128)S(1)} collective-permute-done((f32[64,2304]{1,0:T(8,128)S(1)}, f32[64,2304]{1,0:T(8,128)S(1)}, u32[]{:S(2)}, u32[]{:S(2)}) %collective-permute-start.15) | collective-permute-done | bytes 589856 | tf_op jit(solution)/shard_map/ppermute | solution.py:56
  232.7 6.2 %collective-permute-done.16 = f32[32,2304]{1,0:T(8,128)S(1)} collective-permute-done((f32[32,2304]{1,0:T(8,128)S(1)}, f32[32,2304]{1,0:T(8,128)S(1)}, u32[]{:S(2)}, u32[]{:S(2)}) %collective-permute-start.16) | collective-permute-done | bytes 294944 | tf_op jit(solution)/shard_map/ppermute | solution.py:56
  238.9 3.3 %collective-permute-start.17 = (f32[16,2304]{1,0:T(8,128)S(1)}, f32[16,2304]{1,0:T(8,128)S(1)}, u32[]{:S(2)}, u32[]{:S(2)}) collective-permute-start(f32[16,2304]{1,0:T(8,128)S(1)} %constant_dynamic-slice_fusion.2), channel_id=1, source_target_pairs={{0,16},{16,0},{32,48},{48,32},{64,80},{80,64},{96,112},{112,96},{1... | collective-permute-start | bytes 442376 | tf_op jit(solution)/shard_map/ppermute | solution.py:56
  242.2 3.5 %select_convert_fusion.1 = bf16[16,32,5,256]{3,1,2,0:T(8,128)(2,1)S(1)} fusion(bf16[3,3,256,256]{3,2,1,0:T(8,128)(2,1)S(1)} %copy-done.12, bf16[18,4,7,2,256]{4,2,1,3,0:T(8,128)(2,1)S(1)} %slice.88, bf16[18,4,8,5,256]{4,2,1,3,0:T(8,128)(2,1)S(1)} %copy.48, pred[32,5]{0,1:T(8,128)(4,1)S(1)} %copy-done.14), kind=kOutput, calls=%fused_computation.41 | convolution fusion | flops 3027402752 | bytes 4481184 | tf_op jit(solution)/shard_map/conv_general_dilated | solution.py:63
  247.6 3.4 %select_convert_fusion = bf16[16,32,5,256]{3,1,2,0:T(8,128)(2,1)S(1)} fusion(bf16[3,3,256,256]{3,2,1,0:T(8,128)(2,1)S(1)} %copy-done.12, bf16[18,4,7,2,256]{4,2,1,3,0:T(8,128)(2,1)S(1)} %slice.91, bf16[18,4,8,5,256]{4,2,1,3,0:T(8,128)(2,1)S(1)} %copy.51, pred[32,5]{0,1:T(8,128)(4,1)S(1)} %copy-done.14), kind=kOutput, calls=%fused_computation.40 | convolution fusion | flops 3027402752 | bytes 4481184 | tf_op jit(solution)/shard_map/conv_general_dilated | solution.py:63
  251.8 4.2 %collective-permute-start.19 = (f32[4,2304]{1,0:T(4,128)S(1)}, f32[4,2304]{1,0:T(4,128)S(1)}, u32[]{:S(2)}, u32[]{:S(2)}) collective-permute-start(f32[4,2304]{1,0:T(4,128)S(1)} %constant_dynamic-slice_fusion), channel_id=1, source_target_pairs={{0,64},{16,80},{32,96},{48,112},{64,0},{80,16},{96,32},{112,48},{1... | collective-permute-start | bytes 110600 | tf_op jit(solution)/shard_map/ppermute | solution.py:56
  (211 shorter events, 78.2 us)
Async XLA Ops:
  2.1 9.3 %collective-permute-start.22 = (bf16[2,32,256]{2,0,1:T(2,128)(2,1)S(1)}, bf16[2,32,256]{2,0,1:T(2,128)(2,1)S(1)}, u32[]{:S(2)}, u32[]{:S(2)}) collective-permute-start(bf16[2,32,256]{2,0,1:T(2,128)(2,1)S(1)} %get-tuple-element.72), channel_id=1, source_target_pairs={{16,0},{32,16},{48,32},{64,48},{80,64},{96,80},{112,96},{0,112},{1... | collective-permute-start | bytes 98312 | tf_op jit(solution)/shard_map/ppermute | solution.py:21
  8.4 7.5 %collective-permute-start.21 = (bf16[2,32,256]{2,0,1:T(2,128)(2,1)S(1)}, bf16[2,32,256]{2,0,1:T(2,128)(2,1)S(1)}, u32[]{:S(2)}, u32[]{:S(2)}) collective-permute-start(bf16[2,32,256]{2,0,1:T(2,128)(2,1)S(1)} %get-tuple-element.71), channel_id=1, source_target_pairs={{0,16},{16,32},{32,48},{48,64},{64,80},{80,96},{96,112},{112,0},{1... | collective-permute-start | bytes 98312 | tf_op jit(solution)/shard_map/ppermute | solution.py:19
  15.9 8.8 %collective-permute-start.24 = (bf16[20,2,256]{2,0,1:T(8,128)(2,1)S(1)}, bf16[20,2,256]{2,0,1:T(8,128)(2,1)S(1)}, u32[]{:S(2)}, u32[]{:S(2)}) collective-permute-start(bf16[20,2,256]{2,0,1:T(8,128)(2,1)S(1)} %get-tuple-element.70), channel_id=1, source_target_pairs={{2,0},{4,2},{6,4},{8,6},{10,8},{12,10},{14,12},{0,14},{3,1},{5,3},... | collective-permute-start | bytes 61448 | tf_op jit(solution)/shard_map/ppermute | solution.py:21
  16.9 7.8 %collective-permute-start.23 = (bf16[20,2,256]{2,0,1:T(8,128)(2,1)S(1)}, bf16[20,2,256]{2,0,1:T(8,128)(2,1)S(1)}, u32[]{:S(2)}, u32[]{:S(2)}) collective-permute-start(bf16[20,2,256]{2,0,1:T(8,128)(2,1)S(1)} %get-tuple-element.69), channel_id=1, source_target_pairs={{0,2},{2,4},{4,6},{6,8},{8,10},{10,12},{12,14},{14,0},{1,3},{3,5},... | collective-permute-start | bytes 61448 | tf_op jit(solution)/shard_map/ppermute | solution.py:19
  17.1 9.5 %collective-permute-start.11 = (bf16[8,1,32,256]{3,0,2,1:T(8,128)(2,1)S(1)}, bf16[8,1,32,256]{3,0,2,1:T(8,128)(2,1)S(1)}, u32[]{:S(2)}, u32[]{:S(2)}) collective-permute-start(bf16[8,1,32,256]{3,0,2,1:T(8,128)(2,1)S(1)} %get-tuple-element.68), channel_id=1, source_target_pairs={{16,0},{32,16},{48,32},{64,48},{80,64},{96,80},{112,96},{17,1},{33... | collective-permute-start | bytes 393224 | tf_op jit(solution)/shard_map/ppermute | solution.py:21
  18.4 9.4 %collective-permute-start.10 = (bf16[8,1,32,256]{3,0,2,1:T(8,128)(2,1)S(1)}, bf16[8,1,32,256]{3,0,2,1:T(8,128)(2,1)S(1)}, u32[]{:S(2)}, u32[]{:S(2)}) collective-permute-start(bf16[8,1,32,256]{3,0,2,1:T(8,128)(2,1)S(1)} %get-tuple-element.67), channel_id=1, source_target_pairs={{0,16},{16,32},{32,48},{48,64},{64,80},{80,96},{96,112},{1,17},{17... | collective-permute-start | bytes 393224 | tf_op jit(solution)/shard_map/ppermute | solution.py:19
  27.9 133.1 %collective-permute-start.13 = (bf16[8,18,1,256]{3,0,2,1:T(8,128)(2,1)S(1)}, bf16[8,18,1,256]{3,0,2,1:T(8,128)(2,1)S(1)}, u32[]{:S(2)}, u32[]{:S(2)}) collective-permute-start(bf16[8,18,1,256]{3,0,2,1:T(8,128)(2,1)S(1)} %get-tuple-element.66), channel_id=1, source_target_pairs={{2,0},{4,2},{6,4},{8,6},{10,8},{12,10},{14,12},{3,1},{5,3},{7,5},{... | collective-permute-start | bytes 221192 | tf_op jit(solution)/shard_map/ppermute | solution.py:21
  29.2 131.9 %collective-permute-start.12 = (bf16[8,18,1,256]{3,0,2,1:T(8,128)(2,1)S(1)}, bf16[8,18,1,256]{3,0,2,1:T(8,128)(2,1)S(1)}, u32[]{:S(2)}, u32[]{:S(2)}) collective-permute-start(bf16[8,18,1,256]{3,0,2,1:T(8,128)(2,1)S(1)} %get-tuple-element.65), channel_id=1, source_target_pairs={{0,2},{2,4},{4,6},{6,8},{8,10},{10,12},{12,14},{1,3},{3,5},{5,7},{... | collective-permute-start | bytes 221192 | tf_op jit(solution)/shard_map/ppermute | solution.py:19
  35.8 34.1 %collective-permute-start = (f32[2,32,256]{2,0,1:T(2,128)S(1)}, f32[2,32,256]{2,0,1:T(2,128)S(1)}, u32[]{:S(2)}, u32[]{:S(2)}) collective-permute-start(f32[2,32,256]{2,0,1:T(2,128)S(1)} %slice_bitcast_fusion.11), channel_id=1, source_target_pairs={{16,0},{32,16},{48,32},{64,48},{80,64},{96,80},{112,96},{0,112},{1... | collective-permute-start | bytes 196616 | tf_op jit(solution)/shard_map/while/body/eval_jaxpr/ppermute | solution.py:21
  39.0 31.0 %collective-permute-start.1 = (f32[2,32,256]{2,0,1:T(2,128)S(1)}, f32[2,32,256]{2,0,1:T(2,128)S(1)}, u32[]{:S(2)}, u32[]{:S(2)}) collective-permute-start(f32[2,32,256]{2,0,1:T(2,128)S(1)} %slice_bitcast_fusion.13), channel_id=1, source_target_pairs={{0,16},{16,32},{32,48},{48,64},{64,80},{80,96},{96,112},{112,0},{1... | collective-permute-start | bytes 196616 | tf_op jit(solution)/shard_map/while/body/eval_jaxpr/ppermute | solution.py:19
  41.0 6.1 %collective-permute-start.4 = (f32[]{:T(128)}, f32[]{:T(128)}, u32[]{:S(2)}, u32[]{:S(2)}) collective-permute-start(f32[]{:T(128)} %multiply_reduce_fusion.3), channel_id=1, source_target_pairs={{0,16},{16,0},{32,48},{48,32},{64,80},{80,64},{96,112},{112,96},{1... | collective-permute-start | bytes 20 | tf_op jit(solution)/shard_map/while/body/eval_jaxpr/ppermute | solution.py:33
  48.3 3.6 %collective-permute-start.5 = (f32[]{:T(128)}, f32[]{:T(128)}, u32[]{:S(2)}, u32[]{:S(2)}) collective-permute-start(f32[]{:T(128)} %add.180), channel_id=1, source_target_pairs={{0,32},{16,48},{32,0},{48,16},{64,96},{80,112},{96,64},{112,80},{1... | collective-permute-start | bytes 20 | tf_op jit(solution)/shard_map/while/body/eval_jaxpr/ppermute | solution.py:33
  52.5 5.1 %collective-permute-start.6 = (f32[]{:T(128)}, f32[]{:T(128)}, u32[]{:S(2)}, u32[]{:S(2)}) collective-permute-start(f32[]{:T(128)} %add.181), channel_id=1, source_target_pairs={{0,64},{16,80},{32,96},{48,112},{64,0},{80,16},{96,32},{112,48},{1... | collective-permute-start | bytes 20 | tf_op jit(solution)/shard_map/while/body/eval_jaxpr/ppermute | solution.py:33
  60.0 3.6 %collective-permute-start.8 = (f32[]{:T(128)}, f32[]{:T(128)}, u32[]{:S(2)}, u32[]{:S(2)}) collective-permute-start(f32[]{:T(128)} %add.183), channel_id=1, source_target_pairs={{0,4},{2,6},{4,0},{6,2},{8,12},{10,14},{12,8},{14,10},{1,5},{3,7},... | collective-permute-start | bytes 20 | tf_op jit(solution)/shard_map/while/body/eval_jaxpr/ppermute | solution.py:33
  64.2 5.1 %collective-permute-start.9 = (f32[]{:T(128)}, f32[]{:T(128)}, u32[]{:S(2)}, u32[]{:S(2)}) collective-permute-start(f32[]{:T(128)} %add.184), channel_id=1, source_target_pairs={{0,8},{2,10},{4,12},{6,14},{8,0},{10,2},{12,4},{14,6},{1,9},{3,11}... | collective-permute-start | bytes 20 | tf_op jit(solution)/shard_map/while/body/eval_jaxpr/ppermute | solution.py:33
  70.0 2.2 collective-permute-start.2
  70.5 4.7 %collective-permute-start.3 = (f32[20,2,256]{2,0,1:T(8,128)S(1)}, f32[20,2,256]{2,0,1:T(8,128)S(1)}, u32[]{:S(2)}, u32[]{:S(2)}) collective-permute-start(f32[20,2,256]{2,0,1:T(8,128)S(1)} %get-tuple-element.113), channel_id=1, source_target_pairs={{0,2},{2,4},{4,6},{6,8},{8,10},{10,12},{12,14},{14,0},{1,3},{3,5},... | collective-permute-start | bytes 122888 | tf_op jit(solution)/shard_map/while/body/eval_jaxpr/ppermute | solution.py:19
  78.8 33.7 %collective-permute-start = (f32[2,32,256]{2,0,1:T(2,128)S(1)}, f32[2,32,256]{2,0,1:T(2,128)S(1)}, u32[]{:S(2)}, u32[]{:S(2)}) collective-permute-start(f32[2,32,256]{2,0,1:T(2,128)S(1)} %slice_bitcast_fusion.11), channel_id=1, source_target_pairs={{16,0},{32,16},{48,32},{64,48},{80,64},{96,80},{112,96},{0,112},{1... | collective-permute-start | bytes 196616 | tf_op jit(solution)/shard_map/while/body/eval_jaxpr/ppermute | solution.py:21
  82.7 29.7 %collective-permute-start.1 = (f32[2,32,256]{2,0,1:T(2,128)S(1)}, f32[2,32,256]{2,0,1:T(2,128)S(1)}, u32[]{:S(2)}, u32[]{:S(2)}) collective-permute-start(f32[2,32,256]{2,0,1:T(2,128)S(1)} %slice_bitcast_fusion.13), channel_id=1, source_target_pairs={{0,16},{16,32},{32,48},{48,64},{64,80},{80,96},{96,112},{112,0},{1... | collective-permute-start | bytes 196616 | tf_op jit(solution)/shard_map/while/body/eval_jaxpr/ppermute | solution.py:19
  83.8 5.8 %collective-permute-start.4 = (f32[]{:T(128)}, f32[]{:T(128)}, u32[]{:S(2)}, u32[]{:S(2)}) collective-permute-start(f32[]{:T(128)} %multiply_reduce_fusion.3), channel_id=1, source_target_pairs={{0,16},{16,0},{32,48},{48,32},{64,80},{80,64},{96,112},{112,96},{1... | collective-permute-start | bytes 20 | tf_op jit(solution)/shard_map/while/body/eval_jaxpr/ppermute | solution.py:33
  90.8 3.6 %collective-permute-start.5 = (f32[]{:T(128)}, f32[]{:T(128)}, u32[]{:S(2)}, u32[]{:S(2)}) collective-permute-start(f32[]{:T(128)} %add.180), channel_id=1, source_target_pairs={{0,32},{16,48},{32,0},{48,16},{64,96},{80,112},{96,64},{112,80},{1... | collective-permute-start | bytes 20 | tf_op jit(solution)/shard_map/while/body/eval_jaxpr/ppermute | solution.py:33
  95.0 5.1 %collective-permute-start.6 = (f32[]{:T(128)}, f32[]{:T(128)}, u32[]{:S(2)}, u32[]{:S(2)}) collective-permute-start(f32[]{:T(128)} %add.181), channel_id=1, source_target_pairs={{0,64},{16,80},{32,96},{48,112},{64,0},{80,16},{96,32},{112,48},{1... | collective-permute-start | bytes 20 | tf_op jit(solution)/shard_map/while/body/eval_jaxpr/ppermute | solution.py:33
  100.7 1.2 collective-permute-start.7
  102.5 3.6 %collective-permute-start.8 = (f32[]{:T(128)}, f32[]{:T(128)}, u32[]{:S(2)}, u32[]{:S(2)}) collective-permute-start(f32[]{:T(128)} %add.183), channel_id=1, source_target_pairs={{0,4},{2,6},{4,0},{6,2},{8,12},{10,14},{12,8},{14,10},{1,5},{3,7},... | collective-permute-start | bytes 20 | tf_op jit(solution)/shard_map/while/body/eval_jaxpr/ppermute | solution.py:33
  106.7 5.1 %collective-permute-start.9 = (f32[]{:T(128)}, f32[]{:T(128)}, u32[]{:S(2)}, u32[]{:S(2)}) collective-permute-start(f32[]{:T(128)} %add.184), channel_id=1, source_target_pairs={{0,8},{2,10},{4,12},{6,14},{8,0},{10,2},{12,4},{14,6},{1,9},{3,11}... | collective-permute-start | bytes 20 | tf_op jit(solution)/shard_map/while/body/eval_jaxpr/ppermute | solution.py:33
  112.5 1.8 collective-permute-start.2
  112.5 4.7 %collective-permute-start.3 = (f32[20,2,256]{2,0,1:T(8,128)S(1)}, f32[20,2,256]{2,0,1:T(8,128)S(1)}, u32[]{:S(2)}, u32[]{:S(2)}) collective-permute-start(f32[20,2,256]{2,0,1:T(8,128)S(1)} %get-tuple-element.113), channel_id=1, source_target_pairs={{0,2},{2,4},{4,6},{6,8},{8,10},{10,12},{12,14},{14,0},{1,3},{3,5},... | collective-permute-start | bytes 122888 | tf_op jit(solution)/shard_map/while/body/eval_jaxpr/ppermute | solution.py:19
  120.9 34.2 %collective-permute-start = (f32[2,32,256]{2,0,1:T(2,128)S(1)}, f32[2,32,256]{2,0,1:T(2,128)S(1)}, u32[]{:S(2)}, u32[]{:S(2)}) collective-permute-start(f32[2,32,256]{2,0,1:T(2,128)S(1)} %slice_bitcast_fusion.11), channel_id=1, source_target_pairs={{16,0},{32,16},{48,32},{64,48},{80,64},{96,80},{112,96},{0,112},{1... | collective-permute-start | bytes 196616 | tf_op jit(solution)/shard_map/while/body/eval_jaxpr/ppermute | solution.py:21
  126.0 29.1 %collective-permute-start.1 = (f32[2,32,256]{2,0,1:T(2,128)S(1)}, f32[2,32,256]{2,0,1:T(2,128)S(1)}, u32[]{:S(2)}, u32[]{:S(2)}) collective-permute-start(f32[2,32,256]{2,0,1:T(2,128)S(1)} %slice_bitcast_fusion.13), channel_id=1, source_target_pairs={{0,16},{16,32},{32,48},{48,64},{64,80},{80,96},{96,112},{112,0},{1... | collective-permute-start | bytes 196616 | tf_op jit(solution)/shard_map/while/body/eval_jaxpr/ppermute | solution.py:19
  127.0 5.1 %collective-permute-start.4 = (f32[]{:T(128)}, f32[]{:T(128)}, u32[]{:S(2)}, u32[]{:S(2)}) collective-permute-start(f32[]{:T(128)} %multiply_reduce_fusion.3), channel_id=1, source_target_pairs={{0,16},{16,0},{32,48},{48,32},{64,80},{80,64},{96,112},{112,96},{1... | collective-permute-start | bytes 20 | tf_op jit(solution)/shard_map/while/body/eval_jaxpr/ppermute | solution.py:33
  133.5 3.6 %collective-permute-start.5 = (f32[]{:T(128)}, f32[]{:T(128)}, u32[]{:S(2)}, u32[]{:S(2)}) collective-permute-start(f32[]{:T(128)} %add.180), channel_id=1, source_target_pairs={{0,32},{16,48},{32,0},{48,16},{64,96},{80,112},{96,64},{112,80},{1... | collective-permute-start | bytes 20 | tf_op jit(solution)/shard_map/while/body/eval_jaxpr/ppermute | solution.py:33
  137.7 5.1 %collective-permute-start.6 = (f32[]{:T(128)}, f32[]{:T(128)}, u32[]{:S(2)}, u32[]{:S(2)}) collective-permute-start(f32[]{:T(128)} %add.181), channel_id=1, source_target_pairs={{0,64},{16,80},{32,96},{48,112},{64,0},{80,16},{96,32},{112,48},{1... | collective-permute-start | bytes 20 | tf_op jit(solution)/shard_map/while/body/eval_jaxpr/ppermute | solution.py:33
  145.2 3.6 %collective-permute-start.8 = (f32[]{:T(128)}, f32[]{:T(128)}, u32[]{:S(2)}, u32[]{:S(2)}) collective-permute-start(f32[]{:T(128)} %add.183), channel_id=1, source_target_pairs={{0,4},{2,6},{4,0},{6,2},{8,12},{10,14},{12,8},{14,10},{1,5},{3,7},... | collective-permute-start | bytes 20 | tf_op jit(solution)/shard_map/while/body/eval_jaxpr/ppermute | solution.py:33
  149.4 5.1 %collective-permute-start.9 = (f32[]{:T(128)}, f32[]{:T(128)}, u32[]{:S(2)}, u32[]{:S(2)}) collective-permute-start(f32[]{:T(128)} %add.184), channel_id=1, source_target_pairs={{0,8},{2,10},{4,12},{6,14},{8,0},{10,2},{12,4},{14,6},{1,9},{3,11}... | collective-permute-start | bytes 20 | tf_op jit(solution)/shard_map/while/body/eval_jaxpr/ppermute | solution.py:33
  155.2 1.8 collective-permute-start.2
  155.2 4.7 %collective-permute-start.3 = (f32[20,2,256]{2,0,1:T(8,128)S(1)}, f32[20,2,256]{2,0,1:T(8,128)S(1)}, u32[]{:S(2)}, u32[]{:S(2)}) collective-permute-start(f32[20,2,256]{2,0,1:T(8,128)S(1)} %get-tuple-element.113), channel_id=1, source_target_pairs={{0,2},{2,4},{4,6},{6,8},{8,10},{10,12},{12,14},{14,0},{1,3},{3,5},... | collective-permute-start | bytes 122888 | tf_op jit(solution)/shard_map/while/body/eval_jaxpr/ppermute | solution.py:19
  183.7 32.3 %collective-permute-start.14 = (f32[128,2304]{1,0:T(8,128)S(1)}, f32[128,2304]{1,0:T(8,128)S(1)}, u32[]{:S(2)}, u32[]{:S(2)}) collective-permute-start(f32[128,2304]{1,0:T(8,128)S(1)} %constant_dynamic-slice_fusion.5), channel_id=1, source_target_pairs={{0,2},{2,0},{4,6},{6,4},{8,10},{10,8},{12,14},{14,12},{1,3},{3,1},... | collective-permute-start | bytes 3538952 | tf_op jit(solution)/shard_map/ppermute | solution.py:56
  189.8 5.1 %collective-permute-start.25 = (f32[2]{0:T(128)S(1)}, f32[2]{0:T(128)S(1)}, u32[]{:S(2)}, u32[]{:S(2)}) collective-permute-start(f32[2]{0:T(128)S(1)} %pad_maximum_fusion.14), channel_id=1, source_target_pairs={{0,16},{16,0},{32,48},{48,32},{64,80},{80,64},{96,112},{112,96},{1... | collective-permute-start | bytes 32 | tf_op jit(solution)/shard_map/ppermute | solution.py:33
  196.2 3.6 %collective-permute-start.26 = (f32[2]{0:T(128)S(1)}, f32[2]{0:T(128)S(1)}, u32[]{:S(2)}, u32[]{:S(2)}) collective-permute-start(f32[2]{0:T(128)S(1)} %fusion.93), channel_id=1, source_target_pairs={{0,32},{16,48},{32,0},{48,16},{64,96},{80,112},{96,64},{112,80},{1... | collective-permute-start | bytes 32 | tf_op jit(solution)/shard_map/ppermute | solution.py:33
  201.2 5.1 %collective-permute-start.27 = (f32[2]{0:T(128)S(1)}, f32[2]{0:T(128)S(1)}, u32[]{:S(2)}, u32[]{:S(2)}) collective-permute-start(f32[2]{0:T(128)S(1)} %fusion.94), channel_id=1, source_target_pairs={{0,64},{16,80},{32,96},{48,112},{64,0},{80,16},{96,32},{112,48},{1... | collective-permute-start | bytes 32 | tf_op jit(solution)/shard_map/ppermute | solution.py:33
  207.3 3.5 %collective-permute-start.29 = (f32[2]{0:T(128)S(1)}, f32[2]{0:T(128)S(1)}, u32[]{:S(2)}, u32[]{:S(2)}) collective-permute-start(f32[2]{0:T(128)S(1)} %add.156), channel_id=1, source_target_pairs={{0,4},{2,6},{4,0},{6,2},{8,12},{10,14},{12,8},{14,10},{1,5},{3,7},... | collective-permute-start | bytes 32 | tf_op jit(solution)/shard_map/ppermute | solution.py:33
  210.9 5.0 %collective-permute-start.30 = (f32[2]{0:T(128)S(1)}, f32[2]{0:T(128)S(1)}, u32[]{:S(2)}, u32[]{:S(2)}) collective-permute-start(f32[2]{0:T(128)S(1)} %add.157), channel_id=1, source_target_pairs={{0,8},{2,10},{4,12},{6,14},{8,0},{10,2},{12,4},{14,6},{1,9},{3,11}... | collective-permute-start | bytes 32 | tf_op jit(solution)/shard_map/ppermute | solution.py:33
  216.2 14.3 %collective-permute-start.15 = (f32[64,2304]{1,0:T(8,128)S(1)}, f32[64,2304]{1,0:T(8,128)S(1)}, u32[]{:S(2)}, u32[]{:S(2)}) collective-permute-start(f32[64,2304]{1,0:T(8,128)S(1)} %constant_dynamic-slice_fusion.4), channel_id=1, source_target_pairs={{0,4},{2,6},{4,0},{6,2},{8,12},{10,14},{12,8},{14,10},{1,5},{3,7},... | collective-permute-start | bytes 1769480 | tf_op jit(solution)/shard_map/ppermute | solution.py:56
  230.5 8.3 %collective-permute-start.16 = (f32[32,2304]{1,0:T(8,128)S(1)}, f32[32,2304]{1,0:T(8,128)S(1)}, u32[]{:S(2)}, u32[]{:S(2)}) collective-permute-start(f32[32,2304]{1,0:T(8,128)S(1)} %constant_dynamic-slice_fusion.3), channel_id=1, source_target_pairs={{0,8},{2,10},{4,12},{6,14},{8,0},{10,2},{12,4},{14,6},{1,9},{3,11}... | collective-permute-start | bytes 884744 | tf_op jit(solution)/shard_map/ppermute | solution.py:56
  238.9 8.0 %collective-permute-start.17 = (f32[16,2304]{1,0:T(8,128)S(1)}, f32[16,2304]{1,0:T(8,128)S(1)}, u32[]{:S(2)}, u32[]{:S(2)}) collective-permute-start(f32[16,2304]{1,0:T(8,128)S(1)} %constant_dynamic-slice_fusion.2), channel_id=1, source_target_pairs={{0,16},{16,0},{32,48},{48,32},{64,80},{80,64},{96,112},{112,96},{1... | collective-permute-start | bytes 442376 | tf_op jit(solution)/shard_map/ppermute | solution.py:56
  247.0 4.8 %collective-permute-start.18 = (f32[8,2304]{1,0:T(8,128)S(1)}, f32[8,2304]{1,0:T(8,128)S(1)}, u32[]{:S(2)}, u32[]{:S(2)}) collective-permute-start(f32[8,2304]{1,0:T(8,128)S(1)} %constant_dynamic-slice_fusion.1), channel_id=1, source_target_pairs={{0,32},{16,48},{32,0},{48,16},{64,96},{80,112},{96,64},{112,80},{1... | collective-permute-start | bytes 221192 | tf_op jit(solution)/shard_map/ppermute | solution.py:56
  251.8 6.1 %collective-permute-start.19 = (f32[4,2304]{1,0:T(4,128)S(1)}, f32[4,2304]{1,0:T(4,128)S(1)}, u32[]{:S(2)}, u32[]{:S(2)}) collective-permute-start(f32[4,2304]{1,0:T(4,128)S(1)} %constant_dynamic-slice_fusion), channel_id=1, source_target_pairs={{0,64},{16,80},{32,96},{48,112},{64,0},{80,16},{96,32},{112,48},{1... | collective-permute-start | bytes 110600 | tf_op jit(solution)/shard_map/ppermute | solution.py:56
  258.0 4.0 %collective-permute-start.20 = (f32[4,2304]{1,0:T(4,128)S(1)}, f32[4,2304]{1,0:T(4,128)S(1)}, u32[]{:S(2)}, u32[]{:S(2)}) collective-permute-start(f32[4,2304]{1,0:T(4,128)S(1)} %dynamic-slice_add_fusion.5), channel_id=1, source_target_pairs={{0,1},{1,0},{2,3},{3,2},{4,5},{5,4},{6,7},{7,6},{8,9},{9,8},{10,11... | collective-permute-start | bytes 110600 | tf_op jit(solution)/shard_map/ppermute | solution.py:33
  (23 other events, 106.4 us)

commit v2 on v0

--- a/solution.py
+++ b/solution.py
@@ -79,8 +79,11 @@
         padded_probe, iterate = carry
         image = conv(padded_probe[None], kernel, False).astype(jnp.bfloat16)
         back = conv(image, kernel, True)[0]
-        padded_back = extended(back, field, 2, True)
-        squared = butterfly_sum(jnp.sum(back * back), ("rows", "cols"))
+        row_padded = extended(back, field[:1], 2, True)
+        squared = butterfly_sum(jnp.sum(back * back), ("rows",))
+        squared, row_padded = lax.optimization_barrier((squared, row_padded))
+        padded_back = extended(row_padded, field[1:], 2, True)
+        squared = butterfly_sum(squared, ("cols",))
         scale_now = jnp.sqrt(squared / count + 1e-06)
         iterate = (back / scale_now).astype(jnp.bfloat16)
         padded_probe = (padded_back / scale_now).astype(jnp.bfloat16)

time: 257 us -> 241 us (0.938)
  waiting for transfers between devices: 84.8 us -> 64.8 us
  starting transfers between devices: 92.8 us -> 96.1 us
    ppermute x10, waiting for transfers between devices: 14.7 us -> 5.7 us  [extended(): lax.ppermute(tail, axis, [(i, (i + 1) % count) for i in range(ends)])]
    ppermute x25, waiting for transfers between devices: 53.9 us -> 45.1 us  [butterfly_sum(): lax.ppermute(value, axis, [(i, i ^ step) for i in range(count)])]
    ppermute x10, starting transfers between devices: 22.4 us -> 15.4 us  [extended(): lax.ppermute(head, axis, [((i + 1) % count, i) for i in range(ends)])]
    ppermute x10, starting transfers between devices: 11.5 us -> 16.7 us  [extended(): lax.ppermute(tail, axis, [(i, (i + 1) % count) for i in range(ends)])]
    ppermute x25, starting transfers between devices: 50.6 us -> 55.8 us  [butterfly_sum(): lax.ppermute(value, axis, [(i, i ^ step) for i in range(count)])]
    unnamed x40 -> x48, local copies, waits for them, and re-layouts: 10 us -> 10 us
  transfers between devices with their start and end apart: 51 -> 51, of which waited for: 38 -> 26; matrix products, arithmetic and copies ran while one was open for 18% -> 19% of each run, Pallas kernels for 0% -> 0%
where the time goes in v2:
time: 241 us; the launch traced here: 239 us
  starting transfers between devices  96.1 us (40%)
  waiting for transfers between devices  64.8 us (27%)
  local copies, waits for them, and re-layouts  23.8 us (10%)
  matrix products  23.5 us (10%)
  other arithmetic  13.9 us (6%)
  loops' own time  12.5 us (5%)
  between operations  4.67 us (2%)
    ppermute x25, starting transfers between devices, butterfly_sum(): lax.ppermute(value, axis, [(i, i ^ step) for i in range(count)])  55.8 us
    ppermute x25, waiting for transfers between devices, butterfly_sum(): lax.ppermute(value, axis, [(i, i ^ step) for i in range(count)])  45.1 us
    conv_general_dilated x10, matrix products, conv(): lax.conv_general_dilated(padded, weights, window_strides=(1, 1), padding=...  17.8 us
    ppermute x10, starting transfers between devices, extended(): lax.ppermute(tail, axis, [(i, (i + 1) % count) for i in range(ends)])  16.7 us
    ppermute x10, starting transfers between devices, extended(): lax.ppermute(head, axis, [((i + 1) % count, i) for i in range(ends)])  15.4 us
    another operation x1, loops' own time, per_device(): lax.scan(power_step, (padded_probe, iterate), None, length=ITERS - 1)  12.5 us
    ppermute x6, waiting for transfers between devices, halving_scatter(): lax.ppermute(send, axis, [(i, i ^ step) for i in range(count)])  12.4 us
    unnamed x48, local copies, waits for them, and re-layouts  10 us
  transfers between devices with their start and end apart: 51, of which 26 were waited for; matrix products, arithmetic and copies ran while one was open for 19% of the time, Pallas kernels for 0%

profile of v2, /device:TPU:0, one launch (start us, length us, event | category | flops | bytes accessed | tf_op | source)
XLA Modules:
  0.0 239.3 jit_solution(8166823179362208680)
XLA Ops:
  2.1 6.2 %collective-permute-start.22 = (bf16[2,32,256]{2,0,1:T(2,128)(2,1)S(1)}, bf16[2,32,256]{2,0,1:T(2,128)(2,1)S(1)}, u32[]{:S(2)}, u32[]{:S(2)}) collective-permute-start(bf16[2,32,256]{2,0,1:T(2,128)(2,1)S(1)} %get-tuple-element.70), channel_id=1, source_target_pairs={{16,0},{32,16},{48,32},{64,48},{80,64},{96,80},{112,96},{0,112},{1... | collective-permute-start | bytes 98312 | tf_op jit(solution)/shard_map/ppermute | solution.py:21
  8.4 2.1 copy.25
  11.4 4.5 %collective-permute-done.21 = bf16[2,32,256]{2,0,1:T(2,128)(2,1)S(1)} collective-permute-done((bf16[2,32,256]{2,0,1:T(2,128)(2,1)S(1)}, bf16[2,32,256]{2,0,1:T(2,128)(2,1)S(1)}, u32[]{:S(2)}, u32[]{:S(2)}) %collective-permute-start.21) | collective-permute-done | bytes 32800 | tf_op jit(solution)/shard_map/ppermute | solution.py:19
  18.4 6.1 %collective-permute-start.10 = (bf16[8,1,32,256]{3,0,2,1:T(8,128)(2,1)S(1)}, bf16[8,1,32,256]{3,0,2,1:T(8,128)(2,1)S(1)}, u32[]{:S(2)}, u32[]{:S(2)}) collective-permute-start(bf16[8,1,32,256]{3,0,2,1:T(8,128)(2,1)S(1)} %get-tuple-element.65), channel_id=1, source_target_pairs={{0,16},{16,32},{32,48},{48,64},{64,80},{80,96},{96,112},{1,17},{17... | collective-permute-start | bytes 393224 | tf_op jit(solution)/shard_map/ppermute | solution.py:19
  29.8 3.7 %collective-permute-start.12 = (bf16[8,18,1,256]{3,0,2,1:T(8,128)(2,1)S(1)}, bf16[8,18,1,256]{3,0,2,1:T(8,128)(2,1)}, u32[]{:S(2)}, u32[]{:S(2)}) collective-permute-start(bf16[8,18,1,256]{3,0,2,1:T(8,128)(2,1)S(1)} %get-tuple-element.63), channel_id=1, source_target_pairs={{0,2},{2,4},{4,6},{6,8},{8,10},{10,12},{12,14},{1,3},{3,5},{5,7},{... | collective-permute-start | bytes 221192 | tf_op jit(solution)/shard_map/ppermute | solution.py:19
  33.4 109.5 %while.14 = (s32[]{:T(128)}, bf16[20,36,256]{2,0,1:T(8,128)(2,1)S(1)}, bf16[16,32,256]{2,0,1:T(8,128)(2,1)}, f32[3]{0:T(128)S(1)}, bf16[3,3,256,256]{3,2,1,0:T(8...) while((s32[]{:T(128)}, bf16[20,36,256]{2,0,1:T(8,128)(2,1)S(1)}, ...), condition=%wide.region_2.3_spmd, body=%wide.region_0.2_spmd.sunk | while | flops 1609732096 | bytes 19315492 | solution.py:92
  37.8 4.0 %collective-permute-start = (f32[]{:T(128)}, f32[]{:T(128)}, u32[]{:S(2)}, u32[]{:S(2)}) collective-permute-start(f32[]{:T(128)} %multiply_reduce_fusion.3), channel_id=1, source_target_pairs={{0,16},{16,0},{32,48},{48,32},{64,80},{80,64},{96,112},{112,96},{1... | collective-permute-start | bytes 20 | tf_op jit(solution)/shard_map/while/body/eval_jaxpr/ppermute | solution.py:33
  43.1 2.5 %collective-permute-start.4 = (f32[2,32,256]{2,0,1:T(2,128)S(1)}, f32[2,32,256]{2,0,1:T(2,128)S(1)}, u32[]{:S(2)}, u32[]{:S(2)}) collective-permute-start(f32[2,32,256]{2,0,1:T(2,128)S(1)} %slice_bitcast_fusion.13), channel_id=1, source_target_pairs={{0,16},{16,32},{32,48},{48,64},{64,80},{80,96},{96,112},{112,0},{1... | collective-permute-start | bytes 196616 | tf_op jit(solution)/shard_map/while/body/eval_jaxpr/ppermute | solution.py:19
  48.2 2.3 collective-permute-done.1
  52.4 3.8 %collective-permute-done.2 = f32[]{:T(128)} collective-permute-done((f32[]{:T(128)}, f32[]{:T(128)}, u32[]{:S(2)}, u32[]{:S(2)}) %collective-permute-start.2) | collective-permute-done | bytes 36 | tf_op jit(solution)/shard_map/while/body/eval_jaxpr/ppermute | solution.py:33
  57.5 1.7 collective-permute-start.7
  59.8 2.7 %collective-permute-start.8 = (f32[]{:T(128)}, f32[]{:T(128)}, u32[]{:S(2)}, u32[]{:S(2)}) collective-permute-start(f32[]{:T(128)} %add.182), channel_id=1, source_target_pairs={{0,4},{2,6},{4,0},{6,2},{8,12},{10,14},{12,8},{14,10},{1,5},{3,7},... | collective-permute-start | bytes 20 | tf_op jit(solution)/shard_map/while/body/eval_jaxpr/ppermute | solution.py:33
  64.1 4.5 %collective-permute-start.9 = (f32[]{:T(128)}, f32[]{:T(128)}, u32[]{:S(2)}, u32[]{:S(2)}) collective-permute-start(f32[]{:T(128)} %add.183), channel_id=1, source_target_pairs={{0,8},{2,10},{4,12},{6,14},{8,0},{10,2},{12,4},{14,6},{1,9},{3,11}... | collective-permute-start | bytes 20 | tf_op jit(solution)/shard_map/while/body/eval_jaxpr/ppermute | solution.py:33
  76.7 1.9 collective-permute-start.3
  78.6 1.8 collective-permute-start.4
  81.6 2.2 collective-permute-start.1
  85.9 3.2 %collective-permute-start.2 = (f32[]{:T(128)}, f32[]{:T(128)}, u32[]{:S(2)}, u32[]{:S(2)}) collective-permute-start(f32[]{:T(128)} %add.180), channel_id=1, source_target_pairs={{0,64},{16,80},{32,96},{48,112},{64,0},{80,16},{96,32},{112,48},{1... | collective-permute-start | bytes 20 | tf_op jit(solution)/shard_map/while/body/eval_jaxpr/ppermute | solution.py:33
  89.1 2.0 collective-permute-done.2
  92.4 1.9 collective-permute-start.7
  94.8 3.2 %collective-permute-start.8 = (f32[]{:T(128)}, f32[]{:T(128)}, u32[]{:S(2)}, u32[]{:S(2)}) collective-permute-start(f32[]{:T(128)} %add.182), channel_id=1, source_target_pairs={{0,4},{2,6},{4,0},{6,2},{8,12},{10,14},{12,8},{14,10},{1,5},{3,7},... | collective-permute-start | bytes 20 | tf_op jit(solution)/shard_map/while/body/eval_jaxpr/ppermute | solution.py:33
  99.1 3.9 %collective-permute-start.9 = (f32[]{:T(128)}, f32[]{:T(128)}, u32[]{:S(2)}, u32[]{:S(2)}) collective-permute-start(f32[]{:T(128)} %add.183), channel_id=1, source_target_pairs={{0,8},{2,10},{4,12},{6,14},{8,0},{10,2},{12,4},{14,6},{1,9},{3,11}... | collective-permute-start | bytes 20 | tf_op jit(solution)/shard_map/while/body/eval_jaxpr/ppermute | solution.py:33
  110.1 3.0 %collective-permute-start = (f32[]{:T(128)}, f32[]{:T(128)}, u32[]{:S(2)}, u32[]{:S(2)}) collective-permute-start(f32[]{:T(128)} %multiply_reduce_fusion.3), channel_id=1, source_target_pairs={{0,16},{16,0},{32,48},{48,32},{64,80},{80,64},{96,112},{112,96},{1... | collective-permute-start | bytes 20 | tf_op jit(solution)/shard_map/while/body/eval_jaxpr/ppermute | solution.py:33
  113.2 2.4 %collective-permute-start.3 = (f32[2,32,256]{2,0,1:T(2,128)S(1)}, f32[2,32,256]{2,0,1:T(2,128)S(1)}, u32[]{:S(2)}, u32[]{:S(2)}) collective-permute-start(f32[2,32,256]{2,0,1:T(2,128)S(1)} %slice_bitcast_fusion.11), channel_id=1, source_target_pairs={{16,0},{32,16},{48,32},{64,48},{80,64},{96,80},{112,96},{0,112},{1... | collective-permute-start | bytes 196616 | tf_op jit(solution)/shard_map/while/body/eval_jaxpr/ppermute | solution.py:21
  119.6 2.3 collective-permute-done.1
  122.5 2.3 collective-permute-start.2
  124.8 2.9 %collective-permute-done.2 = f32[]{:T(128)} collective-permute-done((f32[]{:T(128)}, f32[]{:T(128)}, u32[]{:S(2)}, u32[]{:S(2)}) %collective-permute-start.2) | collective-permute-done | bytes 36 | tf_op jit(solution)/shard_map/while/body/eval_jaxpr/ppermute | solution.py:33
  128.9 2.4 %collective-permute-start.7 = (f32[]{:T(128)}, f32[]{:T(128)}, u32[]{:S(2)}, u32[]{:S(2)}) collective-permute-start(f32[]{:T(128)} %add.181), channel_id=1, source_target_pairs={{0,2},{2,0},{4,6},{6,4},{8,10},{10,8},{12,14},{14,12},{1,3},{3,1},... | collective-permute-start | bytes 20 | tf_op jit(solution)/shard_map/while/body/eval_jaxpr/ppermute | solution.py:33
  131.9 2.0 collective-permute-start.8
  133.9 1.7 collective-permute-done.8
  136.2 3.0 %collective-permute-start.9 = (f32[]{:T(128)}, f32[]{:T(128)}, u32[]{:S(2)}, u32[]{:S(2)}) collective-permute-start(f32[]{:T(128)} %add.183), channel_id=1, source_target_pairs={{0,8},{2,10},{4,12},{6,14},{8,0},{10,2},{12,4},{14,6},{1,9},{3,11}... | collective-permute-start | bytes 20 | tf_op jit(solution)/shard_map/while/body/eval_jaxpr/ppermute | solution.py:33
  139.1 2.3 collective-permute-done.9
  143.9 1.6 slice.95
  145.5 2.0 pad_maximum_fusion.1
  147.6 5.6 %fusion.54 = f32[256,3,3,256]{0,3,2,1:T(8,128)S(1)} fusion(bf16[8,18,34,256]{3,0,2,1:T(8,128)(2,1)S(1)} %pad_maximum_fusion.1, bf16[4,16,32,256]{3,2,1,0:T(8,128)(2,1)S(1)} %copy-done.7), kind=kOutput, calls=%fused_computation.66 | convolution fusion | flops 2415919104 | bytes 4661248 | tf_op jit(solution)/shard_map/conv_general_dilated | solution.py:113
  155.8 2.5 %fusion.49 = bf16[18,1,8,5,256]{4,2,3,0,1:T(8,128)(2,1)S(1)} fusion(bf16[3,3,256,256]{3,2,1,0:T(8,128)(2,1)} %get-tuple-element.185, bf16[20,1,7,2,256]{4,2,3,0,1:T(8,128)(2,1)} %slice.95, bf16[20,1,8,5,256]{4,2,3,0,1:T(8,128)(2,1)} %copy.37, pred[8,5]{0,1:T(8,128)(4,1)S(1)} %copy-done.20), kind=kOutput, calls=%fused_computation.57 | convolution fusion | flops 851619840 | bytes 2101288 | tf_op jit(solution)/shard_map/conv_general_dilated | solution.py:56
  159.1 2.4 %select_reduce_fusion = (f32[]{:T(128)}, f32[16,8,5,256]{3,1,2,0:T(8,128)}) fusion(pred[8,5]{0,1:T(8,128)(4,1)S(1)} %copy-done.18, bf16[3,3,256,256]{3,2,1,0:T(8,128)(2,1)S(1)} %copy-done.14, bf16[18,1,7,2,256]{4,2,3,0,1:T(8,128)(2,1)S(1)} %slice.96, bf16[18,1,8,5,256]{4,2,3,0,1:T(8,128)(2,1)S(1)} %fusion.49), kind=kOutput, calls=%fused_computation.69 | convolution fusion | flops 757014528 | bytes 2332716 | tf_op jit(solution)/shard_map/conv_general_dilated | solution.py:56
  162.9 3.5 %collective-permute-start.25 = (f32[2]{0:T(128)S(1)}, f32[2]{0:T(128)S(1)}, u32[]{:S(2)}, u32[]{:S(2)}) collective-permute-start(f32[2]{0:T(128)S(1)} %pad_maximum_fusion.12), channel_id=1, source_target_pairs={{0,16},{16,0},{32,48},{48,32},{64,80},{80,64},{96,112},{112,96},{1... | collective-permute-start | bytes 32 | tf_op jit(solution)/shard_map/ppermute | solution.py:33
  170.7 10.2 %collective-permute-done.26 = f32[2]{0:T(128)S(1)} collective-permute-done((f32[2]{0:T(128)S(1)}, f32[2]{0:T(128)S(1)}, u32[]{:S(2)}, u32[]{:S(2)}) %collective-permute-start.26) | collective-permute-done | bytes 40 | tf_op jit(solution)/shard_map/ppermute | solution.py:33
  182.3 1.8 collective-permute-start.27
  184.1 3.2 %collective-permute-done.27 = f32[2]{0:T(128)S(1)} collective-permute-done((f32[2]{0:T(128)S(1)}, f32[2]{0:T(128)S(1)}, u32[]{:S(2)}, u32[]{:S(2)}) %collective-permute-start.27) | collective-permute-done | bytes 40 | tf_op jit(solution)/shard_map/ppermute | solution.py:33
  189.2 2.9 %collective-permute-done.29 = f32[2]{0:T(128)S(1)} collective-permute-done((f32[2]{0:T(128)S(1)}, f32[2]{0:T(128)S(1)}, u32[]{:S(2)}, u32[]{:S(2)}) %collective-permute-start.29) | collective-permute-done | bytes 40 | tf_op jit(solution)/shard_map/ppermute | solution.py:33
  193.6 3.5 %collective-permute-done.30 = f32[2]{0:T(128)S(1)} collective-permute-done((f32[2]{0:T(128)S(1)}, f32[2]{0:T(128)S(1)}, u32[]{:S(2)}, u32[]{:S(2)}) %collective-permute-start.30) | collective-permute-done | bytes 40 | tf_op jit(solution)/shard_map/ppermute | solution.py:33
  202.5 8.4 %collective-permute-done.15 = f32[64,2304]{1,0:T(8,128)S(1)} collective-permute-done((f32[64,2304]{1,0:T(8,128)S(1)}, f32[64,2304]{1,0:T(8,128)S(1)}, u32[]{:S(2)}, u32[]{:S(2)}) %collective-permute-start.15) | collective-permute-done | bytes 589856 | tf_op jit(solution)/shard_map/ppermute | solution.py:48
  211.0 3.6 %collective-permute-start.16 = (f32[32,2304]{1,0:T(8,128)S(1)}, f32[32,2304]{1,0:T(8,128)S(1)}, u32[]{:S(2)}, u32[]{:S(2)}) collective-permute-start(f32[32,2304]{1,0:T(8,128)S(1)} %constant_dynamic-slice_fusion.3), channel_id=1, source_target_pairs={{0,16},{16,0},{32,48},{48,32},{64,80},{80,64},{96,112},{112,96},{1... | collective-permute-start | bytes 884744 | tf_op jit(solution)/shard_map/ppermute | solution.py:48
  216.6 2.7 %collective-permute-done.16 = f32[32,2304]{1,0:T(8,128)S(1)} collective-permute-done((f32[32,2304]{1,0:T(8,128)S(1)}, f32[32,2304]{1,0:T(8,128)S(1)}, u32[]{:S(2)}, u32[]{:S(2)}) %collective-permute-start.16) | collective-permute-done | bytes 294944 | tf_op jit(solution)/shard_map/ppermute | solution.py:48
  219.4 1.9 collective-permute-start.17
  221.3 3.5 %select_convert_fusion.1 = bf16[16,32,5,256]{3,1,2,0:T(8,128)(2,1)S(1)} fusion(bf16[3,3,256,256]{3,2,1,0:T(8,128)(2,1)S(1)} %copy-done.15, bf16[18,4,7,2,256]{4,2,1,3,0:T(8,128)(2,1)S(1)} %slice.88, bf16[18,4,8,5,256]{4,2,1,3,0:T(8,128)(2,1)S(1)} %copy.27, pred[32,5]{0,1:T(8,128)(4,1)S(1)} %copy-done.17), kind=kOutput, calls=%fused_computation.39 | convolution fusion | flops 3027402752 | bytes 4481184 | tf_op jit(solution)/shard_map/conv_general_dilated | solution.py:56
  227.9 3.4 %select_convert_fusion = bf16[16,32,5,256]{3,1,2,0:T(8,128)(2,1)S(1)} fusion(bf16[3,3,256,256]{3,2,1,0:T(8,128)(2,1)S(1)} %copy-done.15, bf16[18,4,7,2,256]{4,2,1,3,0:T(8,128)(2,1)S(1)} %slice.91, bf16[18,4,8,5,256]{4,2,1,3,0:T(8,128)(2,1)S(1)} %copy.30, pred[32,5]{0,1:T(8,128)(4,1)S(1)} %copy-done.17), kind=kOutput, calls=%fused_computation.38 | convolution fusion | flops 3027402752 | bytes 4481184 | tf_op jit(solution)/shard_map/conv_general_dilated | solution.py:56
  (218 shorter events, 70.7 us)
Async XLA Ops:
  2.1 9.3 %collective-permute-start.22 = (bf16[2,32,256]{2,0,1:T(2,128)(2,1)S(1)}, bf16[2,32,256]{2,0,1:T(2,128)(2,1)S(1)}, u32[]{:S(2)}, u32[]{:S(2)}) collective-permute-start(bf16[2,32,256]{2,0,1:T(2,128)(2,1)S(1)} %get-tuple-element.70), channel_id=1, source_target_pairs={{16,0},{32,16},{48,32},{64,48},{80,64},{96,80},{112,96},{0,112},{1... | collective-permute-start | bytes 98312 | tf_op jit(solution)/shard_map/ppermute | solution.py:21
  8.4 7.5 %collective-permute-start.21 = (bf16[2,32,256]{2,0,1:T(2,128)(2,1)S(1)}, bf16[2,32,256]{2,0,1:T(2,128)(2,1)S(1)}, u32[]{:S(2)}, u32[]{:S(2)}) collective-permute-start(bf16[2,32,256]{2,0,1:T(2,128)(2,1)S(1)} %get-tuple-element.69), channel_id=1, source_target_pairs={{0,16},{16,32},{32,48},{48,64},{64,80},{80,96},{96,112},{112,0},{1... | collective-permute-start | bytes 98312 | tf_op jit(solution)/shard_map/ppermute | solution.py:19
  15.9 8.8 %collective-permute-start.24 = (bf16[20,2,256]{2,0,1:T(8,128)(2,1)S(1)}, bf16[20,2,256]{2,0,1:T(8,128)(2,1)S(1)}, u32[]{:S(2)}, u32[]{:S(2)}) collective-permute-start(bf16[20,2,256]{2,0,1:T(8,128)(2,1)S(1)} %get-tuple-element.68), channel_id=1, source_target_pairs={{2,0},{4,2},{6,4},{8,6},{10,8},{12,10},{14,12},{0,14},{3,1},{5,3},... | collective-permute-start | bytes 61448 | tf_op jit(solution)/shard_map/ppermute | solution.py:21
  16.9 7.8 %collective-permute-start.23 = (bf16[20,2,256]{2,0,1:T(8,128)(2,1)S(1)}, bf16[20,2,256]{2,0,1:T(8,128)(2,1)S(1)}, u32[]{:S(2)}, u32[]{:S(2)}) collective-permute-start(bf16[20,2,256]{2,0,1:T(8,128)(2,1)S(1)} %get-tuple-element.67), channel_id=1, source_target_pairs={{0,2},{2,4},{4,6},{6,8},{8,10},{10,12},{12,14},{14,0},{1,3},{3,5},... | collective-permute-start | bytes 61448 | tf_op jit(solution)/shard_map/ppermute | solution.py:19
  17.1 9.5 %collective-permute-start.11 = (bf16[8,1,32,256]{3,0,2,1:T(8,128)(2,1)S(1)}, bf16[8,1,32,256]{3,0,2,1:T(8,128)(2,1)S(1)}, u32[]{:S(2)}, u32[]{:S(2)}) collective-permute-start(bf16[8,1,32,256]{3,0,2,1:T(8,128)(2,1)S(1)} %get-tuple-element.66), channel_id=1, source_target_pairs={{16,0},{32,16},{48,32},{64,48},{80,64},{96,80},{112,96},{17,1},{33... | collective-permute-start | bytes 393224 | tf_op jit(solution)/shard_map/ppermute | solution.py:21
  18.4 9.4 %collective-permute-start.10 = (bf16[8,1,32,256]{3,0,2,1:T(8,128)(2,1)S(1)}, bf16[8,1,32,256]{3,0,2,1:T(8,128)(2,1)S(1)}, u32[]{:S(2)}, u32[]{:S(2)}) collective-permute-start(bf16[8,1,32,256]{3,0,2,1:T(8,128)(2,1)S(1)} %get-tuple-element.65), channel_id=1, source_target_pairs={{0,16},{16,32},{32,48},{48,64},{64,80},{80,96},{96,112},{1,17},{17... | collective-permute-start | bytes 393224 | tf_op jit(solution)/shard_map/ppermute | solution.py:19
  28.5 117.0 %collective-permute-start.13 = (bf16[8,18,1,256]{3,0,2,1:T(8,128)(2,1)}, bf16[8,18,1,256]{3,0,2,1:T(8,128)(2,1)}, u32[]{:S(2)}, u32[]{:S(2)}) collective-permute-start(bf16[8,18,1,256]{3,0,2,1:T(8,128)(2,1)} %get-tuple-element.64), channel_id=1, source_target_pairs={{2,0},{4,2},{6,4},{8,6},{10,8},{12,10},{14,12},{3,1},{5,3},{7,5},{... | collective-permute-start | bytes 221192 | tf_op jit(solution)/shard_map/ppermute | solution.py:21
  29.8 115.7 %collective-permute-start.12 = (bf16[8,18,1,256]{3,0,2,1:T(8,128)(2,1)S(1)}, bf16[8,18,1,256]{3,0,2,1:T(8,128)(2,1)}, u32[]{:S(2)}, u32[]{:S(2)}) collective-permute-start(bf16[8,18,1,256]{3,0,2,1:T(8,128)(2,1)S(1)} %get-tuple-element.63), channel_id=1, source_target_pairs={{0,2},{2,4},{4,6},{6,8},{8,10},{10,12},{12,14},{1,3},{3,5},{5,7},{... | collective-permute-start | bytes 221192 | tf_op jit(solution)/shard_map/ppermute | solution.py:19
  37.8 7.8 %collective-permute-start = (f32[]{:T(128)}, f32[]{:T(128)}, u32[]{:S(2)}, u32[]{:S(2)}) collective-permute-start(f32[]{:T(128)} %multiply_reduce_fusion.3), channel_id=1, source_target_pairs={{0,16},{16,0},{32,48},{48,32},{64,80},{80,64},{96,112},{112,96},{1... | collective-permute-start | bytes 20 | tf_op jit(solution)/shard_map/while/body/eval_jaxpr/ppermute | solution.py:33
  41.8 15.0 %collective-permute-start.3 = (f32[2,32,256]{2,0,1:T(2,128)S(1)}, f32[2,32,256]{2,0,1:T(2,128)S(1)}, u32[]{:S(2)}, u32[]{:S(2)}) collective-permute-start(f32[2,32,256]{2,0,1:T(2,128)S(1)} %slice_bitcast_fusion.11), channel_id=1, source_target_pairs={{16,0},{32,16},{48,32},{64,48},{80,64},{96,80},{112,96},{0,112},{1... | collective-permute-start | bytes 196616 | tf_op jit(solution)/shard_map/while/body/eval_jaxpr/ppermute | solution.py:21
  43.1 13.8 %collective-permute-start.4 = (f32[2,32,256]{2,0,1:T(2,128)S(1)}, f32[2,32,256]{2,0,1:T(2,128)S(1)}, u32[]{:S(2)}, u32[]{:S(2)}) collective-permute-start(f32[2,32,256]{2,0,1:T(2,128)S(1)} %slice_bitcast_fusion.13), channel_id=1, source_target_pairs={{0,16},{16,32},{32,48},{48,64},{64,80},{80,96},{96,112},{112,0},{1... | collective-permute-start | bytes 196616 | tf_op jit(solution)/shard_map/while/body/eval_jaxpr/ppermute | solution.py:19
  46.8 3.7 %collective-permute-start.1 = (f32[]{:T(128)}, f32[]{:T(128)}, u32[]{:S(2)}, u32[]{:S(2)}) collective-permute-start(f32[]{:T(128)} %add.179), channel_id=1, source_target_pairs={{0,32},{16,48},{32,0},{48,16},{64,96},{80,112},{96,64},{112,80},{1... | collective-permute-start | bytes 20 | tf_op jit(solution)/shard_map/while/body/eval_jaxpr/ppermute | solution.py:33
  51.1 5.2 %collective-permute-start.2 = (f32[]{:T(128)}, f32[]{:T(128)}, u32[]{:S(2)}, u32[]{:S(2)}) collective-permute-start(f32[]{:T(128)} %add.180), channel_id=1, source_target_pairs={{0,64},{16,80},{32,96},{48,112},{64,0},{80,16},{96,32},{112,48},{1... | collective-permute-start | bytes 20 | tf_op jit(solution)/shard_map/while/body/eval_jaxpr/ppermute | solution.py:33
  57.0 13.8 %collective-permute-start.5 = (f32[20,2,256]{2,0,1:T(8,128)S(1)}, f32[20,2,256]{2,0,1:T(8,128)S(1)}, u32[]{:S(2)}, u32[]{:S(2)}) collective-permute-start(f32[20,2,256]{2,0,1:T(8,128)S(1)} %get-tuple-element.113), channel_id=1, source_target_pairs={{2,0},{4,2},{6,4},{8,6},{10,8},{12,10},{14,12},{0,14},{3,1},{5,3},... | collective-permute-start | bytes 122888 | tf_op jit(solution)/shard_map/while/body/eval_jaxpr/ppermute | solution.py:21
  57.0 13.7 %collective-permute-start.6 = (f32[20,2,256]{2,0,1:T(8,128)S(1)}, f32[20,2,256]{2,0,1:T(8,128)S(1)}, u32[]{:S(2)}, u32[]{:S(2)}) collective-permute-start(f32[20,2,256]{2,0,1:T(8,128)S(1)} %get-tuple-element.114), channel_id=1, source_target_pairs={{0,2},{2,4},{4,6},{6,8},{8,10},{10,12},{12,14},{14,0},{1,3},{3,5},... | collective-permute-start | bytes 122888 | tf_op jit(solution)/shard_map/while/body/eval_jaxpr/ppermute | solution.py:19
  59.8 3.7 %collective-permute-start.8 = (f32[]{:T(128)}, f32[]{:T(128)}, u32[]{:S(2)}, u32[]{:S(2)}) collective-permute-start(f32[]{:T(128)} %add.182), channel_id=1, source_target_pairs={{0,4},{2,6},{4,0},{6,2},{8,12},{10,14},{12,8},{14,10},{1,5},{3,7},... | collective-permute-start | bytes 20 | tf_op jit(solution)/shard_map/while/body/eval_jaxpr/ppermute | solution.py:33
  64.1 5.2 %collective-permute-start.9 = (f32[]{:T(128)}, f32[]{:T(128)}, u32[]{:S(2)}, u32[]{:S(2)}) collective-permute-start(f32[]{:T(128)} %add.183), channel_id=1, source_target_pairs={{0,8},{2,10},{4,12},{6,14},{8,0},{10,2},{12,4},{14,6},{1,9},{3,11}... | collective-permute-start | bytes 20 | tf_op jit(solution)/shard_map/while/body/eval_jaxpr/ppermute | solution.py:33
  75.2 5.3 %collective-permute-start = (f32[]{:T(128)}, f32[]{:T(128)}, u32[]{:S(2)}, u32[]{:S(2)}) collective-permute-start(f32[]{:T(128)} %multiply_reduce_fusion.3), channel_id=1, source_target_pairs={{0,16},{16,0},{32,48},{48,32},{64,80},{80,64},{96,112},{112,96},{1... | collective-permute-start | bytes 20 | tf_op jit(solution)/shard_map/while/body/eval_jaxpr/ppermute | solution.py:33
  76.7 15.0 %collective-permute-start.3 = (f32[2,32,256]{2,0,1:T(2,128)S(1)}, f32[2,32,256]{2,0,1:T(2,128)S(1)}, u32[]{:S(2)}, u32[]{:S(2)}) collective-permute-start(f32[2,32,256]{2,0,1:T(2,128)S(1)} %slice_bitcast_fusion.11), channel_id=1, source_target_pairs={{16,0},{32,16},{48,32},{64,48},{80,64},{96,80},{112,96},{0,112},{1... | collective-permute-start | bytes 196616 | tf_op jit(solution)/shard_map/while/body/eval_jaxpr/ppermute | solution.py:21
  78.6 13.1 %collective-permute-start.4 = (f32[2,32,256]{2,0,1:T(2,128)S(1)}, f32[2,32,256]{2,0,1:T(2,128)S(1)}, u32[]{:S(2)}, u32[]{:S(2)}) collective-permute-start(f32[2,32,256]{2,0,1:T(2,128)S(1)} %slice_bitcast_fusion.13), channel_id=1, source_target_pairs={{0,16},{16,32},{32,48},{48,64},{64,80},{80,96},{96,112},{112,0},{1... | collective-permute-start | bytes 196616 | tf_op jit(solution)/shard_map/while/body/eval_jaxpr/ppermute | solution.py:19
  81.6 3.7 %collective-permute-start.1 = (f32[]{:T(128)}, f32[]{:T(128)}, u32[]{:S(2)}, u32[]{:S(2)}) collective-permute-start(f32[]{:T(128)} %add.179), channel_id=1, source_target_pairs={{0,32},{16,48},{32,0},{48,16},{64,96},{80,112},{96,64},{112,80},{1... | collective-permute-start | bytes 20 | tf_op jit(solution)/shard_map/while/body/eval_jaxpr/ppermute | solution.py:33
  85.9 5.2 %collective-permute-start.2 = (f32[]{:T(128)}, f32[]{:T(128)}, u32[]{:S(2)}, u32[]{:S(2)}) collective-permute-start(f32[]{:T(128)} %add.180), channel_id=1, source_target_pairs={{0,64},{16,80},{32,96},{48,112},{64,0},{80,16},{96,32},{112,48},{1... | collective-permute-start | bytes 20 | tf_op jit(solution)/shard_map/while/body/eval_jaxpr/ppermute | solution.py:33
  91.9 13.9 %collective-permute-start.5 = (f32[20,2,256]{2,0,1:T(8,128)S(1)}, f32[20,2,256]{2,0,1:T(8,128)S(1)}, u32[]{:S(2)}, u32[]{:S(2)}) collective-permute-start(f32[20,2,256]{2,0,1:T(8,128)S(1)} %get-tuple-element.113), channel_id=1, source_target_pairs={{2,0},{4,2},{6,4},{8,6},{10,8},{12,10},{14,12},{0,14},{3,1},{5,3},... | collective-permute-start | bytes 122888 | tf_op jit(solution)/shard_map/while/body/eval_jaxpr/ppermute | solution.py:21
  91.9 13.9 %collective-permute-start.6 = (f32[20,2,256]{2,0,1:T(8,128)S(1)}, f32[20,2,256]{2,0,1:T(8,128)S(1)}, u32[]{:S(2)}, u32[]{:S(2)}) collective-permute-start(f32[20,2,256]{2,0,1:T(8,128)S(1)} %get-tuple-element.114), channel_id=1, source_target_pairs={{0,2},{2,4},{4,6},{6,8},{8,10},{10,12},{12,14},{14,0},{1,3},{3,5},... | collective-permute-start | bytes 122888 | tf_op jit(solution)/shard_map/while/body/eval_jaxpr/ppermute | solution.py:19
  92.4 1.9 collective-permute-start.7
  94.8 3.7 %collective-permute-start.8 = (f32[]{:T(128)}, f32[]{:T(128)}, u32[]{:S(2)}, u32[]{:S(2)}) collective-permute-start(f32[]{:T(128)} %add.182), channel_id=1, source_target_pairs={{0,4},{2,6},{4,0},{6,2},{8,12},{10,14},{12,8},{14,10},{1,5},{3,7},... | collective-permute-start | bytes 20 | tf_op jit(solution)/shard_map/while/body/eval_jaxpr/ppermute | solution.py:33
  99.1 5.2 %collective-permute-start.9 = (f32[]{:T(128)}, f32[]{:T(128)}, u32[]{:S(2)}, u32[]{:S(2)}) collective-permute-start(f32[]{:T(128)} %add.183), channel_id=1, source_target_pairs={{0,8},{2,10},{4,12},{6,14},{8,0},{10,2},{12,4},{14,6},{1,9},{3,11}... | collective-permute-start | bytes 20 | tf_op jit(solution)/shard_map/while/body/eval_jaxpr/ppermute | solution.py:33
  110.1 6.9 %collective-permute-start = (f32[]{:T(128)}, f32[]{:T(128)}, u32[]{:S(2)}, u32[]{:S(2)}) collective-permute-start(f32[]{:T(128)} %multiply_reduce_fusion.3), channel_id=1, source_target_pairs={{0,16},{16,0},{32,48},{48,32},{64,80},{80,64},{96,112},{112,96},{1... | collective-permute-start | bytes 20 | tf_op jit(solution)/shard_map/while/body/eval_jaxpr/ppermute | solution.py:33
  113.2 15.0 %collective-permute-start.3 = (f32[2,32,256]{2,0,1:T(2,128)S(1)}, f32[2,32,256]{2,0,1:T(2,128)S(1)}, u32[]{:S(2)}, u32[]{:S(2)}) collective-permute-start(f32[2,32,256]{2,0,1:T(2,128)S(1)} %slice_bitcast_fusion.11), channel_id=1, source_target_pairs={{16,0},{32,16},{48,32},{64,48},{80,64},{96,80},{112,96},{0,112},{1... | collective-permute-start | bytes 196616 | tf_op jit(solution)/shard_map/while/body/eval_jaxpr/ppermute | solution.py:21
  115.7 12.6 %collective-permute-start.4 = (f32[2,32,256]{2,0,1:T(2,128)S(1)}, f32[2,32,256]{2,0,1:T(2,128)S(1)}, u32[]{:S(2)}, u32[]{:S(2)}) collective-permute-start(f32[2,32,256]{2,0,1:T(2,128)S(1)} %slice_bitcast_fusion.13), channel_id=1, source_target_pairs={{0,16},{16,32},{32,48},{48,64},{64,80},{80,96},{96,112},{112,0},{1... | collective-permute-start | bytes 196616 | tf_op jit(solution)/shard_map/while/body/eval_jaxpr/ppermute | solution.py:19
  118.2 3.7 %collective-permute-start.1 = (f32[]{:T(128)}, f32[]{:T(128)}, u32[]{:S(2)}, u32[]{:S(2)}) collective-permute-start(f32[]{:T(128)} %add.179), channel_id=1, source_target_pairs={{0,32},{16,48},{32,0},{48,16},{64,96},{80,112},{96,64},{112,80},{1... | collective-permute-start | bytes 20 | tf_op jit(solution)/shard_map/while/body/eval_jaxpr/ppermute | solution.py:33
  122.5 5.2 %collective-permute-start.2 = (f32[]{:T(128)}, f32[]{:T(128)}, u32[]{:S(2)}, u32[]{:S(2)}) collective-permute-start(f32[]{:T(128)} %add.180), channel_id=1, source_target_pairs={{0,64},{16,80},{32,96},{48,112},{64,0},{80,16},{96,32},{112,48},{1... | collective-permute-start | bytes 20 | tf_op jit(solution)/shard_map/while/body/eval_jaxpr/ppermute | solution.py:33
  128.4 14.4 %collective-permute-start.5 = (f32[20,2,256]{2,0,1:T(8,128)S(1)}, f32[20,2,256]{2,0,1:T(8,128)S(1)}, u32[]{:S(2)}, u32[]{:S(2)}) collective-permute-start(f32[20,2,256]{2,0,1:T(8,128)S(1)} %get-tuple-element.113), channel_id=1, source_target_pairs={{2,0},{4,2},{6,4},{8,6},{10,8},{12,10},{14,12},{0,14},{3,1},{5,3},... | collective-permute-start | bytes 122888 | tf_op jit(solution)/shard_map/while/body/eval_jaxpr/ppermute | solution.py:21
  128.4 14.4 %collective-permute-start.6 = (f32[20,2,256]{2,0,1:T(8,128)S(1)}, f32[20,2,256]{2,0,1:T(8,128)S(1)}, u32[]{:S(2)}, u32[]{:S(2)}) collective-permute-start(f32[20,2,256]{2,0,1:T(8,128)S(1)} %get-tuple-element.114), channel_id=1, source_target_pairs={{0,2},{2,4},{4,6},{6,8},{8,10},{10,12},{12,14},{14,0},{1,3},{3,5},... | collective-permute-start | bytes 122888 | tf_op jit(solution)/shard_map/while/body/eval_jaxpr/ppermute | solution.py:19
  128.9 2.4 %collective-permute-start.7 = (f32[]{:T(128)}, f32[]{:T(128)}, u32[]{:S(2)}, u32[]{:S(2)}) collective-permute-start(f32[]{:T(128)} %add.181), channel_id=1, source_target_pairs={{0,2},{2,0},{4,6},{6,4},{8,10},{10,8},{12,14},{14,12},{1,3},{3,1},... | collective-permute-start | bytes 20 | tf_op jit(solution)/shard_map/while/body/eval_jaxpr/ppermute | solution.py:33
  131.9 3.7 %collective-permute-start.8 = (f32[]{:T(128)}, f32[]{:T(128)}, u32[]{:S(2)}, u32[]{:S(2)}) collective-permute-start(f32[]{:T(128)} %add.182), channel_id=1, source_target_pairs={{0,4},{2,6},{4,0},{6,2},{8,12},{10,14},{12,8},{14,10},{1,5},{3,7},... | collective-permute-start | bytes 20 | tf_op jit(solution)/shard_map/while/body/eval_jaxpr/ppermute | solution.py:33
  136.2 5.2 %collective-permute-start.9 = (f32[]{:T(128)}, f32[]{:T(128)}, u32[]{:S(2)}, u32[]{:S(2)}) collective-permute-start(f32[]{:T(128)} %add.183), channel_id=1, source_target_pairs={{0,8},{2,10},{4,12},{6,14},{8,0},{10,2},{12,4},{14,6},{1,9},{3,11}... | collective-permute-start | bytes 20 | tf_op jit(solution)/shard_map/while/body/eval_jaxpr/ppermute | solution.py:33
  154.9 42.6 %collective-permute-start.14 = (f32[128,2304]{1,0:T(8,128)}, f32[128,2304]{1,0:T(8,128)S(1)}, u32[]{:S(2)}, u32[]{:S(2)}) collective-permute-start(f32[128,2304]{1,0:T(8,128)} %copy.43), channel_id=1, source_target_pairs={{0,64},{16,80},{32,96},{48,112},{64,0},{80,16},{96,32},{112,48},{1... | collective-permute-start | bytes 3538952 | tf_op jit(solution)/shard_map/ppermute | solution.py:48
  162.9 5.1 %collective-permute-start.25 = (f32[2]{0:T(128)S(1)}, f32[2]{0:T(128)S(1)}, u32[]{:S(2)}, u32[]{:S(2)}) collective-permute-start(f32[2]{0:T(128)S(1)} %pad_maximum_fusion.12), channel_id=1, source_target_pairs={{0,16},{16,0},{32,48},{48,32},{64,80},{80,64},{96,112},{112,96},{1... | collective-permute-start | bytes 32 | tf_op jit(solution)/shard_map/ppermute | solution.py:33
  169.3 11.6 %collective-permute-start.26 = (f32[2]{0:T(128)S(1)}, f32[2]{0:T(128)S(1)}, u32[]{:S(2)}, u32[]{:S(2)}) collective-permute-start(f32[2]{0:T(128)S(1)} %fusion.94), channel_id=1, source_target_pairs={{0,32},{16,48},{32,0},{48,16},{64,96},{80,112},{96,64},{112,80},{1... | collective-permute-start | bytes 32 | tf_op jit(solution)/shard_map/ppermute | solution.py:33
  182.3 5.1 %collective-permute-start.27 = (f32[2]{0:T(128)S(1)}, f32[2]{0:T(128)S(1)}, u32[]{:S(2)}, u32[]{:S(2)}) collective-permute-start(f32[2]{0:T(128)S(1)} %fusion.95), channel_id=1, source_target_pairs={{0,64},{16,80},{32,96},{48,112},{64,0},{80,16},{96,32},{112,48},{1... | collective-permute-start | bytes 32 | tf_op jit(solution)/shard_map/ppermute | solution.py:33
  188.5 3.5 %collective-permute-start.29 = (f32[2]{0:T(128)S(1)}, f32[2]{0:T(128)S(1)}, u32[]{:S(2)}, u32[]{:S(2)}) collective-permute-start(f32[2]{0:T(128)S(1)} %add.156), channel_id=1, source_target_pairs={{0,4},{2,6},{4,0},{6,2},{8,12},{10,14},{12,8},{14,10},{1,5},{3,7},... | collective-permute-start | bytes 32 | tf_op jit(solution)/shard_map/ppermute | solution.py:33
  192.0 5.0 %collective-permute-start.30 = (f32[2]{0:T(128)S(1)}, f32[2]{0:T(128)S(1)}, u32[]{:S(2)}, u32[]{:S(2)}) collective-permute-start(f32[2]{0:T(128)S(1)} %add.157), channel_id=1, source_target_pairs={{0,8},{2,10},{4,12},{6,14},{8,0},{10,2},{12,4},{14,6},{1,9},{3,11}... | collective-permute-start | bytes 32 | tf_op jit(solution)/shard_map/ppermute | solution.py:33
  197.7 13.2 %collective-permute-start.15 = (f32[64,2304]{1,0:T(8,128)S(1)}, f32[64,2304]{1,0:T(8,128)S(1)}, u32[]{:S(2)}, u32[]{:S(2)}) collective-permute-start(f32[64,2304]{1,0:T(8,128)S(1)} %constant_dynamic-slice_fusion.4), channel_id=1, source_target_pairs={{0,32},{16,48},{32,0},{48,16},{64,96},{80,112},{96,64},{112,80},{1... | collective-permute-start | bytes 1769480 | tf_op jit(solution)/shard_map/ppermute | solution.py:48
  211.0 8.3 %collective-permute-start.16 = (f32[32,2304]{1,0:T(8,128)S(1)}, f32[32,2304]{1,0:T(8,128)S(1)}, u32[]{:S(2)}, u32[]{:S(2)}) collective-permute-start(f32[32,2304]{1,0:T(8,128)S(1)} %constant_dynamic-slice_fusion.3), channel_id=1, source_target_pairs={{0,16},{16,0},{32,48},{48,32},{64,80},{80,64},{96,112},{112,96},{1... | collective-permute-start | bytes 884744 | tf_op jit(solution)/shard_map/ppermute | solution.py:48
  219.4 7.6 %collective-permute-start.17 = (f32[16,2304]{1,0:T(8,128)S(1)}, f32[16,2304]{1,0:T(8,128)S(1)}, u32[]{:S(2)}, u32[]{:S(2)}) collective-permute-start(f32[16,2304]{1,0:T(8,128)S(1)} %constant_dynamic-slice_fusion.2), channel_id=1, source_target_pairs={{0,8},{2,10},{4,12},{6,14},{8,0},{10,2},{12,4},{14,6},{1,9},{3,11}... | collective-permute-start | bytes 442376 | tf_op jit(solution)/shard_map/ppermute | solution.py:48
  227.0 5.1 %collective-permute-start.18 = (f32[8,2304]{1,0:T(8,128)S(1)}, f32[8,2304]{1,0:T(8,128)S(1)}, u32[]{:S(2)}, u32[]{:S(2)}) collective-permute-start(f32[8,2304]{1,0:T(8,128)S(1)} %constant_dynamic-slice_fusion.1), channel_id=1, source_target_pairs={{0,4},{2,6},{4,0},{6,2},{8,12},{10,14},{12,8},{14,10},{1,5},{3,7},... | collective-permute-start | bytes 221192 | tf_op jit(solution)/shard_map/ppermute | solution.py:48
  233.5 4.0 %collective-permute-start.20 = (f32[4,2304]{1,0:T(4,128)S(1)}, f32[4,2304]{1,0:T(4,128)S(1)}, u32[]{:S(2)}, u32[]{:S(2)}) collective-permute-start(f32[4,2304]{1,0:T(4,128)S(1)} %dynamic-slice_add_fusion.4), channel_id=1, source_target_pairs={{0,1},{1,0},{2,3},{3,2},{4,5},{5,4},{6,7},{7,6},{8,9},{9,8},{10,11... | collective-permute-start | bytes 110600 | tf_op jit(solution)/shard_map/ppermute | solution.py:33
  (26 other events, 138.9 us)

commit v3 on v2

--- a/solution.py
+++ b/solution.py
@@ -89,20 +89,6 @@
         padded_probe = (padded_back / scale_now).astype(jnp.bfloat16)
         return (padded_probe, iterate), scale_now
 
-    (padded_probe, iterate), norm_trace = lax.scan(
-        power_step, (padded_probe, iterate), None, length=ITERS - 1
-    )
-    image = conv(padded_probe[None], kernel, False).astype(jnp.bfloat16)
-    back = conv(image, kernel, True)[0]
-    wide_iter = iterate.astype(jnp.float32)
-    totals = butterfly_sum(
-        jnp.stack([jnp.sum(back * back), jnp.sum(wide_iter * wide_iter)]),
-        ("rows", "cols"),
-    )
-    sum_back = totals[0]
-    sum_probe = totals[1]
-    lipschitz = jnp.sqrt(jnp.sqrt(sum_back / sum_probe))
-    probe_out = back / jnp.sqrt(sum_back / count + 1e-06)
     padded_both = extended(
         jnp.concatenate([inputs, upstream], axis=0), (("rows", 1), ("cols", 2)), 1, False
     )
@@ -118,7 +104,23 @@
         dimension_numbers=("CHWN", "IHWO", "CHWN"),
         preferred_element_type=jnp.float32,
     ).reshape(channels, 9 * channels)
-    owned = halving_scatter(local_grad, ("rows", "cols"))
+    owned = halving_scatter(local_grad, ("rows",))
+    owned, padded_probe = lax.optimization_barrier((owned, padded_probe))
+    (padded_probe, iterate), norm_trace = lax.scan(
+        power_step, (padded_probe, iterate), None, length=ITERS - 1
+    )
+    image = conv(padded_probe[None], kernel, False).astype(jnp.bfloat16)
+    back = conv(image, kernel, True)[0]
+    wide_iter = iterate.astype(jnp.float32)
+    totals = butterfly_sum(
+        jnp.stack([jnp.sum(back * back), jnp.sum(wide_iter * wide_iter)]),
+        ("rows", "cols"),
+    )
+    sum_back = totals[0]
+    sum_probe = totals[1]
+    lipschitz = jnp.sqrt(jnp.sqrt(sum_back / sum_probe))
+    probe_out = back / jnp.sqrt(sum_back / count + 1e-06)
+    owned = halving_scatter(owned, ("cols",))
     owned = butterfly_sum(owned, ("rep",))
     total_cells = batch * lax.axis_size("rep") * height * rows_count * breadth * cols_count
     kernel_grad = owned * (1.0 / math.sqrt(total_cells))

time: 241 us -> 256 us (1.062)
  matrix products: 23.5 us -> 33.8 us
  starting transfers between devices: 96.1 us -> 103 us
  waiting for transfers between devices: 64.8 us -> 60.9 us
    ppermute x6, waiting for transfers between devices: 12.4 us -> 30.4 us  [halving_scatter(): lax.ppermute(send, axis, [(i, i ^ step) for i in range(count)])]
    ppermute x25, waiting for transfers between devices: 45.1 us -> 30.5 us  [butterfly_sum(): lax.ppermute(value, axis, [(i, i ^ step) for i in range(count)])]
    conv_general_dilated x10, matrix products: 17.8 us -> 28.2 us  [conv(): lax.conv_general_dilated(padded, weights, window_strides=(1, 1), padding=...]
    ppermute x10, waiting for transfers between devices: 5.7 us -> 0.03 us  [extended(): lax.ppermute(tail, axis, [(i, (i + 1) % count) for i in range(ends)])]
    ppermute x6, starting transfers between devices: 8.19 us -> 13.2 us  [halving_scatter(): lax.ppermute(send, axis, [(i, i ^ step) for i in range(count)])]
    while x6 -> x0, local copies, waits for them, and re-layouts: 3.25 us -> none
    ppermute x10, starting transfers between devices: 15.4 us -> 18.2 us  [extended(): lax.ppermute(head, axis, [((i + 1) % count, i) for i in range(ends)])]
    unnamed x48 -> x50, local copies, waits for them, and re-layouts: 10 us -> 11.6 us
  transfers between devices with their start and end apart: 51 -> 51, of which waited for: 26 -> 25; matrix products, arithmetic and copies ran while one was open for 19% -> 25% of each run, Pallas kernels for 0% -> 0%
where the time goes in v3:
time: 256 us; the launch traced here: 254 us
  starting transfers between devices  103 us (40%)
  waiting for transfers between devices  60.9 us (24%)
  matrix products  33.8 us (13%)
  local copies, waits for them, and re-layouts  22.2 us (9%)
  other arithmetic  15.1 us (6%)
  loops' own time  14.8 us (6%)
  between operations  4.48 us (2%)
    ppermute x25, starting transfers between devices, butterfly_sum(): lax.ppermute(value, axis, [(i, i ^ step) for i in range(count)])  56.9 us
    ppermute x25, waiting for transfers between devices, butterfly_sum(): lax.ppermute(value, axis, [(i, i ^ step) for i in range(count)])  30.5 us
    ppermute x6, waiting for transfers between devices, halving_scatter(): lax.ppermute(send, axis, [(i, i ^ step) for i in range(count)])  30.4 us
    conv_general_dilated x10, matrix products, conv(): lax.conv_general_dilated(padded, weights, window_strides=(1, 1), padding=...  28.2 us
    ppermute x10, starting transfers between devices, extended(): lax.ppermute(head, axis, [((i + 1) % count, i) for i in range(ends)])  18.2 us
    ppermute x10, starting transfers between devices, extended(): lax.ppermute(tail, axis, [(i, (i + 1) % count) for i in range(ends)])  14.8 us
    another operation x1, loops' own time, per_device(): lax.scan(power_step, (padded_probe, iterate), None, length=ITERS - 1)  14.8 us
    ppermute x6, starting transfers between devices, halving_scatter(): lax.ppermute(send, axis, [(i, i ^ step) for i in range(count)])  13.2 us
  transfers between devices with their start and end apart: 51, of which 25 were waited for; matrix products, arithmetic and copies ran while one was open for 25% of the time, Pallas kernels for 0%

profile of v3, /device:TPU:0, one launch (start us, length us, event | category | flops | bytes accessed | tf_op | source)
XLA Modules:
  0.0 254.4 jit_solution(7237057070941639143)
XLA Ops:
  0.6 2.2 copy.25
  5.2 6.5 %collective-permute-start.10 = (bf16[8,1,32,256]{3,0,2,1:T(8,128)(2,1)S(1)}, bf16[8,1,32,256]{3,0,2,1:T(8,128)(2,1)S(1)}, u32[]{:S(2)}, u32[]{:S(2)}) collective-permute-start(bf16[8,1,32,256]{3,0,2,1:T(8,128)(2,1)S(1)} %get-tuple-element.69), channel_id=1, source_target_pairs={{0,16},{16,32},{32,48},{48,64},{64,80},{80,96},{96,112},{1,17},{17... | collective-permute-start | bytes 393224 | tf_op jit(solution)/shard_map/ppermute | solution.py:19
  13.4 3.3 %collective-permute-start.17 = (bf16[2,32,256]{2,0,1:T(2,128)(2,1)S(1)}, bf16[2,32,256]{2,0,1:T(2,128)(2,1)S(1)}, u32[]{:S(2)}, u32[]{:S(2)}) collective-permute-start(bf16[2,32,256]{2,0,1:T(2,128)(2,1)S(1)} %get-tuple-element.73), channel_id=1, source_target_pairs={{0,16},{16,32},{32,48},{48,64},{64,80},{80,96},{96,112},{112,0},{1... | collective-permute-start | bytes 98312 | tf_op jit(solution)/shard_map/ppermute | solution.py:19
  18.0 3.0 %collective-permute-start.12 = (bf16[8,18,1,256]{3,0,2,1:T(8,128)(2,1)S(1)}, bf16[8,18,1,256]{3,0,2,1:T(8,128)(2,1)S(1)}, u32[]{:S(2)}, u32[]{:S(2)}) collective-permute-start(bf16[8,18,1,256]{3,0,2,1:T(8,128)(2,1)S(1)} %get-tuple-element.67), channel_id=1, source_target_pairs={{0,2},{2,4},{4,6},{6,8},{8,10},{10,12},{12,14},{1,3},{3,5},{5,7},{... | collective-permute-start | bytes 221192 | tf_op jit(solution)/shard_map/ppermute | solution.py:19
  21.8 2.0 collective-permute-start.20
  25.0 5.6 %fusion.54 = f32[256,3,3,256]{0,3,2,1:T(8,128)S(1)} fusion(bf16[8,18,34,256]{3,0,2,1:T(8,128)(2,1)S(1)} %pad_maximum_fusion.1, bf16[4,16,32,256]{3,2,1,0:T(8,128)(2,1)S(1)} %copy-done.10), kind=kOutput, calls=%fused_computation.66 | convolution fusion | flops 2415919104 | bytes 4661248 | tf_op jit(solution)/shard_map/conv_general_dilated | solution.py:99
  32.3 2.9 %copy.43 = f32[128,2304]{1,0:T(8,128)} copy(f32[128,2304]{0,1:T(8,128)} %get-tuple-element.65) | data formatting | bytes 2359296
  35.1 5.5 %collective-permute-start.14 = (f32[128,2304]{1,0:T(8,128)}, f32[128,2304]{1,0:T(8,128)}, u32[]{:S(2)}, u32[]{:S(2)}) collective-permute-start(f32[128,2304]{1,0:T(8,128)} %copy.43), channel_id=1, source_target_pairs={{0,64},{16,80},{32,96},{48,112},{64,0},{80,16},{96,32},{112,48},{1... | collective-permute-start | bytes 3538952 | tf_op jit(solution)/shard_map/ppermute | solution.py:48
  43.8 4.8 %select_convert_fusion.1 = bf16[16,32,5,256]{3,1,2,0:T(8,128)(2,1)S(1)} fusion(bf16[3,3,256,256]{3,2,1,0:T(8,128)(2,1)} %param.8, bf16[18,4,7,2,256]{4,2,1,3,0:T(8,128)(2,1)S(1)} %slice.88, bf16[18,4,8,5,256]{4,2,1,3,0:T(8,128)(2,1)S(1)} %copy.27, pred[32,5]{0,1:T(8,128)(4,1)S(1)} %copy-done.20), kind=kOutput, calls=%fused_computation.39 | convolution fusion | flops 3027402752 | bytes 4481184 | tf_op jit(solution)/shard_map/conv_general_dilated | solution.py:56
  53.0 14.5 %collective-permute-done.14 = f32[128,2304]{1,0:T(8,128)} collective-permute-done((f32[128,2304]{1,0:T(8,128)}, f32[128,2304]{1,0:T(8,128)}, u32[]{:S(2)}, u32[]{:S(2)}) %collective-permute-start.14) | collective-permute-done | bytes 1179680 | tf_op jit(solution)/shard_map/ppermute | solution.py:48
  68.9 2.2 collective-permute-start.15
  71.2 4.7 %select_convert_fusion = bf16[16,32,5,256]{3,1,2,0:T(8,128)(2,1)S(1)} fusion(bf16[3,3,256,256]{3,2,1,0:T(8,128)(2,1)} %param.8, bf16[18,4,7,2,256]{4,2,1,3,0:T(8,128)(2,1)S(1)} %slice.91, bf16[18,4,8,5,256]{4,2,1,3,0:T(8,128)(2,1)S(1)} %copy-done.8, pred[32,5]{0,1:T(8,128)(4,1)S(1)} %copy-done.20), kind=kOutput, calls=%fused_computation.38 | convolution fusion | flops 3027402752 | bytes 4481184 | tf_op jit(solution)/shard_map/conv_general_dilated | solution.py:56
  75.8 8.9 %collective-permute-done.15 = f32[64,2304]{1,0:T(8,128)S(1)} collective-permute-done((f32[64,2304]{1,0:T(8,128)S(1)}, f32[64,2304]{1,0:T(8,128)S(1)}, u32[]{:S(2)}, u32[]{:S(2)}) %collective-permute-start.15) | collective-permute-done | bytes 589856 | tf_op jit(solution)/shard_map/ppermute | solution.py:48
  84.8 2.5 collective-permute-start.16
  90.9 4.2 %collective-permute-done.16 = f32[32,2304]{1,0:T(8,128)S(1)} collective-permute-done((f32[32,2304]{1,0:T(8,128)S(1)}, f32[32,2304]{1,0:T(8,128)S(1)}, u32[]{:S(2)}, u32[]{:S(2)}) %collective-permute-start.16) | collective-permute-done | bytes 294944 | tf_op jit(solution)/shard_map/ppermute | solution.py:48
  96.8 112.3 %while.14 = (s32[]{:T(128)}, bf16[20,36,256]{2,0,1:T(8,128)(2,1)S(1)}, bf16[16,32,256]{2,0,1:T(8,128)(2,1)}, f32[3]{0:T(128)S(1)}, bf16[3,3,256,256]{3,2,1,0:T(8...) while((s32[]{:T(128)}, bf16[20,36,256]{2,0,1:T(8,128)(2,1)S(1)}, ...), condition=%wide.region_2.3_spmd, body=%wide.region_0.2_spmd.sunk | while | flops 1609732096 | bytes 14596871 | solution.py:109
  97.0 2.3 fusion.109
  99.3 2.2 fusion.110
  104.1 4.2 %collective-permute-start.3 = (f32[2,32,256]{2,0,1:T(2,128)S(1)}, f32[2,32,256]{2,0,1:T(2,128)S(1)}, u32[]{:S(2)}, u32[]{:S(2)}) collective-permute-start(f32[2,32,256]{2,0,1:T(2,128)S(1)} %slice_bitcast_fusion.11), channel_id=1, source_target_pairs={{16,0},{32,16},{48,32},{64,48},{80,64},{96,80},{112,96},{0,112},{1... | collective-permute-start | bytes 196616 | tf_op jit(solution)/shard_map/while/body/eval_jaxpr/ppermute | solution.py:21
  109.8 2.3 collective-permute-start.1
  114.0 3.8 %collective-permute-start.2 = (f32[]{:T(128)}, f32[]{:T(128)}, u32[]{:S(2)}, u32[]{:S(2)}) collective-permute-start(f32[]{:T(128)} %add.180), channel_id=1, source_target_pairs={{0,64},{16,80},{32,96},{48,112},{64,0},{80,16},{96,32},{112,48},{1... | collective-permute-start | bytes 20 | tf_op jit(solution)/shard_map/while/body/eval_jaxpr/ppermute | solution.py:33
  122.3 3.0 %collective-permute-start.8 = (f32[]{:T(128)}, f32[]{:T(128)}, u32[]{:S(2)}, u32[]{:S(2)}) collective-permute-start(f32[]{:T(128)} %add.182), channel_id=1, source_target_pairs={{0,4},{2,6},{4,0},{6,2},{8,12},{10,14},{12,8},{14,10},{1,5},{3,7},... | collective-permute-start | bytes 20 | tf_op jit(solution)/shard_map/while/body/eval_jaxpr/ppermute | solution.py:33
  126.5 4.2 %collective-permute-start.9 = (f32[]{:T(128)}, f32[]{:T(128)}, u32[]{:S(2)}, u32[]{:S(2)}) collective-permute-start(f32[]{:T(128)} %add.183), channel_id=1, source_target_pairs={{0,8},{2,10},{4,12},{6,14},{8,0},{10,2},{12,4},{14,6},{1,9},{3,11}... | collective-permute-start | bytes 20 | tf_op jit(solution)/shard_map/while/body/eval_jaxpr/ppermute | solution.py:33
  133.4 2.3 fusion.109
  135.8 2.2 fusion.110
  139.0 2.4 collective-permute-start
  141.4 3.3 %collective-permute-start.3 = (f32[2,32,256]{2,0,1:T(2,128)S(1)}, f32[2,32,256]{2,0,1:T(2,128)S(1)}, u32[]{:S(2)}, u32[]{:S(2)}) collective-permute-start(f32[2,32,256]{2,0,1:T(2,128)S(1)} %slice_bitcast_fusion.11), channel_id=1, source_target_pairs={{16,0},{32,16},{48,32},{64,48},{80,64},{96,80},{112,96},{0,112},{1... | collective-permute-start | bytes 196616 | tf_op jit(solution)/shard_map/while/body/eval_jaxpr/ppermute | solution.py:21
  146.5 2.5 collective-permute-start.1
  150.8 4.7 %collective-permute-start.2 = (f32[]{:T(128)}, f32[]{:T(128)}, u32[]{:S(2)}, u32[]{:S(2)}) collective-permute-start(f32[]{:T(128)} %add.180), channel_id=1, source_target_pairs={{0,64},{16,80},{32,96},{48,112},{64,0},{80,16},{96,32},{112,48},{1... | collective-permute-start | bytes 20 | tf_op jit(solution)/shard_map/while/body/eval_jaxpr/ppermute | solution.py:33
  159.7 2.6 %collective-permute-start.8 = (f32[]{:T(128)}, f32[]{:T(128)}, u32[]{:S(2)}, u32[]{:S(2)}) collective-permute-start(f32[]{:T(128)} %add.182), channel_id=1, source_target_pairs={{0,4},{2,6},{4,0},{6,2},{8,12},{10,14},{12,8},{14,10},{1,5},{3,7},... | collective-permute-start | bytes 20 | tf_op jit(solution)/shard_map/while/body/eval_jaxpr/ppermute | solution.py:33
  164.0 4.0 %collective-permute-start.9 = (f32[]{:T(128)}, f32[]{:T(128)}, u32[]{:S(2)}, u32[]{:S(2)}) collective-permute-start(f32[]{:T(128)} %add.183), channel_id=1, source_target_pairs={{0,8},{2,10},{4,12},{6,14},{8,0},{10,2},{12,4},{14,6},{1,9},{3,11}... | collective-permute-start | bytes 20 | tf_op jit(solution)/shard_map/while/body/eval_jaxpr/ppermute | solution.py:33
  170.9 2.3 fusion.109
  173.2 2.2 fusion.110
  176.4 2.3 collective-permute-start
  178.8 4.8 %collective-permute-start.3 = (f32[2,32,256]{2,0,1:T(2,128)S(1)}, f32[2,32,256]{2,0,1:T(2,128)S(1)}, u32[]{:S(2)}, u32[]{:S(2)}) collective-permute-start(f32[2,32,256]{2,0,1:T(2,128)S(1)} %slice_bitcast_fusion.11), channel_id=1, source_target_pairs={{16,0},{32,16},{48,32},{64,48},{80,64},{96,80},{112,96},{0,112},{1... | collective-permute-start | bytes 196616 | tf_op jit(solution)/shard_map/while/body/eval_jaxpr/ppermute | solution.py:21
  186.5 2.2 collective-permute-done.1
  189.4 3.5 %collective-permute-start.2 = (f32[]{:T(128)}, f32[]{:T(128)}, u32[]{:S(2)}, u32[]{:S(2)}) collective-permute-start(f32[]{:T(128)} %add.180), channel_id=1, source_target_pairs={{0,64},{16,80},{32,96},{48,112},{64,0},{80,16},{96,32},{112,48},{1... | collective-permute-start | bytes 20 | tf_op jit(solution)/shard_map/while/body/eval_jaxpr/ppermute | solution.py:33
  198.1 2.6 %collective-permute-start.8 = (f32[]{:T(128)}, f32[]{:T(128)}, u32[]{:S(2)}, u32[]{:S(2)}) collective-permute-start(f32[]{:T(128)} %add.182), channel_id=1, source_target_pairs={{0,4},{2,6},{4,0},{6,2},{8,12},{10,14},{12,8},{14,10},{1,5},{3,7},... | collective-permute-start | bytes 20 | tf_op jit(solution)/shard_map/while/body/eval_jaxpr/ppermute | solution.py:33
  202.3 3.3 %collective-permute-start.9 = (f32[]{:T(128)}, f32[]{:T(128)}, u32[]{:S(2)}, u32[]{:S(2)}) collective-permute-start(f32[]{:T(128)} %add.183), channel_id=1, source_target_pairs={{0,8},{2,10},{4,12},{6,14},{8,0},{10,2},{12,4},{14,6},{1,9},{3,11}... | collective-permute-start | bytes 20 | tf_op jit(solution)/shard_map/while/body/eval_jaxpr/ppermute | solution.py:33
  209.3 2.3 fusion.49
  212.5 2.9 %select_reduce_fusion = (f32[]{:T(128)}, f32[16,8,5,256]{3,1,2,0:T(8,128)S(1)}) fusion(pred[8,5]{0,1:T(8,128)(4,1)S(1)} %copy-done.18, bf16[3,3,256,256]{3,2,1,0:T(8,128)(2,1)} %param.8, bf16[18,1,7,2,256]{4,2,3,0,1:T(8,128)(2,1)S(1)} %slice.96, bf16[18,1,8,5,256]{4,2,3,0,1:T(8,128)(2,1)S(1)} %fusion.49), kind=kOutput, calls=%fused_computation.69 | convolution fusion | flops 757014528 | bytes 2332716 | tf_op jit(solution)/shard_map/conv_general_dilated | solution.py:56
  216.7 2.1 collective-permute-start.25
  218.8 2.9 %collective-permute-done.25 = f32[2]{0:T(128)S(1)} collective-permute-done((f32[2]{0:T(128)S(1)}, f32[2]{0:T(128)S(1)}, u32[]{:S(2)}, u32[]{:S(2)}) %collective-permute-start.25) | collective-permute-done | bytes 40 | tf_op jit(solution)/shard_map/ppermute | solution.py:33
  223.1 3.5 %collective-permute-done.26 = f32[2]{0:T(128)S(1)} collective-permute-done((f32[2]{0:T(128)S(1)}, f32[2]{0:T(128)S(1)}, u32[]{:S(2)}, u32[]{:S(2)}) %collective-permute-start.26) | collective-permute-done | bytes 40 | tf_op jit(solution)/shard_map/ppermute | solution.py:33
  228.0 2.1 collective-permute-start.27
  230.2 2.9 %collective-permute-done.27 = f32[2]{0:T(128)S(1)} collective-permute-done((f32[2]{0:T(128)S(1)}, f32[2]{0:T(128)S(1)}, u32[]{:S(2)}, u32[]{:S(2)}) %collective-permute-start.27) | collective-permute-done | bytes 40 | tf_op jit(solution)/shard_map/ppermute | solution.py:33
  235.5 2.3 collective-permute-done.29
  239.7 3.1 %collective-permute-done.30 = f32[2]{0:T(128)S(1)} collective-permute-done((f32[2]{0:T(128)S(1)}, f32[2]{0:T(128)S(1)}, u32[]{:S(2)}, u32[]{:S(2)}) %collective-permute-start.30) | collective-permute-done | bytes 40 | tf_op jit(solution)/shard_map/ppermute | solution.py:33
  (214 shorter events, 69.0 us)
Async XLA Ops:
  3.9 12.8 %collective-permute-start.11 = (bf16[8,1,32,256]{3,0,2,1:T(8,128)(2,1)S(1)}, bf16[8,1,32,256]{3,0,2,1:T(8,128)(2,1)S(1)}, u32[]{:S(2)}, u32[]{:S(2)}) collective-permute-start(bf16[8,1,32,256]{3,0,2,1:T(8,128)(2,1)S(1)} %get-tuple-element.70), channel_id=1, source_target_pairs={{16,0},{32,16},{48,32},{64,48},{80,64},{96,80},{112,96},{17,1},{33... | collective-permute-start | bytes 393224 | tf_op jit(solution)/shard_map/ppermute | solution.py:21
  5.2 11.5 %collective-permute-start.10 = (bf16[8,1,32,256]{3,0,2,1:T(8,128)(2,1)S(1)}, bf16[8,1,32,256]{3,0,2,1:T(8,128)(2,1)S(1)}, u32[]{:S(2)}, u32[]{:S(2)}) collective-permute-start(bf16[8,1,32,256]{3,0,2,1:T(8,128)(2,1)S(1)} %get-tuple-element.69), channel_id=1, source_target_pairs={{0,16},{16,32},{32,48},{48,64},{64,80},{80,96},{96,112},{1,17},{17... | collective-permute-start | bytes 393224 | tf_op jit(solution)/shard_map/ppermute | solution.py:19
  12.1 9.0 %collective-permute-start.18 = (bf16[2,32,256]{2,0,1:T(2,128)(2,1)S(1)}, bf16[2,32,256]{2,0,1:T(2,128)(2,1)S(1)}, u32[]{:S(2)}, u32[]{:S(2)}) collective-permute-start(bf16[2,32,256]{2,0,1:T(2,128)(2,1)S(1)} %get-tuple-element.74), channel_id=1, source_target_pairs={{16,0},{32,16},{48,32},{64,48},{80,64},{96,80},{112,96},{0,112},{1... | collective-permute-start | bytes 98312 | tf_op jit(solution)/shard_map/ppermute | solution.py:21
  13.4 7.7 %collective-permute-start.17 = (bf16[2,32,256]{2,0,1:T(2,128)(2,1)S(1)}, bf16[2,32,256]{2,0,1:T(2,128)(2,1)S(1)}, u32[]{:S(2)}, u32[]{:S(2)}) collective-permute-start(bf16[2,32,256]{2,0,1:T(2,128)(2,1)S(1)} %get-tuple-element.73), channel_id=1, source_target_pairs={{0,16},{16,32},{32,48},{48,64},{64,80},{80,96},{96,112},{112,0},{1... | collective-permute-start | bytes 98312 | tf_op jit(solution)/shard_map/ppermute | solution.py:19
  16.7 7.0 %collective-permute-start.13 = (bf16[8,18,1,256]{3,0,2,1:T(8,128)(2,1)S(1)}, bf16[8,18,1,256]{3,0,2,1:T(8,128)(2,1)S(1)}, u32[]{:S(2)}, u32[]{:S(2)}) collective-permute-start(bf16[8,18,1,256]{3,0,2,1:T(8,128)(2,1)S(1)} %get-tuple-element.68), channel_id=1, source_target_pairs={{2,0},{4,2},{6,4},{8,6},{10,8},{12,10},{14,12},{3,1},{5,3},{7,5},{... | collective-permute-start | bytes 221192 | tf_op jit(solution)/shard_map/ppermute | solution.py:21
  18.0 5.7 %collective-permute-start.12 = (bf16[8,18,1,256]{3,0,2,1:T(8,128)(2,1)S(1)}, bf16[8,18,1,256]{3,0,2,1:T(8,128)(2,1)S(1)}, u32[]{:S(2)}, u32[]{:S(2)}) collective-permute-start(bf16[8,18,1,256]{3,0,2,1:T(8,128)(2,1)S(1)} %get-tuple-element.67), channel_id=1, source_target_pairs={{0,2},{2,4},{4,6},{6,8},{8,10},{10,12},{12,14},{1,3},{3,5},{5,7},{... | collective-permute-start | bytes 221192 | tf_op jit(solution)/shard_map/ppermute | solution.py:19
  21.8 18.8 %collective-permute-start.20 = (bf16[20,2,256]{2,0,1:T(8,128)(2,1)}, bf16[20,2,256]{2,0,1:T(8,128)(2,1)}, u32[]{:S(2)}, u32[]{:S(2)}) collective-permute-start(bf16[20,2,256]{2,0,1:T(8,128)(2,1)} %get-tuple-element.72), channel_id=1, source_target_pairs={{2,0},{4,2},{6,4},{8,6},{10,8},{12,10},{14,12},{0,14},{3,1},{5,3},... | collective-permute-start | bytes 61448 | tf_op jit(solution)/shard_map/ppermute | solution.py:21
  23.8 16.8 %collective-permute-start.19 = (bf16[20,2,256]{2,0,1:T(8,128)(2,1)}, bf16[20,2,256]{2,0,1:T(8,128)(2,1)}, u32[]{:S(2)}, u32[]{:S(2)}) collective-permute-start(bf16[20,2,256]{2,0,1:T(8,128)(2,1)} %get-tuple-element.71), channel_id=1, source_target_pairs={{0,2},{2,4},{4,6},{6,8},{8,10},{10,12},{12,14},{14,0},{1,3},{3,5},... | collective-permute-start | bytes 61448 | tf_op jit(solution)/shard_map/ppermute | solution.py:19
  35.1 32.4 %collective-permute-start.14 = (f32[128,2304]{1,0:T(8,128)}, f32[128,2304]{1,0:T(8,128)}, u32[]{:S(2)}, u32[]{:S(2)}) collective-permute-start(f32[128,2304]{1,0:T(8,128)} %copy.43), channel_id=1, source_target_pairs={{0,64},{16,80},{32,96},{48,112},{64,0},{80,16},{96,32},{112,48},{1... | collective-permute-start | bytes 3538952 | tf_op jit(solution)/shard_map/ppermute | solution.py:48
  68.9 15.8 %collective-permute-start.15 = (f32[64,2304]{1,0:T(8,128)S(1)}, f32[64,2304]{1,0:T(8,128)S(1)}, u32[]{:S(2)}, u32[]{:S(2)}) collective-permute-start(f32[64,2304]{1,0:T(8,128)S(1)} %constant_dynamic-slice_fusion.4), channel_id=1, source_target_pairs={{0,32},{16,48},{32,0},{48,16},{64,96},{80,112},{96,64},{112,80},{1... | collective-permute-start | bytes 1769480 | tf_op jit(solution)/shard_map/ppermute | solution.py:48
  84.8 10.2 %collective-permute-start.16 = (f32[32,2304]{1,0:T(8,128)S(1)}, f32[32,2304]{1,0:T(8,128)S(1)}, u32[]{:S(2)}, u32[]{:S(2)}) collective-permute-start(f32[32,2304]{1,0:T(8,128)S(1)} %constant_dynamic-slice_fusion.3), channel_id=1, source_target_pairs={{0,16},{16,0},{32,48},{48,32},{64,80},{80,64},{96,112},{112,96},{1... | collective-permute-start | bytes 884744 | tf_op jit(solution)/shard_map/ppermute | solution.py:48
  95.1 147.7 %collective-permute-start.21 = (f32[16,2304]{1,0:T(8,128)S(1)}, f32[16,2304]{1,0:T(8,128)S(1)}, u32[]{:S(2)}, u32[]{:S(2)}) collective-permute-start(f32[16,2304]{1,0:T(8,128)S(1)} %constant_dynamic-slice_fusion.2), channel_id=1, source_target_pairs={{0,8},{2,10},{4,12},{6,14},{8,0},{10,2},{12,4},{14,6},{1,9},{3,11}... | collective-permute-start | bytes 442376 | tf_op jit(solution)/shard_map/ppermute | solution.py:48
  102.5 5.9 %collective-permute-start = (f32[]{:T(128)}, f32[]{:T(128)}, u32[]{:S(2)}, u32[]{:S(2)}) collective-permute-start(f32[]{:T(128)} %multiply_reduce_fusion.3), channel_id=1, source_target_pairs={{0,16},{16,0},{32,48},{48,32},{64,80},{80,64},{96,112},{112,96},{1... | collective-permute-start | bytes 20 | tf_op jit(solution)/shard_map/while/body/eval_jaxpr/ppermute | solution.py:33
  104.1 15.7 %collective-permute-start.3 = (f32[2,32,256]{2,0,1:T(2,128)S(1)}, f32[2,32,256]{2,0,1:T(2,128)S(1)}, u32[]{:S(2)}, u32[]{:S(2)}) collective-permute-start(f32[2,32,256]{2,0,1:T(2,128)S(1)} %slice_bitcast_fusion.11), channel_id=1, source_target_pairs={{16,0},{32,16},{48,32},{64,48},{80,64},{96,80},{112,96},{0,112},{1... | collective-permute-start | bytes 196616 | tf_op jit(solution)/shard_map/while/body/eval_jaxpr/ppermute | solution.py:21
  108.3 11.5 %collective-permute-start.4 = (f32[2,32,256]{2,0,1:T(2,128)S(1)}, f32[2,32,256]{2,0,1:T(2,128)S(1)}, u32[]{:S(2)}, u32[]{:S(2)}) collective-permute-start(f32[2,32,256]{2,0,1:T(2,128)S(1)} %slice_bitcast_fusion.13), channel_id=1, source_target_pairs={{0,16},{16,32},{32,48},{48,64},{64,80},{80,96},{96,112},{112,0},{1... | collective-permute-start | bytes 196616 | tf_op jit(solution)/shard_map/while/body/eval_jaxpr/ppermute | solution.py:19
  109.8 3.6 %collective-permute-start.1 = (f32[]{:T(128)}, f32[]{:T(128)}, u32[]{:S(2)}, u32[]{:S(2)}) collective-permute-start(f32[]{:T(128)} %add.179), channel_id=1, source_target_pairs={{0,32},{16,48},{32,0},{48,16},{64,96},{80,112},{96,64},{112,80},{1... | collective-permute-start | bytes 20 | tf_op jit(solution)/shard_map/while/body/eval_jaxpr/ppermute | solution.py:33
  114.0 5.1 %collective-permute-start.2 = (f32[]{:T(128)}, f32[]{:T(128)}, u32[]{:S(2)}, u32[]{:S(2)}) collective-permute-start(f32[]{:T(128)} %add.180), channel_id=1, source_target_pairs={{0,64},{16,80},{32,96},{48,112},{64,0},{80,16},{96,32},{112,48},{1... | collective-permute-start | bytes 20 | tf_op jit(solution)/shard_map/while/body/eval_jaxpr/ppermute | solution.py:33
  120.0 13.2 %collective-permute-start.5 = (f32[20,2,256]{2,0,1:T(8,128)S(1)}, f32[20,2,256]{2,0,1:T(8,128)S(1)}, u32[]{:S(2)}, u32[]{:S(2)}) collective-permute-start(f32[20,2,256]{2,0,1:T(8,128)S(1)} %get-tuple-element.117), channel_id=1, source_target_pairs={{2,0},{4,2},{6,4},{8,6},{10,8},{12,10},{14,12},{0,14},{3,1},{5,3},... | collective-permute-start | bytes 122888 | tf_op jit(solution)/shard_map/while/body/eval_jaxpr/ppermute | solution.py:21
  120.0 13.2 %collective-permute-start.6 = (f32[20,2,256]{2,0,1:T(8,128)S(1)}, f32[20,2,256]{2,0,1:T(8,128)S(1)}, u32[]{:S(2)}, u32[]{:S(2)}) collective-permute-start(f32[20,2,256]{2,0,1:T(8,128)S(1)} %get-tuple-element.118), channel_id=1, source_target_pairs={{0,2},{2,4},{4,6},{6,8},{8,10},{10,12},{12,14},{14,0},{1,3},{3,5},... | collective-permute-start | bytes 122888 | tf_op jit(solution)/shard_map/while/body/eval_jaxpr/ppermute | solution.py:19
  122.3 3.6 %collective-permute-start.8 = (f32[]{:T(128)}, f32[]{:T(128)}, u32[]{:S(2)}, u32[]{:S(2)}) collective-permute-start(f32[]{:T(128)} %add.182), channel_id=1, source_target_pairs={{0,4},{2,6},{4,0},{6,2},{8,12},{10,14},{12,8},{14,10},{1,5},{3,7},... | collective-permute-start | bytes 20 | tf_op jit(solution)/shard_map/while/body/eval_jaxpr/ppermute | solution.py:33
  126.5 5.1 %collective-permute-start.9 = (f32[]{:T(128)}, f32[]{:T(128)}, u32[]{:S(2)}, u32[]{:S(2)}) collective-permute-start(f32[]{:T(128)} %add.183), channel_id=1, source_target_pairs={{0,8},{2,10},{4,12},{6,14},{8,0},{10,2},{12,4},{14,6},{1,9},{3,11}... | collective-permute-start | bytes 20 | tf_op jit(solution)/shard_map/while/body/eval_jaxpr/ppermute | solution.py:33
  139.0 6.2 %collective-permute-start = (f32[]{:T(128)}, f32[]{:T(128)}, u32[]{:S(2)}, u32[]{:S(2)}) collective-permute-start(f32[]{:T(128)} %multiply_reduce_fusion.3), channel_id=1, source_target_pairs={{0,16},{16,0},{32,48},{48,32},{64,80},{80,64},{96,112},{112,96},{1... | collective-permute-start | bytes 20 | tf_op jit(solution)/shard_map/while/body/eval_jaxpr/ppermute | solution.py:33
  141.4 15.1 %collective-permute-start.3 = (f32[2,32,256]{2,0,1:T(2,128)S(1)}, f32[2,32,256]{2,0,1:T(2,128)S(1)}, u32[]{:S(2)}, u32[]{:S(2)}) collective-permute-start(f32[2,32,256]{2,0,1:T(2,128)S(1)} %slice_bitcast_fusion.11), channel_id=1, source_target_pairs={{16,0},{32,16},{48,32},{64,48},{80,64},{96,80},{112,96},{0,112},{1... | collective-permute-start | bytes 196616 | tf_op jit(solution)/shard_map/while/body/eval_jaxpr/ppermute | solution.py:21
  144.8 11.7 %collective-permute-start.4 = (f32[2,32,256]{2,0,1:T(2,128)S(1)}, f32[2,32,256]{2,0,1:T(2,128)S(1)}, u32[]{:S(2)}, u32[]{:S(2)}) collective-permute-start(f32[2,32,256]{2,0,1:T(2,128)S(1)} %slice_bitcast_fusion.13), channel_id=1, source_target_pairs={{0,16},{16,32},{32,48},{48,64},{64,80},{80,96},{96,112},{112,0},{1... | collective-permute-start | bytes 196616 | tf_op jit(solution)/shard_map/while/body/eval_jaxpr/ppermute | solution.py:19
  146.5 3.6 %collective-permute-start.1 = (f32[]{:T(128)}, f32[]{:T(128)}, u32[]{:S(2)}, u32[]{:S(2)}) collective-permute-start(f32[]{:T(128)} %add.179), channel_id=1, source_target_pairs={{0,32},{16,48},{32,0},{48,16},{64,96},{80,112},{96,64},{112,80},{1... | collective-permute-start | bytes 20 | tf_op jit(solution)/shard_map/while/body/eval_jaxpr/ppermute | solution.py:33
  150.8 5.1 %collective-permute-start.2 = (f32[]{:T(128)}, f32[]{:T(128)}, u32[]{:S(2)}, u32[]{:S(2)}) collective-permute-start(f32[]{:T(128)} %add.180), channel_id=1, source_target_pairs={{0,64},{16,80},{32,96},{48,112},{64,0},{80,16},{96,32},{112,48},{1... | collective-permute-start | bytes 20 | tf_op jit(solution)/shard_map/while/body/eval_jaxpr/ppermute | solution.py:33
  156.7 13.9 %collective-permute-start.5 = (f32[20,2,256]{2,0,1:T(8,128)S(1)}, f32[20,2,256]{2,0,1:T(8,128)S(1)}, u32[]{:S(2)}, u32[]{:S(2)}) collective-permute-start(f32[20,2,256]{2,0,1:T(8,128)S(1)} %get-tuple-element.117), channel_id=1, source_target_pairs={{2,0},{4,2},{6,4},{8,6},{10,8},{12,10},{14,12},{0,14},{3,1},{5,3},... | collective-permute-start | bytes 122888 | tf_op jit(solution)/shard_map/while/body/eval_jaxpr/ppermute | solution.py:21
  156.7 13.9 %collective-permute-start.6 = (f32[20,2,256]{2,0,1:T(8,128)S(1)}, f32[20,2,256]{2,0,1:T(8,128)S(1)}, u32[]{:S(2)}, u32[]{:S(2)}) collective-permute-start(f32[20,2,256]{2,0,1:T(8,128)S(1)} %get-tuple-element.118), channel_id=1, source_target_pairs={{0,2},{2,4},{4,6},{6,8},{8,10},{10,12},{12,14},{14,0},{1,3},{3,5},... | collective-permute-start | bytes 122888 | tf_op jit(solution)/shard_map/while/body/eval_jaxpr/ppermute | solution.py:19
  157.2 1.8 collective-permute-start.7
  159.7 3.6 %collective-permute-start.8 = (f32[]{:T(128)}, f32[]{:T(128)}, u32[]{:S(2)}, u32[]{:S(2)}) collective-permute-start(f32[]{:T(128)} %add.182), channel_id=1, source_target_pairs={{0,4},{2,6},{4,0},{6,2},{8,12},{10,14},{12,8},{14,10},{1,5},{3,7},... | collective-permute-start | bytes 20 | tf_op jit(solution)/shard_map/while/body/eval_jaxpr/ppermute | solution.py:33
  164.0 5.1 %collective-permute-start.9 = (f32[]{:T(128)}, f32[]{:T(128)}, u32[]{:S(2)}, u32[]{:S(2)}) collective-permute-start(f32[]{:T(128)} %add.183), channel_id=1, source_target_pairs={{0,8},{2,10},{4,12},{6,14},{8,0},{10,2},{12,4},{14,6},{1,9},{3,11}... | collective-permute-start | bytes 20 | tf_op jit(solution)/shard_map/while/body/eval_jaxpr/ppermute | solution.py:33
  176.4 7.4 %collective-permute-start = (f32[]{:T(128)}, f32[]{:T(128)}, u32[]{:S(2)}, u32[]{:S(2)}) collective-permute-start(f32[]{:T(128)} %multiply_reduce_fusion.3), channel_id=1, source_target_pairs={{0,16},{16,0},{32,48},{48,32},{64,80},{80,64},{96,112},{112,96},{1... | collective-permute-start | bytes 20 | tf_op jit(solution)/shard_map/while/body/eval_jaxpr/ppermute | solution.py:33
  178.8 16.3 %collective-permute-start.3 = (f32[2,32,256]{2,0,1:T(2,128)S(1)}, f32[2,32,256]{2,0,1:T(2,128)S(1)}, u32[]{:S(2)}, u32[]{:S(2)}) collective-permute-start(f32[2,32,256]{2,0,1:T(2,128)S(1)} %slice_bitcast_fusion.11), channel_id=1, source_target_pairs={{16,0},{32,16},{48,32},{64,48},{80,64},{96,80},{112,96},{0,112},{1... | collective-permute-start | bytes 196616 | tf_op jit(solution)/shard_map/while/body/eval_jaxpr/ppermute | solution.py:21
  183.7 11.5 %collective-permute-start.4 = (f32[2,32,256]{2,0,1:T(2,128)S(1)}, f32[2,32,256]{2,0,1:T(2,128)S(1)}, u32[]{:S(2)}, u32[]{:S(2)}) collective-permute-start(f32[2,32,256]{2,0,1:T(2,128)S(1)} %slice_bitcast_fusion.13), channel_id=1, source_target_pairs={{0,16},{16,32},{32,48},{48,64},{64,80},{80,96},{96,112},{112,0},{1... | collective-permute-start | bytes 196616 | tf_op jit(solution)/shard_map/while/body/eval_jaxpr/ppermute | solution.py:19
  185.1 3.6 %collective-permute-start.1 = (f32[]{:T(128)}, f32[]{:T(128)}, u32[]{:S(2)}, u32[]{:S(2)}) collective-permute-start(f32[]{:T(128)} %add.179), channel_id=1, source_target_pairs={{0,32},{16,48},{32,0},{48,16},{64,96},{80,112},{96,64},{112,80},{1... | collective-permute-start | bytes 20 | tf_op jit(solution)/shard_map/while/body/eval_jaxpr/ppermute | solution.py:33
  189.4 5.1 %collective-permute-start.2 = (f32[]{:T(128)}, f32[]{:T(128)}, u32[]{:S(2)}, u32[]{:S(2)}) collective-permute-start(f32[]{:T(128)} %add.180), channel_id=1, source_target_pairs={{0,64},{16,80},{32,96},{48,112},{64,0},{80,16},{96,32},{112,48},{1... | collective-permute-start | bytes 20 | tf_op jit(solution)/shard_map/while/body/eval_jaxpr/ppermute | solution.py:33
  195.3 13.7 %collective-permute-start.5 = (f32[20,2,256]{2,0,1:T(8,128)S(1)}, f32[20,2,256]{2,0,1:T(8,128)S(1)}, u32[]{:S(2)}, u32[]{:S(2)}) collective-permute-start(f32[20,2,256]{2,0,1:T(8,128)S(1)} %get-tuple-element.117), channel_id=1, source_target_pairs={{2,0},{4,2},{6,4},{8,6},{10,8},{12,10},{14,12},{0,14},{3,1},{5,3},... | collective-permute-start | bytes 122888 | tf_op jit(solution)/shard_map/while/body/eval_jaxpr/ppermute | solution.py:21
  195.3 13.7 %collective-permute-start.6 = (f32[20,2,256]{2,0,1:T(8,128)S(1)}, f32[20,2,256]{2,0,1:T(8,128)S(1)}, u32[]{:S(2)}, u32[]{:S(2)}) collective-permute-start(f32[20,2,256]{2,0,1:T(8,128)S(1)} %get-tuple-element.118), channel_id=1, source_target_pairs={{0,2},{2,4},{4,6},{6,8},{8,10},{10,12},{12,14},{14,0},{1,3},{3,5},... | collective-permute-start | bytes 122888 | tf_op jit(solution)/shard_map/while/body/eval_jaxpr/ppermute | solution.py:19
  195.8 1.6 collective-permute-start.7
  198.1 3.6 %collective-permute-start.8 = (f32[]{:T(128)}, f32[]{:T(128)}, u32[]{:S(2)}, u32[]{:S(2)}) collective-permute-start(f32[]{:T(128)} %add.182), channel_id=1, source_target_pairs={{0,4},{2,6},{4,0},{6,2},{8,12},{10,14},{12,8},{14,10},{1,5},{3,7},... | collective-permute-start | bytes 20 | tf_op jit(solution)/shard_map/while/body/eval_jaxpr/ppermute | solution.py:33
  202.3 5.1 %collective-permute-start.9 = (f32[]{:T(128)}, f32[]{:T(128)}, u32[]{:S(2)}, u32[]{:S(2)}) collective-permute-start(f32[]{:T(128)} %add.183), channel_id=1, source_target_pairs={{0,8},{2,10},{4,12},{6,14},{8,0},{10,2},{12,4},{14,6},{1,9},{3,11}... | collective-permute-start | bytes 20 | tf_op jit(solution)/shard_map/while/body/eval_jaxpr/ppermute | solution.py:33
  216.7 5.1 %collective-permute-start.25 = (f32[2]{0:T(128)S(1)}, f32[2]{0:T(128)S(1)}, u32[]{:S(2)}, u32[]{:S(2)}) collective-permute-start(f32[2]{0:T(128)S(1)} %pad_maximum_fusion.12), channel_id=1, source_target_pairs={{0,16},{16,0},{32,48},{48,32},{64,80},{80,64},{96,112},{112,96},{1... | collective-permute-start | bytes 32 | tf_op jit(solution)/shard_map/ppermute | solution.py:33
  223.1 3.6 %collective-permute-start.26 = (f32[2]{0:T(128)S(1)}, f32[2]{0:T(128)S(1)}, u32[]{:S(2)}, u32[]{:S(2)}) collective-permute-start(f32[2]{0:T(128)S(1)} %fusion.94), channel_id=1, source_target_pairs={{0,32},{16,48},{32,0},{48,16},{64,96},{80,112},{96,64},{112,80},{1... | collective-permute-start | bytes 32 | tf_op jit(solution)/shard_map/ppermute | solution.py:33
  228.0 5.1 %collective-permute-start.27 = (f32[2]{0:T(128)S(1)}, f32[2]{0:T(128)S(1)}, u32[]{:S(2)}, u32[]{:S(2)}) collective-permute-start(f32[2]{0:T(128)S(1)} %fusion.95), channel_id=1, source_target_pairs={{0,64},{16,80},{32,96},{48,112},{64,0},{80,16},{96,32},{112,48},{1... | collective-permute-start | bytes 32 | tf_op jit(solution)/shard_map/ppermute | solution.py:33
  234.2 3.5 %collective-permute-start.29 = (f32[2]{0:T(128)S(1)}, f32[2]{0:T(128)S(1)}, u32[]{:S(2)}, u32[]{:S(2)}) collective-permute-start(f32[2]{0:T(128)S(1)} %add.156), channel_id=1, source_target_pairs={{0,4},{2,6},{4,0},{6,2},{8,12},{10,14},{12,8},{14,10},{1,5},{3,7},... | collective-permute-start | bytes 32 | tf_op jit(solution)/shard_map/ppermute | solution.py:33
  237.8 5.0 %collective-permute-start.30 = (f32[2]{0:T(128)S(1)}, f32[2]{0:T(128)S(1)}, u32[]{:S(2)}, u32[]{:S(2)}) collective-permute-start(f32[2]{0:T(128)S(1)} %add.157), channel_id=1, source_target_pairs={{0,8},{2,10},{4,12},{6,14},{8,0},{10,2},{12,4},{14,6},{1,9},{3,11}... | collective-permute-start | bytes 32 | tf_op jit(solution)/shard_map/ppermute | solution.py:33
  242.9 4.4 %collective-permute-start.22 = (f32[8,2304]{1,0:T(8,128)S(1)}, f32[8,2304]{1,0:T(8,128)S(1)}, u32[]{:S(2)}, u32[]{:S(2)}) collective-permute-start(f32[8,2304]{1,0:T(8,128)S(1)} %constant_dynamic-slice_fusion.1), channel_id=1, source_target_pairs={{0,4},{2,6},{4,0},{6,2},{8,12},{10,14},{12,8},{14,10},{1,5},{3,7},... | collective-permute-start | bytes 221192 | tf_op jit(solution)/shard_map/ppermute | solution.py:48
  248.6 4.0 %collective-permute-start.24 = (f32[4,2304]{1,0:T(4,128)S(1)}, f32[4,2304]{1,0:T(4,128)S(1)}, u32[]{:S(2)}, u32[]{:S(2)}) collective-permute-start(f32[4,2304]{1,0:T(4,128)S(1)} %dynamic-slice_add_fusion.4), channel_id=1, source_target_pairs={{0,1},{1,0},{2,3},{3,2},{4,5},{5,4},{6,7},{7,6},{8,9},{9,8},{10,11... | collective-permute-start | bytes 110600 | tf_op jit(solution)/shard_map/ppermute | solution.py:33
  (24 other events, 127.6 us)

commit v4 on v3

--- a/solution.py
+++ b/solution.py
@@ -104,8 +104,9 @@
         dimension_numbers=("CHWN", "IHWO", "CHWN"),
         preferred_element_type=jnp.float32,
     ).reshape(channels, 9 * channels)
-    owned = halving_scatter(local_grad, ("rows",))
-    owned, padded_probe = lax.optimization_barrier((owned, padded_probe))
+    local_grad, outputs, input_grad, padded_probe = lax.optimization_barrier(
+        (local_grad, outputs, input_grad, padded_probe)
+    )
     (padded_probe, iterate), norm_trace = lax.scan(
         power_step, (padded_probe, iterate), None, length=ITERS - 1
     )
@@ -120,7 +121,7 @@
     sum_probe = totals[1]
     lipschitz = jnp.sqrt(jnp.sqrt(sum_back / sum_probe))
     probe_out = back / jnp.sqrt(sum_back / count + 1e-06)
-    owned = halving_scatter(owned, ("cols",))
+    owned = halving_scatter(local_grad, ("rows", "cols"))
     owned = butterfly_sum(owned, ("rep",))
     total_cells = batch * lax.axis_size("rep") * height * rows_count * breadth * cols_count
     kernel_grad = owned * (1.0 / math.sqrt(total_cells))

time: 256 us -> 240 us (0.938)
  matrix products: 33.8 us -> 22.1 us
  waiting for transfers between devices: 60.9 us -> 52.8 us
  starting transfers between devices: 103 us -> 107 us
    ppermute x6, waiting for transfers between devices: 30.4 us -> 12.8 us  [halving_scatter(): lax.ppermute(send, axis, [(i, i ^ step) for i in range(count)])]
    conv_general_dilated x10, matrix products: 28.2 us -> 15.2 us  [conv(): lax.conv_general_dilated(padded, weights, window_strides=(1, 1), padding=...]
    ppermute x25, waiting for transfers between devices: 30.5 us -> 38.9 us  [butterfly_sum(): lax.ppermute(value, axis, [(i, i ^ step) for i in range(count)])]
    ppermute x25, starting transfers between devices: 56.9 us -> 63.5 us  [butterfly_sum(): lax.ppermute(value, axis, [(i, i ^ step) for i in range(count)])]
    unnamed x50 -> x32, local copies, waits for them, and re-layouts: 11.6 us -> 8.28 us
    while x0 -> x6, local copies, waits for them, and re-layouts: none -> 3.25 us
  transfers between devices with their start and end apart: 51 -> 51, of which waited for: 25 -> 25; matrix products, arithmetic and copies ran while one was open for 25% -> 11% of each run, Pallas kernels for 0% -> 0%
where the time goes in v4:
time: 240 us; the launch traced here: 239 us
  starting transfers between devices  107 us (45%)
  waiting for transfers between devices  52.8 us (22%)
  local copies, waits for them, and re-layouts  22.1 us (9%)
  matrix products  22.1 us (9%)
  other arithmetic  17.2 us (7%)
  loops' own time  12.7 us (5%)
  between operations  4.62 us (2%)
    ppermute x25, starting transfers between devices, butterfly_sum(): lax.ppermute(value, axis, [(i, i ^ step) for i in range(count)])  63.5 us
    ppermute x25, waiting for transfers between devices, butterfly_sum(): lax.ppermute(value, axis, [(i, i ^ step) for i in range(count)])  38.9 us
    ppermute x10, starting transfers between devices, extended(): lax.ppermute(head, axis, [((i + 1) % count, i) for i in range(ends)])  17.3 us
    conv_general_dilated x10, matrix products, conv(): lax.conv_general_dilated(padded, weights, window_strides=(1, 1), padding=...  15.2 us
    ppermute x10, starting transfers between devices, extended(): lax.ppermute(tail, axis, [(i, (i + 1) % count) for i in range(ends)])  14.8 us
    ppermute x6, waiting for transfers between devices, halving_scatter(): lax.ppermute(send, axis, [(i, i ^ step) for i in range(count)])  12.8 us
    another operation x1, loops' own time, per_device(): lax.scan(power_step, (padded_probe, iterate), None, length=ITERS - 1)  12.7 us
    ppermute x6, starting transfers between devices, halving_scatter(): lax.ppermute(send, axis, [(i, i ^ step) for i in range(count)])  11.4 us
  transfers between devices with their start and end apart: 51, of which 25 were waited for; matrix products, arithmetic and copies ran while one was open for 11% of the time, Pallas kernels for 0%

profile of v4, /device:TPU:0, one launch (start us, length us, event | category | flops | bytes accessed | tf_op | source)
XLA Modules:
  0.0 238.6 jit_solution(6676625644249693477)
XLA Ops:
  2.1 6.2 %collective-permute-start.15 = (bf16[2,32,256]{2,0,1:T(2,128)(2,1)S(1)}, bf16[2,32,256]{2,0,1:T(2,128)(2,1)S(1)}, u32[]{:S(2)}, u32[]{:S(2)}) collective-permute-start(bf16[2,32,256]{2,0,1:T(2,128)(2,1)S(1)} %get-tuple-element.76), channel_id=1, source_target_pairs={{16,0},{32,16},{48,32},{64,48},{80,64},{96,80},{112,96},{0,112},{1... | collective-permute-start | bytes 98312 | tf_op jit(solution)/shard_map/ppermute | solution.py:21
  8.4 2.1 copy.23
  12.8 6.1 %collective-permute-start.10 = (bf16[8,1,32,256]{3,0,2,1:T(8,128)(2,1)S(1)}, bf16[8,1,32,256]{3,0,2,1:T(8,128)(2,1)S(1)}, u32[]{:S(2)}, u32[]{:S(2)}) collective-permute-start(bf16[8,1,32,256]{3,0,2,1:T(8,128)(2,1)S(1)} %get-tuple-element.71), channel_id=1, source_target_pairs={{0,16},{16,32},{32,48},{48,64},{64,80},{80,96},{96,112},{1,17},{17... | collective-permute-start | bytes 393224 | tf_op jit(solution)/shard_map/ppermute | solution.py:19
  23.2 3.0 %collective-permute-start.12 = (bf16[8,18,1,256]{3,0,2,1:T(8,128)(2,1)S(1)}, bf16[8,18,1,256]{3,0,2,1:T(8,128)(2,1)S(1)}, u32[]{:S(2)}, u32[]{:S(2)}) collective-permute-start(bf16[8,18,1,256]{3,0,2,1:T(8,128)(2,1)S(1)} %get-tuple-element.69), channel_id=1, source_target_pairs={{0,2},{2,4},{4,6},{6,8},{8,10},{10,12},{12,14},{1,3},{3,5},{5,7},{... | collective-permute-start | bytes 221192 | tf_op jit(solution)/shard_map/ppermute | solution.py:19
  28.5 6.9 %fusion.46 = f32[256,3,3,256]{0,3,2,1:T(8,128)} fusion(bf16[8,18,34,256]{3,0,2,1:T(8,128)(2,1)S(1)} %pad_maximum_fusion.1, bf16[4,16,32,256]{3,2,1,0:T(8,128)(2,1)S(1)} %copy-done.5), kind=kOutput, calls=%fused_computation.62 | convolution fusion | flops 2415919104 | bytes 4661248 | tf_op jit(solution)/shard_map/conv_general_dilated | solution.py:99
  38.4 3.3 %select_convert_fusion = bf16[16,32,5,256]{3,1,2,0:T(8,128)(2,1)S(1)} fusion(bf16[3,3,256,256]{3,2,1,0:T(8,128)(2,1)S(1)} %copy-done.6, bf16[18,4,8,7,256]{4,1,3,2,0:T(4,128)(2,1)S(1)} %fusion.30, pred[32,5]{0,1:T(8,128)(4,1)S(1)} %copy-done.13), kind=kOutput, calls=%fused_computation.38 | convolution fusion | flops 3021209600 | bytes 4554912 | tf_op jit(solution)/shard_map/conv_general_dilated | solution.py:56
  44.3 3.2 %select_convert_fusion.1 = bf16[16,32,5,256]{3,1,2,0:T(8,128)(2,1)S(1)} fusion(bf16[3,3,256,256]{3,2,1,0:T(8,128)(2,1)S(1)} %copy-done.6, bf16[18,4,8,7,256]{4,1,3,2,0:T(4,128)(2,1)S(1)} %fusion.29, pred[32,5]{0,1:T(8,128)(4,1)S(1)} %copy-done.13), kind=kOutput, calls=%fused_computation.39 | convolution fusion | flops 3021209600 | bytes 4554912 | tf_op jit(solution)/shard_map/conv_general_dilated | solution.py:56
  51.2 2.0 copy.30
  54.4 6.1 %collective-permute-start.18 = (f32[128,2304]{1,0:T(8,128)}, f32[128,2304]{1,0:T(8,128)}, u32[]{:S(2)}, u32[]{:S(2)}) collective-permute-start(f32[128,2304]{1,0:T(8,128)} %constant_dynamic-slice_fusion.5), channel_id=1, source_target_pairs={{0,64},{16,80},{32,96},{48,112},{64,0},{80,16},{96,32},{112,48},{1... | collective-permute-start | bytes 3538952 | tf_op jit(solution)/shard_map/ppermute | solution.py:48
  60.5 121.7 %while.14 = (s32[]{:T(128)}, bf16[20,36,256]{2,0,1:T(8,128)(2,1)S(1)}, bf16[16,32,256]{2,0,1:T(8,128)(2,1)}, f32[3]{0:T(128)S(1)}, bf16[3,3,256,256]{3,2,1,0:T(8...) while((s32[]{:T(128)}, bf16[20,36,256]{2,0,1:T(8,128)(2,1)S(1)}, ...), condition=%wide.region_2.3_spmd, body=%wide.region_0.2_spmd.sunk | while | flops 1609732096 | bytes 19315492 | solution.py:110
  65.7 3.6 %collective-permute-start.3 = (f32[2,32,256]{2,0,1:T(2,128)S(1)}, f32[2,32,256]{2,0,1:T(2,128)S(1)}, u32[]{:S(2)}, u32[]{:S(2)}) collective-permute-start(f32[2,32,256]{2,0,1:T(2,128)S(1)} %slice_bitcast_fusion.11), channel_id=1, source_target_pairs={{16,0},{32,16},{48,32},{64,48},{80,64},{96,80},{112,96},{0,112},{1... | collective-permute-start | bytes 196616 | tf_op jit(solution)/shard_map/while/body/eval_jaxpr/ppermute | solution.py:21
  71.5 15.2 %collective-permute-start.1 = (f32[]{:T(128)}, f32[]{:T(128)}, u32[]{:S(2)}, u32[]{:S(2)}) collective-permute-start(f32[]{:T(128)} %add.180), channel_id=1, source_target_pairs={{0,32},{16,48},{32,0},{48,16},{64,96},{80,112},{96,64},{112,80},{1... | collective-permute-start | bytes 20 | tf_op jit(solution)/shard_map/while/body/eval_jaxpr/ppermute | solution.py:33
  86.7 2.8 %collective-permute-done.1 = f32[]{:T(128)} collective-permute-done((f32[]{:T(128)}, f32[]{:T(128)}, u32[]{:S(2)}, u32[]{:S(2)}) %collective-permute-start.1) | collective-permute-done | bytes 36 | tf_op jit(solution)/shard_map/while/body/eval_jaxpr/ppermute | solution.py:33
  90.0 3.1 %collective-permute-start.2 = (f32[]{:T(128)}, f32[]{:T(128)}, u32[]{:S(2)}, u32[]{:S(2)}) collective-permute-start(f32[]{:T(128)} %add.181), channel_id=1, source_target_pairs={{0,64},{16,80},{32,96},{48,112},{64,0},{80,16},{96,32},{112,48},{1... | collective-permute-start | bytes 20 | tf_op jit(solution)/shard_map/while/body/eval_jaxpr/ppermute | solution.py:33
  93.1 2.1 collective-permute-done.2
  96.4 3.2 %collective-permute-start.7 = (f32[]{:T(128)}, f32[]{:T(128)}, u32[]{:S(2)}, u32[]{:S(2)}) collective-permute-start(f32[]{:T(128)} %add.182), channel_id=1, source_target_pairs={{0,2},{2,0},{4,6},{6,4},{8,10},{10,8},{12,14},{14,12},{1,3},{3,1},... | collective-permute-start | bytes 20 | tf_op jit(solution)/shard_map/while/body/eval_jaxpr/ppermute | solution.py:33
  100.2 2.7 %collective-permute-start.8 = (f32[]{:T(128)}, f32[]{:T(128)}, u32[]{:S(2)}, u32[]{:S(2)}) collective-permute-start(f32[]{:T(128)} %add.183), channel_id=1, source_target_pairs={{0,4},{2,6},{4,0},{6,2},{8,12},{10,14},{12,8},{14,10},{1,5},{3,7},... | collective-permute-start | bytes 20 | tf_op jit(solution)/shard_map/while/body/eval_jaxpr/ppermute | solution.py:33
  104.5 3.4 %collective-permute-start.9 = (f32[]{:T(128)}, f32[]{:T(128)}, u32[]{:S(2)}, u32[]{:S(2)}) collective-permute-start(f32[]{:T(128)} %add.184), channel_id=1, source_target_pairs={{0,8},{2,10},{4,12},{6,14},{8,0},{10,2},{12,4},{14,6},{1,9},{3,11}... | collective-permute-start | bytes 20 | tf_op jit(solution)/shard_map/while/body/eval_jaxpr/ppermute | solution.py:33
  107.8 1.9 collective-permute-done.9
  115.6 2.8 %collective-permute-start.3 = (f32[2,32,256]{2,0,1:T(2,128)S(1)}, f32[2,32,256]{2,0,1:T(2,128)S(1)}, u32[]{:S(2)}, u32[]{:S(2)}) collective-permute-start(f32[2,32,256]{2,0,1:T(2,128)S(1)} %slice_bitcast_fusion.11), channel_id=1, source_target_pairs={{16,0},{32,16},{48,32},{64,48},{80,64},{96,80},{112,96},{0,112},{1... | collective-permute-start | bytes 196616 | tf_op jit(solution)/shard_map/while/body/eval_jaxpr/ppermute | solution.py:21
  122.0 1.7 collective-permute-start.1
  123.8 2.0 collective-permute-done.1
  126.3 3.1 %collective-permute-start.2 = (f32[]{:T(128)}, f32[]{:T(128)}, u32[]{:S(2)}, u32[]{:S(2)}) collective-permute-start(f32[]{:T(128)} %add.181), channel_id=1, source_target_pairs={{0,64},{16,80},{32,96},{48,112},{64,0},{80,16},{96,32},{112,48},{1... | collective-permute-start | bytes 20 | tf_op jit(solution)/shard_map/while/body/eval_jaxpr/ppermute | solution.py:33
  129.4 2.1 collective-permute-done.2
  132.8 1.9 collective-permute-start.7
  135.2 2.0 collective-permute-start.8
  137.2 1.7 collective-permute-done.8
  139.5 2.8 %collective-permute-start.9 = (f32[]{:T(128)}, f32[]{:T(128)}, u32[]{:S(2)}, u32[]{:S(2)}) collective-permute-start(f32[]{:T(128)} %add.184), channel_id=1, source_target_pairs={{0,8},{2,10},{4,12},{6,14},{8,0},{10,2},{12,4},{14,6},{1,9},{3,11}... | collective-permute-start | bytes 20 | tf_op jit(solution)/shard_map/while/body/eval_jaxpr/ppermute | solution.py:33
  142.2 2.5 %collective-permute-done.9 = f32[]{:T(128)} collective-permute-done((f32[]{:T(128)}, f32[]{:T(128)}, u32[]{:S(2)}, u32[]{:S(2)}) %collective-permute-start.9) | collective-permute-done | bytes 36 | tf_op jit(solution)/shard_map/while/body/eval_jaxpr/ppermute | solution.py:33
  150.6 3.0 %collective-permute-start = (f32[]{:T(128)}, f32[]{:T(128)}, u32[]{:S(2)}, u32[]{:S(2)}) collective-permute-start(f32[]{:T(128)} %multiply_reduce_fusion.3), channel_id=1, source_target_pairs={{0,16},{16,0},{32,48},{48,32},{64,80},{80,64},{96,112},{112,96},{1... | collective-permute-start | bytes 20 | tf_op jit(solution)/shard_map/while/body/eval_jaxpr/ppermute | solution.py:33
  154.2 3.2 %collective-permute-start.4 = (f32[2,32,256]{2,0,1:T(2,128)S(1)}, f32[2,32,256]{2,0,1:T(2,128)S(1)}, u32[]{:S(2)}, u32[]{:S(2)}) collective-permute-start(f32[2,32,256]{2,0,1:T(2,128)S(1)} %slice_bitcast_fusion.13), channel_id=1, source_target_pairs={{0,16},{16,32},{32,48},{48,64},{64,80},{80,96},{96,112},{112,0},{1... | collective-permute-start | bytes 196616 | tf_op jit(solution)/shard_map/while/body/eval_jaxpr/ppermute | solution.py:19
  160.0 2.3 collective-permute-done.1
  162.9 3.1 %collective-permute-start.2 = (f32[]{:T(128)}, f32[]{:T(128)}, u32[]{:S(2)}, u32[]{:S(2)}) collective-permute-start(f32[]{:T(128)} %add.181), channel_id=1, source_target_pairs={{0,64},{16,80},{32,96},{48,112},{64,0},{80,16},{96,32},{112,48},{1... | collective-permute-start | bytes 20 | tf_op jit(solution)/shard_map/while/body/eval_jaxpr/ppermute | solution.py:33
  166.0 2.1 collective-permute-done.2
  171.2 2.1 collective-permute-start.8
  173.2 1.7 collective-permute-done.8
  175.4 4.1 %collective-permute-start.9 = (f32[]{:T(128)}, f32[]{:T(128)}, u32[]{:S(2)}, u32[]{:S(2)}) collective-permute-start(f32[]{:T(128)} %add.184), channel_id=1, source_target_pairs={{0,8},{2,10},{4,12},{6,14},{8,0},{10,2},{12,4},{14,6},{1,9},{3,11}... | collective-permute-start | bytes 20 | tf_op jit(solution)/shard_map/while/body/eval_jaxpr/ppermute | solution.py:33
  182.4 1.8 dynamic-slice_add_fusion
  187.9 9.5 %collective-permute-done.19 = f32[64,2304]{1,0:T(8,128)S(1)} collective-permute-done((f32[64,2304]{1,0:T(8,128)S(1)}, f32[64,2304]{1,0:T(8,128)S(1)}, u32[]{:S(2)}, u32[]{:S(2)}) %collective-permute-start.19) | collective-permute-done | bytes 589856 | tf_op jit(solution)/shard_map/ppermute | solution.py:48
  200.4 2.1 collective-permute-start.25
  202.5 3.4 %collective-permute-done.25 = f32[2]{0:T(128)S(1)} collective-permute-done((f32[2]{0:T(128)S(1)}, f32[2]{0:T(128)S(1)}, u32[]{:S(2)}, u32[]{:S(2)}) %collective-permute-start.25) | collective-permute-done | bytes 40 | tf_op jit(solution)/shard_map/ppermute | solution.py:33
  207.6 2.8 %collective-permute-start.21 = (f32[16,2304]{1,0:T(8,128)S(1)}, f32[16,2304]{1,0:T(8,128)S(1)}, u32[]{:S(2)}, u32[]{:S(2)}) collective-permute-start(f32[16,2304]{1,0:T(8,128)S(1)} %constant_dynamic-slice_fusion.2), channel_id=1, source_target_pairs={{0,8},{2,10},{4,12},{6,14},{8,0},{10,2},{12,4},{14,6},{1,9},{3,11}... | collective-permute-start | bytes 442376 | tf_op jit(solution)/shard_map/ppermute | solution.py:48
  212.1 2.1 collective-permute-start.27
  214.2 3.0 %collective-permute-done.27 = f32[2]{0:T(128)S(1)} collective-permute-done((f32[2]{0:T(128)S(1)}, f32[2]{0:T(128)S(1)}, u32[]{:S(2)}, u32[]{:S(2)}) %collective-permute-start.27) | collective-permute-done | bytes 40 | tf_op jit(solution)/shard_map/ppermute | solution.py:33
  219.0 2.9 %collective-permute-done.29 = f32[2]{0:T(128)S(1)} collective-permute-done((f32[2]{0:T(128)S(1)}, f32[2]{0:T(128)S(1)}, u32[]{:S(2)}, u32[]{:S(2)}) %collective-permute-start.29) | collective-permute-done | bytes 40 | tf_op jit(solution)/shard_map/ppermute | solution.py:33
  221.9 2.8 %collective-permute-start.30 = (f32[2]{0:T(128)S(1)}, f32[2]{0:T(128)S(1)}, u32[]{:S(2)}, u32[]{:S(2)}) collective-permute-start(f32[2]{0:T(128)S(1)} %add.157), channel_id=1, source_target_pairs={{0,8},{2,10},{4,12},{6,14},{8,0},{10,2},{12,4},{14,6},{1,9},{3,11}... | collective-permute-start | bytes 32 | tf_op jit(solution)/shard_map/ppermute | solution.py:33
  224.6 2.3 collective-permute-done.30
  229.0 2.4 %collective-permute-done.22 = f32[8,2304]{1,0:T(8,128)S(1)} collective-permute-done((f32[8,2304]{1,0:T(8,128)S(1)}, f32[8,2304]{1,0:T(8,128)S(1)}, u32[]{:S(2)}, u32[]{:S(2)}) %collective-permute-start.22) | collective-permute-done | bytes 73760 | tf_op jit(solution)/shard_map/ppermute | solution.py:48
  (202 shorter events, 65.3 us)
Async XLA Ops:
  2.1 17.0 %collective-permute-start.15 = (bf16[2,32,256]{2,0,1:T(2,128)(2,1)S(1)}, bf16[2,32,256]{2,0,1:T(2,128)(2,1)S(1)}, u32[]{:S(2)}, u32[]{:S(2)}) collective-permute-start(bf16[2,32,256]{2,0,1:T(2,128)(2,1)S(1)} %get-tuple-element.76), channel_id=1, source_target_pairs={{16,0},{32,16},{48,32},{64,48},{80,64},{96,80},{112,96},{0,112},{1... | collective-permute-start | bytes 98312 | tf_op jit(solution)/shard_map/ppermute | solution.py:21
  8.4 10.8 %collective-permute-start.14 = (bf16[2,32,256]{2,0,1:T(2,128)(2,1)S(1)}, bf16[2,32,256]{2,0,1:T(2,128)(2,1)S(1)}, u32[]{:S(2)}, u32[]{:S(2)}) collective-permute-start(bf16[2,32,256]{2,0,1:T(2,128)(2,1)S(1)} %get-tuple-element.75), channel_id=1, source_target_pairs={{0,16},{16,32},{32,48},{48,64},{64,80},{80,96},{96,112},{112,0},{1... | collective-permute-start | bytes 98312 | tf_op jit(solution)/shard_map/ppermute | solution.py:19
  11.5 9.3 %collective-permute-start.11 = (bf16[8,1,32,256]{3,0,2,1:T(8,128)(2,1)S(1)}, bf16[8,1,32,256]{3,0,2,1:T(8,128)(2,1)S(1)}, u32[]{:S(2)}, u32[]{:S(2)}) collective-permute-start(bf16[8,1,32,256]{3,0,2,1:T(8,128)(2,1)S(1)} %get-tuple-element.72), channel_id=1, source_target_pairs={{16,0},{32,16},{48,32},{64,48},{80,64},{96,80},{112,96},{17,1},{33... | collective-permute-start | bytes 393224 | tf_op jit(solution)/shard_map/ppermute | solution.py:21
  12.8 9.0 %collective-permute-start.10 = (bf16[8,1,32,256]{3,0,2,1:T(8,128)(2,1)S(1)}, bf16[8,1,32,256]{3,0,2,1:T(8,128)(2,1)S(1)}, u32[]{:S(2)}, u32[]{:S(2)}) collective-permute-start(bf16[8,1,32,256]{3,0,2,1:T(8,128)(2,1)S(1)} %get-tuple-element.71), channel_id=1, source_target_pairs={{0,16},{16,32},{32,48},{48,64},{64,80},{80,96},{96,112},{1,17},{17... | collective-permute-start | bytes 393224 | tf_op jit(solution)/shard_map/ppermute | solution.py:19
  19.2 7.1 %collective-permute-start.17 = (bf16[20,2,256]{2,0,1:T(8,128)(2,1)S(1)}, bf16[20,2,256]{2,0,1:T(8,128)(2,1)S(1)}, u32[]{:S(2)}, u32[]{:S(2)}) collective-permute-start(bf16[20,2,256]{2,0,1:T(8,128)(2,1)S(1)} %get-tuple-element.74), channel_id=1, source_target_pairs={{2,0},{4,2},{6,4},{8,6},{10,8},{12,10},{14,12},{0,14},{3,1},{5,3},... | collective-permute-start | bytes 61448 | tf_op jit(solution)/shard_map/ppermute | solution.py:21
  20.8 5.5 %collective-permute-start.16 = (bf16[20,2,256]{2,0,1:T(8,128)(2,1)S(1)}, bf16[20,2,256]{2,0,1:T(8,128)(2,1)S(1)}, u32[]{:S(2)}, u32[]{:S(2)}) collective-permute-start(bf16[20,2,256]{2,0,1:T(8,128)(2,1)S(1)} %get-tuple-element.73), channel_id=1, source_target_pairs={{0,2},{2,4},{4,6},{6,8},{8,10},{10,12},{12,14},{14,0},{1,3},{3,5},... | collective-permute-start | bytes 61448 | tf_op jit(solution)/shard_map/ppermute | solution.py:19
  21.9 5.4 %collective-permute-start.13 = (bf16[8,18,1,256]{3,0,2,1:T(8,128)(2,1)S(1)}, bf16[8,18,1,256]{3,0,2,1:T(8,128)(2,1)S(1)}, u32[]{:S(2)}, u32[]{:S(2)}) collective-permute-start(bf16[8,18,1,256]{3,0,2,1:T(8,128)(2,1)S(1)} %get-tuple-element.70), channel_id=1, source_target_pairs={{2,0},{4,2},{6,4},{8,6},{10,8},{12,10},{14,12},{3,1},{5,3},{7,5},{... | collective-permute-start | bytes 221192 | tf_op jit(solution)/shard_map/ppermute | solution.py:21
  23.2 4.1 %collective-permute-start.12 = (bf16[8,18,1,256]{3,0,2,1:T(8,128)(2,1)S(1)}, bf16[8,18,1,256]{3,0,2,1:T(8,128)(2,1)S(1)}, u32[]{:S(2)}, u32[]{:S(2)}) collective-permute-start(bf16[8,18,1,256]{3,0,2,1:T(8,128)(2,1)S(1)} %get-tuple-element.69), channel_id=1, source_target_pairs={{0,2},{2,4},{4,6},{6,8},{8,10},{10,12},{12,14},{1,3},{3,5},{5,7},{... | collective-permute-start | bytes 221192 | tf_op jit(solution)/shard_map/ppermute | solution.py:19
  54.4 128.0 %collective-permute-start.18 = (f32[128,2304]{1,0:T(8,128)}, f32[128,2304]{1,0:T(8,128)}, u32[]{:S(2)}, u32[]{:S(2)}) collective-permute-start(f32[128,2304]{1,0:T(8,128)} %constant_dynamic-slice_fusion.5), channel_id=1, source_target_pairs={{0,64},{16,80},{32,96},{48,112},{64,0},{80,16},{96,32},{112,48},{1... | collective-permute-start | bytes 3538952 | tf_op jit(solution)/shard_map/ppermute | solution.py:48
  65.0 5.3 %collective-permute-start = (f32[]{:T(128)}, f32[]{:T(128)}, u32[]{:S(2)}, u32[]{:S(2)}) collective-permute-start(f32[]{:T(128)} %multiply_reduce_fusion.3), channel_id=1, source_target_pairs={{0,16},{16,0},{32,48},{48,32},{64,80},{80,64},{96,112},{112,96},{1... | collective-permute-start | bytes 20 | tf_op jit(solution)/shard_map/while/body/eval_jaxpr/ppermute | solution.py:33
  65.7 30.0 %collective-permute-start.3 = (f32[2,32,256]{2,0,1:T(2,128)S(1)}, f32[2,32,256]{2,0,1:T(2,128)S(1)}, u32[]{:S(2)}, u32[]{:S(2)}) collective-permute-start(f32[2,32,256]{2,0,1:T(2,128)S(1)} %slice_bitcast_fusion.11), channel_id=1, source_target_pairs={{16,0},{32,16},{48,32},{64,48},{80,64},{96,80},{112,96},{0,112},{1... | collective-permute-start | bytes 196616 | tf_op jit(solution)/shard_map/while/body/eval_jaxpr/ppermute | solution.py:21
  69.3 26.4 %collective-permute-start.4 = (f32[2,32,256]{2,0,1:T(2,128)S(1)}, f32[2,32,256]{2,0,1:T(2,128)S(1)}, u32[]{:S(2)}, u32[]{:S(2)}) collective-permute-start(f32[2,32,256]{2,0,1:T(2,128)S(1)} %slice_bitcast_fusion.13), channel_id=1, source_target_pairs={{0,16},{16,32},{32,48},{48,64},{64,80},{80,96},{96,112},{112,0},{1... | collective-permute-start | bytes 196616 | tf_op jit(solution)/shard_map/while/body/eval_jaxpr/ppermute | solution.py:19
  71.5 17.9 %collective-permute-start.1 = (f32[]{:T(128)}, f32[]{:T(128)}, u32[]{:S(2)}, u32[]{:S(2)}) collective-permute-start(f32[]{:T(128)} %add.180), channel_id=1, source_target_pairs={{0,32},{16,48},{32,0},{48,16},{64,96},{80,112},{96,64},{112,80},{1... | collective-permute-start | bytes 20 | tf_op jit(solution)/shard_map/while/body/eval_jaxpr/ppermute | solution.py:33
  90.0 5.2 %collective-permute-start.2 = (f32[]{:T(128)}, f32[]{:T(128)}, u32[]{:S(2)}, u32[]{:S(2)}) collective-permute-start(f32[]{:T(128)} %add.181), channel_id=1, source_target_pairs={{0,64},{16,80},{32,96},{48,112},{64,0},{80,16},{96,32},{112,48},{1... | collective-permute-start | bytes 20 | tf_op jit(solution)/shard_map/while/body/eval_jaxpr/ppermute | solution.py:33
  95.9 15.3 %collective-permute-start.5 = (f32[20,2,256]{2,0,1:T(8,128)S(1)}, f32[20,2,256]{2,0,1:T(8,128)S(1)}, u32[]{:S(2)}, u32[]{:S(2)}) collective-permute-start(f32[20,2,256]{2,0,1:T(8,128)S(1)} %get-tuple-element.121), channel_id=1, source_target_pairs={{2,0},{4,2},{6,4},{8,6},{10,8},{12,10},{14,12},{0,14},{3,1},{5,3},... | collective-permute-start | bytes 122888 | tf_op jit(solution)/shard_map/while/body/eval_jaxpr/ppermute | solution.py:21
  95.9 15.2 %collective-permute-start.6 = (f32[20,2,256]{2,0,1:T(8,128)S(1)}, f32[20,2,256]{2,0,1:T(8,128)S(1)}, u32[]{:S(2)}, u32[]{:S(2)}) collective-permute-start(f32[20,2,256]{2,0,1:T(8,128)S(1)} %get-tuple-element.122), channel_id=1, source_target_pairs={{0,2},{2,4},{4,6},{6,8},{8,10},{10,12},{12,14},{14,0},{1,3},{3,5},... | collective-permute-start | bytes 122888 | tf_op jit(solution)/shard_map/while/body/eval_jaxpr/ppermute | solution.py:19
  96.4 3.2 %collective-permute-start.7 = (f32[]{:T(128)}, f32[]{:T(128)}, u32[]{:S(2)}, u32[]{:S(2)}) collective-permute-start(f32[]{:T(128)} %add.182), channel_id=1, source_target_pairs={{0,2},{2,0},{4,6},{6,4},{8,10},{10,8},{12,14},{14,12},{1,3},{3,1},... | collective-permute-start | bytes 20 | tf_op jit(solution)/shard_map/while/body/eval_jaxpr/ppermute | solution.py:33
  100.2 3.7 %collective-permute-start.8 = (f32[]{:T(128)}, f32[]{:T(128)}, u32[]{:S(2)}, u32[]{:S(2)}) collective-permute-start(f32[]{:T(128)} %add.183), channel_id=1, source_target_pairs={{0,4},{2,6},{4,0},{6,2},{8,12},{10,14},{12,8},{14,10},{1,5},{3,7},... | collective-permute-start | bytes 20 | tf_op jit(solution)/shard_map/while/body/eval_jaxpr/ppermute | solution.py:33
  104.5 5.2 %collective-permute-start.9 = (f32[]{:T(128)}, f32[]{:T(128)}, u32[]{:S(2)}, u32[]{:S(2)}) collective-permute-start(f32[]{:T(128)} %add.184), channel_id=1, source_target_pairs={{0,8},{2,10},{4,12},{6,14},{8,0},{10,2},{12,4},{14,6},{1,9},{3,11}... | collective-permute-start | bytes 20 | tf_op jit(solution)/shard_map/while/body/eval_jaxpr/ppermute | solution.py:33
  115.6 5.3 %collective-permute-start = (f32[]{:T(128)}, f32[]{:T(128)}, u32[]{:S(2)}, u32[]{:S(2)}) collective-permute-start(f32[]{:T(128)} %multiply_reduce_fusion.3), channel_id=1, source_target_pairs={{0,16},{16,0},{32,48},{48,32},{64,80},{80,64},{96,112},{112,96},{1... | collective-permute-start | bytes 20 | tf_op jit(solution)/shard_map/while/body/eval_jaxpr/ppermute | solution.py:33
  115.6 16.5 %collective-permute-start.3 = (f32[2,32,256]{2,0,1:T(2,128)S(1)}, f32[2,32,256]{2,0,1:T(2,128)S(1)}, u32[]{:S(2)}, u32[]{:S(2)}) collective-permute-start(f32[2,32,256]{2,0,1:T(2,128)S(1)} %slice_bitcast_fusion.11), channel_id=1, source_target_pairs={{16,0},{32,16},{48,32},{64,48},{80,64},{96,80},{112,96},{0,112},{1... | collective-permute-start | bytes 196616 | tf_op jit(solution)/shard_map/while/body/eval_jaxpr/ppermute | solution.py:21
  118.5 13.6 %collective-permute-start.4 = (f32[2,32,256]{2,0,1:T(2,128)S(1)}, f32[2,32,256]{2,0,1:T(2,128)S(1)}, u32[]{:S(2)}, u32[]{:S(2)}) collective-permute-start(f32[2,32,256]{2,0,1:T(2,128)S(1)} %slice_bitcast_fusion.13), channel_id=1, source_target_pairs={{0,16},{16,32},{32,48},{48,64},{64,80},{80,96},{96,112},{112,0},{1... | collective-permute-start | bytes 196616 | tf_op jit(solution)/shard_map/while/body/eval_jaxpr/ppermute | solution.py:19
  122.0 3.7 %collective-permute-start.1 = (f32[]{:T(128)}, f32[]{:T(128)}, u32[]{:S(2)}, u32[]{:S(2)}) collective-permute-start(f32[]{:T(128)} %add.180), channel_id=1, source_target_pairs={{0,32},{16,48},{32,0},{48,16},{64,96},{80,112},{96,64},{112,80},{1... | collective-permute-start | bytes 20 | tf_op jit(solution)/shard_map/while/body/eval_jaxpr/ppermute | solution.py:33
  126.3 5.2 %collective-permute-start.2 = (f32[]{:T(128)}, f32[]{:T(128)}, u32[]{:S(2)}, u32[]{:S(2)}) collective-permute-start(f32[]{:T(128)} %add.181), channel_id=1, source_target_pairs={{0,64},{16,80},{32,96},{48,112},{64,0},{80,16},{96,32},{112,48},{1... | collective-permute-start | bytes 20 | tf_op jit(solution)/shard_map/while/body/eval_jaxpr/ppermute | solution.py:33
  132.3 13.9 %collective-permute-start.5 = (f32[20,2,256]{2,0,1:T(8,128)S(1)}, f32[20,2,256]{2,0,1:T(8,128)S(1)}, u32[]{:S(2)}, u32[]{:S(2)}) collective-permute-start(f32[20,2,256]{2,0,1:T(8,128)S(1)} %get-tuple-element.121), channel_id=1, source_target_pairs={{2,0},{4,2},{6,4},{8,6},{10,8},{12,10},{14,12},{0,14},{3,1},{5,3},... | collective-permute-start | bytes 122888 | tf_op jit(solution)/shard_map/while/body/eval_jaxpr/ppermute | solution.py:21
  132.3 13.9 %collective-permute-start.6 = (f32[20,2,256]{2,0,1:T(8,128)S(1)}, f32[20,2,256]{2,0,1:T(8,128)S(1)}, u32[]{:S(2)}, u32[]{:S(2)}) collective-permute-start(f32[20,2,256]{2,0,1:T(8,128)S(1)} %get-tuple-element.122), channel_id=1, source_target_pairs={{0,2},{2,4},{4,6},{6,8},{8,10},{10,12},{12,14},{14,0},{1,3},{3,5},... | collective-permute-start | bytes 122888 | tf_op jit(solution)/shard_map/while/body/eval_jaxpr/ppermute | solution.py:19
  132.8 1.9 collective-permute-start.7
  135.2 3.7 %collective-permute-start.8 = (f32[]{:T(128)}, f32[]{:T(128)}, u32[]{:S(2)}, u32[]{:S(2)}) collective-permute-start(f32[]{:T(128)} %add.183), channel_id=1, source_target_pairs={{0,4},{2,6},{4,0},{6,2},{8,12},{10,14},{12,8},{14,10},{1,5},{3,7},... | collective-permute-start | bytes 20 | tf_op jit(solution)/shard_map/while/body/eval_jaxpr/ppermute | solution.py:33
  139.5 5.2 %collective-permute-start.9 = (f32[]{:T(128)}, f32[]{:T(128)}, u32[]{:S(2)}, u32[]{:S(2)}) collective-permute-start(f32[]{:T(128)} %add.184), channel_id=1, source_target_pairs={{0,8},{2,10},{4,12},{6,14},{8,0},{10,2},{12,4},{14,6},{1,9},{3,11}... | collective-permute-start | bytes 20 | tf_op jit(solution)/shard_map/while/body/eval_jaxpr/ppermute | solution.py:33
  150.6 6.9 %collective-permute-start = (f32[]{:T(128)}, f32[]{:T(128)}, u32[]{:S(2)}, u32[]{:S(2)}) collective-permute-start(f32[]{:T(128)} %multiply_reduce_fusion.3), channel_id=1, source_target_pairs={{0,16},{16,0},{32,48},{48,32},{64,80},{80,64},{96,112},{112,96},{1... | collective-permute-start | bytes 20 | tf_op jit(solution)/shard_map/while/body/eval_jaxpr/ppermute | solution.py:33
  153.6 15.0 %collective-permute-start.3 = (f32[2,32,256]{2,0,1:T(2,128)S(1)}, f32[2,32,256]{2,0,1:T(2,128)S(1)}, u32[]{:S(2)}, u32[]{:S(2)}) collective-permute-start(f32[2,32,256]{2,0,1:T(2,128)S(1)} %slice_bitcast_fusion.11), channel_id=1, source_target_pairs={{16,0},{32,16},{48,32},{64,48},{80,64},{96,80},{112,96},{0,112},{1... | collective-permute-start | bytes 196616 | tf_op jit(solution)/shard_map/while/body/eval_jaxpr/ppermute | solution.py:21
  154.2 14.5 %collective-permute-start.4 = (f32[2,32,256]{2,0,1:T(2,128)S(1)}, f32[2,32,256]{2,0,1:T(2,128)S(1)}, u32[]{:S(2)}, u32[]{:S(2)}) collective-permute-start(f32[2,32,256]{2,0,1:T(2,128)S(1)} %slice_bitcast_fusion.13), channel_id=1, source_target_pairs={{0,16},{16,32},{32,48},{48,64},{64,80},{80,96},{96,112},{112,0},{1... | collective-permute-start | bytes 196616 | tf_op jit(solution)/shard_map/while/body/eval_jaxpr/ppermute | solution.py:19
  158.6 3.7 %collective-permute-start.1 = (f32[]{:T(128)}, f32[]{:T(128)}, u32[]{:S(2)}, u32[]{:S(2)}) collective-permute-start(f32[]{:T(128)} %add.180), channel_id=1, source_target_pairs={{0,32},{16,48},{32,0},{48,16},{64,96},{80,112},{96,64},{112,80},{1... | collective-permute-start | bytes 20 | tf_op jit(solution)/shard_map/while/body/eval_jaxpr/ppermute | solution.py:33
  162.9 5.2 %collective-permute-start.2 = (f32[]{:T(128)}, f32[]{:T(128)}, u32[]{:S(2)}, u32[]{:S(2)}) collective-permute-start(f32[]{:T(128)} %add.181), channel_id=1, source_target_pairs={{0,64},{16,80},{32,96},{48,112},{64,0},{80,16},{96,32},{112,48},{1... | collective-permute-start | bytes 20 | tf_op jit(solution)/shard_map/while/body/eval_jaxpr/ppermute | solution.py:33
  168.8 13.3 %collective-permute-start.5 = (f32[20,2,256]{2,0,1:T(8,128)S(1)}, f32[20,2,256]{2,0,1:T(8,128)S(1)}, u32[]{:S(2)}, u32[]{:S(2)}) collective-permute-start(f32[20,2,256]{2,0,1:T(8,128)S(1)} %get-tuple-element.121), channel_id=1, source_target_pairs={{2,0},{4,2},{6,4},{8,6},{10,8},{12,10},{14,12},{0,14},{3,1},{5,3},... | collective-permute-start | bytes 122888 | tf_op jit(solution)/shard_map/while/body/eval_jaxpr/ppermute | solution.py:21
  168.9 13.3 %collective-permute-start.6 = (f32[20,2,256]{2,0,1:T(8,128)S(1)}, f32[20,2,256]{2,0,1:T(8,128)S(1)}, u32[]{:S(2)}, u32[]{:S(2)}) collective-permute-start(f32[20,2,256]{2,0,1:T(8,128)S(1)} %get-tuple-element.122), channel_id=1, source_target_pairs={{0,2},{2,4},{4,6},{6,8},{8,10},{10,12},{12,14},{14,0},{1,3},{3,5},... | collective-permute-start | bytes 122888 | tf_op jit(solution)/shard_map/while/body/eval_jaxpr/ppermute | solution.py:19
  171.2 3.7 %collective-permute-start.8 = (f32[]{:T(128)}, f32[]{:T(128)}, u32[]{:S(2)}, u32[]{:S(2)}) collective-permute-start(f32[]{:T(128)} %add.183), channel_id=1, source_target_pairs={{0,4},{2,6},{4,0},{6,2},{8,12},{10,14},{12,8},{14,10},{1,5},{3,7},... | collective-permute-start | bytes 20 | tf_op jit(solution)/shard_map/while/body/eval_jaxpr/ppermute | solution.py:33
  175.4 5.2 %collective-permute-start.9 = (f32[]{:T(128)}, f32[]{:T(128)}, u32[]{:S(2)}, u32[]{:S(2)}) collective-permute-start(f32[]{:T(128)} %add.184), channel_id=1, source_target_pairs={{0,8},{2,10},{4,12},{6,14},{8,0},{10,2},{12,4},{14,6},{1,9},{3,11}... | collective-permute-start | bytes 20 | tf_op jit(solution)/shard_map/while/body/eval_jaxpr/ppermute | solution.py:33
  184.4 13.0 %collective-permute-start.19 = (f32[64,2304]{1,0:T(8,128)S(1)}, f32[64,2304]{1,0:T(8,128)S(1)}, u32[]{:S(2)}, u32[]{:S(2)}) collective-permute-start(f32[64,2304]{1,0:T(8,128)S(1)} %constant_dynamic-slice_fusion.4), channel_id=1, source_target_pairs={{0,32},{16,48},{32,0},{48,16},{64,96},{80,112},{96,64},{112,80},{1... | collective-permute-start | bytes 1769480 | tf_op jit(solution)/shard_map/ppermute | solution.py:48
  197.5 10.0 %collective-permute-start.20 = (f32[32,2304]{1,0:T(8,128)S(1)}, f32[32,2304]{1,0:T(8,128)S(1)}, u32[]{:S(2)}, u32[]{:S(2)}) collective-permute-start(f32[32,2304]{1,0:T(8,128)S(1)} %constant_dynamic-slice_fusion.3), channel_id=1, source_target_pairs={{0,16},{16,0},{32,48},{48,32},{64,80},{80,64},{96,112},{112,96},{1... | collective-permute-start | bytes 884744 | tf_op jit(solution)/shard_map/ppermute | solution.py:48
  200.4 5.5 %collective-permute-start.25 = (f32[2]{0:T(128)S(1)}, f32[2]{0:T(128)S(1)}, u32[]{:S(2)}, u32[]{:S(2)}) collective-permute-start(f32[2]{0:T(128)S(1)} %pad_maximum_fusion.12), channel_id=1, source_target_pairs={{0,16},{16,0},{32,48},{48,32},{64,80},{80,64},{96,112},{112,96},{1... | collective-permute-start | bytes 32 | tf_op jit(solution)/shard_map/ppermute | solution.py:33
  207.2 3.6 %collective-permute-start.26 = (f32[2]{0:T(128)S(1)}, f32[2]{0:T(128)S(1)}, u32[]{:S(2)}, u32[]{:S(2)}) collective-permute-start(f32[2]{0:T(128)S(1)} %fusion.80), channel_id=1, source_target_pairs={{0,32},{16,48},{32,0},{48,16},{64,96},{80,112},{96,64},{112,80},{1... | collective-permute-start | bytes 32 | tf_op jit(solution)/shard_map/ppermute | solution.py:33
  207.6 19.3 %collective-permute-start.21 = (f32[16,2304]{1,0:T(8,128)S(1)}, f32[16,2304]{1,0:T(8,128)S(1)}, u32[]{:S(2)}, u32[]{:S(2)}) collective-permute-start(f32[16,2304]{1,0:T(8,128)S(1)} %constant_dynamic-slice_fusion.2), channel_id=1, source_target_pairs={{0,8},{2,10},{4,12},{6,14},{8,0},{10,2},{12,4},{14,6},{1,9},{3,11}... | collective-permute-start | bytes 442376 | tf_op jit(solution)/shard_map/ppermute | solution.py:48
  212.1 5.1 %collective-permute-start.27 = (f32[2]{0:T(128)S(1)}, f32[2]{0:T(128)S(1)}, u32[]{:S(2)}, u32[]{:S(2)}) collective-permute-start(f32[2]{0:T(128)S(1)} %fusion.81), channel_id=1, source_target_pairs={{0,64},{16,80},{32,96},{48,112},{64,0},{80,16},{96,32},{112,48},{1... | collective-permute-start | bytes 32 | tf_op jit(solution)/shard_map/ppermute | solution.py:33
  218.3 3.5 %collective-permute-start.29 = (f32[2]{0:T(128)S(1)}, f32[2]{0:T(128)S(1)}, u32[]{:S(2)}, u32[]{:S(2)}) collective-permute-start(f32[2]{0:T(128)S(1)} %add.156), channel_id=1, source_target_pairs={{0,4},{2,6},{4,0},{6,2},{8,12},{10,14},{12,8},{14,10},{1,5},{3,7},... | collective-permute-start | bytes 32 | tf_op jit(solution)/shard_map/ppermute | solution.py:33
  221.9 5.0 %collective-permute-start.30 = (f32[2]{0:T(128)S(1)}, f32[2]{0:T(128)S(1)}, u32[]{:S(2)}, u32[]{:S(2)}) collective-permute-start(f32[2]{0:T(128)S(1)} %add.157), channel_id=1, source_target_pairs={{0,8},{2,10},{4,12},{6,14},{8,0},{10,2},{12,4},{14,6},{1,9},{3,11}... | collective-permute-start | bytes 32 | tf_op jit(solution)/shard_map/ppermute | solution.py:33
  227.0 4.4 %collective-permute-start.22 = (f32[8,2304]{1,0:T(8,128)S(1)}, f32[8,2304]{1,0:T(8,128)S(1)}, u32[]{:S(2)}, u32[]{:S(2)}) collective-permute-start(f32[8,2304]{1,0:T(8,128)S(1)} %constant_dynamic-slice_fusion.1), channel_id=1, source_target_pairs={{0,4},{2,6},{4,0},{6,2},{8,12},{10,14},{12,8},{14,10},{1,5},{3,7},... | collective-permute-start | bytes 221192 | tf_op jit(solution)/shard_map/ppermute | solution.py:48
  232.8 4.0 %collective-permute-start.24 = (f32[4,2304]{1,0:T(4,128)S(1)}, f32[4,2304]{1,0:T(4,128)S(1)}, u32[]{:S(2)}, u32[]{:S(2)}) collective-permute-start(f32[4,2304]{1,0:T(4,128)S(1)} %dynamic-slice_add_fusion.5), channel_id=1, source_target_pairs={{0,1},{1,0},{2,3},{3,2},{4,5},{5,4},{6,7},{7,6},{8,9},{9,8},{10,11... | collective-permute-start | bytes 110600 | tf_op jit(solution)/shard_map/ppermute | solution.py:33
  (19 other events, 81.5 us)

commit v5 on v4

--- a/solution.py
+++ b/solution.py
@@ -35,18 +35,25 @@
     return value
 
 
-def halving_scatter(value, axes):
+def halving_order(axes):
+    order = []
     for axis in axes:
+        step = 1
+        while step < lax.axis_size(axis):
+            order.append((axis, step))
+            step *= 2
+    return order
+
+
+def halving_scatter(value, order):
+    for axis, step in order:
         count = lax.axis_size(axis)
         index = lax.axis_index(axis)
-        step = count // 2
-        while step >= 1:
-            half = value.shape[0] // 2
-            upper = (index // step) % 2
-            keep = lax.dynamic_slice_in_dim(value, upper * half, half, axis=0)
-            send = lax.dynamic_slice_in_dim(value, (1 - upper) * half, half, axis=0)
-            value = keep + lax.ppermute(send, axis, [(i, i ^ step) for i in range(count)])
-            step //= 2
+        half = value.shape[0] // 2
+        upper = (index // step) % 2
+        keep = lax.dynamic_slice_in_dim(value, upper * half, half, axis=0)
+        send = lax.dynamic_slice_in_dim(value, (1 - upper) * half, half, axis=0)
+        value = keep + lax.ppermute(send, axis, [(i, i ^ step) for i in range(count)])
     return value
 
 
@@ -104,6 +111,10 @@
         dimension_numbers=("CHWN", "IHWO", "CHWN"),
         preferred_element_type=jnp.float32,
     ).reshape(channels, 9 * channels)
+    order = halving_order(("cols", "rows"))
+    bits = len(order)
+    local_grad = local_grad.reshape((2,) * bits + (channels >> bits, 9 * channels))
+    local_grad = local_grad.transpose(tuple(reversed(range(bits))) + (bits, bits + 1))
     local_grad, outputs, input_grad, padded_probe = lax.optimization_barrier(
         (local_grad, outputs, input_grad, padded_probe)
     )
@@ -121,7 +132,7 @@
     sum_probe = totals[1]
     lipschitz = jnp.sqrt(jnp.sqrt(sum_back / sum_probe))
     probe_out = back / jnp.sqrt(sum_back / count + 1e-06)
-    owned = halving_scatter(local_grad, ("rows", "cols"))
+    owned = halving_scatter(local_grad.reshape(channels, 9 * channels), order)
     owned = butterfly_sum(owned, ("rep",))
     total_cells = batch * lax.axis_size("rep") * height * rows_count * breadth * cols_count
     kernel_grad = owned * (1.0 / math.sqrt(total_cells))

time: 240 us -> 262 us (1.092); the launches traced: 239 us -> 257 us
  local copies, waits for them, and re-layouts: 22.1 us -> 37.9 us
  loops' own time: 12.7 us -> 24.5 us
  waiting for transfers between devices: 52.8 us -> 46.2 us
  starting transfers between devices: 107 us -> 101 us
  other arithmetic: 17.2 us -> 21 us
    ppermute x25, waiting for transfers between devices: 38.9 us -> 26.4 us  [butterfly_sum(): lax.ppermute(value, axis, [(i, i ^ step) for i in range(count)])]
    another operation x1, loops' own time: 12.7 us -> 24.5 us  [per_device(): lax.scan(power_step, (padded_probe, iterate), None, length=ITERS - 1)]
    ppermute x25, starting transfers between devices: 63.5 us -> 55.5 us  [butterfly_sum(): lax.ppermute(value, axis, [(i, i ^ step) for i in range(count)])]
    ppermute x10, starting transfers between devices: 17.3 us -> 23.8 us  [extended(): lax.ppermute(head, axis, [((i + 1) % count, i) for i in range(ends)])]
    ppermute x10, starting transfers between devices: 14.8 us -> 9.02 us  [extended(): lax.ppermute(tail, axis, [(i, (i + 1) % count) for i in range(ends)])]
    ppermute x10, waiting for transfers between devices: 0.03 us -> 5.37 us  [extended(): lax.ppermute(head, axis, [((i + 1) % count, i) for i in range(ends)])]
    convert_element_type x2, local copies, waits for them, and re-layouts: 0.93 us -> 4.99 us  [per_device(): input_grad = conv(padded_up, kernel, True).astype(jnp.bfloat16)]
    another operation x0 -> x1, local copies, waits for them, and re-layouts: none -> 3.22 us  [per_device(): local_grad.reshape((2,) * bits + (channels >> bits, 9 * channels))]
  transfers between devices with their start and end apart: 51 -> 51, of which waited for: 25 -> 23; matrix products, arithmetic and copies ran while one was open for 11% -> 13% of each run, Pallas kernels for 0% -> 0%
where the time goes in v5:
time: 262 us; the launch traced here: 257 us
  starting transfers between devices  101 us (39%)
  waiting for transfers between devices  46.2 us (18%)
  local copies, waits for them, and re-layouts  37.9 us (14%)
  loops' own time  24.5 us (9%)
  matrix products  21.9 us (8%)
  other arithmetic  21 us (8%)
  between operations  4.73 us (2%)
    ppermute x25, starting transfers between devices, butterfly_sum(): lax.ppermute(value, axis, [(i, i ^ step) for i in range(count)])  55.5 us
    ppermute x25, waiting for transfers between devices, butterfly_sum(): lax.ppermute(value, axis, [(i, i ^ step) for i in range(count)])  26.4 us
    another operation x1, loops' own time, per_device(): lax.scan(power_step, (padded_probe, iterate), None, length=ITERS - 1)  24.5 us
    ppermute x10, starting transfers between devices, extended(): lax.ppermute(head, axis, [((i + 1) % count, i) for i in range(ends)])  23.8 us
    conv_general_dilated x10, matrix products, conv(): lax.conv_general_dilated(padded, weights, window_strides=(1, 1), padding=...  15.2 us
    ppermute x6, waiting for transfers between devices, halving_scatter(): lax.ppermute(send, axis, [(i, i ^ step) for i in range(count)])  14.4 us
    ppermute x6, starting transfers between devices, halving_scatter(): lax.ppermute(send, axis, [(i, i ^ step) for i in range(count)])  12.5 us
    ppermute x10, starting transfers between devices, extended(): lax.ppermute(tail, axis, [(i, (i + 1) % count) for i in range(ends)])  9.02 us
  transfers between devices with their start and end apart: 51, of which 23 were waited for; matrix products, arithmetic and copies ran while one was open for 13% of the time, Pallas kernels for 0%

profile of v5, /device:TPU:0, one launch (start us, length us, event | category | flops | bytes accessed | tf_op | source)
XLA Modules:
  0.0 257.0 jit_solution(12304978498940193927)
XLA Ops:
  2.8 4.0 %collective-permute-start.14 = (bf16[2,32,256]{2,0,1:T(2,128)(2,1)}, bf16[2,32,256]{2,0,1:T(2,128)(2,1)}, u32[]{:S(2)}, u32[]{:S(2)}) collective-permute-start(bf16[2,32,256]{2,0,1:T(2,128)(2,1)} %get-tuple-element.81), channel_id=1, source_target_pairs={{0,16},{16,32},{32,48},{48,64},{64,80},{80,96},{96,112},{112,0},{1... | collective-permute-start | bytes 98312 | tf_op jit(solution)/shard_map/ppermute | solution.py:19
  6.7 2.2 collective-permute-start.15
  8.9 2.1 copy.41
  12.8 3.2 %collective-permute-start.10 = (bf16[8,1,32,256]{3,0,2,1:T(8,128)(2,1)}, bf16[8,1,32,256]{3,0,2,1:T(8,128)(2,1)S(1)}, u32[]{:S(2)}, u32[]{:S(2)}) collective-permute-start(bf16[8,1,32,256]{3,0,2,1:T(8,128)(2,1)} %get-tuple-element.77), channel_id=1, source_target_pairs={{0,16},{16,32},{32,48},{48,64},{64,80},{80,96},{96,112},{1,17},{17... | collective-permute-start | bytes 393224 | tf_op jit(solution)/shard_map/ppermute | solution.py:19
  18.3 2.9 %collective-permute-start.17 = (bf16[20,2,256]{2,0,1:T(8,128)(2,1)S(1)}, bf16[20,2,256]{2,0,1:T(8,128)(2,1)S(1)}, u32[]{:S(2)}, u32[]{:S(2)}) collective-permute-start(bf16[20,2,256]{2,0,1:T(8,128)(2,1)S(1)} %get-tuple-element.80), channel_id=1, source_target_pairs={{2,0},{4,2},{6,4},{8,6},{10,8},{12,10},{14,12},{0,14},{3,1},{5,3},... | collective-permute-start | bytes 61448 | tf_op jit(solution)/shard_map/ppermute | solution.py:21
  21.2 3.5 %collective-permute-done.11 = bf16[8,1,32,256]{3,0,2,1:T(8,128)(2,1)} collective-permute-done((bf16[8,1,32,256]{3,0,2,1:T(8,128)(2,1)}, bf16[8,1,32,256]{3,0,2,1:T(8,128)(2,1)}, u32[]{:S(2)}, u32[]{:S(2)}) %collective-permute-start.11) | collective-permute-done | bytes 131104 | tf_op jit(solution)/shard_map/ppermute | solution.py:21
  29.9 1.9 collective-permute-done.13
  31.7 2.0 pad_maximum_fusion.1
  33.7 2.3 slice_bitcast_fusion.3
  36.1 6.7 %fusion.46 = f32[256,3,3,256]{0,3,2,1:T(8,128)} fusion(bf16[8,18,34,256]{3,0,2,1:T(8,128)(2,1)S(1)} %pad_maximum_fusion.1, bf16[4,16,32,256]{3,2,1,0:T(8,128)(2,1)S(1)} %copy-done.9), kind=kOutput, calls=%fused_computation.62 | convolution fusion | flops 2415919104 | bytes 4661248 | tf_op jit(solution)/shard_map/conv_general_dilated | solution.py:106
  45.0 3.3 %select_convert_fusion.1 = bf16[16,32,5,256]{3,1,2,0:T(8,128)(2,1)S(1)} fusion(bf16[3,3,256,256]{3,2,1,0:T(8,128)(2,1)S(1)} %copy-done.10, bf16[18,4,8,7,256]{4,1,3,2,0:T(4,128)(2,1)S(1)} %fusion.29, pred[32,5]{0,1:T(8,128)(4,1)S(1)} %copy-done.17), kind=kOutput, calls=%fused_computation.39 | convolution fusion | flops 3021209600 | bytes 4554912 | tf_op jit(solution)/shard_map/conv_general_dilated | solution.py:63
  52.1 3.3 %select_convert_fusion = bf16[16,32,5,256]{3,1,2,0:T(8,128)(2,1)S(1)} fusion(bf16[3,3,256,256]{3,2,1,0:T(8,128)(2,1)S(1)} %copy-done.10, bf16[18,4,8,7,256]{4,1,3,2,0:T(4,128)(2,1)S(1)} %fusion.30, pred[32,5]{0,1:T(8,128)(4,1)S(1)} %copy-done.17), kind=kOutput, calls=%fused_computation.38 | convolution fusion | flops 3021209600 | bytes 4554912 | tf_op jit(solution)/shard_map/conv_general_dilated | solution.py:63
  55.3 1.8 copy.48
  57.2 3.1 %copy.44 = f32[256,3,3,256]{3,2,1,0:T(4,128)S(1)} copy(f32[256,3,3,256]{0,3,2,1:T(8,128)} %fusion.46) | data formatting | bytes 4718592 | tf_op jit(solution)/shard_map/conv_general_dilated | solution.py:106
  60.3 3.2 %reshape_reshape.3 = f32[2,2,2,2,2,2,4,2304]{7,6,5,4,3,2,1,0:T(4,128)} reshape(f32[256,3,3,256]{3,2,1,0:T(4,128)S(1)} %copy.44) | data formatting | bytes 4718592 | tf_op jit(solution)/shard_map/reshape;reshape | solution.py:116
  63.5 3.1 %slice_bitcast_fusion.4 = (bf16[4,16,32,256]{3,1,2,0:T(8,128)(2,1)}, bf16[4,16,32,256]{3,1,2,0:T(8,128)(2,1)}) fusion(bf16[16,4,40,256]{3,0,2,1:T(8,128)(2,1)} %bitcast.118, bf16[16,4,40,256]{3,0,2,1:T(8,128)(2,1)} %bitcast.117), kind=kLoop, calls=%fused_computation.57 | loop fusion | bytes 4194304 | tf_op jit(solution)/shard_map/convert_element_type | solution.py:105
  68.3 2.6 %reshape.28 = f32[256,2304]{1,0:T(8,128)S(1)} reshape(f32[2,2,2,2,2,2,4,2304]{7,6,5,4,3,2,1,0:T(4,128)} %copy.50) | data formatting | bytes 4718592 | tf_op jit(solution)/shard_map/reshape | solution.py:135
  72.1 3.0 %collective-permute-start.18 = (f32[128,2304]{1,0:T(8,128)}, f32[128,2304]{1,0:T(8,128)}, u32[]{:S(2)}, u32[]{:S(2)}) collective-permute-start(f32[128,2304]{1,0:T(8,128)} %constant_dynamic-slice_fusion.5), channel_id=1, source_target_pairs={{0,2},{2,0},{4,6},{6,4},{8,10},{10,8},{12,14},{14,12},{1,3},{3,1},... | collective-permute-start | bytes 3538952 | tf_op jit(solution)/shard_map/ppermute | solution.py:56
  75.1 118.9 %while.14 = (s32[]{:T(128)}, bf16[20,36,256]{2,0,1:T(8,128)(2,1)S(1)}, bf16[16,32,256]{2,0,1:T(8,128)(2,1)}, f32[3]{0:T(128)S(1)}, bf16[3,3,256,256]{3,2,1,0:T(8...) while((s32[]{:T(128)}, bf16[20,36,256]{2,0,1:T(8,128)(2,1)S(1)}, ...), condition=%wide.region_2.3_spmd, body=%wide.region_0.2_spmd.sunk | while | flops 1609732096 | bytes 19315492 | solution.py:121
  88.9 2.4 collective-permute-start
  91.3 3.4 %collective-permute-start.3 = (f32[2,32,256]{2,0,1:T(2,128)S(1)}, f32[2,32,256]{2,0,1:T(2,128)S(1)}, u32[]{:S(2)}, u32[]{:S(2)}) collective-permute-start(f32[2,32,256]{2,0,1:T(2,128)S(1)} %slice_bitcast_fusion.11), channel_id=1, source_target_pairs={{16,0},{32,16},{48,32},{64,48},{80,64},{96,80},{112,96},{0,112},{1... | collective-permute-start | bytes 196616 | tf_op jit(solution)/shard_map/while/body/eval_jaxpr/ppermute | solution.py:21
  96.5 2.9 %collective-permute-start.1 = (f32[]{:T(128)}, f32[]{:T(128)}, u32[]{:S(2)}, u32[]{:S(2)}) collective-permute-start(f32[]{:T(128)} %add.180), channel_id=1, source_target_pairs={{0,32},{16,48},{32,0},{48,16},{64,96},{80,112},{96,64},{112,80},{1... | collective-permute-start | bytes 20 | tf_op jit(solution)/shard_map/while/body/eval_jaxpr/ppermute | solution.py:33
  100.7 4.1 %collective-permute-start.2 = (f32[]{:T(128)}, f32[]{:T(128)}, u32[]{:S(2)}, u32[]{:S(2)}) collective-permute-start(f32[]{:T(128)} %add.181), channel_id=1, source_target_pairs={{0,64},{16,80},{32,96},{48,112},{64,0},{80,16},{96,32},{112,48},{1... | collective-permute-start | bytes 20 | tf_op jit(solution)/shard_map/while/body/eval_jaxpr/ppermute | solution.py:33
  114.3 3.4 %collective-permute-start.9 = (f32[]{:T(128)}, f32[]{:T(128)}, u32[]{:S(2)}, u32[]{:S(2)}) collective-permute-start(f32[]{:T(128)} %add.184), channel_id=1, source_target_pairs={{0,8},{2,10},{4,12},{6,14},{8,0},{10,2},{12,4},{14,6},{1,9},{3,11}... | collective-permute-start | bytes 20 | tf_op jit(solution)/shard_map/while/body/eval_jaxpr/ppermute | solution.py:33
  125.3 2.1 collective-permute-start
  127.5 3.5 %collective-permute-start.3 = (f32[2,32,256]{2,0,1:T(2,128)S(1)}, f32[2,32,256]{2,0,1:T(2,128)S(1)}, u32[]{:S(2)}, u32[]{:S(2)}) collective-permute-start(f32[2,32,256]{2,0,1:T(2,128)S(1)} %slice_bitcast_fusion.11), channel_id=1, source_target_pairs={{16,0},{32,16},{48,32},{64,48},{80,64},{96,80},{112,96},{0,112},{1... | collective-permute-start | bytes 196616 | tf_op jit(solution)/shard_map/while/body/eval_jaxpr/ppermute | solution.py:21
  132.6 2.9 %collective-permute-start.1 = (f32[]{:T(128)}, f32[]{:T(128)}, u32[]{:S(2)}, u32[]{:S(2)}) collective-permute-start(f32[]{:T(128)} %add.180), channel_id=1, source_target_pairs={{0,32},{16,48},{32,0},{48,16},{64,96},{80,112},{96,64},{112,80},{1... | collective-permute-start | bytes 20 | tf_op jit(solution)/shard_map/while/body/eval_jaxpr/ppermute | solution.py:33
  136.9 4.8 %collective-permute-start.2 = (f32[]{:T(128)}, f32[]{:T(128)}, u32[]{:S(2)}, u32[]{:S(2)}) collective-permute-start(f32[]{:T(128)} %add.181), channel_id=1, source_target_pairs={{0,64},{16,80},{32,96},{48,112},{64,0},{80,16},{96,32},{112,48},{1... | collective-permute-start | bytes 20 | tf_op jit(solution)/shard_map/while/body/eval_jaxpr/ppermute | solution.py:33
  143.7 1.9 collective-permute-start.5
  147.9 2.0 collective-permute-done.8
  150.6 2.0 collective-permute-start.9
  152.6 3.1 %collective-permute-done.9 = f32[]{:T(128)} collective-permute-done((f32[]{:T(128)}, f32[]{:T(128)}, u32[]{:S(2)}, u32[]{:S(2)}) %collective-permute-start.9) | collective-permute-done | bytes 36 | tf_op jit(solution)/shard_map/while/body/eval_jaxpr/ppermute | solution.py:33
  161.7 2.4 collective-permute-start
  164.1 4.6 %collective-permute-start.3 = (f32[2,32,256]{2,0,1:T(2,128)S(1)}, f32[2,32,256]{2,0,1:T(2,128)S(1)}, u32[]{:S(2)}, u32[]{:S(2)}) collective-permute-start(f32[2,32,256]{2,0,1:T(2,128)S(1)} %slice_bitcast_fusion.11), channel_id=1, source_target_pairs={{16,0},{32,16},{48,32},{64,48},{80,64},{96,80},{112,96},{0,112},{1... | collective-permute-start | bytes 196616 | tf_op jit(solution)/shard_map/while/body/eval_jaxpr/ppermute | solution.py:21
  174.6 3.5 %collective-permute-start.2 = (f32[]{:T(128)}, f32[]{:T(128)}, u32[]{:S(2)}, u32[]{:S(2)}) collective-permute-start(f32[]{:T(128)} %add.181), channel_id=1, source_target_pairs={{0,64},{16,80},{32,96},{48,112},{64,0},{80,16},{96,32},{112,48},{1... | collective-permute-start | bytes 20 | tf_op jit(solution)/shard_map/while/body/eval_jaxpr/ppermute | solution.py:33
  182.9 2.7 %collective-permute-start.8 = (f32[]{:T(128)}, f32[]{:T(128)}, u32[]{:S(2)}, u32[]{:S(2)}) collective-permute-start(f32[]{:T(128)} %add.183), channel_id=1, source_target_pairs={{0,4},{2,6},{4,0},{6,2},{8,12},{10,14},{12,8},{14,10},{1,5},{3,7},... | collective-permute-start | bytes 20 | tf_op jit(solution)/shard_map/while/body/eval_jaxpr/ppermute | solution.py:33
  187.2 2.9 %collective-permute-start.9 = (f32[]{:T(128)}, f32[]{:T(128)}, u32[]{:S(2)}, u32[]{:S(2)}) collective-permute-start(f32[]{:T(128)} %add.184), channel_id=1, source_target_pairs={{0,8},{2,10},{4,12},{6,14},{8,0},{10,2},{12,4},{14,6},{1,9},{3,11}... | collective-permute-start | bytes 20 | tf_op jit(solution)/shard_map/while/body/eval_jaxpr/ppermute | solution.py:33
  190.1 2.2 collective-permute-done.9
  194.2 1.8 dynamic-slice_add_fusion
  200.9 10.1 %collective-permute-done.19 = f32[64,2304]{1,0:T(8,128)S(1)} collective-permute-done((f32[64,2304]{1,0:T(8,128)S(1)}, f32[64,2304]{1,0:T(8,128)S(1)}, u32[]{:S(2)}, u32[]{:S(2)}) %collective-permute-start.19) | collective-permute-done | bytes 589856 | tf_op jit(solution)/shard_map/ppermute | solution.py:56
  214.1 2.1 collective-permute-start.25
  221.7 2.4 collective-permute-start.21
  225.6 4.1 %collective-permute-start.27 = (f32[2]{0:T(128)S(1)}, f32[2]{0:T(128)S(1)}, u32[]{:S(2)}, u32[]{:S(2)}) collective-permute-start(f32[2]{0:T(128)S(1)} %fusion.81), channel_id=1, source_target_pairs={{0,64},{16,80},{32,96},{48,112},{64,0},{80,16},{96,32},{112,48},{1... | collective-permute-start | bytes 32 | tf_op jit(solution)/shard_map/ppermute | solution.py:33
  233.5 2.4 collective-permute-done.29
  235.9 2.0 collective-permute-start.30
  237.9 3.0 %collective-permute-done.30 = f32[2]{0:T(128)S(1)} collective-permute-done((f32[2]{0:T(128)S(1)}, f32[2]{0:T(128)S(1)}, u32[]{:S(2)}, u32[]{:S(2)}) %collective-permute-start.30) | collective-permute-done | bytes 40 | tf_op jit(solution)/shard_map/ppermute | solution.py:33
  242.8 2.7 %collective-permute-done.22 = f32[8,2304]{1,0:T(8,128)S(1)} collective-permute-done((f32[8,2304]{1,0:T(8,128)S(1)}, f32[8,2304]{1,0:T(8,128)S(1)}, u32[]{:S(2)}, u32[]{:S(2)}) %collective-permute-start.22) | collective-permute-done | bytes 73760 | tf_op jit(solution)/shard_map/ppermute | solution.py:56
  245.5 3.6 %collective-permute-start.23 = (f32[4,2304]{1,0:T(4,128)S(1)}, f32[4,2304]{1,0:T(4,128)S(1)}, u32[]{:S(2)}, u32[]{:S(2)}) collective-permute-start(f32[4,2304]{1,0:T(4,128)S(1)} %constant_dynamic-slice_fusion), channel_id=1, source_target_pairs={{0,64},{16,80},{32,96},{48,112},{64,0},{80,16},{96,32},{112,48},{1... | collective-permute-start | bytes 110600 | tf_op jit(solution)/shard_map/ppermute | solution.py:56
  (213 shorter events, 82.5 us)
Async XLA Ops:
  2.8 14.7 %collective-permute-start.14 = (bf16[2,32,256]{2,0,1:T(2,128)(2,1)}, bf16[2,32,256]{2,0,1:T(2,128)(2,1)}, u32[]{:S(2)}, u32[]{:S(2)}) collective-permute-start(bf16[2,32,256]{2,0,1:T(2,128)(2,1)} %get-tuple-element.81), channel_id=1, source_target_pairs={{0,16},{16,32},{32,48},{48,64},{64,80},{80,96},{96,112},{112,0},{1... | collective-permute-start | bytes 98312 | tf_op jit(solution)/shard_map/ppermute | solution.py:19
  6.7 10.8 %collective-permute-start.15 = (bf16[2,32,256]{2,0,1:T(2,128)(2,1)}, bf16[2,32,256]{2,0,1:T(2,128)(2,1)}, u32[]{:S(2)}, u32[]{:S(2)}) collective-permute-start(bf16[2,32,256]{2,0,1:T(2,128)(2,1)} %get-tuple-element.82), channel_id=1, source_target_pairs={{16,0},{32,16},{48,32},{64,48},{80,64},{96,80},{112,96},{0,112},{1... | collective-permute-start | bytes 98312 | tf_op jit(solution)/shard_map/ppermute | solution.py:21
  12.8 8.4 %collective-permute-start.10 = (bf16[8,1,32,256]{3,0,2,1:T(8,128)(2,1)}, bf16[8,1,32,256]{3,0,2,1:T(8,128)(2,1)S(1)}, u32[]{:S(2)}, u32[]{:S(2)}) collective-permute-start(bf16[8,1,32,256]{3,0,2,1:T(8,128)(2,1)} %get-tuple-element.77), channel_id=1, source_target_pairs={{0,16},{16,32},{32,48},{48,64},{64,80},{80,96},{96,112},{1,17},{17... | collective-permute-start | bytes 393224 | tf_op jit(solution)/shard_map/ppermute | solution.py:19
  16.0 8.7 %collective-permute-start.11 = (bf16[8,1,32,256]{3,0,2,1:T(8,128)(2,1)}, bf16[8,1,32,256]{3,0,2,1:T(8,128)(2,1)}, u32[]{:S(2)}, u32[]{:S(2)}) collective-permute-start(bf16[8,1,32,256]{3,0,2,1:T(8,128)(2,1)} %get-tuple-element.78), channel_id=1, source_target_pairs={{16,0},{32,16},{48,32},{64,48},{80,64},{96,80},{112,96},{17,1},{33... | collective-permute-start | bytes 393224 | tf_op jit(solution)/shard_map/ppermute | solution.py:21
  18.2 9.8 %collective-permute-start.16 = (bf16[20,2,256]{2,0,1:T(8,128)(2,1)S(1)}, bf16[20,2,256]{2,0,1:T(8,128)(2,1)S(1)}, u32[]{:S(2)}, u32[]{:S(2)}) collective-permute-start(bf16[20,2,256]{2,0,1:T(8,128)(2,1)S(1)} %get-tuple-element.79), channel_id=1, source_target_pairs={{0,2},{2,4},{4,6},{6,8},{8,10},{10,12},{12,14},{14,0},{1,3},{3,5},... | collective-permute-start | bytes 61448 | tf_op jit(solution)/shard_map/ppermute | solution.py:19
  18.3 9.8 %collective-permute-start.17 = (bf16[20,2,256]{2,0,1:T(8,128)(2,1)S(1)}, bf16[20,2,256]{2,0,1:T(8,128)(2,1)S(1)}, u32[]{:S(2)}, u32[]{:S(2)}) collective-permute-start(bf16[20,2,256]{2,0,1:T(8,128)(2,1)S(1)} %get-tuple-element.80), channel_id=1, source_target_pairs={{2,0},{4,2},{6,4},{8,6},{10,8},{12,10},{14,12},{0,14},{3,1},{5,3},... | collective-permute-start | bytes 61448 | tf_op jit(solution)/shard_map/ppermute | solution.py:21
  25.5 4.4 %collective-permute-start.12 = (bf16[8,18,1,256]{3,0,2,1:T(8,128)(2,1)S(1)}, bf16[8,18,1,256]{3,0,2,1:T(8,128)(2,1)S(1)}, u32[]{:S(2)}, u32[]{:S(2)}) collective-permute-start(bf16[8,18,1,256]{3,0,2,1:T(8,128)(2,1)S(1)} %get-tuple-element.75), channel_id=1, source_target_pairs={{0,2},{2,4},{4,6},{6,8},{8,10},{10,12},{12,14},{1,3},{3,5},{5,7},{... | collective-permute-start | bytes 221192 | tf_op jit(solution)/shard_map/ppermute | solution.py:19
  26.8 5.0 %collective-permute-start.13 = (bf16[8,18,1,256]{3,0,2,1:T(8,128)(2,1)S(1)}, bf16[8,18,1,256]{3,0,2,1:T(8,128)(2,1)S(1)}, u32[]{:S(2)}, u32[]{:S(2)}) collective-permute-start(bf16[8,18,1,256]{3,0,2,1:T(8,128)(2,1)S(1)} %get-tuple-element.76), channel_id=1, source_target_pairs={{2,0},{4,2},{6,4},{8,6},{10,8},{12,10},{14,12},{3,1},{5,3},{7,5},{... | collective-permute-start | bytes 221192 | tf_op jit(solution)/shard_map/ppermute | solution.py:21
  72.1 122.1 %collective-permute-start.18 = (f32[128,2304]{1,0:T(8,128)}, f32[128,2304]{1,0:T(8,128)}, u32[]{:S(2)}, u32[]{:S(2)}) collective-permute-start(f32[128,2304]{1,0:T(8,128)} %constant_dynamic-slice_fusion.5), channel_id=1, source_target_pairs={{0,2},{2,0},{4,6},{6,4},{8,10},{10,8},{12,14},{14,12},{1,3},{3,1},... | collective-permute-start | bytes 3538952 | tf_op jit(solution)/shard_map/ppermute | solution.py:56
  88.9 6.2 %collective-permute-start = (f32[]{:T(128)}, f32[]{:T(128)}, u32[]{:S(2)}, u32[]{:S(2)}) collective-permute-start(f32[]{:T(128)} %multiply_reduce_fusion.3), channel_id=1, source_target_pairs={{0,16},{16,0},{32,48},{48,32},{64,80},{80,64},{96,112},{112,96},{1... | collective-permute-start | bytes 20 | tf_op jit(solution)/shard_map/while/body/eval_jaxpr/ppermute | solution.py:33
  91.3 15.2 %collective-permute-start.3 = (f32[2,32,256]{2,0,1:T(2,128)S(1)}, f32[2,32,256]{2,0,1:T(2,128)S(1)}, u32[]{:S(2)}, u32[]{:S(2)}) collective-permute-start(f32[2,32,256]{2,0,1:T(2,128)S(1)} %slice_bitcast_fusion.11), channel_id=1, source_target_pairs={{16,0},{32,16},{48,32},{64,48},{80,64},{96,80},{112,96},{0,112},{1... | collective-permute-start | bytes 196616 | tf_op jit(solution)/shard_map/while/body/eval_jaxpr/ppermute | solution.py:21
  94.8 11.7 %collective-permute-start.4 = (f32[2,32,256]{2,0,1:T(2,128)S(1)}, f32[2,32,256]{2,0,1:T(2,128)S(1)}, u32[]{:S(2)}, u32[]{:S(2)}) collective-permute-start(f32[2,32,256]{2,0,1:T(2,128)S(1)} %slice_bitcast_fusion.13), channel_id=1, source_target_pairs={{0,16},{16,32},{32,48},{48,64},{64,80},{80,96},{96,112},{112,0},{1... | collective-permute-start | bytes 196616 | tf_op jit(solution)/shard_map/while/body/eval_jaxpr/ppermute | solution.py:19
  96.5 3.6 %collective-permute-start.1 = (f32[]{:T(128)}, f32[]{:T(128)}, u32[]{:S(2)}, u32[]{:S(2)}) collective-permute-start(f32[]{:T(128)} %add.180), channel_id=1, source_target_pairs={{0,32},{16,48},{32,0},{48,16},{64,96},{80,112},{96,64},{112,80},{1... | collective-permute-start | bytes 20 | tf_op jit(solution)/shard_map/while/body/eval_jaxpr/ppermute | solution.py:33
  100.7 5.1 %collective-permute-start.2 = (f32[]{:T(128)}, f32[]{:T(128)}, u32[]{:S(2)}, u32[]{:S(2)}) collective-permute-start(f32[]{:T(128)} %add.181), channel_id=1, source_target_pairs={{0,64},{16,80},{32,96},{48,112},{64,0},{80,16},{96,32},{112,48},{1... | collective-permute-start | bytes 20 | tf_op jit(solution)/shard_map/while/body/eval_jaxpr/ppermute | solution.py:33
  107.6 13.4 %collective-permute-start.5 = (f32[20,2,256]{2,0,1:T(8,128)S(1)}, f32[20,2,256]{2,0,1:T(8,128)S(1)}, u32[]{:S(2)}, u32[]{:S(2)}) collective-permute-start(f32[20,2,256]{2,0,1:T(8,128)S(1)} %get-tuple-element.127), channel_id=1, source_target_pairs={{2,0},{4,2},{6,4},{8,6},{10,8},{12,10},{14,12},{0,14},{3,1},{5,3},... | collective-permute-start | bytes 122888 | tf_op jit(solution)/shard_map/while/body/eval_jaxpr/ppermute | solution.py:21
  109.3 11.6 %collective-permute-start.6 = (f32[20,2,256]{2,0,1:T(8,128)S(1)}, f32[20,2,256]{2,0,1:T(8,128)S(1)}, u32[]{:S(2)}, u32[]{:S(2)}) collective-permute-start(f32[20,2,256]{2,0,1:T(8,128)S(1)} %get-tuple-element.128), channel_id=1, source_target_pairs={{0,2},{2,4},{4,6},{6,8},{8,10},{10,12},{12,14},{14,0},{1,3},{3,5},... | collective-permute-start | bytes 122888 | tf_op jit(solution)/shard_map/while/body/eval_jaxpr/ppermute | solution.py:19
  110.0 3.6 %collective-permute-start.8 = (f32[]{:T(128)}, f32[]{:T(128)}, u32[]{:S(2)}, u32[]{:S(2)}) collective-permute-start(f32[]{:T(128)} %add.183), channel_id=1, source_target_pairs={{0,4},{2,6},{4,0},{6,2},{8,12},{10,14},{12,8},{14,10},{1,5},{3,7},... | collective-permute-start | bytes 20 | tf_op jit(solution)/shard_map/while/body/eval_jaxpr/ppermute | solution.py:33
  114.3 5.1 %collective-permute-start.9 = (f32[]{:T(128)}, f32[]{:T(128)}, u32[]{:S(2)}, u32[]{:S(2)}) collective-permute-start(f32[]{:T(128)} %add.184), channel_id=1, source_target_pairs={{0,8},{2,10},{4,12},{6,14},{8,0},{10,2},{12,4},{14,6},{1,9},{3,11}... | collective-permute-start | bytes 20 | tf_op jit(solution)/shard_map/while/body/eval_jaxpr/ppermute | solution.py:33
  125.3 5.9 %collective-permute-start = (f32[]{:T(128)}, f32[]{:T(128)}, u32[]{:S(2)}, u32[]{:S(2)}) collective-permute-start(f32[]{:T(128)} %multiply_reduce_fusion.3), channel_id=1, source_target_pairs={{0,16},{16,0},{32,48},{48,32},{64,80},{80,64},{96,112},{112,96},{1... | collective-permute-start | bytes 20 | tf_op jit(solution)/shard_map/while/body/eval_jaxpr/ppermute | solution.py:33
  127.5 15.2 %collective-permute-start.3 = (f32[2,32,256]{2,0,1:T(2,128)S(1)}, f32[2,32,256]{2,0,1:T(2,128)S(1)}, u32[]{:S(2)}, u32[]{:S(2)}) collective-permute-start(f32[2,32,256]{2,0,1:T(2,128)S(1)} %slice_bitcast_fusion.11), channel_id=1, source_target_pairs={{16,0},{32,16},{48,32},{64,48},{80,64},{96,80},{112,96},{0,112},{1... | collective-permute-start | bytes 196616 | tf_op jit(solution)/shard_map/while/body/eval_jaxpr/ppermute | solution.py:21
  131.0 11.6 %collective-permute-start.4 = (f32[2,32,256]{2,0,1:T(2,128)S(1)}, f32[2,32,256]{2,0,1:T(2,128)S(1)}, u32[]{:S(2)}, u32[]{:S(2)}) collective-permute-start(f32[2,32,256]{2,0,1:T(2,128)S(1)} %slice_bitcast_fusion.13), channel_id=1, source_target_pairs={{0,16},{16,32},{32,48},{48,64},{64,80},{80,96},{96,112},{112,0},{1... | collective-permute-start | bytes 196616 | tf_op jit(solution)/shard_map/while/body/eval_jaxpr/ppermute | solution.py:19
  132.6 3.6 %collective-permute-start.1 = (f32[]{:T(128)}, f32[]{:T(128)}, u32[]{:S(2)}, u32[]{:S(2)}) collective-permute-start(f32[]{:T(128)} %add.180), channel_id=1, source_target_pairs={{0,32},{16,48},{32,0},{48,16},{64,96},{80,112},{96,64},{112,80},{1... | collective-permute-start | bytes 20 | tf_op jit(solution)/shard_map/while/body/eval_jaxpr/ppermute | solution.py:33
  136.9 5.1 %collective-permute-start.2 = (f32[]{:T(128)}, f32[]{:T(128)}, u32[]{:S(2)}, u32[]{:S(2)}) collective-permute-start(f32[]{:T(128)} %add.181), channel_id=1, source_target_pairs={{0,64},{16,80},{32,96},{48,112},{64,0},{80,16},{96,32},{112,48},{1... | collective-permute-start | bytes 20 | tf_op jit(solution)/shard_map/while/body/eval_jaxpr/ppermute | solution.py:33
  142.8 2.9 %collective-permute-start.7 = (f32[]{:T(128)}, f32[]{:T(128)}, u32[]{:S(2)}, u32[]{:S(2)}) collective-permute-start(f32[]{:T(128)} %add.182), channel_id=1, source_target_pairs={{0,2},{2,0},{4,6},{6,4},{8,10},{10,8},{12,14},{14,12},{1,3},{3,1},... | collective-permute-start | bytes 20 | tf_op jit(solution)/shard_map/while/body/eval_jaxpr/ppermute | solution.py:33
  143.7 13.6 %collective-permute-start.5 = (f32[20,2,256]{2,0,1:T(8,128)S(1)}, f32[20,2,256]{2,0,1:T(8,128)S(1)}, u32[]{:S(2)}, u32[]{:S(2)}) collective-permute-start(f32[20,2,256]{2,0,1:T(8,128)S(1)} %get-tuple-element.127), channel_id=1, source_target_pairs={{2,0},{4,2},{6,4},{8,6},{10,8},{12,10},{14,12},{0,14},{3,1},{5,3},... | collective-permute-start | bytes 122888 | tf_op jit(solution)/shard_map/while/body/eval_jaxpr/ppermute | solution.py:21
  145.6 11.6 %collective-permute-start.6 = (f32[20,2,256]{2,0,1:T(8,128)S(1)}, f32[20,2,256]{2,0,1:T(8,128)S(1)}, u32[]{:S(2)}, u32[]{:S(2)}) collective-permute-start(f32[20,2,256]{2,0,1:T(8,128)S(1)} %get-tuple-element.128), channel_id=1, source_target_pairs={{0,2},{2,4},{4,6},{6,8},{8,10},{10,12},{12,14},{14,0},{1,3},{3,5},... | collective-permute-start | bytes 122888 | tf_op jit(solution)/shard_map/while/body/eval_jaxpr/ppermute | solution.py:19
  146.3 3.6 %collective-permute-start.8 = (f32[]{:T(128)}, f32[]{:T(128)}, u32[]{:S(2)}, u32[]{:S(2)}) collective-permute-start(f32[]{:T(128)} %add.183), channel_id=1, source_target_pairs={{0,4},{2,6},{4,0},{6,2},{8,12},{10,14},{12,8},{14,10},{1,5},{3,7},... | collective-permute-start | bytes 20 | tf_op jit(solution)/shard_map/while/body/eval_jaxpr/ppermute | solution.py:33
  150.6 5.1 %collective-permute-start.9 = (f32[]{:T(128)}, f32[]{:T(128)}, u32[]{:S(2)}, u32[]{:S(2)}) collective-permute-start(f32[]{:T(128)} %add.184), channel_id=1, source_target_pairs={{0,8},{2,10},{4,12},{6,14},{8,0},{10,2},{12,4},{14,6},{1,9},{3,11}... | collective-permute-start | bytes 20 | tf_op jit(solution)/shard_map/while/body/eval_jaxpr/ppermute | solution.py:33
  161.7 7.3 %collective-permute-start = (f32[]{:T(128)}, f32[]{:T(128)}, u32[]{:S(2)}, u32[]{:S(2)}) collective-permute-start(f32[]{:T(128)} %multiply_reduce_fusion.3), channel_id=1, source_target_pairs={{0,16},{16,0},{32,48},{48,32},{64,80},{80,64},{96,112},{112,96},{1... | collective-permute-start | bytes 20 | tf_op jit(solution)/shard_map/while/body/eval_jaxpr/ppermute | solution.py:33
  164.1 16.2 %collective-permute-start.3 = (f32[2,32,256]{2,0,1:T(2,128)S(1)}, f32[2,32,256]{2,0,1:T(2,128)S(1)}, u32[]{:S(2)}, u32[]{:S(2)}) collective-permute-start(f32[2,32,256]{2,0,1:T(2,128)S(1)} %slice_bitcast_fusion.11), channel_id=1, source_target_pairs={{16,0},{32,16},{48,32},{64,48},{80,64},{96,80},{112,96},{0,112},{1... | collective-permute-start | bytes 196616 | tf_op jit(solution)/shard_map/while/body/eval_jaxpr/ppermute | solution.py:21
  168.8 11.5 %collective-permute-start.4 = (f32[2,32,256]{2,0,1:T(2,128)S(1)}, f32[2,32,256]{2,0,1:T(2,128)S(1)}, u32[]{:S(2)}, u32[]{:S(2)}) collective-permute-start(f32[2,32,256]{2,0,1:T(2,128)S(1)} %slice_bitcast_fusion.13), channel_id=1, source_target_pairs={{0,16},{16,32},{32,48},{48,64},{64,80},{80,96},{96,112},{112,0},{1... | collective-permute-start | bytes 196616 | tf_op jit(solution)/shard_map/while/body/eval_jaxpr/ppermute | solution.py:19
  170.3 3.6 %collective-permute-start.1 = (f32[]{:T(128)}, f32[]{:T(128)}, u32[]{:S(2)}, u32[]{:S(2)}) collective-permute-start(f32[]{:T(128)} %add.180), channel_id=1, source_target_pairs={{0,32},{16,48},{32,0},{48,16},{64,96},{80,112},{96,64},{112,80},{1... | collective-permute-start | bytes 20 | tf_op jit(solution)/shard_map/while/body/eval_jaxpr/ppermute | solution.py:33
  174.6 5.1 %collective-permute-start.2 = (f32[]{:T(128)}, f32[]{:T(128)}, u32[]{:S(2)}, u32[]{:S(2)}) collective-permute-start(f32[]{:T(128)} %add.181), channel_id=1, source_target_pairs={{0,64},{16,80},{32,96},{48,112},{64,0},{80,16},{96,32},{112,48},{1... | collective-permute-start | bytes 20 | tf_op jit(solution)/shard_map/while/body/eval_jaxpr/ppermute | solution.py:33
  181.4 12.5 %collective-permute-start.5 = (f32[20,2,256]{2,0,1:T(8,128)S(1)}, f32[20,2,256]{2,0,1:T(8,128)S(1)}, u32[]{:S(2)}, u32[]{:S(2)}) collective-permute-start(f32[20,2,256]{2,0,1:T(8,128)S(1)} %get-tuple-element.127), channel_id=1, source_target_pairs={{2,0},{4,2},{6,4},{8,6},{10,8},{12,10},{14,12},{0,14},{3,1},{5,3},... | collective-permute-start | bytes 122888 | tf_op jit(solution)/shard_map/while/body/eval_jaxpr/ppermute | solution.py:21
  182.2 11.6 %collective-permute-start.6 = (f32[20,2,256]{2,0,1:T(8,128)S(1)}, f32[20,2,256]{2,0,1:T(8,128)S(1)}, u32[]{:S(2)}, u32[]{:S(2)}) collective-permute-start(f32[20,2,256]{2,0,1:T(8,128)S(1)} %get-tuple-element.128), channel_id=1, source_target_pairs={{0,2},{2,4},{4,6},{6,8},{8,10},{10,12},{12,14},{14,0},{1,3},{3,5},... | collective-permute-start | bytes 122888 | tf_op jit(solution)/shard_map/while/body/eval_jaxpr/ppermute | solution.py:19
  182.9 3.6 %collective-permute-start.8 = (f32[]{:T(128)}, f32[]{:T(128)}, u32[]{:S(2)}, u32[]{:S(2)}) collective-permute-start(f32[]{:T(128)} %add.183), channel_id=1, source_target_pairs={{0,4},{2,6},{4,0},{6,2},{8,12},{10,14},{12,8},{14,10},{1,5},{3,7},... | collective-permute-start | bytes 20 | tf_op jit(solution)/shard_map/while/body/eval_jaxpr/ppermute | solution.py:33
  187.2 5.1 %collective-permute-start.9 = (f32[]{:T(128)}, f32[]{:T(128)}, u32[]{:S(2)}, u32[]{:S(2)}) collective-permute-start(f32[]{:T(128)} %add.184), channel_id=1, source_target_pairs={{0,8},{2,10},{4,12},{6,14},{8,0},{10,2},{12,4},{14,6},{1,9},{3,11}... | collective-permute-start | bytes 20 | tf_op jit(solution)/shard_map/while/body/eval_jaxpr/ppermute | solution.py:33
  196.1 14.9 %collective-permute-start.19 = (f32[64,2304]{1,0:T(8,128)S(1)}, f32[64,2304]{1,0:T(8,128)S(1)}, u32[]{:S(2)}, u32[]{:S(2)}) collective-permute-start(f32[64,2304]{1,0:T(8,128)S(1)} %constant_dynamic-slice_fusion.4), channel_id=1, source_target_pairs={{0,4},{2,6},{4,0},{6,2},{8,12},{10,14},{12,8},{14,10},{1,5},{3,7},... | collective-permute-start | bytes 1769480 | tf_op jit(solution)/shard_map/ppermute | solution.py:56
  211.1 10.6 %collective-permute-start.20 = (f32[32,2304]{1,0:T(8,128)S(1)}, f32[32,2304]{1,0:T(8,128)S(1)}, u32[]{:S(2)}, u32[]{:S(2)}) collective-permute-start(f32[32,2304]{1,0:T(8,128)S(1)} %constant_dynamic-slice_fusion.3), channel_id=1, source_target_pairs={{0,8},{2,10},{4,12},{6,14},{8,0},{10,2},{12,4},{14,6},{1,9},{3,11}... | collective-permute-start | bytes 884744 | tf_op jit(solution)/shard_map/ppermute | solution.py:56
  214.1 5.1 %collective-permute-start.25 = (f32[2]{0:T(128)S(1)}, f32[2]{0:T(128)S(1)}, u32[]{:S(2)}, u32[]{:S(2)}) collective-permute-start(f32[2]{0:T(128)S(1)} %pad_maximum_fusion.12), channel_id=1, source_target_pairs={{0,16},{16,0},{32,48},{48,32},{64,80},{80,64},{96,112},{112,96},{1... | collective-permute-start | bytes 32 | tf_op jit(solution)/shard_map/ppermute | solution.py:33
  220.5 3.7 %collective-permute-start.26 = (f32[2]{0:T(128)S(1)}, f32[2]{0:T(128)S(1)}, u32[]{:S(2)}, u32[]{:S(2)}) collective-permute-start(f32[2]{0:T(128)S(1)} %fusion.80), channel_id=1, source_target_pairs={{0,32},{16,48},{32,0},{48,16},{64,96},{80,112},{96,64},{112,80},{1... | collective-permute-start | bytes 32 | tf_op jit(solution)/shard_map/ppermute | solution.py:33
  221.7 19.2 %collective-permute-start.21 = (f32[16,2304]{1,0:T(8,128)S(1)}, f32[16,2304]{1,0:T(8,128)S(1)}, u32[]{:S(2)}, u32[]{:S(2)}) collective-permute-start(f32[16,2304]{1,0:T(8,128)S(1)} %constant_dynamic-slice_fusion.2), channel_id=1, source_target_pairs={{0,16},{16,0},{32,48},{48,32},{64,80},{80,64},{96,112},{112,96},{1... | collective-permute-start | bytes 442376 | tf_op jit(solution)/shard_map/ppermute | solution.py:56
  225.6 5.7 %collective-permute-start.27 = (f32[2]{0:T(128)S(1)}, f32[2]{0:T(128)S(1)}, u32[]{:S(2)}, u32[]{:S(2)}) collective-permute-start(f32[2]{0:T(128)S(1)} %fusion.81), channel_id=1, source_target_pairs={{0,64},{16,80},{32,96},{48,112},{64,0},{80,16},{96,32},{112,48},{1... | collective-permute-start | bytes 32 | tf_op jit(solution)/shard_map/ppermute | solution.py:33
  232.4 3.5 %collective-permute-start.29 = (f32[2]{0:T(128)S(1)}, f32[2]{0:T(128)S(1)}, u32[]{:S(2)}, u32[]{:S(2)}) collective-permute-start(f32[2]{0:T(128)S(1)} %add.156), channel_id=1, source_target_pairs={{0,4},{2,6},{4,0},{6,2},{8,12},{10,14},{12,8},{14,10},{1,5},{3,7},... | collective-permute-start | bytes 32 | tf_op jit(solution)/shard_map/ppermute | solution.py:33
  235.9 5.0 %collective-permute-start.30 = (f32[2]{0:T(128)S(1)}, f32[2]{0:T(128)S(1)}, u32[]{:S(2)}, u32[]{:S(2)}) collective-permute-start(f32[2]{0:T(128)S(1)} %add.157), channel_id=1, source_target_pairs={{0,8},{2,10},{4,12},{6,14},{8,0},{10,2},{12,4},{14,6},{1,9},{3,11}... | collective-permute-start | bytes 32 | tf_op jit(solution)/shard_map/ppermute | solution.py:33
  241.0 4.4 %collective-permute-start.22 = (f32[8,2304]{1,0:T(8,128)S(1)}, f32[8,2304]{1,0:T(8,128)S(1)}, u32[]{:S(2)}, u32[]{:S(2)}) collective-permute-start(f32[8,2304]{1,0:T(8,128)S(1)} %constant_dynamic-slice_fusion.1), channel_id=1, source_target_pairs={{0,32},{16,48},{32,0},{48,16},{64,96},{80,112},{96,64},{112,80},{1... | collective-permute-start | bytes 221192 | tf_op jit(solution)/shard_map/ppermute | solution.py:56
  245.5 5.5 %collective-permute-start.23 = (f32[4,2304]{1,0:T(4,128)S(1)}, f32[4,2304]{1,0:T(4,128)S(1)}, u32[]{:S(2)}, u32[]{:S(2)}) collective-permute-start(f32[4,2304]{1,0:T(4,128)S(1)} %constant_dynamic-slice_fusion), channel_id=1, source_target_pairs={{0,64},{16,80},{32,96},{48,112},{64,0},{80,16},{96,32},{112,48},{1... | collective-permute-start | bytes 110600 | tf_op jit(solution)/shard_map/ppermute | solution.py:56
  251.0 4.0 %collective-permute-start.24 = (f32[4,2304]{1,0:T(4,128)S(1)}, f32[4,2304]{1,0:T(4,128)S(1)}, u32[]{:S(2)}, u32[]{:S(2)}) collective-permute-start(f32[4,2304]{1,0:T(4,128)S(1)} %dynamic-slice_add_fusion.5), channel_id=1, source_target_pairs={{0,1},{1,0},{2,3},{3,2},{4,5},{5,4},{6,7},{7,6},{8,9},{9,8},{10,11... | collective-permute-start | bytes 110600 | tf_op jit(solution)/shard_map/ppermute | solution.py:33
  (23 other events, 119.7 us)

commit v6 on v4

--- a/solution.py
+++ b/solution.py
@@ -110,6 +110,7 @@
     (padded_probe, iterate), norm_trace = lax.scan(
         power_step, (padded_probe, iterate), None, length=ITERS - 1
     )
+    local_grad, padded_probe = lax.optimization_barrier((local_grad, padded_probe))
     image = conv(padded_probe[None], kernel, False).astype(jnp.bfloat16)
     back = conv(image, kernel, True)[0]
     wide_iter = iterate.astype(jnp.float32)

time: 240 us -> 261 us (1.087)
  matrix products: 22.1 us -> 34.7 us
  waiting for transfers between devices: 52.8 us -> 61.9 us
    ppermute x6, waiting for transfers between devices: 12.8 us -> 31.2 us  [halving_scatter(): lax.ppermute(send, axis, [(i, i ^ step) for i in range(count)])]
    conv_general_dilated x10, matrix products: 15.2 us -> 27.8 us  [conv(): lax.conv_general_dilated(padded, weights, window_strides=(1, 1), padding=...]
    ppermute x25, waiting for transfers between devices: 38.9 us -> 29.4 us  [butterfly_sum(): lax.ppermute(value, axis, [(i, i ^ step) for i in range(count)])]
    ppermute x10, starting transfers between devices: 17.3 us -> 24.3 us  [extended(): lax.ppermute(head, axis, [((i + 1) % count, i) for i in range(ends)])]
    ppermute x10, starting transfers between devices: 14.8 us -> 10.6 us  [extended(): lax.ppermute(tail, axis, [(i, (i + 1) % count) for i in range(ends)])]
    while x6 -> x0, local copies, waits for them, and re-layouts: 3.25 us -> none
    ppermute x6, starting transfers between devices: 11.4 us -> 8.16 us  [halving_scatter(): lax.ppermute(send, axis, [(i, i ^ step) for i in range(count)])]
    another operation x1, loops' own time: 12.7 us -> 15.3 us  [per_device(): lax.scan(power_step, (padded_probe, iterate), None, length=ITERS - 1)]
  transfers between devices with their start and end apart: 51 -> 51, of which waited for: 25 -> 24; matrix products, arithmetic and copies ran while one was open for 11% -> 9% of each run, Pallas kernels for 0% -> 0%
where the time goes in v6:
time: 261 us; the launch traced here: 259 us
  starting transfers between devices  105 us (40%)
  waiting for transfers between devices  61.9 us (24%)
  matrix products  34.7 us (13%)
  local copies, waits for them, and re-layouts  21.5 us (8%)
  other arithmetic  16.7 us (6%)
  loops' own time  15.3 us (6%)
  between operations  4.38 us (2%)
    ppermute x25, starting transfers between devices, butterfly_sum(): lax.ppermute(value, axis, [(i, i ^ step) for i in range(count)])  61.8 us
    ppermute x6, waiting for transfers between devices, halving_scatter(): lax.ppermute(send, axis, [(i, i ^ step) for i in range(count)])  31.2 us
    ppermute x25, waiting for transfers between devices, butterfly_sum(): lax.ppermute(value, axis, [(i, i ^ step) for i in range(count)])  29.4 us
    conv_general_dilated x10, matrix products, conv(): lax.conv_general_dilated(padded, weights, window_strides=(1, 1), padding=...  27.8 us
    ppermute x10, starting transfers between devices, extended(): lax.ppermute(head, axis, [((i + 1) % count, i) for i in range(ends)])  24.3 us
    another operation x1, loops' own time, per_device(): lax.scan(power_step, (padded_probe, iterate), None, length=ITERS - 1)  15.3 us
    ppermute x10, starting transfers between devices, extended(): lax.ppermute(tail, axis, [(i, (i + 1) % count) for i in range(ends)])  10.6 us
    unnamed x28, local copies, waits for them, and re-layouts  9.57 us
  transfers between devices with their start and end apart: 51, of which 24 were waited for; matrix products, arithmetic and copies ran while one was open for 9% of the time, Pallas kernels for 0%

profile of v6, /device:TPU:0, one launch (start us, length us, event | category | flops | bytes accessed | tf_op | source)
XLA Modules:
  0.0 259.2 jit_solution(4312715804871462074)
XLA Ops:
  2.1 6.2 %collective-permute-start.15 = (bf16[2,32,256]{2,0,1:T(2,128)(2,1)S(1)}, bf16[2,32,256]{2,0,1:T(2,128)(2,1)S(1)}, u32[]{:S(2)}, u32[]{:S(2)}) collective-permute-start(bf16[2,32,256]{2,0,1:T(2,128)(2,1)S(1)} %get-tuple-element.80), channel_id=1, source_target_pairs={{16,0},{32,16},{48,32},{64,48},{80,64},{96,80},{112,96},{0,112},{1... | collective-permute-start | bytes 98312 | tf_op jit(solution)/shard_map/ppermute | solution.py:21
  8.4 2.1 copy.23
  12.8 6.1 %collective-permute-start.10 = (bf16[8,1,32,256]{3,0,2,1:T(8,128)(2,1)S(1)}, bf16[8,1,32,256]{3,0,2,1:T(8,128)(2,1)S(1)}, u32[]{:S(2)}, u32[]{:S(2)}) collective-permute-start(bf16[8,1,32,256]{3,0,2,1:T(8,128)(2,1)S(1)} %get-tuple-element.75), channel_id=1, source_target_pairs={{0,16},{16,32},{32,48},{48,64},{64,80},{80,96},{96,112},{1,17},{17... | collective-permute-start | bytes 393224 | tf_op jit(solution)/shard_map/ppermute | solution.py:19
  23.2 3.0 %collective-permute-start.12 = (bf16[8,18,1,256]{3,0,2,1:T(8,128)(2,1)S(1)}, bf16[8,18,1,256]{3,0,2,1:T(8,128)(2,1)S(1)}, u32[]{:S(2)}, u32[]{:S(2)}) collective-permute-start(bf16[8,18,1,256]{3,0,2,1:T(8,128)(2,1)S(1)} %get-tuple-element.73), channel_id=1, source_target_pairs={{0,2},{2,4},{4,6},{6,8},{8,10},{10,12},{12,14},{1,3},{3,5},{5,7},{... | collective-permute-start | bytes 221192 | tf_op jit(solution)/shard_map/ppermute | solution.py:19
  28.5 6.9 %fusion.46 = f32[256,3,3,256]{0,3,2,1:T(8,128)} fusion(bf16[8,18,34,256]{3,0,2,1:T(8,128)(2,1)S(1)} %pad_maximum_fusion.1, bf16[4,16,32,256]{3,2,1,0:T(8,128)(2,1)S(1)} %copy-done.5), kind=kOutput, calls=%fused_computation.62 | convolution fusion | flops 2415919104 | bytes 4661248 | tf_op jit(solution)/shard_map/conv_general_dilated | solution.py:99
  38.3 4.5 %select_convert_fusion = bf16[16,32,5,256]{3,1,2,0:T(8,128)(2,1)S(1)} fusion(bf16[3,3,256,256]{3,2,1,0:T(8,128)(2,1)} %param.8, bf16[18,4,8,7,256]{4,1,3,2,0:T(4,128)(2,1)S(1)} %fusion.30, pred[32,5]{0,1:T(8,128)(4,1)S(1)} %copy-done.10), kind=kOutput, calls=%fused_computation.38 | convolution fusion | flops 3021209600 | bytes 4554912 | tf_op jit(solution)/shard_map/conv_general_dilated | solution.py:56
  45.6 4.5 %select_convert_fusion.1 = bf16[16,32,5,256]{3,1,2,0:T(8,128)(2,1)S(1)} fusion(bf16[3,3,256,256]{3,2,1,0:T(8,128)(2,1)} %param.8, bf16[18,4,8,7,256]{4,1,3,2,0:T(4,128)(2,1)S(1)} %fusion.29, pred[32,5]{0,1:T(8,128)(4,1)S(1)} %copy-done.10), kind=kOutput, calls=%fused_computation.39 | convolution fusion | flops 3021209600 | bytes 4554912 | tf_op jit(solution)/shard_map/conv_general_dilated | solution.py:56
  52.4 119.5 %while.14 = (s32[]{:T(128)}, bf16[20,36,256]{2,0,1:T(8,128)(2,1)S(1)}, bf16[16,32,256]{2,0,1:T(8,128)(2,1)}, f32[3]{0:T(128)S(1)}, bf16[3,3,256,256]{3,2,1,0:T(8...) while((s32[]{:T(128)}, bf16[20,36,256]{2,0,1:T(8,128)(2,1)S(1)}, ...), condition=%wide.region_2.3_spmd, body=%wide.region_0.2_spmd.sunk | while | flops 1609732096 | bytes 14596871 | solution.py:110
  52.8 2.3 fusion.95
  55.2 2.2 fusion.96
  58.4 4.0 %collective-permute-start = (f32[]{:T(128)}, f32[]{:T(128)}, u32[]{:S(2)}, u32[]{:S(2)}) collective-permute-start(f32[]{:T(128)} %multiply_reduce_fusion.3), channel_id=1, source_target_pairs={{0,16},{16,0},{32,48},{48,32},{64,80},{80,64},{96,112},{112,96},{1... | collective-permute-start | bytes 20 | tf_op jit(solution)/shard_map/while/body/eval_jaxpr/ppermute | solution.py:33
  62.4 5.2 %collective-permute-start.3 = (f32[2,32,256]{2,0,1:T(2,128)S(1)}, f32[2,32,256]{2,0,1:T(2,128)S(1)}, u32[]{:S(2)}, u32[]{:S(2)}) collective-permute-start(f32[2,32,256]{2,0,1:T(2,128)S(1)} %slice_bitcast_fusion.11), channel_id=1, source_target_pairs={{16,0},{32,16},{48,32},{64,48},{80,64},{96,80},{112,96},{0,112},{1... | collective-permute-start | bytes 196616 | tf_op jit(solution)/shard_map/while/body/eval_jaxpr/ppermute | solution.py:21
  70.8 1.9 collective-permute-done.1
  73.4 3.2 %collective-permute-start.2 = (f32[]{:T(128)}, f32[]{:T(128)}, u32[]{:S(2)}, u32[]{:S(2)}) collective-permute-start(f32[]{:T(128)} %add.181), channel_id=1, source_target_pairs={{0,64},{16,80},{32,96},{48,112},{64,0},{80,16},{96,32},{112,48},{1... | collective-permute-start | bytes 20 | tf_op jit(solution)/shard_map/while/body/eval_jaxpr/ppermute | solution.py:33
  76.6 1.9 collective-permute-done.2
  79.9 4.2 %collective-permute-start.7 = (f32[]{:T(128)}, f32[]{:T(128)}, u32[]{:S(2)}, u32[]{:S(2)}) collective-permute-start(f32[]{:T(128)} %add.182), channel_id=1, source_target_pairs={{0,2},{2,0},{4,6},{6,4},{8,10},{10,8},{12,14},{14,12},{1,3},{3,1},... | collective-permute-start | bytes 20 | tf_op jit(solution)/shard_map/while/body/eval_jaxpr/ppermute | solution.py:33
  84.8 3.0 %collective-permute-start.8 = (f32[]{:T(128)}, f32[]{:T(128)}, u32[]{:S(2)}, u32[]{:S(2)}) collective-permute-start(f32[]{:T(128)} %add.183), channel_id=1, source_target_pairs={{0,4},{2,6},{4,0},{6,2},{8,12},{10,14},{12,8},{14,10},{1,5},{3,7},... | collective-permute-start | bytes 20 | tf_op jit(solution)/shard_map/while/body/eval_jaxpr/ppermute | solution.py:33
  89.0 4.3 %collective-permute-start.9 = (f32[]{:T(128)}, f32[]{:T(128)}, u32[]{:S(2)}, u32[]{:S(2)}) collective-permute-start(f32[]{:T(128)} %add.184), channel_id=1, source_target_pairs={{0,8},{2,10},{4,12},{6,14},{8,0},{10,2},{12,4},{14,6},{1,9},{3,11}... | collective-permute-start | bytes 20 | tf_op jit(solution)/shard_map/while/body/eval_jaxpr/ppermute | solution.py:33
  96.0 2.3 fusion.95
  98.3 2.2 fusion.96
  101.5 2.1 collective-permute-start
  103.7 3.6 %collective-permute-start.3 = (f32[2,32,256]{2,0,1:T(2,128)S(1)}, f32[2,32,256]{2,0,1:T(2,128)S(1)}, u32[]{:S(2)}, u32[]{:S(2)}) collective-permute-start(f32[2,32,256]{2,0,1:T(2,128)S(1)} %slice_bitcast_fusion.11), channel_id=1, source_target_pairs={{16,0},{32,16},{48,32},{64,48},{80,64},{96,80},{112,96},{0,112},{1... | collective-permute-start | bytes 196616 | tf_op jit(solution)/shard_map/while/body/eval_jaxpr/ppermute | solution.py:21
  108.8 2.8 %collective-permute-start.1 = (f32[]{:T(128)}, f32[]{:T(128)}, u32[]{:S(2)}, u32[]{:S(2)}) collective-permute-start(f32[]{:T(128)} %add.180), channel_id=1, source_target_pairs={{0,32},{16,48},{32,0},{48,16},{64,96},{80,112},{96,64},{112,80},{1... | collective-permute-start | bytes 20 | tf_op jit(solution)/shard_map/while/body/eval_jaxpr/ppermute | solution.py:33
  113.1 4.9 %collective-permute-start.2 = (f32[]{:T(128)}, f32[]{:T(128)}, u32[]{:S(2)}, u32[]{:S(2)}) collective-permute-start(f32[]{:T(128)} %add.181), channel_id=1, source_target_pairs={{0,64},{16,80},{32,96},{48,112},{64,0},{80,16},{96,32},{112,48},{1... | collective-permute-start | bytes 20 | tf_op jit(solution)/shard_map/while/body/eval_jaxpr/ppermute | solution.py:33
  119.6 2.0 collective-permute-start.7
  122.3 2.7 %collective-permute-start.8 = (f32[]{:T(128)}, f32[]{:T(128)}, u32[]{:S(2)}, u32[]{:S(2)}) collective-permute-start(f32[]{:T(128)} %add.183), channel_id=1, source_target_pairs={{0,4},{2,6},{4,0},{6,2},{8,12},{10,14},{12,8},{14,10},{1,5},{3,7},... | collective-permute-start | bytes 20 | tf_op jit(solution)/shard_map/while/body/eval_jaxpr/ppermute | solution.py:33
  126.6 3.3 %collective-permute-start.9 = (f32[]{:T(128)}, f32[]{:T(128)}, u32[]{:S(2)}, u32[]{:S(2)}) collective-permute-start(f32[]{:T(128)} %add.184), channel_id=1, source_target_pairs={{0,8},{2,10},{4,12},{6,14},{8,0},{10,2},{12,4},{14,6},{1,9},{3,11}... | collective-permute-start | bytes 20 | tf_op jit(solution)/shard_map/while/body/eval_jaxpr/ppermute | solution.py:33
  133.5 2.3 fusion.95
  135.8 2.2 fusion.96
  139.0 2.3 collective-permute-start
  141.4 4.8 %collective-permute-start.3 = (f32[2,32,256]{2,0,1:T(2,128)S(1)}, f32[2,32,256]{2,0,1:T(2,128)S(1)}, u32[]{:S(2)}, u32[]{:S(2)}) collective-permute-start(f32[2,32,256]{2,0,1:T(2,128)S(1)} %slice_bitcast_fusion.11), channel_id=1, source_target_pairs={{16,0},{32,16},{48,32},{64,48},{80,64},{96,80},{112,96},{0,112},{1... | collective-permute-start | bytes 196616 | tf_op jit(solution)/shard_map/while/body/eval_jaxpr/ppermute | solution.py:21
  149.2 2.2 collective-permute-done.1
  152.0 3.5 %collective-permute-start.2 = (f32[]{:T(128)}, f32[]{:T(128)}, u32[]{:S(2)}, u32[]{:S(2)}) collective-permute-start(f32[]{:T(128)} %add.181), channel_id=1, source_target_pairs={{0,64},{16,80},{32,96},{48,112},{64,0},{80,16},{96,32},{112,48},{1... | collective-permute-start | bytes 20 | tf_op jit(solution)/shard_map/while/body/eval_jaxpr/ppermute | solution.py:33
  160.9 2.0 collective-permute-start.8
  165.2 3.2 %collective-permute-start.9 = (f32[]{:T(128)}, f32[]{:T(128)}, u32[]{:S(2)}, u32[]{:S(2)}) collective-permute-start(f32[]{:T(128)} %add.184), channel_id=1, source_target_pairs={{0,8},{2,10},{4,12},{6,14},{8,0},{10,2},{12,4},{14,6},{1,9},{3,11}... | collective-permute-start | bytes 20 | tf_op jit(solution)/shard_map/while/body/eval_jaxpr/ppermute | solution.py:33
  171.9 2.0 copy.30
  175.1 2.1 collective-permute-start.18
  177.2 2.6 %copy.35 = bf16[4,16,32,256]{3,2,1,0:T(8,128)(2,1)} copy(bf16[4,16,32,256]{3,1,2,0:T(8,128)(2,1)} %get-tuple-element.51) | data formatting | bytes 2097152
  181.4 21.7 %collective-permute-done.18 = f32[128,2304]{1,0:T(8,128)} collective-permute-done((f32[128,2304]{1,0:T(8,128)}, f32[128,2304]{1,0:T(8,128)}, u32[]{:S(2)}, u32[]{:S(2)}) %collective-permute-start.18) | collective-permute-done | bytes 1179680 | tf_op jit(solution)/shard_map/ppermute | solution.py:48
  204.9 2.3 fusion.43
  208.0 2.8 %select_reduce_fusion = (f32[]{:T(128)}, f32[16,8,5,256]{3,1,2,0:T(8,128)S(1)}) fusion(pred[8,5]{0,1:T(8,128)(4,1)S(1)} %copy-done.9, bf16[3,3,256,256]{3,2,1,0:T(8,128)(2,1)} %param.8, bf16[18,1,7,2,256]{4,2,3,0,1:T(8,128)(2,1)S(1)} %slice.96, bf16[18,1,8,5,256]{4,2,3,0,1:T(8,128)(2,1)S(1)} %fusion.43), kind=kOutput, calls=%fused_computation.64 | convolution fusion | flops 757014528 | bytes 2332716 | tf_op jit(solution)/shard_map/conv_general_dilated | solution.py:56
  210.9 6.4 %collective-permute-done.19 = f32[64,2304]{1,0:T(8,128)S(1)} collective-permute-done((f32[64,2304]{1,0:T(8,128)S(1)}, f32[64,2304]{1,0:T(8,128)S(1)}, u32[]{:S(2)}, u32[]{:S(2)}) %collective-permute-start.19) | collective-permute-done | bytes 589856 | tf_op jit(solution)/shard_map/ppermute | solution.py:48
  217.4 2.7 %collective-permute-start.20 = (f32[32,2304]{1,0:T(8,128)S(1)}, f32[32,2304]{1,0:T(8,128)S(1)}, u32[]{:S(2)}, u32[]{:S(2)}) collective-permute-start(f32[32,2304]{1,0:T(8,128)S(1)} %constant_dynamic-slice_fusion.3), channel_id=1, source_target_pairs={{0,16},{16,0},{32,48},{48,32},{64,80},{80,64},{96,112},{112,96},{1... | collective-permute-start | bytes 884744 | tf_op jit(solution)/shard_map/ppermute | solution.py:48
  222.3 4.2 %collective-permute-done.25 = f32[2]{0:T(128)S(1)} collective-permute-done((f32[2]{0:T(128)S(1)}, f32[2]{0:T(128)S(1)}, u32[]{:S(2)}, u32[]{:S(2)}) %collective-permute-start.25) | collective-permute-done | bytes 40 | tf_op jit(solution)/shard_map/ppermute | solution.py:33
  232.8 3.4 %collective-permute-start.27 = (f32[2]{0:T(128)S(1)}, f32[2]{0:T(128)S(1)}, u32[]{:S(2)}, u32[]{:S(2)}) collective-permute-start(f32[2]{0:T(128)S(1)} %fusion.81), channel_id=1, source_target_pairs={{0,64},{16,80},{32,96},{48,112},{64,0},{80,16},{96,32},{112,48},{1... | collective-permute-start | bytes 32 | tf_op jit(solution)/shard_map/ppermute | solution.py:33
  239.9 2.6 %collective-permute-done.29 = f32[2]{0:T(128)S(1)} collective-permute-done((f32[2]{0:T(128)S(1)}, f32[2]{0:T(128)S(1)}, u32[]{:S(2)}, u32[]{:S(2)}) %collective-permute-start.29) | collective-permute-done | bytes 40 | tf_op jit(solution)/shard_map/ppermute | solution.py:33
  244.4 3.2 %collective-permute-done.30 = f32[2]{0:T(128)S(1)} collective-permute-done((f32[2]{0:T(128)S(1)}, f32[2]{0:T(128)S(1)}, u32[]{:S(2)}, u32[]{:S(2)}) %collective-permute-start.30) | collective-permute-done | bytes 40 | tf_op jit(solution)/shard_map/ppermute | solution.py:33
  249.9 2.2 collective-permute-done.22
  (192 shorter events, 67.1 us)
Async XLA Ops:
  2.1 16.8 %collective-permute-start.15 = (bf16[2,32,256]{2,0,1:T(2,128)(2,1)S(1)}, bf16[2,32,256]{2,0,1:T(2,128)(2,1)S(1)}, u32[]{:S(2)}, u32[]{:S(2)}) collective-permute-start(bf16[2,32,256]{2,0,1:T(2,128)(2,1)S(1)} %get-tuple-element.80), channel_id=1, source_target_pairs={{16,0},{32,16},{48,32},{64,48},{80,64},{96,80},{112,96},{0,112},{1... | collective-permute-start | bytes 98312 | tf_op jit(solution)/shard_map/ppermute | solution.py:21
  8.4 10.6 %collective-permute-start.14 = (bf16[2,32,256]{2,0,1:T(2,128)(2,1)S(1)}, bf16[2,32,256]{2,0,1:T(2,128)(2,1)S(1)}, u32[]{:S(2)}, u32[]{:S(2)}) collective-permute-start(bf16[2,32,256]{2,0,1:T(2,128)(2,1)S(1)} %get-tuple-element.79), channel_id=1, source_target_pairs={{0,16},{16,32},{32,48},{48,64},{64,80},{80,96},{96,112},{112,0},{1... | collective-permute-start | bytes 98312 | tf_op jit(solution)/shard_map/ppermute | solution.py:19
  11.5 9.1 %collective-permute-start.11 = (bf16[8,1,32,256]{3,0,2,1:T(8,128)(2,1)S(1)}, bf16[8,1,32,256]{3,0,2,1:T(8,128)(2,1)S(1)}, u32[]{:S(2)}, u32[]{:S(2)}) collective-permute-start(bf16[8,1,32,256]{3,0,2,1:T(8,128)(2,1)S(1)} %get-tuple-element.76), channel_id=1, source_target_pairs={{16,0},{32,16},{48,32},{64,48},{80,64},{96,80},{112,96},{17,1},{33... | collective-permute-start | bytes 393224 | tf_op jit(solution)/shard_map/ppermute | solution.py:21
  12.8 9.0 %collective-permute-start.10 = (bf16[8,1,32,256]{3,0,2,1:T(8,128)(2,1)S(1)}, bf16[8,1,32,256]{3,0,2,1:T(8,128)(2,1)S(1)}, u32[]{:S(2)}, u32[]{:S(2)}) collective-permute-start(bf16[8,1,32,256]{3,0,2,1:T(8,128)(2,1)S(1)} %get-tuple-element.75), channel_id=1, source_target_pairs={{0,16},{16,32},{32,48},{48,64},{64,80},{80,96},{96,112},{1,17},{17... | collective-permute-start | bytes 393224 | tf_op jit(solution)/shard_map/ppermute | solution.py:19
  19.0 7.3 %collective-permute-start.17 = (bf16[20,2,256]{2,0,1:T(8,128)(2,1)S(1)}, bf16[20,2,256]{2,0,1:T(8,128)(2,1)S(1)}, u32[]{:S(2)}, u32[]{:S(2)}) collective-permute-start(bf16[20,2,256]{2,0,1:T(8,128)(2,1)S(1)} %get-tuple-element.78), channel_id=1, source_target_pairs={{2,0},{4,2},{6,4},{8,6},{10,8},{12,10},{14,12},{0,14},{3,1},{5,3},... | collective-permute-start | bytes 61448 | tf_op jit(solution)/shard_map/ppermute | solution.py:21
  20.6 5.7 %collective-permute-start.16 = (bf16[20,2,256]{2,0,1:T(8,128)(2,1)S(1)}, bf16[20,2,256]{2,0,1:T(8,128)(2,1)S(1)}, u32[]{:S(2)}, u32[]{:S(2)}) collective-permute-start(bf16[20,2,256]{2,0,1:T(8,128)(2,1)S(1)} %get-tuple-element.77), channel_id=1, source_target_pairs={{0,2},{2,4},{4,6},{6,8},{8,10},{10,12},{12,14},{14,0},{1,3},{3,5},... | collective-permute-start | bytes 61448 | tf_op jit(solution)/shard_map/ppermute | solution.py:19
  21.9 5.4 %collective-permute-start.13 = (bf16[8,18,1,256]{3,0,2,1:T(8,128)(2,1)S(1)}, bf16[8,18,1,256]{3,0,2,1:T(8,128)(2,1)S(1)}, u32[]{:S(2)}, u32[]{:S(2)}) collective-permute-start(bf16[8,18,1,256]{3,0,2,1:T(8,128)(2,1)S(1)} %get-tuple-element.74), channel_id=1, source_target_pairs={{2,0},{4,2},{6,4},{8,6},{10,8},{12,10},{14,12},{3,1},{5,3},{7,5},{... | collective-permute-start | bytes 221192 | tf_op jit(solution)/shard_map/ppermute | solution.py:21
  23.2 4.1 %collective-permute-start.12 = (bf16[8,18,1,256]{3,0,2,1:T(8,128)(2,1)S(1)}, bf16[8,18,1,256]{3,0,2,1:T(8,128)(2,1)S(1)}, u32[]{:S(2)}, u32[]{:S(2)}) collective-permute-start(bf16[8,18,1,256]{3,0,2,1:T(8,128)(2,1)S(1)} %get-tuple-element.73), channel_id=1, source_target_pairs={{0,2},{2,4},{4,6},{6,8},{8,10},{10,12},{12,14},{1,3},{3,5},{5,7},{... | collective-permute-start | bytes 221192 | tf_op jit(solution)/shard_map/ppermute | solution.py:19
  58.4 9.4 %collective-permute-start = (f32[]{:T(128)}, f32[]{:T(128)}, u32[]{:S(2)}, u32[]{:S(2)}) collective-permute-start(f32[]{:T(128)} %multiply_reduce_fusion.3), channel_id=1, source_target_pairs={{0,16},{16,0},{32,48},{48,32},{64,80},{80,64},{96,112},{112,96},{1... | collective-permute-start | bytes 20 | tf_op jit(solution)/shard_map/while/body/eval_jaxpr/ppermute | solution.py:33
  62.4 16.8 %collective-permute-start.3 = (f32[2,32,256]{2,0,1:T(2,128)S(1)}, f32[2,32,256]{2,0,1:T(2,128)S(1)}, u32[]{:S(2)}, u32[]{:S(2)}) collective-permute-start(f32[2,32,256]{2,0,1:T(2,128)S(1)} %slice_bitcast_fusion.11), channel_id=1, source_target_pairs={{16,0},{32,16},{48,32},{64,48},{80,64},{96,80},{112,96},{0,112},{1... | collective-permute-start | bytes 196616 | tf_op jit(solution)/shard_map/while/body/eval_jaxpr/ppermute | solution.py:21
  67.7 11.5 %collective-permute-start.4 = (f32[2,32,256]{2,0,1:T(2,128)S(1)}, f32[2,32,256]{2,0,1:T(2,128)S(1)}, u32[]{:S(2)}, u32[]{:S(2)}) collective-permute-start(f32[2,32,256]{2,0,1:T(2,128)S(1)} %slice_bitcast_fusion.13), channel_id=1, source_target_pairs={{0,16},{16,32},{32,48},{48,64},{64,80},{80,96},{96,112},{112,0},{1... | collective-permute-start | bytes 196616 | tf_op jit(solution)/shard_map/while/body/eval_jaxpr/ppermute | solution.py:19
  69.1 3.6 %collective-permute-start.1 = (f32[]{:T(128)}, f32[]{:T(128)}, u32[]{:S(2)}, u32[]{:S(2)}) collective-permute-start(f32[]{:T(128)} %add.180), channel_id=1, source_target_pairs={{0,32},{16,48},{32,0},{48,16},{64,96},{80,112},{96,64},{112,80},{1... | collective-permute-start | bytes 20 | tf_op jit(solution)/shard_map/while/body/eval_jaxpr/ppermute | solution.py:33
  73.4 5.1 %collective-permute-start.2 = (f32[]{:T(128)}, f32[]{:T(128)}, u32[]{:S(2)}, u32[]{:S(2)}) collective-permute-start(f32[]{:T(128)} %add.181), channel_id=1, source_target_pairs={{0,64},{16,80},{32,96},{48,112},{64,0},{80,16},{96,32},{112,48},{1... | collective-permute-start | bytes 20 | tf_op jit(solution)/shard_map/while/body/eval_jaxpr/ppermute | solution.py:33
  79.3 16.4 %collective-permute-start.5 = (f32[20,2,256]{2,0,1:T(8,128)S(1)}, f32[20,2,256]{2,0,1:T(8,128)S(1)}, u32[]{:S(2)}, u32[]{:S(2)}) collective-permute-start(f32[20,2,256]{2,0,1:T(8,128)S(1)} %get-tuple-element.125), channel_id=1, source_target_pairs={{2,0},{4,2},{6,4},{8,6},{10,8},{12,10},{14,12},{0,14},{3,1},{5,3},... | collective-permute-start | bytes 122888 | tf_op jit(solution)/shard_map/while/body/eval_jaxpr/ppermute | solution.py:21
  79.6 16.1 %collective-permute-start.6 = (f32[20,2,256]{2,0,1:T(8,128)S(1)}, f32[20,2,256]{2,0,1:T(8,128)S(1)}, u32[]{:S(2)}, u32[]{:S(2)}) collective-permute-start(f32[20,2,256]{2,0,1:T(8,128)S(1)} %get-tuple-element.126), channel_id=1, source_target_pairs={{0,2},{2,4},{4,6},{6,8},{8,10},{10,12},{12,14},{14,0},{1,3},{3,5},... | collective-permute-start | bytes 122888 | tf_op jit(solution)/shard_map/while/body/eval_jaxpr/ppermute | solution.py:19
  79.9 4.2 %collective-permute-start.7 = (f32[]{:T(128)}, f32[]{:T(128)}, u32[]{:S(2)}, u32[]{:S(2)}) collective-permute-start(f32[]{:T(128)} %add.182), channel_id=1, source_target_pairs={{0,2},{2,0},{4,6},{6,4},{8,10},{10,8},{12,14},{14,12},{1,3},{3,1},... | collective-permute-start | bytes 20 | tf_op jit(solution)/shard_map/while/body/eval_jaxpr/ppermute | solution.py:33
  84.8 3.6 %collective-permute-start.8 = (f32[]{:T(128)}, f32[]{:T(128)}, u32[]{:S(2)}, u32[]{:S(2)}) collective-permute-start(f32[]{:T(128)} %add.183), channel_id=1, source_target_pairs={{0,4},{2,6},{4,0},{6,2},{8,12},{10,14},{12,8},{14,10},{1,5},{3,7},... | collective-permute-start | bytes 20 | tf_op jit(solution)/shard_map/while/body/eval_jaxpr/ppermute | solution.py:33
  89.0 5.1 %collective-permute-start.9 = (f32[]{:T(128)}, f32[]{:T(128)}, u32[]{:S(2)}, u32[]{:S(2)}) collective-permute-start(f32[]{:T(128)} %add.184), channel_id=1, source_target_pairs={{0,8},{2,10},{4,12},{6,14},{8,0},{10,2},{12,4},{14,6},{1,9},{3,11}... | collective-permute-start | bytes 20 | tf_op jit(solution)/shard_map/while/body/eval_jaxpr/ppermute | solution.py:33
  101.5 6.0 %collective-permute-start = (f32[]{:T(128)}, f32[]{:T(128)}, u32[]{:S(2)}, u32[]{:S(2)}) collective-permute-start(f32[]{:T(128)} %multiply_reduce_fusion.3), channel_id=1, source_target_pairs={{0,16},{16,0},{32,48},{48,32},{64,80},{80,64},{96,112},{112,96},{1... | collective-permute-start | bytes 20 | tf_op jit(solution)/shard_map/while/body/eval_jaxpr/ppermute | solution.py:33
  103.7 15.2 %collective-permute-start.3 = (f32[2,32,256]{2,0,1:T(2,128)S(1)}, f32[2,32,256]{2,0,1:T(2,128)S(1)}, u32[]{:S(2)}, u32[]{:S(2)}) collective-permute-start(f32[2,32,256]{2,0,1:T(2,128)S(1)} %slice_bitcast_fusion.11), channel_id=1, source_target_pairs={{16,0},{32,16},{48,32},{64,48},{80,64},{96,80},{112,96},{0,112},{1... | collective-permute-start | bytes 196616 | tf_op jit(solution)/shard_map/while/body/eval_jaxpr/ppermute | solution.py:21
  107.4 11.5 %collective-permute-start.4 = (f32[2,32,256]{2,0,1:T(2,128)S(1)}, f32[2,32,256]{2,0,1:T(2,128)S(1)}, u32[]{:S(2)}, u32[]{:S(2)}) collective-permute-start(f32[2,32,256]{2,0,1:T(2,128)S(1)} %slice_bitcast_fusion.13), channel_id=1, source_target_pairs={{0,16},{16,32},{32,48},{48,64},{64,80},{80,96},{96,112},{112,0},{1... | collective-permute-start | bytes 196616 | tf_op jit(solution)/shard_map/while/body/eval_jaxpr/ppermute | solution.py:19
  108.8 3.6 %collective-permute-start.1 = (f32[]{:T(128)}, f32[]{:T(128)}, u32[]{:S(2)}, u32[]{:S(2)}) collective-permute-start(f32[]{:T(128)} %add.180), channel_id=1, source_target_pairs={{0,32},{16,48},{32,0},{48,16},{64,96},{80,112},{96,64},{112,80},{1... | collective-permute-start | bytes 20 | tf_op jit(solution)/shard_map/while/body/eval_jaxpr/ppermute | solution.py:33
  113.1 5.1 %collective-permute-start.2 = (f32[]{:T(128)}, f32[]{:T(128)}, u32[]{:S(2)}, u32[]{:S(2)}) collective-permute-start(f32[]{:T(128)} %add.181), channel_id=1, source_target_pairs={{0,64},{16,80},{32,96},{48,112},{64,0},{80,16},{96,32},{112,48},{1... | collective-permute-start | bytes 20 | tf_op jit(solution)/shard_map/while/body/eval_jaxpr/ppermute | solution.py:33
  119.0 14.2 %collective-permute-start.5 = (f32[20,2,256]{2,0,1:T(8,128)S(1)}, f32[20,2,256]{2,0,1:T(8,128)S(1)}, u32[]{:S(2)}, u32[]{:S(2)}) collective-permute-start(f32[20,2,256]{2,0,1:T(8,128)S(1)} %get-tuple-element.125), channel_id=1, source_target_pairs={{2,0},{4,2},{6,4},{8,6},{10,8},{12,10},{14,12},{0,14},{3,1},{5,3},... | collective-permute-start | bytes 122888 | tf_op jit(solution)/shard_map/while/body/eval_jaxpr/ppermute | solution.py:21
  119.1 14.2 %collective-permute-start.6 = (f32[20,2,256]{2,0,1:T(8,128)S(1)}, f32[20,2,256]{2,0,1:T(8,128)S(1)}, u32[]{:S(2)}, u32[]{:S(2)}) collective-permute-start(f32[20,2,256]{2,0,1:T(8,128)S(1)} %get-tuple-element.126), channel_id=1, source_target_pairs={{0,2},{2,4},{4,6},{6,8},{8,10},{10,12},{12,14},{14,0},{1,3},{3,5},... | collective-permute-start | bytes 122888 | tf_op jit(solution)/shard_map/while/body/eval_jaxpr/ppermute | solution.py:19
  119.6 2.0 collective-permute-start.7
  122.3 3.6 %collective-permute-start.8 = (f32[]{:T(128)}, f32[]{:T(128)}, u32[]{:S(2)}, u32[]{:S(2)}) collective-permute-start(f32[]{:T(128)} %add.183), channel_id=1, source_target_pairs={{0,4},{2,6},{4,0},{6,2},{8,12},{10,14},{12,8},{14,10},{1,5},{3,7},... | collective-permute-start | bytes 20 | tf_op jit(solution)/shard_map/while/body/eval_jaxpr/ppermute | solution.py:33
  126.6 5.1 %collective-permute-start.9 = (f32[]{:T(128)}, f32[]{:T(128)}, u32[]{:S(2)}, u32[]{:S(2)}) collective-permute-start(f32[]{:T(128)} %add.184), channel_id=1, source_target_pairs={{0,8},{2,10},{4,12},{6,14},{8,0},{10,2},{12,4},{14,6},{1,9},{3,11}... | collective-permute-start | bytes 20 | tf_op jit(solution)/shard_map/while/body/eval_jaxpr/ppermute | solution.py:33
  139.0 7.4 %collective-permute-start = (f32[]{:T(128)}, f32[]{:T(128)}, u32[]{:S(2)}, u32[]{:S(2)}) collective-permute-start(f32[]{:T(128)} %multiply_reduce_fusion.3), channel_id=1, source_target_pairs={{0,16},{16,0},{32,48},{48,32},{64,80},{80,64},{96,112},{112,96},{1... | collective-permute-start | bytes 20 | tf_op jit(solution)/shard_map/while/body/eval_jaxpr/ppermute | solution.py:33
  141.4 16.4 %collective-permute-start.3 = (f32[2,32,256]{2,0,1:T(2,128)S(1)}, f32[2,32,256]{2,0,1:T(2,128)S(1)}, u32[]{:S(2)}, u32[]{:S(2)}) collective-permute-start(f32[2,32,256]{2,0,1:T(2,128)S(1)} %slice_bitcast_fusion.11), channel_id=1, source_target_pairs={{16,0},{32,16},{48,32},{64,48},{80,64},{96,80},{112,96},{0,112},{1... | collective-permute-start | bytes 196616 | tf_op jit(solution)/shard_map/while/body/eval_jaxpr/ppermute | solution.py:21
  146.3 11.5 %collective-permute-start.4 = (f32[2,32,256]{2,0,1:T(2,128)S(1)}, f32[2,32,256]{2,0,1:T(2,128)S(1)}, u32[]{:S(2)}, u32[]{:S(2)}) collective-permute-start(f32[2,32,256]{2,0,1:T(2,128)S(1)} %slice_bitcast_fusion.13), channel_id=1, source_target_pairs={{0,16},{16,32},{32,48},{48,64},{64,80},{80,96},{96,112},{112,0},{1... | collective-permute-start | bytes 196616 | tf_op jit(solution)/shard_map/while/body/eval_jaxpr/ppermute | solution.py:19
  147.8 3.6 %collective-permute-start.1 = (f32[]{:T(128)}, f32[]{:T(128)}, u32[]{:S(2)}, u32[]{:S(2)}) collective-permute-start(f32[]{:T(128)} %add.180), channel_id=1, source_target_pairs={{0,32},{16,48},{32,0},{48,16},{64,96},{80,112},{96,64},{112,80},{1... | collective-permute-start | bytes 20 | tf_op jit(solution)/shard_map/while/body/eval_jaxpr/ppermute | solution.py:33
  152.0 5.1 %collective-permute-start.2 = (f32[]{:T(128)}, f32[]{:T(128)}, u32[]{:S(2)}, u32[]{:S(2)}) collective-permute-start(f32[]{:T(128)} %add.181), channel_id=1, source_target_pairs={{0,64},{16,80},{32,96},{48,112},{64,0},{80,16},{96,32},{112,48},{1... | collective-permute-start | bytes 20 | tf_op jit(solution)/shard_map/while/body/eval_jaxpr/ppermute | solution.py:33
  158.0 13.9 %collective-permute-start.5 = (f32[20,2,256]{2,0,1:T(8,128)S(1)}, f32[20,2,256]{2,0,1:T(8,128)S(1)}, u32[]{:S(2)}, u32[]{:S(2)}) collective-permute-start(f32[20,2,256]{2,0,1:T(8,128)S(1)} %get-tuple-element.125), channel_id=1, source_target_pairs={{2,0},{4,2},{6,4},{8,6},{10,8},{12,10},{14,12},{0,14},{3,1},{5,3},... | collective-permute-start | bytes 122888 | tf_op jit(solution)/shard_map/while/body/eval_jaxpr/ppermute | solution.py:21
  158.0 13.9 %collective-permute-start.6 = (f32[20,2,256]{2,0,1:T(8,128)S(1)}, f32[20,2,256]{2,0,1:T(8,128)S(1)}, u32[]{:S(2)}, u32[]{:S(2)}) collective-permute-start(f32[20,2,256]{2,0,1:T(8,128)S(1)} %get-tuple-element.126), channel_id=1, source_target_pairs={{0,2},{2,4},{4,6},{6,8},{8,10},{10,12},{12,14},{14,0},{1,3},{3,5},... | collective-permute-start | bytes 122888 | tf_op jit(solution)/shard_map/while/body/eval_jaxpr/ppermute | solution.py:19
  160.9 3.6 %collective-permute-start.8 = (f32[]{:T(128)}, f32[]{:T(128)}, u32[]{:S(2)}, u32[]{:S(2)}) collective-permute-start(f32[]{:T(128)} %add.183), channel_id=1, source_target_pairs={{0,4},{2,6},{4,0},{6,2},{8,12},{10,14},{12,8},{14,10},{1,5},{3,7},... | collective-permute-start | bytes 20 | tf_op jit(solution)/shard_map/while/body/eval_jaxpr/ppermute | solution.py:33
  165.2 5.1 %collective-permute-start.9 = (f32[]{:T(128)}, f32[]{:T(128)}, u32[]{:S(2)}, u32[]{:S(2)}) collective-permute-start(f32[]{:T(128)} %add.184), channel_id=1, source_target_pairs={{0,8},{2,10},{4,12},{6,14},{8,0},{10,2},{12,4},{14,6},{1,9},{3,11}... | collective-permute-start | bytes 20 | tf_op jit(solution)/shard_map/while/body/eval_jaxpr/ppermute | solution.py:33
  175.1 28.0 %collective-permute-start.18 = (f32[128,2304]{1,0:T(8,128)}, f32[128,2304]{1,0:T(8,128)}, u32[]{:S(2)}, u32[]{:S(2)}) collective-permute-start(f32[128,2304]{1,0:T(8,128)} %constant_dynamic-slice_fusion.5), channel_id=1, source_target_pairs={{0,64},{16,80},{32,96},{48,112},{64,0},{80,16},{96,32},{112,48},{1... | collective-permute-start | bytes 3538952 | tf_op jit(solution)/shard_map/ppermute | solution.py:48
  204.6 12.7 %collective-permute-start.19 = (f32[64,2304]{1,0:T(8,128)S(1)}, f32[64,2304]{1,0:T(8,128)S(1)}, u32[]{:S(2)}, u32[]{:S(2)}) collective-permute-start(f32[64,2304]{1,0:T(8,128)S(1)} %constant_dynamic-slice_fusion.4), channel_id=1, source_target_pairs={{0,32},{16,48},{32,0},{48,16},{64,96},{80,112},{96,64},{112,80},{1... | collective-permute-start | bytes 1769480 | tf_op jit(solution)/shard_map/ppermute | solution.py:48
  217.4 12.0 %collective-permute-start.20 = (f32[32,2304]{1,0:T(8,128)S(1)}, f32[32,2304]{1,0:T(8,128)S(1)}, u32[]{:S(2)}, u32[]{:S(2)}) collective-permute-start(f32[32,2304]{1,0:T(8,128)S(1)} %constant_dynamic-slice_fusion.3), channel_id=1, source_target_pairs={{0,16},{16,0},{32,48},{48,32},{64,80},{80,64},{96,112},{112,96},{1... | collective-permute-start | bytes 884744 | tf_op jit(solution)/shard_map/ppermute | solution.py:48
  221.5 5.1 %collective-permute-start.25 = (f32[2]{0:T(128)S(1)}, f32[2]{0:T(128)S(1)}, u32[]{:S(2)}, u32[]{:S(2)}) collective-permute-start(f32[2]{0:T(128)S(1)} %pad_maximum_fusion.12), channel_id=1, source_target_pairs={{0,16},{16,0},{32,48},{48,32},{64,80},{80,64},{96,112},{112,96},{1... | collective-permute-start | bytes 32 | tf_op jit(solution)/shard_map/ppermute | solution.py:33
  227.9 3.6 %collective-permute-start.26 = (f32[2]{0:T(128)S(1)}, f32[2]{0:T(128)S(1)}, u32[]{:S(2)}, u32[]{:S(2)}) collective-permute-start(f32[2]{0:T(128)S(1)} %fusion.80), channel_id=1, source_target_pairs={{0,32},{16,48},{32,0},{48,16},{64,96},{80,112},{96,64},{112,80},{1... | collective-permute-start | bytes 32 | tf_op jit(solution)/shard_map/ppermute | solution.py:33
  229.4 18.2 %collective-permute-start.21 = (f32[16,2304]{1,0:T(8,128)S(1)}, f32[16,2304]{1,0:T(8,128)S(1)}, u32[]{:S(2)}, u32[]{:S(2)}) collective-permute-start(f32[16,2304]{1,0:T(8,128)S(1)} %constant_dynamic-slice_fusion.2), channel_id=1, source_target_pairs={{0,8},{2,10},{4,12},{6,14},{8,0},{10,2},{12,4},{14,6},{1,9},{3,11}... | collective-permute-start | bytes 442376 | tf_op jit(solution)/shard_map/ppermute | solution.py:48
  232.8 5.1 %collective-permute-start.27 = (f32[2]{0:T(128)S(1)}, f32[2]{0:T(128)S(1)}, u32[]{:S(2)}, u32[]{:S(2)}) collective-permute-start(f32[2]{0:T(128)S(1)} %fusion.81), channel_id=1, source_target_pairs={{0,64},{16,80},{32,96},{48,112},{64,0},{80,16},{96,32},{112,48},{1... | collective-permute-start | bytes 32 | tf_op jit(solution)/shard_map/ppermute | solution.py:33
  239.0 3.5 %collective-permute-start.29 = (f32[2]{0:T(128)S(1)}, f32[2]{0:T(128)S(1)}, u32[]{:S(2)}, u32[]{:S(2)}) collective-permute-start(f32[2]{0:T(128)S(1)} %add.156), channel_id=1, source_target_pairs={{0,4},{2,6},{4,0},{6,2},{8,12},{10,14},{12,8},{14,10},{1,5},{3,7},... | collective-permute-start | bytes 32 | tf_op jit(solution)/shard_map/ppermute | solution.py:33
  242.6 5.0 %collective-permute-start.30 = (f32[2]{0:T(128)S(1)}, f32[2]{0:T(128)S(1)}, u32[]{:S(2)}, u32[]{:S(2)}) collective-permute-start(f32[2]{0:T(128)S(1)} %add.157), channel_id=1, source_target_pairs={{0,8},{2,10},{4,12},{6,14},{8,0},{10,2},{12,4},{14,6},{1,9},{3,11}... | collective-permute-start | bytes 32 | tf_op jit(solution)/shard_map/ppermute | solution.py:33
  247.7 4.4 %collective-permute-start.22 = (f32[8,2304]{1,0:T(8,128)S(1)}, f32[8,2304]{1,0:T(8,128)S(1)}, u32[]{:S(2)}, u32[]{:S(2)}) collective-permute-start(f32[8,2304]{1,0:T(8,128)S(1)} %constant_dynamic-slice_fusion.1), channel_id=1, source_target_pairs={{0,4},{2,6},{4,0},{6,2},{8,12},{10,14},{12,8},{14,10},{1,5},{3,7},... | collective-permute-start | bytes 221192 | tf_op jit(solution)/shard_map/ppermute | solution.py:48
  253.4 4.0 %collective-permute-start.24 = (f32[4,2304]{1,0:T(4,128)S(1)}, f32[4,2304]{1,0:T(4,128)S(1)}, u32[]{:S(2)}, u32[]{:S(2)}) collective-permute-start(f32[4,2304]{1,0:T(4,128)S(1)} %dynamic-slice_add_fusion.5), channel_id=1, source_target_pairs={{0,1},{1,0},{2,3},{3,2},{4,5},{5,4},{6,7},{7,6},{8,9},{9,8},{10,11... | collective-permute-start | bytes 110600 | tf_op jit(solution)/shard_map/ppermute | solution.py:33
  (14 other events, 56.2 us)

commit v7 on v4

--- a/solution.py
+++ b/solution.py
@@ -45,7 +45,10 @@
             upper = (index // step) % 2
             keep = lax.dynamic_slice_in_dim(value, upper * half, half, axis=0)
             send = lax.dynamic_slice_in_dim(value, (1 - upper) * half, half, axis=0)
-            value = keep + lax.ppermute(send, axis, [(i, i ^ step) for i in range(count)])
+            if send.size * 4 > 256 * 2304:
+                send = send.astype(jnp.bfloat16)
+            received = lax.ppermute(send, axis, [(i, i ^ step) for i in range(count)])
+            value = keep + received.astype(jnp.float32)
             step //= 2
     return value
 

time: 240 us -> 228 us (0.950)
  starting transfers between devices: 107 us -> 99.7 us
  waiting for transfers between devices: 52.8 us -> 47.5 us
    ppermute x25, starting transfers between devices: 63.5 us -> 54.8 us  [butterfly_sum(): lax.ppermute(value, axis, [(i, i ^ step) for i in range(count)])]
    ppermute x25, waiting for transfers between devices: 38.9 us -> 33.6 us  [butterfly_sum(): lax.ppermute(value, axis, [(i, i ^ step) for i in range(count)])]
    ppermute x10, starting transfers between devices: 17.3 us -> 20 us  [extended(): lax.ppermute(head, axis, [((i + 1) % count, i) for i in range(ends)])]
  transfers between devices with their start and end apart: 51 -> 51, of which waited for: 25 -> 24; matrix products, arithmetic and copies ran while one was open for 11% -> 12% of each run, Pallas kernels for 0% -> 0%
where the time goes in v7:
time: 228 us; the launch traced here: 226 us
  starting transfers between devices  99.7 us (44%)
  waiting for transfers between devices  47.5 us (21%)
  matrix products  22.1 us (10%)
  local copies, waits for them, and re-layouts  21.1 us (9%)
  other arithmetic  16.9 us (7%)
  loops' own time  14.1 us (6%)
  between operations  4.59 us (2%)
    ppermute x25, starting transfers between devices, butterfly_sum(): lax.ppermute(value, axis, [(i, i ^ step) for i in range(count)])  54.8 us
    ppermute x25, waiting for transfers between devices, butterfly_sum(): lax.ppermute(value, axis, [(i, i ^ step) for i in range(count)])  33.6 us
    ppermute x10, starting transfers between devices, extended(): lax.ppermute(head, axis, [((i + 1) % count, i) for i in range(ends)])  20 us
    conv_general_dilated x10, matrix products, conv(): lax.conv_general_dilated(padded, weights, window_strides=(1, 1), padding=...  15.2 us
    another operation x1, loops' own time, per_device(): lax.scan(power_step, (padded_probe, iterate), None, length=ITERS - 1)  14.1 us
    ppermute x6, waiting for transfers between devices, halving_scatter(): received = lax.ppermute(send, axis, [(i, i ^ step) for i in range(count)])  12.8 us
    ppermute x10, starting transfers between devices, extended(): lax.ppermute(tail, axis, [(i, (i + 1) % count) for i in range(ends)])  12.6 us
    ppermute x6, starting transfers between devices, halving_scatter(): received = lax.ppermute(send, axis, [(i, i ^ step) for i in range(count)])  12.3 us
  transfers between devices with their start and end apart: 51, of which 24 were waited for; matrix products, arithmetic and copies ran while one was open for 12% of the time, Pallas kernels for 0%

profile of v7, /device:TPU:0, one launch (start us, length us, event | category | flops | bytes accessed | tf_op | source)
XLA Modules:
  0.0 226.1 jit_solution(4568974612567020473)
XLA Ops:
  2.1 6.2 %collective-permute-start.15 = (bf16[2,32,256]{2,0,1:T(2,128)(2,1)S(1)}, bf16[2,32,256]{2,0,1:T(2,128)(2,1)S(1)}, u32[]{:S(2)}, u32[]{:S(2)}) collective-permute-start(bf16[2,32,256]{2,0,1:T(2,128)(2,1)S(1)} %get-tuple-element.76), channel_id=1, source_target_pairs={{16,0},{32,16},{48,32},{64,48},{80,64},{96,80},{112,96},{0,112},{1... | collective-permute-start | bytes 98312 | tf_op jit(solution)/shard_map/ppermute | solution.py:21
  8.4 2.1 copy.23
  12.8 6.1 %collective-permute-start.10 = (bf16[8,1,32,256]{3,0,2,1:T(8,128)(2,1)S(1)}, bf16[8,1,32,256]{3,0,2,1:T(8,128)(2,1)S(1)}, u32[]{:S(2)}, u32[]{:S(2)}) collective-permute-start(bf16[8,1,32,256]{3,0,2,1:T(8,128)(2,1)S(1)} %get-tuple-element.71), channel_id=1, source_target_pairs={{0,16},{16,32},{32,48},{48,64},{64,80},{80,96},{96,112},{1,17},{17... | collective-permute-start | bytes 393224 | tf_op jit(solution)/shard_map/ppermute | solution.py:19
  19.2 1.6 collective-permute-start.17
  23.2 3.0 %collective-permute-start.12 = (bf16[8,18,1,256]{3,0,2,1:T(8,128)(2,1)S(1)}, bf16[8,18,1,256]{3,0,2,1:T(8,128)(2,1)S(1)}, u32[]{:S(2)}, u32[]{:S(2)}) collective-permute-start(bf16[8,18,1,256]{3,0,2,1:T(8,128)(2,1)S(1)} %get-tuple-element.69), channel_id=1, source_target_pairs={{0,2},{2,4},{4,6},{6,8},{8,10},{10,12},{12,14},{1,3},{3,5},{5,7},{... | collective-permute-start | bytes 221192 | tf_op jit(solution)/shard_map/ppermute | solution.py:19
  28.5 6.9 %fusion.46 = f32[256,3,3,256]{0,3,2,1:T(8,128)} fusion(bf16[8,18,34,256]{3,0,2,1:T(8,128)(2,1)S(1)} %pad_maximum_fusion.1, bf16[4,16,32,256]{3,2,1,0:T(8,128)(2,1)S(1)} %copy-done.5), kind=kOutput, calls=%fused_computation.63 | convolution fusion | flops 2415919104 | bytes 4661248 | tf_op jit(solution)/shard_map/conv_general_dilated | solution.py:102
  38.4 3.3 %select_convert_fusion = bf16[16,32,5,256]{3,1,2,0:T(8,128)(2,1)S(1)} fusion(bf16[3,3,256,256]{3,2,1,0:T(8,128)(2,1)S(1)} %copy-done.6, bf16[18,4,8,7,256]{4,1,3,2,0:T(4,128)(2,1)S(1)} %fusion.30, pred[32,5]{0,1:T(8,128)(4,1)S(1)} %copy-done.13), kind=kOutput, calls=%fused_computation.38 | convolution fusion | flops 3021209600 | bytes 4554912 | tf_op jit(solution)/shard_map/conv_general_dilated | solution.py:59
  44.3 3.2 %select_convert_fusion.1 = bf16[16,32,5,256]{3,1,2,0:T(8,128)(2,1)S(1)} fusion(bf16[3,3,256,256]{3,2,1,0:T(8,128)(2,1)S(1)} %copy-done.6, bf16[18,4,8,7,256]{4,1,3,2,0:T(4,128)(2,1)S(1)} %fusion.29, pred[32,5]{0,1:T(8,128)(4,1)S(1)} %copy-done.13), kind=kOutput, calls=%fused_computation.39 | convolution fusion | flops 3021209600 | bytes 4554912 | tf_op jit(solution)/shard_map/conv_general_dilated | solution.py:59
  51.2 2.1 copy.30
  53.4 6.2 %collective-permute-start.18 = (bf16[128,2304]{1,0:T(8,128)(2,1)S(1)}, bf16[128,2304]{1,0:T(8,128)(2,1)}, u32[]{:S(2)}, u32[]{:S(2)}) collective-permute-start(bf16[128,2304]{1,0:T(8,128)(2,1)S(1)} %dynamic-slice_convert_fusion), channel_id=1, source_target_pairs={{0,64},{16,80},{32,96},{48,112},{64,0},{80,16},{96,32},{112,48},{1... | collective-permute-start | bytes 1769480 | tf_op jit(solution)/shard_map/ppermute | solution.py:50
  59.6 109.1 %while.14 = (s32[]{:T(128)}, bf16[20,36,256]{2,0,1:T(8,128)(2,1)S(1)}, bf16[16,32,256]{2,0,1:T(8,128)(2,1)}, f32[3]{0:T(128)S(1)}, bf16[3,3,256,256]{3,2,1,0:T(8...) while((s32[]{:T(128)}, bf16[20,36,256]{2,0,1:T(8,128)(2,1)S(1)}, ...), condition=%wide.region_2.3_spmd, body=%wide.region_0.2_spmd.sunk | while | flops 1609732096 | bytes 19315492 | solution.py:113
  64.8 3.5 %collective-permute-start.3 = (f32[2,32,256]{2,0,1:T(2,128)S(1)}, f32[2,32,256]{2,0,1:T(2,128)S(1)}, u32[]{:S(2)}, u32[]{:S(2)}) collective-permute-start(f32[2,32,256]{2,0,1:T(2,128)S(1)} %slice_bitcast_fusion.11), channel_id=1, source_target_pairs={{16,0},{32,16},{48,32},{64,48},{80,64},{96,80},{112,96},{0,112},{1... | collective-permute-start | bytes 196616 | tf_op jit(solution)/shard_map/while/body/eval_jaxpr/ppermute | solution.py:21
  70.5 2.3 %collective-permute-start.1 = (f32[]{:T(128)}, f32[]{:T(128)}, u32[]{:S(2)}, u32[]{:S(2)}) collective-permute-start(f32[]{:T(128)} %add.180), channel_id=1, source_target_pairs={{0,32},{16,48},{32,0},{48,16},{64,96},{80,112},{96,64},{112,80},{1... | collective-permute-start | bytes 20 | tf_op jit(solution)/shard_map/while/body/eval_jaxpr/ppermute | solution.py:33
  72.8 2.7 %collective-permute-done.1 = f32[]{:T(128)} collective-permute-done((f32[]{:T(128)}, f32[]{:T(128)}, u32[]{:S(2)}, u32[]{:S(2)}) %collective-permute-start.1) | collective-permute-done | bytes 36 | tf_op jit(solution)/shard_map/while/body/eval_jaxpr/ppermute | solution.py:33
  76.1 3.1 %collective-permute-start.2 = (f32[]{:T(128)}, f32[]{:T(128)}, u32[]{:S(2)}, u32[]{:S(2)}) collective-permute-start(f32[]{:T(128)} %add.181), channel_id=1, source_target_pairs={{0,64},{16,80},{32,96},{48,112},{64,0},{80,16},{96,32},{112,48},{1... | collective-permute-start | bytes 20 | tf_op jit(solution)/shard_map/while/body/eval_jaxpr/ppermute | solution.py:33
  79.2 2.0 collective-permute-done.2
  82.5 3.1 %collective-permute-start.7 = (f32[]{:T(128)}, f32[]{:T(128)}, u32[]{:S(2)}, u32[]{:S(2)}) collective-permute-start(f32[]{:T(128)} %add.182), channel_id=1, source_target_pairs={{0,2},{2,0},{4,6},{6,4},{8,10},{10,8},{12,14},{14,12},{1,3},{3,1},... | collective-permute-start | bytes 20 | tf_op jit(solution)/shard_map/while/body/eval_jaxpr/ppermute | solution.py:33
  86.2 2.7 %collective-permute-start.8 = (f32[]{:T(128)}, f32[]{:T(128)}, u32[]{:S(2)}, u32[]{:S(2)}) collective-permute-start(f32[]{:T(128)} %add.183), channel_id=1, source_target_pairs={{0,4},{2,6},{4,0},{6,2},{8,12},{10,14},{12,8},{14,10},{1,5},{3,7},... | collective-permute-start | bytes 20 | tf_op jit(solution)/shard_map/while/body/eval_jaxpr/ppermute | solution.py:33
  90.4 4.0 %collective-permute-start.9 = (f32[]{:T(128)}, f32[]{:T(128)}, u32[]{:S(2)}, u32[]{:S(2)}) collective-permute-start(f32[]{:T(128)} %add.184), channel_id=1, source_target_pairs={{0,8},{2,10},{4,12},{6,14},{8,0},{10,2},{12,4},{14,6},{1,9},{3,11}... | collective-permute-start | bytes 20 | tf_op jit(solution)/shard_map/while/body/eval_jaxpr/ppermute | solution.py:33
  101.4 2.9 %collective-permute-start = (f32[]{:T(128)}, f32[]{:T(128)}, u32[]{:S(2)}, u32[]{:S(2)}) collective-permute-start(f32[]{:T(128)} %multiply_reduce_fusion.3), channel_id=1, source_target_pairs={{0,16},{16,0},{32,48},{48,32},{64,80},{80,64},{96,112},{112,96},{1... | collective-permute-start | bytes 20 | tf_op jit(solution)/shard_map/while/body/eval_jaxpr/ppermute | solution.py:33
  104.4 1.9 collective-permute-start.3
  106.3 1.8 collective-permute-start.4
  109.4 2.3 %collective-permute-start.1 = (f32[]{:T(128)}, f32[]{:T(128)}, u32[]{:S(2)}, u32[]{:S(2)}) collective-permute-start(f32[]{:T(128)} %add.180), channel_id=1, source_target_pairs={{0,32},{16,48},{32,0},{48,16},{64,96},{80,112},{96,64},{112,80},{1... | collective-permute-start | bytes 20 | tf_op jit(solution)/shard_map/while/body/eval_jaxpr/ppermute | solution.py:33
  113.6 3.2 %collective-permute-start.2 = (f32[]{:T(128)}, f32[]{:T(128)}, u32[]{:S(2)}, u32[]{:S(2)}) collective-permute-start(f32[]{:T(128)} %add.181), channel_id=1, source_target_pairs={{0,64},{16,80},{32,96},{48,112},{64,0},{80,16},{96,32},{112,48},{1... | collective-permute-start | bytes 20 | tf_op jit(solution)/shard_map/while/body/eval_jaxpr/ppermute | solution.py:33
  116.8 1.9 collective-permute-done.2
  120.0 2.0 collective-permute-start.7
  122.7 2.7 %collective-permute-start.8 = (f32[]{:T(128)}, f32[]{:T(128)}, u32[]{:S(2)}, u32[]{:S(2)}) collective-permute-start(f32[]{:T(128)} %add.183), channel_id=1, source_target_pairs={{0,4},{2,6},{4,0},{6,2},{8,12},{10,14},{12,8},{14,10},{1,5},{3,7},... | collective-permute-start | bytes 20 | tf_op jit(solution)/shard_map/while/body/eval_jaxpr/ppermute | solution.py:33
  126.9 3.4 %collective-permute-start.9 = (f32[]{:T(128)}, f32[]{:T(128)}, u32[]{:S(2)}, u32[]{:S(2)}) collective-permute-start(f32[]{:T(128)} %add.184), channel_id=1, source_target_pairs={{0,8},{2,10},{4,12},{6,14},{8,0},{10,2},{12,4},{14,6},{1,9},{3,11}... | collective-permute-start | bytes 20 | tf_op jit(solution)/shard_map/while/body/eval_jaxpr/ppermute | solution.py:33
  130.2 1.7 collective-permute-done.9
  139.2 4.1 %collective-permute-start.3 = (f32[2,32,256]{2,0,1:T(2,128)S(1)}, f32[2,32,256]{2,0,1:T(2,128)S(1)}, u32[]{:S(2)}, u32[]{:S(2)}) collective-permute-start(f32[2,32,256]{2,0,1:T(2,128)S(1)} %slice_bitcast_fusion.11), channel_id=1, source_target_pairs={{16,0},{32,16},{48,32},{64,48},{80,64},{96,80},{112,96},{0,112},{1... | collective-permute-start | bytes 196616 | tf_op jit(solution)/shard_map/while/body/eval_jaxpr/ppermute | solution.py:21
  144.8 1.7 collective-permute-start.1
  146.5 1.8 collective-permute-done.1
  149.0 3.5 %collective-permute-start.2 = (f32[]{:T(128)}, f32[]{:T(128)}, u32[]{:S(2)}, u32[]{:S(2)}) collective-permute-start(f32[]{:T(128)} %add.181), channel_id=1, source_target_pairs={{0,64},{16,80},{32,96},{48,112},{64,0},{80,16},{96,32},{112,48},{1... | collective-permute-start | bytes 20 | tf_op jit(solution)/shard_map/while/body/eval_jaxpr/ppermute | solution.py:33
  152.5 1.6 collective-permute-done.2
  155.4 1.7 collective-permute-start.7
  157.7 2.0 collective-permute-start.8
  161.9 3.2 %collective-permute-start.9 = (f32[]{:T(128)}, f32[]{:T(128)}, u32[]{:S(2)}, u32[]{:S(2)}) collective-permute-start(f32[]{:T(128)} %add.184), channel_id=1, source_target_pairs={{0,8},{2,10},{4,12},{6,14},{8,0},{10,2},{12,4},{14,6},{1,9},{3,11}... | collective-permute-start | bytes 20 | tf_op jit(solution)/shard_map/while/body/eval_jaxpr/ppermute | solution.py:33
  165.2 1.9 collective-permute-done.9
  168.8 1.6 convert_add_fusion
  174.4 9.7 %collective-permute-done.19 = f32[64,2304]{1,0:T(8,128)S(1)} collective-permute-done((f32[64,2304]{1,0:T(8,128)S(1)}, f32[64,2304]{1,0:T(8,128)S(1)}, u32[]{:S(2)}, u32[]{:S(2)}) %collective-permute-start.19) | collective-permute-done | bytes 589856 | tf_op jit(solution)/shard_map/ppermute | solution.py:50
  184.3 2.7 %collective-permute-start.20 = (f32[32,2304]{1,0:T(8,128)S(1)}, f32[32,2304]{1,0:T(8,128)S(1)}, u32[]{:S(2)}, u32[]{:S(2)}) collective-permute-start(f32[32,2304]{1,0:T(8,128)S(1)} %constant_dynamic-slice_fusion.3), channel_id=1, source_target_pairs={{0,16},{16,0},{32,48},{48,32},{64,80},{80,64},{96,112},{112,96},{1... | collective-permute-start | bytes 884744 | tf_op jit(solution)/shard_map/ppermute | solution.py:50
  189.3 4.1 %collective-permute-done.25 = f32[2]{0:T(128)S(1)} collective-permute-done((f32[2]{0:T(128)S(1)}, f32[2]{0:T(128)S(1)}, u32[]{:S(2)}, u32[]{:S(2)}) %collective-permute-start.25) | collective-permute-done | bytes 40 | tf_op jit(solution)/shard_map/ppermute | solution.py:33
  195.8 1.9 collective-permute-start.21
  199.7 3.5 %collective-permute-start.27 = (f32[2]{0:T(128)S(1)}, f32[2]{0:T(128)S(1)}, u32[]{:S(2)}, u32[]{:S(2)}) collective-permute-start(f32[2]{0:T(128)S(1)} %fusion.81), channel_id=1, source_target_pairs={{0,64},{16,80},{32,96},{48,112},{64,0},{80,16},{96,32},{112,48},{1... | collective-permute-start | bytes 32 | tf_op jit(solution)/shard_map/ppermute | solution.py:33
  206.8 2.6 %collective-permute-done.29 = f32[2]{0:T(128)S(1)} collective-permute-done((f32[2]{0:T(128)S(1)}, f32[2]{0:T(128)S(1)}, u32[]{:S(2)}, u32[]{:S(2)}) %collective-permute-start.29) | collective-permute-done | bytes 40 | tf_op jit(solution)/shard_map/ppermute | solution.py:33
  209.4 1.8 collective-permute-start.30
  211.3 3.2 %collective-permute-done.30 = f32[2]{0:T(128)S(1)} collective-permute-done((f32[2]{0:T(128)S(1)}, f32[2]{0:T(128)S(1)}, u32[]{:S(2)}, u32[]{:S(2)}) %collective-permute-start.30) | collective-permute-done | bytes 40 | tf_op jit(solution)/shard_map/ppermute | solution.py:33
  216.8 2.2 collective-permute-done.22
  (202 shorter events, 64.6 us)
Async XLA Ops:
  2.1 17.0 %collective-permute-start.15 = (bf16[2,32,256]{2,0,1:T(2,128)(2,1)S(1)}, bf16[2,32,256]{2,0,1:T(2,128)(2,1)S(1)}, u32[]{:S(2)}, u32[]{:S(2)}) collective-permute-start(bf16[2,32,256]{2,0,1:T(2,128)(2,1)S(1)} %get-tuple-element.76), channel_id=1, source_target_pairs={{16,0},{32,16},{48,32},{64,48},{80,64},{96,80},{112,96},{0,112},{1... | collective-permute-start | bytes 98312 | tf_op jit(solution)/shard_map/ppermute | solution.py:21
  8.4 10.8 %collective-permute-start.14 = (bf16[2,32,256]{2,0,1:T(2,128)(2,1)S(1)}, bf16[2,32,256]{2,0,1:T(2,128)(2,1)S(1)}, u32[]{:S(2)}, u32[]{:S(2)}) collective-permute-start(bf16[2,32,256]{2,0,1:T(2,128)(2,1)S(1)} %get-tuple-element.75), channel_id=1, source_target_pairs={{0,16},{16,32},{32,48},{48,64},{64,80},{80,96},{96,112},{112,0},{1... | collective-permute-start | bytes 98312 | tf_op jit(solution)/shard_map/ppermute | solution.py:19
  11.5 9.3 %collective-permute-start.11 = (bf16[8,1,32,256]{3,0,2,1:T(8,128)(2,1)S(1)}, bf16[8,1,32,256]{3,0,2,1:T(8,128)(2,1)S(1)}, u32[]{:S(2)}, u32[]{:S(2)}) collective-permute-start(bf16[8,1,32,256]{3,0,2,1:T(8,128)(2,1)S(1)} %get-tuple-element.72), channel_id=1, source_target_pairs={{16,0},{32,16},{48,32},{64,48},{80,64},{96,80},{112,96},{17,1},{33... | collective-permute-start | bytes 393224 | tf_op jit(solution)/shard_map/ppermute | solution.py:21
  12.8 9.0 %collective-permute-start.10 = (bf16[8,1,32,256]{3,0,2,1:T(8,128)(2,1)S(1)}, bf16[8,1,32,256]{3,0,2,1:T(8,128)(2,1)S(1)}, u32[]{:S(2)}, u32[]{:S(2)}) collective-permute-start(bf16[8,1,32,256]{3,0,2,1:T(8,128)(2,1)S(1)} %get-tuple-element.71), channel_id=1, source_target_pairs={{0,16},{16,32},{32,48},{48,64},{64,80},{80,96},{96,112},{1,17},{17... | collective-permute-start | bytes 393224 | tf_op jit(solution)/shard_map/ppermute | solution.py:19
  19.2 7.1 %collective-permute-start.17 = (bf16[20,2,256]{2,0,1:T(8,128)(2,1)S(1)}, bf16[20,2,256]{2,0,1:T(8,128)(2,1)S(1)}, u32[]{:S(2)}, u32[]{:S(2)}) collective-permute-start(bf16[20,2,256]{2,0,1:T(8,128)(2,1)S(1)} %get-tuple-element.74), channel_id=1, source_target_pairs={{2,0},{4,2},{6,4},{8,6},{10,8},{12,10},{14,12},{0,14},{3,1},{5,3},... | collective-permute-start | bytes 61448 | tf_op jit(solution)/shard_map/ppermute | solution.py:21
  20.8 5.5 %collective-permute-start.16 = (bf16[20,2,256]{2,0,1:T(8,128)(2,1)S(1)}, bf16[20,2,256]{2,0,1:T(8,128)(2,1)S(1)}, u32[]{:S(2)}, u32[]{:S(2)}) collective-permute-start(bf16[20,2,256]{2,0,1:T(8,128)(2,1)S(1)} %get-tuple-element.73), channel_id=1, source_target_pairs={{0,2},{2,4},{4,6},{6,8},{8,10},{10,12},{12,14},{14,0},{1,3},{3,5},... | collective-permute-start | bytes 61448 | tf_op jit(solution)/shard_map/ppermute | solution.py:19
  21.9 5.4 %collective-permute-start.13 = (bf16[8,18,1,256]{3,0,2,1:T(8,128)(2,1)S(1)}, bf16[8,18,1,256]{3,0,2,1:T(8,128)(2,1)S(1)}, u32[]{:S(2)}, u32[]{:S(2)}) collective-permute-start(bf16[8,18,1,256]{3,0,2,1:T(8,128)(2,1)S(1)} %get-tuple-element.70), channel_id=1, source_target_pairs={{2,0},{4,2},{6,4},{8,6},{10,8},{12,10},{14,12},{3,1},{5,3},{7,5},{... | collective-permute-start | bytes 221192 | tf_op jit(solution)/shard_map/ppermute | solution.py:21
  23.2 4.1 %collective-permute-start.12 = (bf16[8,18,1,256]{3,0,2,1:T(8,128)(2,1)S(1)}, bf16[8,18,1,256]{3,0,2,1:T(8,128)(2,1)S(1)}, u32[]{:S(2)}, u32[]{:S(2)}) collective-permute-start(bf16[8,18,1,256]{3,0,2,1:T(8,128)(2,1)S(1)} %get-tuple-element.69), channel_id=1, source_target_pairs={{0,2},{2,4},{4,6},{6,8},{8,10},{10,12},{12,14},{1,3},{3,5},{5,7},{... | collective-permute-start | bytes 221192 | tf_op jit(solution)/shard_map/ppermute | solution.py:19
  53.4 115.4 %collective-permute-start.18 = (bf16[128,2304]{1,0:T(8,128)(2,1)S(1)}, bf16[128,2304]{1,0:T(8,128)(2,1)}, u32[]{:S(2)}, u32[]{:S(2)}) collective-permute-start(bf16[128,2304]{1,0:T(8,128)(2,1)S(1)} %dynamic-slice_convert_fusion), channel_id=1, source_target_pairs={{0,64},{16,80},{32,96},{48,112},{64,0},{80,16},{96,32},{112,48},{1... | collective-permute-start | bytes 1769480 | tf_op jit(solution)/shard_map/ppermute | solution.py:50
  64.1 5.1 %collective-permute-start = (f32[]{:T(128)}, f32[]{:T(128)}, u32[]{:S(2)}, u32[]{:S(2)}) collective-permute-start(f32[]{:T(128)} %multiply_reduce_fusion.3), channel_id=1, source_target_pairs={{0,16},{16,0},{32,48},{48,32},{64,80},{80,64},{96,112},{112,96},{1... | collective-permute-start | bytes 20 | tf_op jit(solution)/shard_map/while/body/eval_jaxpr/ppermute | solution.py:33
  64.8 17.0 %collective-permute-start.3 = (f32[2,32,256]{2,0,1:T(2,128)S(1)}, f32[2,32,256]{2,0,1:T(2,128)S(1)}, u32[]{:S(2)}, u32[]{:S(2)}) collective-permute-start(f32[2,32,256]{2,0,1:T(2,128)S(1)} %slice_bitcast_fusion.11), channel_id=1, source_target_pairs={{16,0},{32,16},{48,32},{64,48},{80,64},{96,80},{112,96},{0,112},{1... | collective-permute-start | bytes 196616 | tf_op jit(solution)/shard_map/while/body/eval_jaxpr/ppermute | solution.py:21
  68.4 13.4 %collective-permute-start.4 = (f32[2,32,256]{2,0,1:T(2,128)S(1)}, f32[2,32,256]{2,0,1:T(2,128)S(1)}, u32[]{:S(2)}, u32[]{:S(2)}) collective-permute-start(f32[2,32,256]{2,0,1:T(2,128)S(1)} %slice_bitcast_fusion.13), channel_id=1, source_target_pairs={{0,16},{16,32},{32,48},{48,64},{64,80},{80,96},{96,112},{112,0},{1... | collective-permute-start | bytes 196616 | tf_op jit(solution)/shard_map/while/body/eval_jaxpr/ppermute | solution.py:19
  70.5 5.0 %collective-permute-start.1 = (f32[]{:T(128)}, f32[]{:T(128)}, u32[]{:S(2)}, u32[]{:S(2)}) collective-permute-start(f32[]{:T(128)} %add.180), channel_id=1, source_target_pairs={{0,32},{16,48},{32,0},{48,16},{64,96},{80,112},{96,64},{112,80},{1... | collective-permute-start | bytes 20 | tf_op jit(solution)/shard_map/while/body/eval_jaxpr/ppermute | solution.py:33
  76.1 5.1 %collective-permute-start.2 = (f32[]{:T(128)}, f32[]{:T(128)}, u32[]{:S(2)}, u32[]{:S(2)}) collective-permute-start(f32[]{:T(128)} %add.181), channel_id=1, source_target_pairs={{0,64},{16,80},{32,96},{48,112},{64,0},{80,16},{96,32},{112,48},{1... | collective-permute-start | bytes 20 | tf_op jit(solution)/shard_map/while/body/eval_jaxpr/ppermute | solution.py:33
  82.0 15.0 %collective-permute-start.5 = (f32[20,2,256]{2,0,1:T(8,128)S(1)}, f32[20,2,256]{2,0,1:T(8,128)S(1)}, u32[]{:S(2)}, u32[]{:S(2)}) collective-permute-start(f32[20,2,256]{2,0,1:T(8,128)S(1)} %get-tuple-element.121), channel_id=1, source_target_pairs={{2,0},{4,2},{6,4},{8,6},{10,8},{12,10},{14,12},{0,14},{3,1},{5,3},... | collective-permute-start | bytes 122888 | tf_op jit(solution)/shard_map/while/body/eval_jaxpr/ppermute | solution.py:21
  82.0 15.0 %collective-permute-start.6 = (f32[20,2,256]{2,0,1:T(8,128)S(1)}, f32[20,2,256]{2,0,1:T(8,128)S(1)}, u32[]{:S(2)}, u32[]{:S(2)}) collective-permute-start(f32[20,2,256]{2,0,1:T(8,128)S(1)} %get-tuple-element.122), channel_id=1, source_target_pairs={{0,2},{2,4},{4,6},{6,8},{8,10},{10,12},{12,14},{14,0},{1,3},{3,5},... | collective-permute-start | bytes 122888 | tf_op jit(solution)/shard_map/while/body/eval_jaxpr/ppermute | solution.py:19
  82.5 3.1 %collective-permute-start.7 = (f32[]{:T(128)}, f32[]{:T(128)}, u32[]{:S(2)}, u32[]{:S(2)}) collective-permute-start(f32[]{:T(128)} %add.182), channel_id=1, source_target_pairs={{0,2},{2,0},{4,6},{6,4},{8,10},{10,8},{12,14},{14,12},{1,3},{3,1},... | collective-permute-start | bytes 20 | tf_op jit(solution)/shard_map/while/body/eval_jaxpr/ppermute | solution.py:33
  86.2 3.6 %collective-permute-start.8 = (f32[]{:T(128)}, f32[]{:T(128)}, u32[]{:S(2)}, u32[]{:S(2)}) collective-permute-start(f32[]{:T(128)} %add.183), channel_id=1, source_target_pairs={{0,4},{2,6},{4,0},{6,2},{8,12},{10,14},{12,8},{14,10},{1,5},{3,7},... | collective-permute-start | bytes 20 | tf_op jit(solution)/shard_map/while/body/eval_jaxpr/ppermute | solution.py:33
  90.4 5.1 %collective-permute-start.9 = (f32[]{:T(128)}, f32[]{:T(128)}, u32[]{:S(2)}, u32[]{:S(2)}) collective-permute-start(f32[]{:T(128)} %add.184), channel_id=1, source_target_pairs={{0,8},{2,10},{4,12},{6,14},{8,0},{10,2},{12,4},{14,6},{1,9},{3,11}... | collective-permute-start | bytes 20 | tf_op jit(solution)/shard_map/while/body/eval_jaxpr/ppermute | solution.py:33
  101.4 6.7 %collective-permute-start = (f32[]{:T(128)}, f32[]{:T(128)}, u32[]{:S(2)}, u32[]{:S(2)}) collective-permute-start(f32[]{:T(128)} %multiply_reduce_fusion.3), channel_id=1, source_target_pairs={{0,16},{16,0},{32,48},{48,32},{64,80},{80,64},{96,112},{112,96},{1... | collective-permute-start | bytes 20 | tf_op jit(solution)/shard_map/while/body/eval_jaxpr/ppermute | solution.py:33
  104.4 15.0 %collective-permute-start.3 = (f32[2,32,256]{2,0,1:T(2,128)S(1)}, f32[2,32,256]{2,0,1:T(2,128)S(1)}, u32[]{:S(2)}, u32[]{:S(2)}) collective-permute-start(f32[2,32,256]{2,0,1:T(2,128)S(1)} %slice_bitcast_fusion.11), channel_id=1, source_target_pairs={{16,0},{32,16},{48,32},{64,48},{80,64},{96,80},{112,96},{0,112},{1... | collective-permute-start | bytes 196616 | tf_op jit(solution)/shard_map/while/body/eval_jaxpr/ppermute | solution.py:21
  106.3 13.0 %collective-permute-start.4 = (f32[2,32,256]{2,0,1:T(2,128)S(1)}, f32[2,32,256]{2,0,1:T(2,128)S(1)}, u32[]{:S(2)}, u32[]{:S(2)}) collective-permute-start(f32[2,32,256]{2,0,1:T(2,128)S(1)} %slice_bitcast_fusion.13), channel_id=1, source_target_pairs={{0,16},{16,32},{32,48},{48,64},{64,80},{80,96},{96,112},{112,0},{1... | collective-permute-start | bytes 196616 | tf_op jit(solution)/shard_map/while/body/eval_jaxpr/ppermute | solution.py:19
  109.4 3.6 %collective-permute-start.1 = (f32[]{:T(128)}, f32[]{:T(128)}, u32[]{:S(2)}, u32[]{:S(2)}) collective-permute-start(f32[]{:T(128)} %add.180), channel_id=1, source_target_pairs={{0,32},{16,48},{32,0},{48,16},{64,96},{80,112},{96,64},{112,80},{1... | collective-permute-start | bytes 20 | tf_op jit(solution)/shard_map/while/body/eval_jaxpr/ppermute | solution.py:33
  113.6 5.1 %collective-permute-start.2 = (f32[]{:T(128)}, f32[]{:T(128)}, u32[]{:S(2)}, u32[]{:S(2)}) collective-permute-start(f32[]{:T(128)} %add.181), channel_id=1, source_target_pairs={{0,64},{16,80},{32,96},{48,112},{64,0},{80,16},{96,32},{112,48},{1... | collective-permute-start | bytes 20 | tf_op jit(solution)/shard_map/while/body/eval_jaxpr/ppermute | solution.py:33
  119.5 14.0 %collective-permute-start.5 = (f32[20,2,256]{2,0,1:T(8,128)S(1)}, f32[20,2,256]{2,0,1:T(8,128)S(1)}, u32[]{:S(2)}, u32[]{:S(2)}) collective-permute-start(f32[20,2,256]{2,0,1:T(8,128)S(1)} %get-tuple-element.121), channel_id=1, source_target_pairs={{2,0},{4,2},{6,4},{8,6},{10,8},{12,10},{14,12},{0,14},{3,1},{5,3},... | collective-permute-start | bytes 122888 | tf_op jit(solution)/shard_map/while/body/eval_jaxpr/ppermute | solution.py:21
  119.5 13.9 %collective-permute-start.6 = (f32[20,2,256]{2,0,1:T(8,128)S(1)}, f32[20,2,256]{2,0,1:T(8,128)S(1)}, u32[]{:S(2)}, u32[]{:S(2)}) collective-permute-start(f32[20,2,256]{2,0,1:T(8,128)S(1)} %get-tuple-element.122), channel_id=1, source_target_pairs={{0,2},{2,4},{4,6},{6,8},{8,10},{10,12},{12,14},{14,0},{1,3},{3,5},... | collective-permute-start | bytes 122888 | tf_op jit(solution)/shard_map/while/body/eval_jaxpr/ppermute | solution.py:19
  120.0 2.0 collective-permute-start.7
  122.7 3.6 %collective-permute-start.8 = (f32[]{:T(128)}, f32[]{:T(128)}, u32[]{:S(2)}, u32[]{:S(2)}) collective-permute-start(f32[]{:T(128)} %add.183), channel_id=1, source_target_pairs={{0,4},{2,6},{4,0},{6,2},{8,12},{10,14},{12,8},{14,10},{1,5},{3,7},... | collective-permute-start | bytes 20 | tf_op jit(solution)/shard_map/while/body/eval_jaxpr/ppermute | solution.py:33
  126.9 5.1 %collective-permute-start.9 = (f32[]{:T(128)}, f32[]{:T(128)}, u32[]{:S(2)}, u32[]{:S(2)}) collective-permute-start(f32[]{:T(128)} %add.184), channel_id=1, source_target_pairs={{0,8},{2,10},{4,12},{6,14},{8,0},{10,2},{12,4},{14,6},{1,9},{3,11}... | collective-permute-start | bytes 20 | tf_op jit(solution)/shard_map/while/body/eval_jaxpr/ppermute | solution.py:33
  137.9 5.7 %collective-permute-start = (f32[]{:T(128)}, f32[]{:T(128)}, u32[]{:S(2)}, u32[]{:S(2)}) collective-permute-start(f32[]{:T(128)} %multiply_reduce_fusion.3), channel_id=1, source_target_pairs={{0,16},{16,0},{32,48},{48,32},{64,80},{80,64},{96,112},{112,96},{1... | collective-permute-start | bytes 20 | tf_op jit(solution)/shard_map/while/body/eval_jaxpr/ppermute | solution.py:33
  139.2 15.5 %collective-permute-start.3 = (f32[2,32,256]{2,0,1:T(2,128)S(1)}, f32[2,32,256]{2,0,1:T(2,128)S(1)}, u32[]{:S(2)}, u32[]{:S(2)}) collective-permute-start(f32[2,32,256]{2,0,1:T(2,128)S(1)} %slice_bitcast_fusion.11), channel_id=1, source_target_pairs={{16,0},{32,16},{48,32},{64,48},{80,64},{96,80},{112,96},{0,112},{1... | collective-permute-start | bytes 196616 | tf_op jit(solution)/shard_map/while/body/eval_jaxpr/ppermute | solution.py:21
  143.4 11.3 %collective-permute-start.4 = (f32[2,32,256]{2,0,1:T(2,128)S(1)}, f32[2,32,256]{2,0,1:T(2,128)S(1)}, u32[]{:S(2)}, u32[]{:S(2)}) collective-permute-start(f32[2,32,256]{2,0,1:T(2,128)S(1)} %slice_bitcast_fusion.13), channel_id=1, source_target_pairs={{0,16},{16,32},{32,48},{48,64},{64,80},{80,96},{96,112},{112,0},{1... | collective-permute-start | bytes 196616 | tf_op jit(solution)/shard_map/while/body/eval_jaxpr/ppermute | solution.py:19
  144.8 3.6 %collective-permute-start.1 = (f32[]{:T(128)}, f32[]{:T(128)}, u32[]{:S(2)}, u32[]{:S(2)}) collective-permute-start(f32[]{:T(128)} %add.180), channel_id=1, source_target_pairs={{0,32},{16,48},{32,0},{48,16},{64,96},{80,112},{96,64},{112,80},{1... | collective-permute-start | bytes 20 | tf_op jit(solution)/shard_map/while/body/eval_jaxpr/ppermute | solution.py:33
  149.0 5.1 %collective-permute-start.2 = (f32[]{:T(128)}, f32[]{:T(128)}, u32[]{:S(2)}, u32[]{:S(2)}) collective-permute-start(f32[]{:T(128)} %add.181), channel_id=1, source_target_pairs={{0,64},{16,80},{32,96},{48,112},{64,0},{80,16},{96,32},{112,48},{1... | collective-permute-start | bytes 20 | tf_op jit(solution)/shard_map/while/body/eval_jaxpr/ppermute | solution.py:33
  154.9 13.7 %collective-permute-start.5 = (f32[20,2,256]{2,0,1:T(8,128)S(1)}, f32[20,2,256]{2,0,1:T(8,128)S(1)}, u32[]{:S(2)}, u32[]{:S(2)}) collective-permute-start(f32[20,2,256]{2,0,1:T(8,128)S(1)} %get-tuple-element.121), channel_id=1, source_target_pairs={{2,0},{4,2},{6,4},{8,6},{10,8},{12,10},{14,12},{0,14},{3,1},{5,3},... | collective-permute-start | bytes 122888 | tf_op jit(solution)/shard_map/while/body/eval_jaxpr/ppermute | solution.py:21
  154.9 13.7 %collective-permute-start.6 = (f32[20,2,256]{2,0,1:T(8,128)S(1)}, f32[20,2,256]{2,0,1:T(8,128)S(1)}, u32[]{:S(2)}, u32[]{:S(2)}) collective-permute-start(f32[20,2,256]{2,0,1:T(8,128)S(1)} %get-tuple-element.122), channel_id=1, source_target_pairs={{0,2},{2,4},{4,6},{6,8},{8,10},{10,12},{12,14},{14,0},{1,3},{3,5},... | collective-permute-start | bytes 122888 | tf_op jit(solution)/shard_map/while/body/eval_jaxpr/ppermute | solution.py:19
  157.7 3.6 %collective-permute-start.8 = (f32[]{:T(128)}, f32[]{:T(128)}, u32[]{:S(2)}, u32[]{:S(2)}) collective-permute-start(f32[]{:T(128)} %add.183), channel_id=1, source_target_pairs={{0,4},{2,6},{4,0},{6,2},{8,12},{10,14},{12,8},{14,10},{1,5},{3,7},... | collective-permute-start | bytes 20 | tf_op jit(solution)/shard_map/while/body/eval_jaxpr/ppermute | solution.py:33
  161.9 5.1 %collective-permute-start.9 = (f32[]{:T(128)}, f32[]{:T(128)}, u32[]{:S(2)}, u32[]{:S(2)}) collective-permute-start(f32[]{:T(128)} %add.184), channel_id=1, source_target_pairs={{0,8},{2,10},{4,12},{6,14},{8,0},{10,2},{12,4},{14,6},{1,9},{3,11}... | collective-permute-start | bytes 20 | tf_op jit(solution)/shard_map/while/body/eval_jaxpr/ppermute | solution.py:33
  170.6 13.6 %collective-permute-start.19 = (f32[64,2304]{1,0:T(8,128)S(1)}, f32[64,2304]{1,0:T(8,128)S(1)}, u32[]{:S(2)}, u32[]{:S(2)}) collective-permute-start(f32[64,2304]{1,0:T(8,128)S(1)} %constant_dynamic-slice_fusion.4), channel_id=1, source_target_pairs={{0,32},{16,48},{32,0},{48,16},{64,96},{80,112},{96,64},{112,80},{1... | collective-permute-start | bytes 1769480 | tf_op jit(solution)/shard_map/ppermute | solution.py:50
  184.3 11.4 %collective-permute-start.20 = (f32[32,2304]{1,0:T(8,128)S(1)}, f32[32,2304]{1,0:T(8,128)S(1)}, u32[]{:S(2)}, u32[]{:S(2)}) collective-permute-start(f32[32,2304]{1,0:T(8,128)S(1)} %constant_dynamic-slice_fusion.3), channel_id=1, source_target_pairs={{0,16},{16,0},{32,48},{48,32},{64,80},{80,64},{96,112},{112,96},{1... | collective-permute-start | bytes 884744 | tf_op jit(solution)/shard_map/ppermute | solution.py:50
  188.4 5.1 %collective-permute-start.25 = (f32[2]{0:T(128)S(1)}, f32[2]{0:T(128)S(1)}, u32[]{:S(2)}, u32[]{:S(2)}) collective-permute-start(f32[2]{0:T(128)S(1)} %pad_maximum_fusion.12), channel_id=1, source_target_pairs={{0,16},{16,0},{32,48},{48,32},{64,80},{80,64},{96,112},{112,96},{1... | collective-permute-start | bytes 32 | tf_op jit(solution)/shard_map/ppermute | solution.py:33
  194.8 3.6 %collective-permute-start.26 = (f32[2]{0:T(128)S(1)}, f32[2]{0:T(128)S(1)}, u32[]{:S(2)}, u32[]{:S(2)}) collective-permute-start(f32[2]{0:T(128)S(1)} %fusion.80), channel_id=1, source_target_pairs={{0,32},{16,48},{32,0},{48,16},{64,96},{80,112},{96,64},{112,80},{1... | collective-permute-start | bytes 32 | tf_op jit(solution)/shard_map/ppermute | solution.py:33
  195.8 18.7 %collective-permute-start.21 = (f32[16,2304]{1,0:T(8,128)S(1)}, f32[16,2304]{1,0:T(8,128)S(1)}, u32[]{:S(2)}, u32[]{:S(2)}) collective-permute-start(f32[16,2304]{1,0:T(8,128)S(1)} %constant_dynamic-slice_fusion.2), channel_id=1, source_target_pairs={{0,8},{2,10},{4,12},{6,14},{8,0},{10,2},{12,4},{14,6},{1,9},{3,11}... | collective-permute-start | bytes 442376 | tf_op jit(solution)/shard_map/ppermute | solution.py:50
  199.7 5.1 %collective-permute-start.27 = (f32[2]{0:T(128)S(1)}, f32[2]{0:T(128)S(1)}, u32[]{:S(2)}, u32[]{:S(2)}) collective-permute-start(f32[2]{0:T(128)S(1)} %fusion.81), channel_id=1, source_target_pairs={{0,64},{16,80},{32,96},{48,112},{64,0},{80,16},{96,32},{112,48},{1... | collective-permute-start | bytes 32 | tf_op jit(solution)/shard_map/ppermute | solution.py:33
  205.9 3.5 %collective-permute-start.29 = (f32[2]{0:T(128)S(1)}, f32[2]{0:T(128)S(1)}, u32[]{:S(2)}, u32[]{:S(2)}) collective-permute-start(f32[2]{0:T(128)S(1)} %add.156), channel_id=1, source_target_pairs={{0,4},{2,6},{4,0},{6,2},{8,12},{10,14},{12,8},{14,10},{1,5},{3,7},... | collective-permute-start | bytes 32 | tf_op jit(solution)/shard_map/ppermute | solution.py:33
  209.4 5.0 %collective-permute-start.30 = (f32[2]{0:T(128)S(1)}, f32[2]{0:T(128)S(1)}, u32[]{:S(2)}, u32[]{:S(2)}) collective-permute-start(f32[2]{0:T(128)S(1)} %add.157), channel_id=1, source_target_pairs={{0,8},{2,10},{4,12},{6,14},{8,0},{10,2},{12,4},{14,6},{1,9},{3,11}... | collective-permute-start | bytes 32 | tf_op jit(solution)/shard_map/ppermute | solution.py:33
  214.5 4.4 %collective-permute-start.22 = (f32[8,2304]{1,0:T(8,128)S(1)}, f32[8,2304]{1,0:T(8,128)S(1)}, u32[]{:S(2)}, u32[]{:S(2)}) collective-permute-start(f32[8,2304]{1,0:T(8,128)S(1)} %constant_dynamic-slice_fusion.1), channel_id=1, source_target_pairs={{0,4},{2,6},{4,0},{6,2},{8,12},{10,14},{12,8},{14,10},{1,5},{3,7},... | collective-permute-start | bytes 221192 | tf_op jit(solution)/shard_map/ppermute | solution.py:50
  220.3 4.0 %collective-permute-start.24 = (f32[4,2304]{1,0:T(4,128)S(1)}, f32[4,2304]{1,0:T(4,128)S(1)}, u32[]{:S(2)}, u32[]{:S(2)}) collective-permute-start(f32[4,2304]{1,0:T(4,128)S(1)} %dynamic-slice_add_fusion.4), channel_id=1, source_target_pairs={{0,1},{1,0},{2,3},{3,2},{4,5},{5,4},{6,7},{7,6},{8,9},{9,8},{10,11... | collective-permute-start | bytes 110600 | tf_op jit(solution)/shard_map/ppermute | solution.py:33
  (19 other events, 85.0 us)

commit v8 on v7

--- a/solution.py
+++ b/solution.py
@@ -45,7 +45,7 @@
             upper = (index // step) % 2
             keep = lax.dynamic_slice_in_dim(value, upper * half, half, axis=0)
             send = lax.dynamic_slice_in_dim(value, (1 - upper) * half, half, axis=0)
-            if send.size * 4 > 256 * 2304:
+            if send.size * 8 > 256 * 2304:
                 send = send.astype(jnp.bfloat16)
             received = lax.ppermute(send, axis, [(i, i ^ step) for i in range(count)])
             value = keep + received.astype(jnp.float32)

time: 228 us -> 223 us (0.978)
  waiting for transfers between devices: 47.5 us -> 40.6 us
  local copies, waits for them, and re-layouts: 21.1 us -> 24.1 us
    ppermute x6, waiting for transfers between devices: 12.8 us -> 4.26 us  [halving_scatter(): received = lax.ppermute(send, axis, [(i, i ^ step) for i in range(count)])]
    unnamed x32 -> x38, local copies, waits for them, and re-layouts: 8.27 us -> 9.93 us
  transfers between devices with their start and end apart: 51 -> 51, of which waited for: 24 -> 24; matrix products, arithmetic and copies ran while one was open for 12% -> 13% of each run, Pallas kernels for 0% -> 0%
where the time goes in v8:
time: 223 us; the launch traced here: 222 us
  starting transfers between devices  100 us (45%)
  waiting for transfers between devices  40.6 us (18%)
  local copies, waits for them, and re-layouts  24.1 us (11%)
  matrix products  22.1 us (10%)
  other arithmetic  16.5 us (7%)
  loops' own time  13.2 us (6%)
  between operations  4.59 us (2%)
    ppermute x25, starting transfers between devices, butterfly_sum(): lax.ppermute(value, axis, [(i, i ^ step) for i in range(count)])  55.6 us
    ppermute x25, waiting for transfers between devices, butterfly_sum(): lax.ppermute(value, axis, [(i, i ^ step) for i in range(count)])  35.3 us
    ppermute x10, starting transfers between devices, extended(): lax.ppermute(head, axis, [((i + 1) % count, i) for i in range(ends)])  19.8 us
    conv_general_dilated x10, matrix products, conv(): lax.conv_general_dilated(padded, weights, window_strides=(1, 1), padding=...  15.2 us
    another operation x1, loops' own time, per_device(): lax.scan(power_step, (padded_probe, iterate), None, length=ITERS - 1)  13.2 us
    ppermute x10, starting transfers between devices, extended(): lax.ppermute(tail, axis, [(i, (i + 1) % count) for i in range(ends)])  12.6 us
    ppermute x6, starting transfers between devices, halving_scatter(): received = lax.ppermute(send, axis, [(i, i ^ step) for i in range(count)])  12.5 us
    unnamed x38, local copies, waits for them, and re-layouts  9.93 us
  transfers between devices with their start and end apart: 51, of which 24 were waited for; matrix products, arithmetic and copies ran while one was open for 13% of the time, Pallas kernels for 0%

profile of v8, /device:TPU:0, one launch (start us, length us, event | category | flops | bytes accessed | tf_op | source)
XLA Modules:
  0.0 221.6 jit_solution(1312428080186412296)
XLA Ops:
  2.1 6.2 %collective-permute-start.15 = (bf16[2,32,256]{2,0,1:T(2,128)(2,1)S(1)}, bf16[2,32,256]{2,0,1:T(2,128)(2,1)S(1)}, u32[]{:S(2)}, u32[]{:S(2)}) collective-permute-start(bf16[2,32,256]{2,0,1:T(2,128)(2,1)S(1)} %get-tuple-element.76), channel_id=1, source_target_pairs={{16,0},{32,16},{48,32},{64,48},{80,64},{96,80},{112,96},{0,112},{1... | collective-permute-start | bytes 98312 | tf_op jit(solution)/shard_map/ppermute | solution.py:21
  8.4 2.1 copy.23
  12.8 6.1 %collective-permute-start.10 = (bf16[8,1,32,256]{3,0,2,1:T(8,128)(2,1)S(1)}, bf16[8,1,32,256]{3,0,2,1:T(8,128)(2,1)S(1)}, u32[]{:S(2)}, u32[]{:S(2)}) collective-permute-start(bf16[8,1,32,256]{3,0,2,1:T(8,128)(2,1)S(1)} %get-tuple-element.71), channel_id=1, source_target_pairs={{0,16},{16,32},{32,48},{48,64},{64,80},{80,96},{96,112},{1,17},{17... | collective-permute-start | bytes 393224 | tf_op jit(solution)/shard_map/ppermute | solution.py:19
  19.2 1.6 collective-permute-start.17
  23.2 3.0 %collective-permute-start.12 = (bf16[8,18,1,256]{3,0,2,1:T(8,128)(2,1)S(1)}, bf16[8,18,1,256]{3,0,2,1:T(8,128)(2,1)S(1)}, u32[]{:S(2)}, u32[]{:S(2)}) collective-permute-start(bf16[8,18,1,256]{3,0,2,1:T(8,128)(2,1)S(1)} %get-tuple-element.69), channel_id=1, source_target_pairs={{0,2},{2,4},{4,6},{6,8},{8,10},{10,12},{12,14},{1,3},{3,5},{5,7},{... | collective-permute-start | bytes 221192 | tf_op jit(solution)/shard_map/ppermute | solution.py:19
  28.5 6.9 %fusion.46 = f32[256,3,3,256]{0,3,2,1:T(8,128)} fusion(bf16[8,18,34,256]{3,0,2,1:T(8,128)(2,1)S(1)} %pad_maximum_fusion.1, bf16[4,16,32,256]{3,2,1,0:T(8,128)(2,1)S(1)} %copy-done.8), kind=kOutput, calls=%fused_computation.63 | convolution fusion | flops 2415919104 | bytes 4661248 | tf_op jit(solution)/shard_map/conv_general_dilated | solution.py:102
  38.3 3.3 %select_convert_fusion = bf16[16,32,5,256]{3,1,2,0:T(8,128)(2,1)S(1)} fusion(bf16[3,3,256,256]{3,2,1,0:T(8,128)(2,1)S(1)} %copy-done.9, bf16[18,4,8,7,256]{4,1,3,2,0:T(4,128)(2,1)S(1)} %fusion.30, pred[32,5]{0,1:T(8,128)(4,1)S(1)} %copy-done.16), kind=kOutput, calls=%fused_computation.38 | convolution fusion | flops 3021209600 | bytes 4554912 | tf_op jit(solution)/shard_map/conv_general_dilated | solution.py:59
  44.3 3.2 %select_convert_fusion.1 = bf16[16,32,5,256]{3,1,2,0:T(8,128)(2,1)S(1)} fusion(bf16[3,3,256,256]{3,2,1,0:T(8,128)(2,1)S(1)} %copy-done.9, bf16[18,4,8,7,256]{4,1,3,2,0:T(4,128)(2,1)S(1)} %fusion.29, pred[32,5]{0,1:T(8,128)(4,1)S(1)} %copy-done.16), kind=kOutput, calls=%fused_computation.39 | convolution fusion | flops 3021209600 | bytes 4554912 | tf_op jit(solution)/shard_map/conv_general_dilated | solution.py:59
  49.8 2.1 copy.30
  52.0 6.2 %collective-permute-start.18 = (bf16[128,2304]{1,0:T(8,128)(2,1)S(1)}, bf16[128,2304]{1,0:T(8,128)(2,1)}, u32[]{:S(2)}, u32[]{:S(2)}) collective-permute-start(bf16[128,2304]{1,0:T(8,128)(2,1)S(1)} %dynamic-slice_convert_fusion), channel_id=1, source_target_pairs={{0,64},{16,80},{32,96},{48,112},{64,0},{80,16},{96,32},{112,48},{1... | collective-permute-start | bytes 1769480 | tf_op jit(solution)/shard_map/ppermute | solution.py:50
  58.2 110.4 %while.14 = (s32[]{:T(128)}, bf16[20,36,256]{2,0,1:T(8,128)(2,1)S(1)}, bf16[16,32,256]{2,0,1:T(8,128)(2,1)}, f32[3]{0:T(128)S(1)}, bf16[3,3,256,256]{3,2,1,0:T(8...) while((s32[]{:T(128)}, bf16[20,36,256]{2,0,1:T(8,128)(2,1)S(1)}, ...), condition=%wide.region_2.3_spmd, body=%wide.region_0.2_spmd.sunk | while | flops 1609732096 | bytes 19315492 | solution.py:113
  63.5 3.5 %collective-permute-start.3 = (f32[2,32,256]{2,0,1:T(2,128)S(1)}, f32[2,32,256]{2,0,1:T(2,128)S(1)}, u32[]{:S(2)}, u32[]{:S(2)}) collective-permute-start(f32[2,32,256]{2,0,1:T(2,128)S(1)} %slice_bitcast_fusion.11), channel_id=1, source_target_pairs={{16,0},{32,16},{48,32},{64,48},{80,64},{96,80},{112,96},{0,112},{1... | collective-permute-start | bytes 196616 | tf_op jit(solution)/shard_map/while/body/eval_jaxpr/ppermute | solution.py:21
  69.2 2.3 %collective-permute-start.1 = (f32[]{:T(128)}, f32[]{:T(128)}, u32[]{:S(2)}, u32[]{:S(2)}) collective-permute-start(f32[]{:T(128)} %add.180), channel_id=1, source_target_pairs={{0,32},{16,48},{32,0},{48,16},{64,96},{80,112},{96,64},{112,80},{1... | collective-permute-start | bytes 20 | tf_op jit(solution)/shard_map/while/body/eval_jaxpr/ppermute | solution.py:33
  71.5 2.8 %collective-permute-done.1 = f32[]{:T(128)} collective-permute-done((f32[]{:T(128)}, f32[]{:T(128)}, u32[]{:S(2)}, u32[]{:S(2)}) %collective-permute-start.1) | collective-permute-done | bytes 36 | tf_op jit(solution)/shard_map/while/body/eval_jaxpr/ppermute | solution.py:33
  74.9 3.1 %collective-permute-start.2 = (f32[]{:T(128)}, f32[]{:T(128)}, u32[]{:S(2)}, u32[]{:S(2)}) collective-permute-start(f32[]{:T(128)} %add.181), channel_id=1, source_target_pairs={{0,64},{16,80},{32,96},{48,112},{64,0},{80,16},{96,32},{112,48},{1... | collective-permute-start | bytes 20 | tf_op jit(solution)/shard_map/while/body/eval_jaxpr/ppermute | solution.py:33
  78.0 2.1 collective-permute-done.2
  81.4 3.2 %collective-permute-start.7 = (f32[]{:T(128)}, f32[]{:T(128)}, u32[]{:S(2)}, u32[]{:S(2)}) collective-permute-start(f32[]{:T(128)} %add.182), channel_id=1, source_target_pairs={{0,2},{2,0},{4,6},{6,4},{8,10},{10,8},{12,14},{14,12},{1,3},{3,1},... | collective-permute-start | bytes 20 | tf_op jit(solution)/shard_map/while/body/eval_jaxpr/ppermute | solution.py:33
  85.1 2.8 %collective-permute-start.8 = (f32[]{:T(128)}, f32[]{:T(128)}, u32[]{:S(2)}, u32[]{:S(2)}) collective-permute-start(f32[]{:T(128)} %add.183), channel_id=1, source_target_pairs={{0,4},{2,6},{4,0},{6,2},{8,12},{10,14},{12,8},{14,10},{1,5},{3,7},... | collective-permute-start | bytes 20 | tf_op jit(solution)/shard_map/while/body/eval_jaxpr/ppermute | solution.py:33
  89.5 4.1 %collective-permute-start.9 = (f32[]{:T(128)}, f32[]{:T(128)}, u32[]{:S(2)}, u32[]{:S(2)}) collective-permute-start(f32[]{:T(128)} %add.184), channel_id=1, source_target_pairs={{0,8},{2,10},{4,12},{6,14},{8,0},{10,2},{12,4},{14,6},{1,9},{3,11}... | collective-permute-start | bytes 20 | tf_op jit(solution)/shard_map/while/body/eval_jaxpr/ppermute | solution.py:33
  100.5 2.8 %collective-permute-start = (f32[]{:T(128)}, f32[]{:T(128)}, u32[]{:S(2)}, u32[]{:S(2)}) collective-permute-start(f32[]{:T(128)} %multiply_reduce_fusion.3), channel_id=1, source_target_pairs={{0,16},{16,0},{32,48},{48,32},{64,80},{80,64},{96,112},{112,96},{1... | collective-permute-start | bytes 20 | tf_op jit(solution)/shard_map/while/body/eval_jaxpr/ppermute | solution.py:33
  103.5 1.8 collective-permute-start.3
  105.4 1.8 collective-permute-start.4
  108.5 2.3 %collective-permute-start.1 = (f32[]{:T(128)}, f32[]{:T(128)}, u32[]{:S(2)}, u32[]{:S(2)}) collective-permute-start(f32[]{:T(128)} %add.180), channel_id=1, source_target_pairs={{0,32},{16,48},{32,0},{48,16},{64,96},{80,112},{96,64},{112,80},{1... | collective-permute-start | bytes 20 | tf_op jit(solution)/shard_map/while/body/eval_jaxpr/ppermute | solution.py:33
  112.8 3.2 %collective-permute-start.2 = (f32[]{:T(128)}, f32[]{:T(128)}, u32[]{:S(2)}, u32[]{:S(2)}) collective-permute-start(f32[]{:T(128)} %add.181), channel_id=1, source_target_pairs={{0,64},{16,80},{32,96},{48,112},{64,0},{80,16},{96,32},{112,48},{1... | collective-permute-start | bytes 20 | tf_op jit(solution)/shard_map/while/body/eval_jaxpr/ppermute | solution.py:33
  115.9 2.1 collective-permute-done.2
  119.3 2.2 collective-permute-start.7
  122.0 2.7 %collective-permute-start.8 = (f32[]{:T(128)}, f32[]{:T(128)}, u32[]{:S(2)}, u32[]{:S(2)}) collective-permute-start(f32[]{:T(128)} %add.183), channel_id=1, source_target_pairs={{0,4},{2,6},{4,0},{6,2},{8,12},{10,14},{12,8},{14,10},{1,5},{3,7},... | collective-permute-start | bytes 20 | tf_op jit(solution)/shard_map/while/body/eval_jaxpr/ppermute | solution.py:33
  126.3 3.4 %collective-permute-start.9 = (f32[]{:T(128)}, f32[]{:T(128)}, u32[]{:S(2)}, u32[]{:S(2)}) collective-permute-start(f32[]{:T(128)} %add.184), channel_id=1, source_target_pairs={{0,8},{2,10},{4,12},{6,14},{8,0},{10,2},{12,4},{14,6},{1,9},{3,11}... | collective-permute-start | bytes 20 | tf_op jit(solution)/shard_map/while/body/eval_jaxpr/ppermute | solution.py:33
  129.7 1.9 collective-permute-done.9
  138.9 4.0 %collective-permute-start.3 = (f32[2,32,256]{2,0,1:T(2,128)S(1)}, f32[2,32,256]{2,0,1:T(2,128)S(1)}, u32[]{:S(2)}, u32[]{:S(2)}) collective-permute-start(f32[2,32,256]{2,0,1:T(2,128)S(1)} %slice_bitcast_fusion.11), channel_id=1, source_target_pairs={{16,0},{32,16},{48,32},{64,48},{80,64},{96,80},{112,96},{0,112},{1... | collective-permute-start | bytes 196616 | tf_op jit(solution)/shard_map/while/body/eval_jaxpr/ppermute | solution.py:21
  144.3 1.9 collective-permute-start.1
  146.2 1.8 collective-permute-done.1
  148.6 3.5 %collective-permute-start.2 = (f32[]{:T(128)}, f32[]{:T(128)}, u32[]{:S(2)}, u32[]{:S(2)}) collective-permute-start(f32[]{:T(128)} %add.181), channel_id=1, source_target_pairs={{0,64},{16,80},{32,96},{48,112},{64,0},{80,16},{96,32},{112,48},{1... | collective-permute-start | bytes 20 | tf_op jit(solution)/shard_map/while/body/eval_jaxpr/ppermute | solution.py:33
  152.1 1.7 collective-permute-done.2
  155.1 1.9 collective-permute-start.7
  157.5 2.0 collective-permute-start.8
  159.6 1.7 collective-permute-done.8
  161.8 3.2 %collective-permute-start.9 = (f32[]{:T(128)}, f32[]{:T(128)}, u32[]{:S(2)}, u32[]{:S(2)}) collective-permute-start(f32[]{:T(128)} %add.184), channel_id=1, source_target_pairs={{0,8},{2,10},{4,12},{6,14},{8,0},{10,2},{12,4},{14,6},{1,9},{3,11}... | collective-permute-start | bytes 20 | tf_op jit(solution)/shard_map/while/body/eval_jaxpr/ppermute | solution.py:33
  165.0 2.0 collective-permute-done.9
  179.7 2.7 %collective-permute-start.20 = (f32[32,2304]{1,0:T(8,128)S(1)}, f32[32,2304]{1,0:T(8,128)S(1)}, u32[]{:S(2)}, u32[]{:S(2)}) collective-permute-start(f32[32,2304]{1,0:T(8,128)S(1)} %constant_dynamic-slice_fusion.3), channel_id=1, source_target_pairs={{0,16},{16,0},{32,48},{48,32},{64,80},{80,64},{96,112},{112,96},{1... | collective-permute-start | bytes 884744 | tf_op jit(solution)/shard_map/ppermute | solution.py:50
  184.7 4.1 %collective-permute-done.25 = f32[2]{0:T(128)S(1)} collective-permute-done((f32[2]{0:T(128)S(1)}, f32[2]{0:T(128)S(1)}, u32[]{:S(2)}, u32[]{:S(2)}) %collective-permute-start.25) | collective-permute-done | bytes 40 | tf_op jit(solution)/shard_map/ppermute | solution.py:33
  191.2 1.9 collective-permute-start.21
  195.2 3.5 %collective-permute-start.27 = (f32[2]{0:T(128)S(1)}, f32[2]{0:T(128)S(1)}, u32[]{:S(2)}, u32[]{:S(2)}) collective-permute-start(f32[2]{0:T(128)S(1)} %fusion.81), channel_id=1, source_target_pairs={{0,64},{16,80},{32,96},{48,112},{64,0},{80,16},{96,32},{112,48},{1... | collective-permute-start | bytes 32 | tf_op jit(solution)/shard_map/ppermute | solution.py:33
  198.6 1.6 collective-permute-done.27
  202.3 2.6 %collective-permute-done.29 = f32[2]{0:T(128)S(1)} collective-permute-done((f32[2]{0:T(128)S(1)}, f32[2]{0:T(128)S(1)}, u32[]{:S(2)}, u32[]{:S(2)}) %collective-permute-start.29) | collective-permute-done | bytes 40 | tf_op jit(solution)/shard_map/ppermute | solution.py:33
  204.9 1.8 collective-permute-start.30
  206.7 3.2 %collective-permute-done.30 = f32[2]{0:T(128)S(1)} collective-permute-done((f32[2]{0:T(128)S(1)}, f32[2]{0:T(128)S(1)}, u32[]{:S(2)}, u32[]{:S(2)}) %collective-permute-start.30) | collective-permute-done | bytes 40 | tf_op jit(solution)/shard_map/ppermute | solution.py:33
  212.3 2.2 collective-permute-done.22
  (208 shorter events, 67.7 us)
Async XLA Ops:
  2.1 17.0 %collective-permute-start.15 = (bf16[2,32,256]{2,0,1:T(2,128)(2,1)S(1)}, bf16[2,32,256]{2,0,1:T(2,128)(2,1)S(1)}, u32[]{:S(2)}, u32[]{:S(2)}) collective-permute-start(bf16[2,32,256]{2,0,1:T(2,128)(2,1)S(1)} %get-tuple-element.76), channel_id=1, source_target_pairs={{16,0},{32,16},{48,32},{64,48},{80,64},{96,80},{112,96},{0,112},{1... | collective-permute-start | bytes 98312 | tf_op jit(solution)/shard_map/ppermute | solution.py:21
  8.4 10.8 %collective-permute-start.14 = (bf16[2,32,256]{2,0,1:T(2,128)(2,1)S(1)}, bf16[2,32,256]{2,0,1:T(2,128)(2,1)S(1)}, u32[]{:S(2)}, u32[]{:S(2)}) collective-permute-start(bf16[2,32,256]{2,0,1:T(2,128)(2,1)S(1)} %get-tuple-element.75), channel_id=1, source_target_pairs={{0,16},{16,32},{32,48},{48,64},{64,80},{80,96},{96,112},{112,0},{1... | collective-permute-start | bytes 98312 | tf_op jit(solution)/shard_map/ppermute | solution.py:19
  11.5 9.3 %collective-permute-start.11 = (bf16[8,1,32,256]{3,0,2,1:T(8,128)(2,1)S(1)}, bf16[8,1,32,256]{3,0,2,1:T(8,128)(2,1)S(1)}, u32[]{:S(2)}, u32[]{:S(2)}) collective-permute-start(bf16[8,1,32,256]{3,0,2,1:T(8,128)(2,1)S(1)} %get-tuple-element.72), channel_id=1, source_target_pairs={{16,0},{32,16},{48,32},{64,48},{80,64},{96,80},{112,96},{17,1},{33... | collective-permute-start | bytes 393224 | tf_op jit(solution)/shard_map/ppermute | solution.py:21
  12.8 9.0 %collective-permute-start.10 = (bf16[8,1,32,256]{3,0,2,1:T(8,128)(2,1)S(1)}, bf16[8,1,32,256]{3,0,2,1:T(8,128)(2,1)S(1)}, u32[]{:S(2)}, u32[]{:S(2)}) collective-permute-start(bf16[8,1,32,256]{3,0,2,1:T(8,128)(2,1)S(1)} %get-tuple-element.71), channel_id=1, source_target_pairs={{0,16},{16,32},{32,48},{48,64},{64,80},{80,96},{96,112},{1,17},{17... | collective-permute-start | bytes 393224 | tf_op jit(solution)/shard_map/ppermute | solution.py:19
  19.2 7.1 %collective-permute-start.17 = (bf16[20,2,256]{2,0,1:T(8,128)(2,1)S(1)}, bf16[20,2,256]{2,0,1:T(8,128)(2,1)S(1)}, u32[]{:S(2)}, u32[]{:S(2)}) collective-permute-start(bf16[20,2,256]{2,0,1:T(8,128)(2,1)S(1)} %get-tuple-element.74), channel_id=1, source_target_pairs={{2,0},{4,2},{6,4},{8,6},{10,8},{12,10},{14,12},{0,14},{3,1},{5,3},... | collective-permute-start | bytes 61448 | tf_op jit(solution)/shard_map/ppermute | solution.py:21
  20.8 5.5 %collective-permute-start.16 = (bf16[20,2,256]{2,0,1:T(8,128)(2,1)S(1)}, bf16[20,2,256]{2,0,1:T(8,128)(2,1)S(1)}, u32[]{:S(2)}, u32[]{:S(2)}) collective-permute-start(bf16[20,2,256]{2,0,1:T(8,128)(2,1)S(1)} %get-tuple-element.73), channel_id=1, source_target_pairs={{0,2},{2,4},{4,6},{6,8},{8,10},{10,12},{12,14},{14,0},{1,3},{3,5},... | collective-permute-start | bytes 61448 | tf_op jit(solution)/shard_map/ppermute | solution.py:19
  21.9 5.4 %collective-permute-start.13 = (bf16[8,18,1,256]{3,0,2,1:T(8,128)(2,1)S(1)}, bf16[8,18,1,256]{3,0,2,1:T(8,128)(2,1)S(1)}, u32[]{:S(2)}, u32[]{:S(2)}) collective-permute-start(bf16[8,18,1,256]{3,0,2,1:T(8,128)(2,1)S(1)} %get-tuple-element.70), channel_id=1, source_target_pairs={{2,0},{4,2},{6,4},{8,6},{10,8},{12,10},{14,12},{3,1},{5,3},{7,5},{... | collective-permute-start | bytes 221192 | tf_op jit(solution)/shard_map/ppermute | solution.py:21
  23.2 4.1 %collective-permute-start.12 = (bf16[8,18,1,256]{3,0,2,1:T(8,128)(2,1)S(1)}, bf16[8,18,1,256]{3,0,2,1:T(8,128)(2,1)S(1)}, u32[]{:S(2)}, u32[]{:S(2)}) collective-permute-start(bf16[8,18,1,256]{3,0,2,1:T(8,128)(2,1)S(1)} %get-tuple-element.69), channel_id=1, source_target_pairs={{0,2},{2,4},{4,6},{6,8},{8,10},{10,12},{12,14},{1,3},{3,5},{5,7},{... | collective-permute-start | bytes 221192 | tf_op jit(solution)/shard_map/ppermute | solution.py:19
  52.0 119.0 %collective-permute-start.18 = (bf16[128,2304]{1,0:T(8,128)(2,1)S(1)}, bf16[128,2304]{1,0:T(8,128)(2,1)}, u32[]{:S(2)}, u32[]{:S(2)}) collective-permute-start(bf16[128,2304]{1,0:T(8,128)(2,1)S(1)} %dynamic-slice_convert_fusion), channel_id=1, source_target_pairs={{0,64},{16,80},{32,96},{48,112},{64,0},{80,16},{96,32},{112,48},{1... | collective-permute-start | bytes 1769480 | tf_op jit(solution)/shard_map/ppermute | solution.py:50
  62.7 5.3 %collective-permute-start = (f32[]{:T(128)}, f32[]{:T(128)}, u32[]{:S(2)}, u32[]{:S(2)}) collective-permute-start(f32[]{:T(128)} %multiply_reduce_fusion.3), channel_id=1, source_target_pairs={{0,16},{16,0},{32,48},{48,32},{64,80},{80,64},{96,112},{112,96},{1... | collective-permute-start | bytes 20 | tf_op jit(solution)/shard_map/while/body/eval_jaxpr/ppermute | solution.py:33
  63.5 17.2 %collective-permute-start.3 = (f32[2,32,256]{2,0,1:T(2,128)S(1)}, f32[2,32,256]{2,0,1:T(2,128)S(1)}, u32[]{:S(2)}, u32[]{:S(2)}) collective-permute-start(f32[2,32,256]{2,0,1:T(2,128)S(1)} %slice_bitcast_fusion.11), channel_id=1, source_target_pairs={{16,0},{32,16},{48,32},{64,48},{80,64},{96,80},{112,96},{0,112},{1... | collective-permute-start | bytes 196616 | tf_op jit(solution)/shard_map/while/body/eval_jaxpr/ppermute | solution.py:21
  67.1 13.6 %collective-permute-start.4 = (f32[2,32,256]{2,0,1:T(2,128)S(1)}, f32[2,32,256]{2,0,1:T(2,128)S(1)}, u32[]{:S(2)}, u32[]{:S(2)}) collective-permute-start(f32[2,32,256]{2,0,1:T(2,128)S(1)} %slice_bitcast_fusion.13), channel_id=1, source_target_pairs={{0,16},{16,32},{32,48},{48,64},{64,80},{80,96},{96,112},{112,0},{1... | collective-permute-start | bytes 196616 | tf_op jit(solution)/shard_map/while/body/eval_jaxpr/ppermute | solution.py:19
  69.2 5.1 %collective-permute-start.1 = (f32[]{:T(128)}, f32[]{:T(128)}, u32[]{:S(2)}, u32[]{:S(2)}) collective-permute-start(f32[]{:T(128)} %add.180), channel_id=1, source_target_pairs={{0,32},{16,48},{32,0},{48,16},{64,96},{80,112},{96,64},{112,80},{1... | collective-permute-start | bytes 20 | tf_op jit(solution)/shard_map/while/body/eval_jaxpr/ppermute | solution.py:33
  74.9 5.2 %collective-permute-start.2 = (f32[]{:T(128)}, f32[]{:T(128)}, u32[]{:S(2)}, u32[]{:S(2)}) collective-permute-start(f32[]{:T(128)} %add.181), channel_id=1, source_target_pairs={{0,64},{16,80},{32,96},{48,112},{64,0},{80,16},{96,32},{112,48},{1... | collective-permute-start | bytes 20 | tf_op jit(solution)/shard_map/while/body/eval_jaxpr/ppermute | solution.py:33
  80.8 15.3 %collective-permute-start.5 = (f32[20,2,256]{2,0,1:T(8,128)S(1)}, f32[20,2,256]{2,0,1:T(8,128)S(1)}, u32[]{:S(2)}, u32[]{:S(2)}) collective-permute-start(f32[20,2,256]{2,0,1:T(8,128)S(1)} %get-tuple-element.121), channel_id=1, source_target_pairs={{2,0},{4,2},{6,4},{8,6},{10,8},{12,10},{14,12},{0,14},{3,1},{5,3},... | collective-permute-start | bytes 122888 | tf_op jit(solution)/shard_map/while/body/eval_jaxpr/ppermute | solution.py:21
  80.9 15.3 %collective-permute-start.6 = (f32[20,2,256]{2,0,1:T(8,128)S(1)}, f32[20,2,256]{2,0,1:T(8,128)S(1)}, u32[]{:S(2)}, u32[]{:S(2)}) collective-permute-start(f32[20,2,256]{2,0,1:T(8,128)S(1)} %get-tuple-element.122), channel_id=1, source_target_pairs={{0,2},{2,4},{4,6},{6,8},{8,10},{10,12},{12,14},{14,0},{1,3},{3,5},... | collective-permute-start | bytes 122888 | tf_op jit(solution)/shard_map/while/body/eval_jaxpr/ppermute | solution.py:19
  81.4 3.2 %collective-permute-start.7 = (f32[]{:T(128)}, f32[]{:T(128)}, u32[]{:S(2)}, u32[]{:S(2)}) collective-permute-start(f32[]{:T(128)} %add.182), channel_id=1, source_target_pairs={{0,2},{2,0},{4,6},{6,4},{8,10},{10,8},{12,14},{14,12},{1,3},{3,1},... | collective-permute-start | bytes 20 | tf_op jit(solution)/shard_map/while/body/eval_jaxpr/ppermute | solution.py:33
  85.1 3.7 %collective-permute-start.8 = (f32[]{:T(128)}, f32[]{:T(128)}, u32[]{:S(2)}, u32[]{:S(2)}) collective-permute-start(f32[]{:T(128)} %add.183), channel_id=1, source_target_pairs={{0,4},{2,6},{4,0},{6,2},{8,12},{10,14},{12,8},{14,10},{1,5},{3,7},... | collective-permute-start | bytes 20 | tf_op jit(solution)/shard_map/while/body/eval_jaxpr/ppermute | solution.py:33
  89.5 5.2 %collective-permute-start.9 = (f32[]{:T(128)}, f32[]{:T(128)}, u32[]{:S(2)}, u32[]{:S(2)}) collective-permute-start(f32[]{:T(128)} %add.184), channel_id=1, source_target_pairs={{0,8},{2,10},{4,12},{6,14},{8,0},{10,2},{12,4},{14,6},{1,9},{3,11}... | collective-permute-start | bytes 20 | tf_op jit(solution)/shard_map/while/body/eval_jaxpr/ppermute | solution.py:33
  100.5 6.7 %collective-permute-start = (f32[]{:T(128)}, f32[]{:T(128)}, u32[]{:S(2)}, u32[]{:S(2)}) collective-permute-start(f32[]{:T(128)} %multiply_reduce_fusion.3), channel_id=1, source_target_pairs={{0,16},{16,0},{32,48},{48,32},{64,80},{80,64},{96,112},{112,96},{1... | collective-permute-start | bytes 20 | tf_op jit(solution)/shard_map/while/body/eval_jaxpr/ppermute | solution.py:33
  103.5 15.1 %collective-permute-start.3 = (f32[2,32,256]{2,0,1:T(2,128)S(1)}, f32[2,32,256]{2,0,1:T(2,128)S(1)}, u32[]{:S(2)}, u32[]{:S(2)}) collective-permute-start(f32[2,32,256]{2,0,1:T(2,128)S(1)} %slice_bitcast_fusion.11), channel_id=1, source_target_pairs={{16,0},{32,16},{48,32},{64,48},{80,64},{96,80},{112,96},{0,112},{1... | collective-permute-start | bytes 196616 | tf_op jit(solution)/shard_map/while/body/eval_jaxpr/ppermute | solution.py:21
  105.4 13.2 %collective-permute-start.4 = (f32[2,32,256]{2,0,1:T(2,128)S(1)}, f32[2,32,256]{2,0,1:T(2,128)S(1)}, u32[]{:S(2)}, u32[]{:S(2)}) collective-permute-start(f32[2,32,256]{2,0,1:T(2,128)S(1)} %slice_bitcast_fusion.13), channel_id=1, source_target_pairs={{0,16},{16,32},{32,48},{48,64},{64,80},{80,96},{96,112},{112,0},{1... | collective-permute-start | bytes 196616 | tf_op jit(solution)/shard_map/while/body/eval_jaxpr/ppermute | solution.py:19
  108.5 3.7 %collective-permute-start.1 = (f32[]{:T(128)}, f32[]{:T(128)}, u32[]{:S(2)}, u32[]{:S(2)}) collective-permute-start(f32[]{:T(128)} %add.180), channel_id=1, source_target_pairs={{0,32},{16,48},{32,0},{48,16},{64,96},{80,112},{96,64},{112,80},{1... | collective-permute-start | bytes 20 | tf_op jit(solution)/shard_map/while/body/eval_jaxpr/ppermute | solution.py:33
  112.8 5.2 %collective-permute-start.2 = (f32[]{:T(128)}, f32[]{:T(128)}, u32[]{:S(2)}, u32[]{:S(2)}) collective-permute-start(f32[]{:T(128)} %add.181), channel_id=1, source_target_pairs={{0,64},{16,80},{32,96},{48,112},{64,0},{80,16},{96,32},{112,48},{1... | collective-permute-start | bytes 20 | tf_op jit(solution)/shard_map/while/body/eval_jaxpr/ppermute | solution.py:33
  118.7 14.3 %collective-permute-start.5 = (f32[20,2,256]{2,0,1:T(8,128)S(1)}, f32[20,2,256]{2,0,1:T(8,128)S(1)}, u32[]{:S(2)}, u32[]{:S(2)}) collective-permute-start(f32[20,2,256]{2,0,1:T(8,128)S(1)} %get-tuple-element.121), channel_id=1, source_target_pairs={{2,0},{4,2},{6,4},{8,6},{10,8},{12,10},{14,12},{0,14},{3,1},{5,3},... | collective-permute-start | bytes 122888 | tf_op jit(solution)/shard_map/while/body/eval_jaxpr/ppermute | solution.py:21
  118.8 14.2 %collective-permute-start.6 = (f32[20,2,256]{2,0,1:T(8,128)S(1)}, f32[20,2,256]{2,0,1:T(8,128)S(1)}, u32[]{:S(2)}, u32[]{:S(2)}) collective-permute-start(f32[20,2,256]{2,0,1:T(8,128)S(1)} %get-tuple-element.122), channel_id=1, source_target_pairs={{0,2},{2,4},{4,6},{6,8},{8,10},{10,12},{12,14},{14,0},{1,3},{3,5},... | collective-permute-start | bytes 122888 | tf_op jit(solution)/shard_map/while/body/eval_jaxpr/ppermute | solution.py:19
  119.3 2.2 collective-permute-start.7
  122.0 3.7 %collective-permute-start.8 = (f32[]{:T(128)}, f32[]{:T(128)}, u32[]{:S(2)}, u32[]{:S(2)}) collective-permute-start(f32[]{:T(128)} %add.183), channel_id=1, source_target_pairs={{0,4},{2,6},{4,0},{6,2},{8,12},{10,14},{12,8},{14,10},{1,5},{3,7},... | collective-permute-start | bytes 20 | tf_op jit(solution)/shard_map/while/body/eval_jaxpr/ppermute | solution.py:33
  126.3 5.2 %collective-permute-start.9 = (f32[]{:T(128)}, f32[]{:T(128)}, u32[]{:S(2)}, u32[]{:S(2)}) collective-permute-start(f32[]{:T(128)} %add.184), channel_id=1, source_target_pairs={{0,8},{2,10},{4,12},{6,14},{8,0},{10,2},{12,4},{14,6},{1,9},{3,11}... | collective-permute-start | bytes 20 | tf_op jit(solution)/shard_map/while/body/eval_jaxpr/ppermute | solution.py:33
  137.4 5.7 %collective-permute-start = (f32[]{:T(128)}, f32[]{:T(128)}, u32[]{:S(2)}, u32[]{:S(2)}) collective-permute-start(f32[]{:T(128)} %multiply_reduce_fusion.3), channel_id=1, source_target_pairs={{0,16},{16,0},{32,48},{48,32},{64,80},{80,64},{96,112},{112,96},{1... | collective-permute-start | bytes 20 | tf_op jit(solution)/shard_map/while/body/eval_jaxpr/ppermute | solution.py:33
  138.9 15.5 %collective-permute-start.3 = (f32[2,32,256]{2,0,1:T(2,128)S(1)}, f32[2,32,256]{2,0,1:T(2,128)S(1)}, u32[]{:S(2)}, u32[]{:S(2)}) collective-permute-start(f32[2,32,256]{2,0,1:T(2,128)S(1)} %slice_bitcast_fusion.11), channel_id=1, source_target_pairs={{16,0},{32,16},{48,32},{64,48},{80,64},{96,80},{112,96},{0,112},{1... | collective-permute-start | bytes 196616 | tf_op jit(solution)/shard_map/while/body/eval_jaxpr/ppermute | solution.py:21
  142.9 11.5 %collective-permute-start.4 = (f32[2,32,256]{2,0,1:T(2,128)S(1)}, f32[2,32,256]{2,0,1:T(2,128)S(1)}, u32[]{:S(2)}, u32[]{:S(2)}) collective-permute-start(f32[2,32,256]{2,0,1:T(2,128)S(1)} %slice_bitcast_fusion.13), channel_id=1, source_target_pairs={{0,16},{16,32},{32,48},{48,64},{64,80},{80,96},{96,112},{112,0},{1... | collective-permute-start | bytes 196616 | tf_op jit(solution)/shard_map/while/body/eval_jaxpr/ppermute | solution.py:19
  144.3 3.7 %collective-permute-start.1 = (f32[]{:T(128)}, f32[]{:T(128)}, u32[]{:S(2)}, u32[]{:S(2)}) collective-permute-start(f32[]{:T(128)} %add.180), channel_id=1, source_target_pairs={{0,32},{16,48},{32,0},{48,16},{64,96},{80,112},{96,64},{112,80},{1... | collective-permute-start | bytes 20 | tf_op jit(solution)/shard_map/while/body/eval_jaxpr/ppermute | solution.py:33
  148.6 5.2 %collective-permute-start.2 = (f32[]{:T(128)}, f32[]{:T(128)}, u32[]{:S(2)}, u32[]{:S(2)}) collective-permute-start(f32[]{:T(128)} %add.181), channel_id=1, source_target_pairs={{0,64},{16,80},{32,96},{48,112},{64,0},{80,16},{96,32},{112,48},{1... | collective-permute-start | bytes 20 | tf_op jit(solution)/shard_map/while/body/eval_jaxpr/ppermute | solution.py:33
  154.6 14.0 %collective-permute-start.5 = (f32[20,2,256]{2,0,1:T(8,128)S(1)}, f32[20,2,256]{2,0,1:T(8,128)S(1)}, u32[]{:S(2)}, u32[]{:S(2)}) collective-permute-start(f32[20,2,256]{2,0,1:T(8,128)S(1)} %get-tuple-element.121), channel_id=1, source_target_pairs={{2,0},{4,2},{6,4},{8,6},{10,8},{12,10},{14,12},{0,14},{3,1},{5,3},... | collective-permute-start | bytes 122888 | tf_op jit(solution)/shard_map/while/body/eval_jaxpr/ppermute | solution.py:21
  154.6 14.0 %collective-permute-start.6 = (f32[20,2,256]{2,0,1:T(8,128)S(1)}, f32[20,2,256]{2,0,1:T(8,128)S(1)}, u32[]{:S(2)}, u32[]{:S(2)}) collective-permute-start(f32[20,2,256]{2,0,1:T(8,128)S(1)} %get-tuple-element.122), channel_id=1, source_target_pairs={{0,2},{2,4},{4,6},{6,8},{8,10},{10,12},{12,14},{14,0},{1,3},{3,5},... | collective-permute-start | bytes 122888 | tf_op jit(solution)/shard_map/while/body/eval_jaxpr/ppermute | solution.py:19
  157.5 3.7 %collective-permute-start.8 = (f32[]{:T(128)}, f32[]{:T(128)}, u32[]{:S(2)}, u32[]{:S(2)}) collective-permute-start(f32[]{:T(128)} %add.183), channel_id=1, source_target_pairs={{0,4},{2,6},{4,0},{6,2},{8,12},{10,14},{12,8},{14,10},{1,5},{3,7},... | collective-permute-start | bytes 20 | tf_op jit(solution)/shard_map/while/body/eval_jaxpr/ppermute | solution.py:33
  161.8 5.2 %collective-permute-start.9 = (f32[]{:T(128)}, f32[]{:T(128)}, u32[]{:S(2)}, u32[]{:S(2)}) collective-permute-start(f32[]{:T(128)} %add.184), channel_id=1, source_target_pairs={{0,8},{2,10},{4,12},{6,14},{8,0},{10,2},{12,4},{14,6},{1,9},{3,11}... | collective-permute-start | bytes 20 | tf_op jit(solution)/shard_map/while/body/eval_jaxpr/ppermute | solution.py:33
  172.8 6.8 %collective-permute-start.19 = (bf16[64,2304]{1,0:T(8,128)(2,1)S(1)}, bf16[64,2304]{1,0:T(8,128)(2,1)S(1)}, u32[]{:S(2)}, u32[]{:S(2)}) collective-permute-start(bf16[64,2304]{1,0:T(8,128)(2,1)S(1)} %dynamic-slice_convert_fusion.1), channel_id=1, source_target_pairs={{0,32},{16,48},{32,0},{48,16},{64,96},{80,112},{96,64},{112,80},{1... | collective-permute-start | bytes 884744 | tf_op jit(solution)/shard_map/ppermute | solution.py:50
  179.7 11.4 %collective-permute-start.20 = (f32[32,2304]{1,0:T(8,128)S(1)}, f32[32,2304]{1,0:T(8,128)S(1)}, u32[]{:S(2)}, u32[]{:S(2)}) collective-permute-start(f32[32,2304]{1,0:T(8,128)S(1)} %constant_dynamic-slice_fusion.3), channel_id=1, source_target_pairs={{0,16},{16,0},{32,48},{48,32},{64,80},{80,64},{96,112},{112,96},{1... | collective-permute-start | bytes 884744 | tf_op jit(solution)/shard_map/ppermute | solution.py:50
  183.8 5.1 %collective-permute-start.25 = (f32[2]{0:T(128)S(1)}, f32[2]{0:T(128)S(1)}, u32[]{:S(2)}, u32[]{:S(2)}) collective-permute-start(f32[2]{0:T(128)S(1)} %pad_maximum_fusion.12), channel_id=1, source_target_pairs={{0,16},{16,0},{32,48},{48,32},{64,80},{80,64},{96,112},{112,96},{1... | collective-permute-start | bytes 32 | tf_op jit(solution)/shard_map/ppermute | solution.py:33
  190.2 3.6 %collective-permute-start.26 = (f32[2]{0:T(128)S(1)}, f32[2]{0:T(128)S(1)}, u32[]{:S(2)}, u32[]{:S(2)}) collective-permute-start(f32[2]{0:T(128)S(1)} %fusion.80), channel_id=1, source_target_pairs={{0,32},{16,48},{32,0},{48,16},{64,96},{80,112},{96,64},{112,80},{1... | collective-permute-start | bytes 32 | tf_op jit(solution)/shard_map/ppermute | solution.py:33
  191.2 18.7 %collective-permute-start.21 = (f32[16,2304]{1,0:T(8,128)S(1)}, f32[16,2304]{1,0:T(8,128)S(1)}, u32[]{:S(2)}, u32[]{:S(2)}) collective-permute-start(f32[16,2304]{1,0:T(8,128)S(1)} %constant_dynamic-slice_fusion.2), channel_id=1, source_target_pairs={{0,8},{2,10},{4,12},{6,14},{8,0},{10,2},{12,4},{14,6},{1,9},{3,11}... | collective-permute-start | bytes 442376 | tf_op jit(solution)/shard_map/ppermute | solution.py:50
  195.2 5.1 %collective-permute-start.27 = (f32[2]{0:T(128)S(1)}, f32[2]{0:T(128)S(1)}, u32[]{:S(2)}, u32[]{:S(2)}) collective-permute-start(f32[2]{0:T(128)S(1)} %fusion.81), channel_id=1, source_target_pairs={{0,64},{16,80},{32,96},{48,112},{64,0},{80,16},{96,32},{112,48},{1... | collective-permute-start | bytes 32 | tf_op jit(solution)/shard_map/ppermute | solution.py:33
  201.4 3.5 %collective-permute-start.29 = (f32[2]{0:T(128)S(1)}, f32[2]{0:T(128)S(1)}, u32[]{:S(2)}, u32[]{:S(2)}) collective-permute-start(f32[2]{0:T(128)S(1)} %add.156), channel_id=1, source_target_pairs={{0,4},{2,6},{4,0},{6,2},{8,12},{10,14},{12,8},{14,10},{1,5},{3,7},... | collective-permute-start | bytes 32 | tf_op jit(solution)/shard_map/ppermute | solution.py:33
  204.9 5.0 %collective-permute-start.30 = (f32[2]{0:T(128)S(1)}, f32[2]{0:T(128)S(1)}, u32[]{:S(2)}, u32[]{:S(2)}) collective-permute-start(f32[2]{0:T(128)S(1)} %add.157), channel_id=1, source_target_pairs={{0,8},{2,10},{4,12},{6,14},{8,0},{10,2},{12,4},{14,6},{1,9},{3,11}... | collective-permute-start | bytes 32 | tf_op jit(solution)/shard_map/ppermute | solution.py:33
  210.0 4.4 %collective-permute-start.22 = (f32[8,2304]{1,0:T(8,128)S(1)}, f32[8,2304]{1,0:T(8,128)S(1)}, u32[]{:S(2)}, u32[]{:S(2)}) collective-permute-start(f32[8,2304]{1,0:T(8,128)S(1)} %constant_dynamic-slice_fusion.1), channel_id=1, source_target_pairs={{0,4},{2,6},{4,0},{6,2},{8,12},{10,14},{12,8},{14,10},{1,5},{3,7},... | collective-permute-start | bytes 221192 | tf_op jit(solution)/shard_map/ppermute | solution.py:50
  215.8 4.0 %collective-permute-start.24 = (f32[4,2304]{1,0:T(4,128)S(1)}, f32[4,2304]{1,0:T(4,128)S(1)}, u32[]{:S(2)}, u32[]{:S(2)}) collective-permute-start(f32[4,2304]{1,0:T(4,128)S(1)} %dynamic-slice_add_fusion.3), channel_id=1, source_target_pairs={{0,1},{1,0},{2,3},{3,2},{4,5},{5,4},{6,7},{7,6},{8,9},{9,8},{10,11... | collective-permute-start | bytes 110600 | tf_op jit(solution)/shard_map/ppermute | solution.py:33
  (22 other events, 93.6 us)

commit v9 on v8

--- a/solution.py
+++ b/solution.py
@@ -45,7 +45,7 @@
             upper = (index // step) % 2
             keep = lax.dynamic_slice_in_dim(value, upper * half, half, axis=0)
             send = lax.dynamic_slice_in_dim(value, (1 - upper) * half, half, axis=0)
-            if send.size * 8 > 256 * 2304:
+            if send.size * 32 > 256 * 2304:
                 send = send.astype(jnp.bfloat16)
             received = lax.ppermute(send, axis, [(i, i ^ step) for i in range(count)])
             value = keep + received.astype(jnp.float32)

time: 223 us -> 221 us (level)
  waiting for transfers between devices: 40.6 us -> 37.8 us
    ppermute x25, waiting for transfers between devices: 35.3 us -> 31.8 us  [butterfly_sum(): lax.ppermute(value, axis, [(i, i ^ step) for i in range(count)])]
    ppermute x25, starting transfers between devices: 55.6 us -> 58.9 us  [butterfly_sum(): lax.ppermute(value, axis, [(i, i ^ step) for i in range(count)])]
  transfers between devices with their start and end apart: 51 -> 51, of which waited for: 24 -> 23; matrix products, arithmetic and copies ran while one was open for 13% -> 13% of each run, Pallas kernels for 0% -> 0%
where the time goes in v9:
time: 221 us; the launch traced here: 220 us
  starting transfers between devices  102 us (46%)
  waiting for transfers between devices  37.8 us (17%)
  local copies, waits for them, and re-layouts  24.1 us (11%)
  matrix products  22.1 us (10%)
  other arithmetic  16.5 us (7%)
  loops' own time  13.2 us (6%)
  between operations  4.58 us (2%)
    ppermute x25, starting transfers between devices, butterfly_sum(): lax.ppermute(value, axis, [(i, i ^ step) for i in range(count)])  58.9 us
    ppermute x25, waiting for transfers between devices, butterfly_sum(): lax.ppermute(value, axis, [(i, i ^ step) for i in range(count)])  31.8 us
    ppermute x10, starting transfers between devices, extended(): lax.ppermute(head, axis, [((i + 1) % count, i) for i in range(ends)])  19.8 us
    conv_general_dilated x10, matrix products, conv(): lax.conv_general_dilated(padded, weights, window_strides=(1, 1), padding=...  15.2 us
    another operation x1, loops' own time, per_device(): lax.scan(power_step, (padded_probe, iterate), None, length=ITERS - 1)  13.2 us
    ppermute x10, starting transfers between devices, extended(): lax.ppermute(tail, axis, [(i, (i + 1) % count) for i in range(ends)])  12.6 us
    ppermute x6, starting transfers between devices, halving_scatter(): received = lax.ppermute(send, axis, [(i, i ^ step) for i in range(count)])  10.4 us
    unnamed x38, local copies, waits for them, and re-layouts  9.89 us
  transfers between devices with their start and end apart: 51, of which 23 were waited for; matrix products, arithmetic and copies ran while one was open for 13% of the time, Pallas kernels for 0%

profile of v9, /device:TPU:0, one launch (start us, length us, event | category | flops | bytes accessed | tf_op | source)
XLA Modules:
  0.0 220.0 jit_solution(3383929386946188674)
XLA Ops:
  2.1 6.2 %collective-permute-start.15 = (bf16[2,32,256]{2,0,1:T(2,128)(2,1)S(1)}, bf16[2,32,256]{2,0,1:T(2,128)(2,1)S(1)}, u32[]{:S(2)}, u32[]{:S(2)}) collective-permute-start(bf16[2,32,256]{2,0,1:T(2,128)(2,1)S(1)} %get-tuple-element.76), channel_id=1, source_target_pairs={{16,0},{32,16},{48,32},{64,48},{80,64},{96,80},{112,96},{0,112},{1... | collective-permute-start | bytes 98312 | tf_op jit(solution)/shard_map/ppermute | solution.py:21
  8.4 2.1 copy.23
  12.8 6.1 %collective-permute-start.10 = (bf16[8,1,32,256]{3,0,2,1:T(8,128)(2,1)S(1)}, bf16[8,1,32,256]{3,0,2,1:T(8,128)(2,1)S(1)}, u32[]{:S(2)}, u32[]{:S(2)}) collective-permute-start(bf16[8,1,32,256]{3,0,2,1:T(8,128)(2,1)S(1)} %get-tuple-element.71), channel_id=1, source_target_pairs={{0,16},{16,32},{32,48},{48,64},{64,80},{80,96},{96,112},{1,17},{17... | collective-permute-start | bytes 393224 | tf_op jit(solution)/shard_map/ppermute | solution.py:19
  19.2 1.6 collective-permute-start.17
  23.2 3.0 %collective-permute-start.12 = (bf16[8,18,1,256]{3,0,2,1:T(8,128)(2,1)S(1)}, bf16[8,18,1,256]{3,0,2,1:T(8,128)(2,1)S(1)}, u32[]{:S(2)}, u32[]{:S(2)}) collective-permute-start(bf16[8,18,1,256]{3,0,2,1:T(8,128)(2,1)S(1)} %get-tuple-element.69), channel_id=1, source_target_pairs={{0,2},{2,4},{4,6},{6,8},{8,10},{10,12},{12,14},{1,3},{3,5},{5,7},{... | collective-permute-start | bytes 221192 | tf_op jit(solution)/shard_map/ppermute | solution.py:19
  28.5 6.9 %fusion.46 = f32[256,3,3,256]{0,3,2,1:T(8,128)} fusion(bf16[8,18,34,256]{3,0,2,1:T(8,128)(2,1)S(1)} %pad_maximum_fusion.1, bf16[4,16,32,256]{3,2,1,0:T(8,128)(2,1)S(1)} %copy-done.8), kind=kOutput, calls=%fused_computation.63 | convolution fusion | flops 2415919104 | bytes 4661248 | tf_op jit(solution)/shard_map/conv_general_dilated | solution.py:102
  38.3 3.3 %select_convert_fusion = bf16[16,32,5,256]{3,1,2,0:T(8,128)(2,1)S(1)} fusion(bf16[3,3,256,256]{3,2,1,0:T(8,128)(2,1)S(1)} %copy-done.9, bf16[18,4,8,7,256]{4,1,3,2,0:T(4,128)(2,1)S(1)} %fusion.30, pred[32,5]{0,1:T(8,128)(4,1)S(1)} %copy-done.16), kind=kOutput, calls=%fused_computation.38 | convolution fusion | flops 3021209600 | bytes 4554912 | tf_op jit(solution)/shard_map/conv_general_dilated | solution.py:59
  44.3 3.2 %select_convert_fusion.1 = bf16[16,32,5,256]{3,1,2,0:T(8,128)(2,1)S(1)} fusion(bf16[3,3,256,256]{3,2,1,0:T(8,128)(2,1)S(1)} %copy-done.9, bf16[18,4,8,7,256]{4,1,3,2,0:T(4,128)(2,1)S(1)} %fusion.29, pred[32,5]{0,1:T(8,128)(4,1)S(1)} %copy-done.16), kind=kOutput, calls=%fused_computation.39 | convolution fusion | flops 3021209600 | bytes 4554912 | tf_op jit(solution)/shard_map/conv_general_dilated | solution.py:59
  49.8 2.1 copy.30
  52.0 6.2 %collective-permute-start.18 = (bf16[128,2304]{1,0:T(8,128)(2,1)S(1)}, bf16[128,2304]{1,0:T(8,128)(2,1)}, u32[]{:S(2)}, u32[]{:S(2)}) collective-permute-start(bf16[128,2304]{1,0:T(8,128)(2,1)S(1)} %dynamic-slice_convert_fusion), channel_id=1, source_target_pairs={{0,64},{16,80},{32,96},{48,112},{64,0},{80,16},{96,32},{112,48},{1... | collective-permute-start | bytes 1769480 | tf_op jit(solution)/shard_map/ppermute | solution.py:50
  58.2 110.4 %while.14 = (s32[]{:T(128)}, bf16[20,36,256]{2,0,1:T(8,128)(2,1)S(1)}, bf16[16,32,256]{2,0,1:T(8,128)(2,1)}, f32[3]{0:T(128)S(1)}, bf16[3,3,256,256]{3,2,1,0:T(8...) while((s32[]{:T(128)}, bf16[20,36,256]{2,0,1:T(8,128)(2,1)S(1)}, ...), condition=%wide.region_2.3_spmd, body=%wide.region_0.2_spmd.sunk | while | flops 1609732096 | bytes 19315492 | solution.py:113
  63.5 3.5 %collective-permute-start.3 = (f32[2,32,256]{2,0,1:T(2,128)S(1)}, f32[2,32,256]{2,0,1:T(2,128)S(1)}, u32[]{:S(2)}, u32[]{:S(2)}) collective-permute-start(f32[2,32,256]{2,0,1:T(2,128)S(1)} %slice_bitcast_fusion.11), channel_id=1, source_target_pairs={{16,0},{32,16},{48,32},{64,48},{80,64},{96,80},{112,96},{0,112},{1... | collective-permute-start | bytes 196616 | tf_op jit(solution)/shard_map/while/body/eval_jaxpr/ppermute | solution.py:21
  69.2 2.3 %collective-permute-start.1 = (f32[]{:T(128)}, f32[]{:T(128)}, u32[]{:S(2)}, u32[]{:S(2)}) collective-permute-start(f32[]{:T(128)} %add.180), channel_id=1, source_target_pairs={{0,32},{16,48},{32,0},{48,16},{64,96},{80,112},{96,64},{112,80},{1... | collective-permute-start | bytes 20 | tf_op jit(solution)/shard_map/while/body/eval_jaxpr/ppermute | solution.py:33
  71.5 2.8 %collective-permute-done.1 = f32[]{:T(128)} collective-permute-done((f32[]{:T(128)}, f32[]{:T(128)}, u32[]{:S(2)}, u32[]{:S(2)}) %collective-permute-start.1) | collective-permute-done | bytes 36 | tf_op jit(solution)/shard_map/while/body/eval_jaxpr/ppermute | solution.py:33
  74.9 3.1 %collective-permute-start.2 = (f32[]{:T(128)}, f32[]{:T(128)}, u32[]{:S(2)}, u32[]{:S(2)}) collective-permute-start(f32[]{:T(128)} %add.181), channel_id=1, source_target_pairs={{0,64},{16,80},{32,96},{48,112},{64,0},{80,16},{96,32},{112,48},{1... | collective-permute-start | bytes 20 | tf_op jit(solution)/shard_map/while/body/eval_jaxpr/ppermute | solution.py:33
  78.0 2.1 collective-permute-done.2
  81.4 3.2 %collective-permute-start.7 = (f32[]{:T(128)}, f32[]{:T(128)}, u32[]{:S(2)}, u32[]{:S(2)}) collective-permute-start(f32[]{:T(128)} %add.182), channel_id=1, source_target_pairs={{0,2},{2,0},{4,6},{6,4},{8,10},{10,8},{12,14},{14,12},{1,3},{3,1},... | collective-permute-start | bytes 20 | tf_op jit(solution)/shard_map/while/body/eval_jaxpr/ppermute | solution.py:33
  85.1 2.8 %collective-permute-start.8 = (f32[]{:T(128)}, f32[]{:T(128)}, u32[]{:S(2)}, u32[]{:S(2)}) collective-permute-start(f32[]{:T(128)} %add.183), channel_id=1, source_target_pairs={{0,4},{2,6},{4,0},{6,2},{8,12},{10,14},{12,8},{14,10},{1,5},{3,7},... | collective-permute-start | bytes 20 | tf_op jit(solution)/shard_map/while/body/eval_jaxpr/ppermute | solution.py:33
  89.5 4.1 %collective-permute-start.9 = (f32[]{:T(128)}, f32[]{:T(128)}, u32[]{:S(2)}, u32[]{:S(2)}) collective-permute-start(f32[]{:T(128)} %add.184), channel_id=1, source_target_pairs={{0,8},{2,10},{4,12},{6,14},{8,0},{10,2},{12,4},{14,6},{1,9},{3,11}... | collective-permute-start | bytes 20 | tf_op jit(solution)/shard_map/while/body/eval_jaxpr/ppermute | solution.py:33
  100.5 2.8 %collective-permute-start = (f32[]{:T(128)}, f32[]{:T(128)}, u32[]{:S(2)}, u32[]{:S(2)}) collective-permute-start(f32[]{:T(128)} %multiply_reduce_fusion.3), channel_id=1, source_target_pairs={{0,16},{16,0},{32,48},{48,32},{64,80},{80,64},{96,112},{112,96},{1... | collective-permute-start | bytes 20 | tf_op jit(solution)/shard_map/while/body/eval_jaxpr/ppermute | solution.py:33
  103.5 1.8 collective-permute-start.3
  105.4 1.8 collective-permute-start.4
  108.5 2.3 %collective-permute-start.1 = (f32[]{:T(128)}, f32[]{:T(128)}, u32[]{:S(2)}, u32[]{:S(2)}) collective-permute-start(f32[]{:T(128)} %add.180), channel_id=1, source_target_pairs={{0,32},{16,48},{32,0},{48,16},{64,96},{80,112},{96,64},{112,80},{1... | collective-permute-start | bytes 20 | tf_op jit(solution)/shard_map/while/body/eval_jaxpr/ppermute | solution.py:33
  112.8 3.2 %collective-permute-start.2 = (f32[]{:T(128)}, f32[]{:T(128)}, u32[]{:S(2)}, u32[]{:S(2)}) collective-permute-start(f32[]{:T(128)} %add.181), channel_id=1, source_target_pairs={{0,64},{16,80},{32,96},{48,112},{64,0},{80,16},{96,32},{112,48},{1... | collective-permute-start | bytes 20 | tf_op jit(solution)/shard_map/while/body/eval_jaxpr/ppermute | solution.py:33
  115.9 2.1 collective-permute-done.2
  119.3 2.2 collective-permute-start.7
  122.0 2.7 %collective-permute-start.8 = (f32[]{:T(128)}, f32[]{:T(128)}, u32[]{:S(2)}, u32[]{:S(2)}) collective-permute-start(f32[]{:T(128)} %add.183), channel_id=1, source_target_pairs={{0,4},{2,6},{4,0},{6,2},{8,12},{10,14},{12,8},{14,10},{1,5},{3,7},... | collective-permute-start | bytes 20 | tf_op jit(solution)/shard_map/while/body/eval_jaxpr/ppermute | solution.py:33
  126.3 3.4 %collective-permute-start.9 = (f32[]{:T(128)}, f32[]{:T(128)}, u32[]{:S(2)}, u32[]{:S(2)}) collective-permute-start(f32[]{:T(128)} %add.184), channel_id=1, source_target_pairs={{0,8},{2,10},{4,12},{6,14},{8,0},{10,2},{12,4},{14,6},{1,9},{3,11}... | collective-permute-start | bytes 20 | tf_op jit(solution)/shard_map/while/body/eval_jaxpr/ppermute | solution.py:33
  129.7 1.9 collective-permute-done.9
  138.9 4.0 %collective-permute-start.3 = (f32[2,32,256]{2,0,1:T(2,128)S(1)}, f32[2,32,256]{2,0,1:T(2,128)S(1)}, u32[]{:S(2)}, u32[]{:S(2)}) collective-permute-start(f32[2,32,256]{2,0,1:T(2,128)S(1)} %slice_bitcast_fusion.11), channel_id=1, source_target_pairs={{16,0},{32,16},{48,32},{64,48},{80,64},{96,80},{112,96},{0,112},{1... | collective-permute-start | bytes 196616 | tf_op jit(solution)/shard_map/while/body/eval_jaxpr/ppermute | solution.py:21
  144.3 1.9 collective-permute-start.1
  146.2 1.8 collective-permute-done.1
  148.6 3.5 %collective-permute-start.2 = (f32[]{:T(128)}, f32[]{:T(128)}, u32[]{:S(2)}, u32[]{:S(2)}) collective-permute-start(f32[]{:T(128)} %add.181), channel_id=1, source_target_pairs={{0,64},{16,80},{32,96},{48,112},{64,0},{80,16},{96,32},{112,48},{1... | collective-permute-start | bytes 20 | tf_op jit(solution)/shard_map/while/body/eval_jaxpr/ppermute | solution.py:33
  152.1 1.7 collective-permute-done.2
  155.1 1.9 collective-permute-start.7
  157.5 2.0 collective-permute-start.8
  159.6 1.7 collective-permute-done.8
  161.8 3.2 %collective-permute-start.9 = (f32[]{:T(128)}, f32[]{:T(128)}, u32[]{:S(2)}, u32[]{:S(2)}) collective-permute-start(f32[]{:T(128)} %add.184), channel_id=1, source_target_pairs={{0,8},{2,10},{4,12},{6,14},{8,0},{10,2},{12,4},{14,6},{1,9},{3,11}... | collective-permute-start | bytes 20 | tf_op jit(solution)/shard_map/while/body/eval_jaxpr/ppermute | solution.py:33
  165.0 2.0 collective-permute-done.9
  173.4 1.6 select_reduce_fusion
  179.8 3.0 %collective-permute-start.25 = (f32[2]{0:T(128)S(1)}, f32[2]{0:T(128)S(1)}, u32[]{:S(2)}, u32[]{:S(2)}) collective-permute-start(f32[2]{0:T(128)S(1)} %pad_maximum_fusion.12), channel_id=1, source_target_pairs={{0,16},{16,0},{32,48},{48,32},{64,80},{80,64},{96,112},{112,96},{1... | collective-permute-start | bytes 32 | tf_op jit(solution)/shard_map/ppermute | solution.py:33
  187.7 1.9 collective-permute-done.20
  189.7 1.9 collective-permute-start.21
  193.0 4.1 %collective-permute-start.27 = (f32[2]{0:T(128)S(1)}, f32[2]{0:T(128)S(1)}, u32[]{:S(2)}, u32[]{:S(2)}) collective-permute-start(f32[2]{0:T(128)S(1)} %fusion.81), channel_id=1, source_target_pairs={{0,64},{16,80},{32,96},{48,112},{64,0},{80,16},{96,32},{112,48},{1... | collective-permute-start | bytes 32 | tf_op jit(solution)/shard_map/ppermute | solution.py:33
  200.7 2.6 %collective-permute-done.29 = f32[2]{0:T(128)S(1)} collective-permute-done((f32[2]{0:T(128)S(1)}, f32[2]{0:T(128)S(1)}, u32[]{:S(2)}, u32[]{:S(2)}) %collective-permute-start.29) | collective-permute-done | bytes 40 | tf_op jit(solution)/shard_map/ppermute | solution.py:33
  203.3 1.7 collective-permute-start.30
  205.0 3.3 %collective-permute-done.30 = f32[2]{0:T(128)S(1)} collective-permute-done((f32[2]{0:T(128)S(1)}, f32[2]{0:T(128)S(1)}, u32[]{:S(2)}, u32[]{:S(2)}) %collective-permute-start.30) | collective-permute-done | bytes 40 | tf_op jit(solution)/shard_map/ppermute | solution.py:33
  210.7 2.1 collective-permute-done.22
  (208 shorter events, 67.6 us)
Async XLA Ops:
  2.1 17.0 %collective-permute-start.15 = (bf16[2,32,256]{2,0,1:T(2,128)(2,1)S(1)}, bf16[2,32,256]{2,0,1:T(2,128)(2,1)S(1)}, u32[]{:S(2)}, u32[]{:S(2)}) collective-permute-start(bf16[2,32,256]{2,0,1:T(2,128)(2,1)S(1)} %get-tuple-element.76), channel_id=1, source_target_pairs={{16,0},{32,16},{48,32},{64,48},{80,64},{96,80},{112,96},{0,112},{1... | collective-permute-start | bytes 98312 | tf_op jit(solution)/shard_map/ppermute | solution.py:21
  8.4 10.8 %collective-permute-start.14 = (bf16[2,32,256]{2,0,1:T(2,128)(2,1)S(1)}, bf16[2,32,256]{2,0,1:T(2,128)(2,1)S(1)}, u32[]{:S(2)}, u32[]{:S(2)}) collective-permute-start(bf16[2,32,256]{2,0,1:T(2,128)(2,1)S(1)} %get-tuple-element.75), channel_id=1, source_target_pairs={{0,16},{16,32},{32,48},{48,64},{64,80},{80,96},{96,112},{112,0},{1... | collective-permute-start | bytes 98312 | tf_op jit(solution)/shard_map/ppermute | solution.py:19
  11.5 9.3 %collective-permute-start.11 = (bf16[8,1,32,256]{3,0,2,1:T(8,128)(2,1)S(1)}, bf16[8,1,32,256]{3,0,2,1:T(8,128)(2,1)S(1)}, u32[]{:S(2)}, u32[]{:S(2)}) collective-permute-start(bf16[8,1,32,256]{3,0,2,1:T(8,128)(2,1)S(1)} %get-tuple-element.72), channel_id=1, source_target_pairs={{16,0},{32,16},{48,32},{64,48},{80,64},{96,80},{112,96},{17,1},{33... | collective-permute-start | bytes 393224 | tf_op jit(solution)/shard_map/ppermute | solution.py:21
  12.8 9.0 %collective-permute-start.10 = (bf16[8,1,32,256]{3,0,2,1:T(8,128)(2,1)S(1)}, bf16[8,1,32,256]{3,0,2,1:T(8,128)(2,1)S(1)}, u32[]{:S(2)}, u32[]{:S(2)}) collective-permute-start(bf16[8,1,32,256]{3,0,2,1:T(8,128)(2,1)S(1)} %get-tuple-element.71), channel_id=1, source_target_pairs={{0,16},{16,32},{32,48},{48,64},{64,80},{80,96},{96,112},{1,17},{17... | collective-permute-start | bytes 393224 | tf_op jit(solution)/shard_map/ppermute | solution.py:19
  19.2 7.1 %collective-permute-start.17 = (bf16[20,2,256]{2,0,1:T(8,128)(2,1)S(1)}, bf16[20,2,256]{2,0,1:T(8,128)(2,1)S(1)}, u32[]{:S(2)}, u32[]{:S(2)}) collective-permute-start(bf16[20,2,256]{2,0,1:T(8,128)(2,1)S(1)} %get-tuple-element.74), channel_id=1, source_target_pairs={{2,0},{4,2},{6,4},{8,6},{10,8},{12,10},{14,12},{0,14},{3,1},{5,3},... | collective-permute-start | bytes 61448 | tf_op jit(solution)/shard_map/ppermute | solution.py:21
  20.8 5.5 %collective-permute-start.16 = (bf16[20,2,256]{2,0,1:T(8,128)(2,1)S(1)}, bf16[20,2,256]{2,0,1:T(8,128)(2,1)S(1)}, u32[]{:S(2)}, u32[]{:S(2)}) collective-permute-start(bf16[20,2,256]{2,0,1:T(8,128)(2,1)S(1)} %get-tuple-element.73), channel_id=1, source_target_pairs={{0,2},{2,4},{4,6},{6,8},{8,10},{10,12},{12,14},{14,0},{1,3},{3,5},... | collective-permute-start | bytes 61448 | tf_op jit(solution)/shard_map/ppermute | solution.py:19
  21.9 5.4 %collective-permute-start.13 = (bf16[8,18,1,256]{3,0,2,1:T(8,128)(2,1)S(1)}, bf16[8,18,1,256]{3,0,2,1:T(8,128)(2,1)S(1)}, u32[]{:S(2)}, u32[]{:S(2)}) collective-permute-start(bf16[8,18,1,256]{3,0,2,1:T(8,128)(2,1)S(1)} %get-tuple-element.70), channel_id=1, source_target_pairs={{2,0},{4,2},{6,4},{8,6},{10,8},{12,10},{14,12},{3,1},{5,3},{7,5},{... | collective-permute-start | bytes 221192 | tf_op jit(solution)/shard_map/ppermute | solution.py:21
  23.2 4.1 %collective-permute-start.12 = (bf16[8,18,1,256]{3,0,2,1:T(8,128)(2,1)S(1)}, bf16[8,18,1,256]{3,0,2,1:T(8,128)(2,1)S(1)}, u32[]{:S(2)}, u32[]{:S(2)}) collective-permute-start(bf16[8,18,1,256]{3,0,2,1:T(8,128)(2,1)S(1)} %get-tuple-element.69), channel_id=1, source_target_pairs={{0,2},{2,4},{4,6},{6,8},{8,10},{10,12},{12,14},{1,3},{3,5},{5,7},{... | collective-permute-start | bytes 221192 | tf_op jit(solution)/shard_map/ppermute | solution.py:19
  52.0 119.0 %collective-permute-start.18 = (bf16[128,2304]{1,0:T(8,128)(2,1)S(1)}, bf16[128,2304]{1,0:T(8,128)(2,1)}, u32[]{:S(2)}, u32[]{:S(2)}) collective-permute-start(bf16[128,2304]{1,0:T(8,128)(2,1)S(1)} %dynamic-slice_convert_fusion), channel_id=1, source_target_pairs={{0,64},{16,80},{32,96},{48,112},{64,0},{80,16},{96,32},{112,48},{1... | collective-permute-start | bytes 1769480 | tf_op jit(solution)/shard_map/ppermute | solution.py:50
  62.7 5.3 %collective-permute-start = (f32[]{:T(128)}, f32[]{:T(128)}, u32[]{:S(2)}, u32[]{:S(2)}) collective-permute-start(f32[]{:T(128)} %multiply_reduce_fusion.3), channel_id=1, source_target_pairs={{0,16},{16,0},{32,48},{48,32},{64,80},{80,64},{96,112},{112,96},{1... | collective-permute-start | bytes 20 | tf_op jit(solution)/shard_map/while/body/eval_jaxpr/ppermute | solution.py:33
  63.5 17.2 %collective-permute-start.3 = (f32[2,32,256]{2,0,1:T(2,128)S(1)}, f32[2,32,256]{2,0,1:T(2,128)S(1)}, u32[]{:S(2)}, u32[]{:S(2)}) collective-permute-start(f32[2,32,256]{2,0,1:T(2,128)S(1)} %slice_bitcast_fusion.11), channel_id=1, source_target_pairs={{16,0},{32,16},{48,32},{64,48},{80,64},{96,80},{112,96},{0,112},{1... | collective-permute-start | bytes 196616 | tf_op jit(solution)/shard_map/while/body/eval_jaxpr/ppermute | solution.py:21
  67.1 13.6 %collective-permute-start.4 = (f32[2,32,256]{2,0,1:T(2,128)S(1)}, f32[2,32,256]{2,0,1:T(2,128)S(1)}, u32[]{:S(2)}, u32[]{:S(2)}) collective-permute-start(f32[2,32,256]{2,0,1:T(2,128)S(1)} %slice_bitcast_fusion.13), channel_id=1, source_target_pairs={{0,16},{16,32},{32,48},{48,64},{64,80},{80,96},{96,112},{112,0},{1... | collective-permute-start | bytes 196616 | tf_op jit(solution)/shard_map/while/body/eval_jaxpr/ppermute | solution.py:19
  69.2 5.1 %collective-permute-start.1 = (f32[]{:T(128)}, f32[]{:T(128)}, u32[]{:S(2)}, u32[]{:S(2)}) collective-permute-start(f32[]{:T(128)} %add.180), channel_id=1, source_target_pairs={{0,32},{16,48},{32,0},{48,16},{64,96},{80,112},{96,64},{112,80},{1... | collective-permute-start | bytes 20 | tf_op jit(solution)/shard_map/while/body/eval_jaxpr/ppermute | solution.py:33
  74.9 5.2 %collective-permute-start.2 = (f32[]{:T(128)}, f32[]{:T(128)}, u32[]{:S(2)}, u32[]{:S(2)}) collective-permute-start(f32[]{:T(128)} %add.181), channel_id=1, source_target_pairs={{0,64},{16,80},{32,96},{48,112},{64,0},{80,16},{96,32},{112,48},{1... | collective-permute-start | bytes 20 | tf_op jit(solution)/shard_map/while/body/eval_jaxpr/ppermute | solution.py:33
  80.8 15.3 %collective-permute-start.5 = (f32[20,2,256]{2,0,1:T(8,128)S(1)}, f32[20,2,256]{2,0,1:T(8,128)S(1)}, u32[]{:S(2)}, u32[]{:S(2)}) collective-permute-start(f32[20,2,256]{2,0,1:T(8,128)S(1)} %get-tuple-element.121), channel_id=1, source_target_pairs={{2,0},{4,2},{6,4},{8,6},{10,8},{12,10},{14,12},{0,14},{3,1},{5,3},... | collective-permute-start | bytes 122888 | tf_op jit(solution)/shard_map/while/body/eval_jaxpr/ppermute | solution.py:21
  80.9 15.3 %collective-permute-start.6 = (f32[20,2,256]{2,0,1:T(8,128)S(1)}, f32[20,2,256]{2,0,1:T(8,128)S(1)}, u32[]{:S(2)}, u32[]{:S(2)}) collective-permute-start(f32[20,2,256]{2,0,1:T(8,128)S(1)} %get-tuple-element.122), channel_id=1, source_target_pairs={{0,2},{2,4},{4,6},{6,8},{8,10},{10,12},{12,14},{14,0},{1,3},{3,5},... | collective-permute-start | bytes 122888 | tf_op jit(solution)/shard_map/while/body/eval_jaxpr/ppermute | solution.py:19
  81.4 3.2 %collective-permute-start.7 = (f32[]{:T(128)}, f32[]{:T(128)}, u32[]{:S(2)}, u32[]{:S(2)}) collective-permute-start(f32[]{:T(128)} %add.182), channel_id=1, source_target_pairs={{0,2},{2,0},{4,6},{6,4},{8,10},{10,8},{12,14},{14,12},{1,3},{3,1},... | collective-permute-start | bytes 20 | tf_op jit(solution)/shard_map/while/body/eval_jaxpr/ppermute | solution.py:33
  85.1 3.7 %collective-permute-start.8 = (f32[]{:T(128)}, f32[]{:T(128)}, u32[]{:S(2)}, u32[]{:S(2)}) collective-permute-start(f32[]{:T(128)} %add.183), channel_id=1, source_target_pairs={{0,4},{2,6},{4,0},{6,2},{8,12},{10,14},{12,8},{14,10},{1,5},{3,7},... | collective-permute-start | bytes 20 | tf_op jit(solution)/shard_map/while/body/eval_jaxpr/ppermute | solution.py:33
  89.5 5.2 %collective-permute-start.9 = (f32[]{:T(128)}, f32[]{:T(128)}, u32[]{:S(2)}, u32[]{:S(2)}) collective-permute-start(f32[]{:T(128)} %add.184), channel_id=1, source_target_pairs={{0,8},{2,10},{4,12},{6,14},{8,0},{10,2},{12,4},{14,6},{1,9},{3,11}... | collective-permute-start | bytes 20 | tf_op jit(solution)/shard_map/while/body/eval_jaxpr/ppermute | solution.py:33
  100.5 6.7 %collective-permute-start = (f32[]{:T(128)}, f32[]{:T(128)}, u32[]{:S(2)}, u32[]{:S(2)}) collective-permute-start(f32[]{:T(128)} %multiply_reduce_fusion.3), channel_id=1, source_target_pairs={{0,16},{16,0},{32,48},{48,32},{64,80},{80,64},{96,112},{112,96},{1... | collective-permute-start | bytes 20 | tf_op jit(solution)/shard_map/while/body/eval_jaxpr/ppermute | solution.py:33
  103.5 15.1 %collective-permute-start.3 = (f32[2,32,256]{2,0,1:T(2,128)S(1)}, f32[2,32,256]{2,0,1:T(2,128)S(1)}, u32[]{:S(2)}, u32[]{:S(2)}) collective-permute-start(f32[2,32,256]{2,0,1:T(2,128)S(1)} %slice_bitcast_fusion.11), channel_id=1, source_target_pairs={{16,0},{32,16},{48,32},{64,48},{80,64},{96,80},{112,96},{0,112},{1... | collective-permute-start | bytes 196616 | tf_op jit(solution)/shard_map/while/body/eval_jaxpr/ppermute | solution.py:21
  105.4 13.2 %collective-permute-start.4 = (f32[2,32,256]{2,0,1:T(2,128)S(1)}, f32[2,32,256]{2,0,1:T(2,128)S(1)}, u32[]{:S(2)}, u32[]{:S(2)}) collective-permute-start(f32[2,32,256]{2,0,1:T(2,128)S(1)} %slice_bitcast_fusion.13), channel_id=1, source_target_pairs={{0,16},{16,32},{32,48},{48,64},{64,80},{80,96},{96,112},{112,0},{1... | collective-permute-start | bytes 196616 | tf_op jit(solution)/shard_map/while/body/eval_jaxpr/ppermute | solution.py:19
  108.5 3.7 %collective-permute-start.1 = (f32[]{:T(128)}, f32[]{:T(128)}, u32[]{:S(2)}, u32[]{:S(2)}) collective-permute-start(f32[]{:T(128)} %add.180), channel_id=1, source_target_pairs={{0,32},{16,48},{32,0},{48,16},{64,96},{80,112},{96,64},{112,80},{1... | collective-permute-start | bytes 20 | tf_op jit(solution)/shard_map/while/body/eval_jaxpr/ppermute | solution.py:33
  112.8 5.2 %collective-permute-start.2 = (f32[]{:T(128)}, f32[]{:T(128)}, u32[]{:S(2)}, u32[]{:S(2)}) collective-permute-start(f32[]{:T(128)} %add.181), channel_id=1, source_target_pairs={{0,64},{16,80},{32,96},{48,112},{64,0},{80,16},{96,32},{112,48},{1... | collective-permute-start | bytes 20 | tf_op jit(solution)/shard_map/while/body/eval_jaxpr/ppermute | solution.py:33
  118.7 14.3 %collective-permute-start.5 = (f32[20,2,256]{2,0,1:T(8,128)S(1)}, f32[20,2,256]{2,0,1:T(8,128)S(1)}, u32[]{:S(2)}, u32[]{:S(2)}) collective-permute-start(f32[20,2,256]{2,0,1:T(8,128)S(1)} %get-tuple-element.121), channel_id=1, source_target_pairs={{2,0},{4,2},{6,4},{8,6},{10,8},{12,10},{14,12},{0,14},{3,1},{5,3},... | collective-permute-start | bytes 122888 | tf_op jit(solution)/shard_map/while/body/eval_jaxpr/ppermute | solution.py:21
  118.8 14.2 %collective-permute-start.6 = (f32[20,2,256]{2,0,1:T(8,128)S(1)}, f32[20,2,256]{2,0,1:T(8,128)S(1)}, u32[]{:S(2)}, u32[]{:S(2)}) collective-permute-start(f32[20,2,256]{2,0,1:T(8,128)S(1)} %get-tuple-element.122), channel_id=1, source_target_pairs={{0,2},{2,4},{4,6},{6,8},{8,10},{10,12},{12,14},{14,0},{1,3},{3,5},... | collective-permute-start | bytes 122888 | tf_op jit(solution)/shard_map/while/body/eval_jaxpr/ppermute | solution.py:19
  119.3 2.2 collective-permute-start.7
  122.0 3.7 %collective-permute-start.8 = (f32[]{:T(128)}, f32[]{:T(128)}, u32[]{:S(2)}, u32[]{:S(2)}) collective-permute-start(f32[]{:T(128)} %add.183), channel_id=1, source_target_pairs={{0,4},{2,6},{4,0},{6,2},{8,12},{10,14},{12,8},{14,10},{1,5},{3,7},... | collective-permute-start | bytes 20 | tf_op jit(solution)/shard_map/while/body/eval_jaxpr/ppermute | solution.py:33
  126.3 5.2 %collective-permute-start.9 = (f32[]{:T(128)}, f32[]{:T(128)}, u32[]{:S(2)}, u32[]{:S(2)}) collective-permute-start(f32[]{:T(128)} %add.184), channel_id=1, source_target_pairs={{0,8},{2,10},{4,12},{6,14},{8,0},{10,2},{12,4},{14,6},{1,9},{3,11}... | collective-permute-start | bytes 20 | tf_op jit(solution)/shard_map/while/body/eval_jaxpr/ppermute | solution.py:33
  137.4 5.7 %collective-permute-start = (f32[]{:T(128)}, f32[]{:T(128)}, u32[]{:S(2)}, u32[]{:S(2)}) collective-permute-start(f32[]{:T(128)} %multiply_reduce_fusion.3), channel_id=1, source_target_pairs={{0,16},{16,0},{32,48},{48,32},{64,80},{80,64},{96,112},{112,96},{1... | collective-permute-start | bytes 20 | tf_op jit(solution)/shard_map/while/body/eval_jaxpr/ppermute | solution.py:33
  138.9 15.5 %collective-permute-start.3 = (f32[2,32,256]{2,0,1:T(2,128)S(1)}, f32[2,32,256]{2,0,1:T(2,128)S(1)}, u32[]{:S(2)}, u32[]{:S(2)}) collective-permute-start(f32[2,32,256]{2,0,1:T(2,128)S(1)} %slice_bitcast_fusion.11), channel_id=1, source_target_pairs={{16,0},{32,16},{48,32},{64,48},{80,64},{96,80},{112,96},{0,112},{1... | collective-permute-start | bytes 196616 | tf_op jit(solution)/shard_map/while/body/eval_jaxpr/ppermute | solution.py:21
  142.9 11.5 %collective-permute-start.4 = (f32[2,32,256]{2,0,1:T(2,128)S(1)}, f32[2,32,256]{2,0,1:T(2,128)S(1)}, u32[]{:S(2)}, u32[]{:S(2)}) collective-permute-start(f32[2,32,256]{2,0,1:T(2,128)S(1)} %slice_bitcast_fusion.13), channel_id=1, source_target_pairs={{0,16},{16,32},{32,48},{48,64},{64,80},{80,96},{96,112},{112,0},{1... | collective-permute-start | bytes 196616 | tf_op jit(solution)/shard_map/while/body/eval_jaxpr/ppermute | solution.py:19
  144.3 3.7 %collective-permute-start.1 = (f32[]{:T(128)}, f32[]{:T(128)}, u32[]{:S(2)}, u32[]{:S(2)}) collective-permute-start(f32[]{:T(128)} %add.180), channel_id=1, source_target_pairs={{0,32},{16,48},{32,0},{48,16},{64,96},{80,112},{96,64},{112,80},{1... | collective-permute-start | bytes 20 | tf_op jit(solution)/shard_map/while/body/eval_jaxpr/ppermute | solution.py:33
  148.6 5.2 %collective-permute-start.2 = (f32[]{:T(128)}, f32[]{:T(128)}, u32[]{:S(2)}, u32[]{:S(2)}) collective-permute-start(f32[]{:T(128)} %add.181), channel_id=1, source_target_pairs={{0,64},{16,80},{32,96},{48,112},{64,0},{80,16},{96,32},{112,48},{1... | collective-permute-start | bytes 20 | tf_op jit(solution)/shard_map/while/body/eval_jaxpr/ppermute | solution.py:33
  154.6 14.0 %collective-permute-start.5 = (f32[20,2,256]{2,0,1:T(8,128)S(1)}, f32[20,2,256]{2,0,1:T(8,128)S(1)}, u32[]{:S(2)}, u32[]{:S(2)}) collective-permute-start(f32[20,2,256]{2,0,1:T(8,128)S(1)} %get-tuple-element.121), channel_id=1, source_target_pairs={{2,0},{4,2},{6,4},{8,6},{10,8},{12,10},{14,12},{0,14},{3,1},{5,3},... | collective-permute-start | bytes 122888 | tf_op jit(solution)/shard_map/while/body/eval_jaxpr/ppermute | solution.py:21
  154.6 14.0 %collective-permute-start.6 = (f32[20,2,256]{2,0,1:T(8,128)S(1)}, f32[20,2,256]{2,0,1:T(8,128)S(1)}, u32[]{:S(2)}, u32[]{:S(2)}) collective-permute-start(f32[20,2,256]{2,0,1:T(8,128)S(1)} %get-tuple-element.122), channel_id=1, source_target_pairs={{0,2},{2,4},{4,6},{6,8},{8,10},{10,12},{12,14},{14,0},{1,3},{3,5},... | collective-permute-start | bytes 122888 | tf_op jit(solution)/shard_map/while/body/eval_jaxpr/ppermute | solution.py:19
  157.5 3.7 %collective-permute-start.8 = (f32[]{:T(128)}, f32[]{:T(128)}, u32[]{:S(2)}, u32[]{:S(2)}) collective-permute-start(f32[]{:T(128)} %add.183), channel_id=1, source_target_pairs={{0,4},{2,6},{4,0},{6,2},{8,12},{10,14},{12,8},{14,10},{1,5},{3,7},... | collective-permute-start | bytes 20 | tf_op jit(solution)/shard_map/while/body/eval_jaxpr/ppermute | solution.py:33
  161.8 5.2 %collective-permute-start.9 = (f32[]{:T(128)}, f32[]{:T(128)}, u32[]{:S(2)}, u32[]{:S(2)}) collective-permute-start(f32[]{:T(128)} %add.184), channel_id=1, source_target_pairs={{0,8},{2,10},{4,12},{6,14},{8,0},{10,2},{12,4},{14,6},{1,9},{3,11}... | collective-permute-start | bytes 20 | tf_op jit(solution)/shard_map/while/body/eval_jaxpr/ppermute | solution.py:33
  172.8 10.0 %collective-permute-start.19 = (bf16[64,2304]{1,0:T(8,128)(2,1)S(1)}, bf16[64,2304]{1,0:T(8,128)(2,1)S(1)}, u32[]{:S(2)}, u32[]{:S(2)}) collective-permute-start(bf16[64,2304]{1,0:T(8,128)(2,1)S(1)} %dynamic-slice_convert_fusion.1), channel_id=1, source_target_pairs={{0,32},{16,48},{32,0},{48,16},{64,96},{80,112},{96,64},{112,80},{1... | collective-permute-start | bytes 884744 | tf_op jit(solution)/shard_map/ppermute | solution.py:50
  179.8 5.1 %collective-permute-start.25 = (f32[2]{0:T(128)S(1)}, f32[2]{0:T(128)S(1)}, u32[]{:S(2)}, u32[]{:S(2)}) collective-permute-start(f32[2]{0:T(128)S(1)} %pad_maximum_fusion.12), channel_id=1, source_target_pairs={{0,16},{16,0},{32,48},{48,32},{64,80},{80,64},{96,112},{112,96},{1... | collective-permute-start | bytes 32 | tf_op jit(solution)/shard_map/ppermute | solution.py:33
  182.9 6.7 %collective-permute-start.20 = (bf16[32,2304]{1,0:T(8,128)(2,1)S(1)}, bf16[32,2304]{1,0:T(8,128)(2,1)S(1)}, u32[]{:S(2)}, u32[]{:S(2)}) collective-permute-start(bf16[32,2304]{1,0:T(8,128)(2,1)S(1)} %dynamic-slice_convert_fusion.2), channel_id=1, source_target_pairs={{0,16},{16,0},{32,48},{48,32},{64,80},{80,64},{96,112},{112,96},{1... | collective-permute-start | bytes 442376 | tf_op jit(solution)/shard_map/ppermute | solution.py:50
  186.2 5.4 %collective-permute-start.26 = (f32[2]{0:T(128)S(1)}, f32[2]{0:T(128)S(1)}, u32[]{:S(2)}, u32[]{:S(2)}) collective-permute-start(f32[2]{0:T(128)S(1)} %fusion.80), channel_id=1, source_target_pairs={{0,32},{16,48},{32,0},{48,16},{64,96},{80,112},{96,64},{112,80},{1... | collective-permute-start | bytes 32 | tf_op jit(solution)/shard_map/ppermute | solution.py:33
  189.7 18.7 %collective-permute-start.21 = (bf16[16,2304]{1,0:T(8,128)(2,1)S(1)}, bf16[16,2304]{1,0:T(8,128)(2,1)S(1)}, u32[]{:S(2)}, u32[]{:S(2)}) collective-permute-start(bf16[16,2304]{1,0:T(8,128)(2,1)S(1)} %dynamic-slice_convert_fusion.3), channel_id=1, source_target_pairs={{0,8},{2,10},{4,12},{6,14},{8,0},{10,2},{12,4},{14,6},{1,9},{3,11}... | collective-permute-start | bytes 221192 | tf_op jit(solution)/shard_map/ppermute | solution.py:50
  193.0 5.7 %collective-permute-start.27 = (f32[2]{0:T(128)S(1)}, f32[2]{0:T(128)S(1)}, u32[]{:S(2)}, u32[]{:S(2)}) collective-permute-start(f32[2]{0:T(128)S(1)} %fusion.81), channel_id=1, source_target_pairs={{0,64},{16,80},{32,96},{48,112},{64,0},{80,16},{96,32},{112,48},{1... | collective-permute-start | bytes 32 | tf_op jit(solution)/shard_map/ppermute | solution.py:33
  199.7 3.5 %collective-permute-start.29 = (f32[2]{0:T(128)S(1)}, f32[2]{0:T(128)S(1)}, u32[]{:S(2)}, u32[]{:S(2)}) collective-permute-start(f32[2]{0:T(128)S(1)} %add.156), channel_id=1, source_target_pairs={{0,4},{2,6},{4,0},{6,2},{8,12},{10,14},{12,8},{14,10},{1,5},{3,7},... | collective-permute-start | bytes 32 | tf_op jit(solution)/shard_map/ppermute | solution.py:33
  203.3 5.0 %collective-permute-start.30 = (f32[2]{0:T(128)S(1)}, f32[2]{0:T(128)S(1)}, u32[]{:S(2)}, u32[]{:S(2)}) collective-permute-start(f32[2]{0:T(128)S(1)} %add.157), channel_id=1, source_target_pairs={{0,8},{2,10},{4,12},{6,14},{8,0},{10,2},{12,4},{14,6},{1,9},{3,11}... | collective-permute-start | bytes 32 | tf_op jit(solution)/shard_map/ppermute | solution.py:33
  208.4 4.4 %collective-permute-start.22 = (f32[8,2304]{1,0:T(8,128)S(1)}, f32[8,2304]{1,0:T(8,128)S(1)}, u32[]{:S(2)}, u32[]{:S(2)}) collective-permute-start(f32[8,2304]{1,0:T(8,128)S(1)} %constant_dynamic-slice_fusion.1), channel_id=1, source_target_pairs={{0,4},{2,6},{4,0},{6,2},{8,12},{10,14},{12,8},{14,10},{1,5},{3,7},... | collective-permute-start | bytes 221192 | tf_op jit(solution)/shard_map/ppermute | solution.py:50
  214.2 4.0 %collective-permute-start.24 = (f32[4,2304]{1,0:T(4,128)S(1)}, f32[4,2304]{1,0:T(4,128)S(1)}, u32[]{:S(2)}, u32[]{:S(2)}) collective-permute-start(f32[4,2304]{1,0:T(4,128)S(1)} %dynamic-slice_add_fusion.1), channel_id=1, source_target_pairs={{0,1},{1,0},{2,3},{3,2},{4,5},{5,4},{6,7},{7,6},{8,9},{9,8},{10,11... | collective-permute-start | bytes 110600 | tf_op jit(solution)/shard_map/ppermute | solution.py:33
  (22 other events, 91.2 us)

commit v10 on v9

--- a/solution.py
+++ b/solution.py
@@ -33,6 +33,45 @@
             value = value + lax.ppermute(value, axis, [(i, i ^ step) for i in range(count)])
             step *= 2
     return value
+
+
+def extended_pair(field, cells, sides, field_width):
+    for axis, field_dim, cells_dim in sides:
+        count = lax.axis_size(axis)
+        index = lax.axis_index(axis)
+        parts = []
+        for start, width, dim, array in (
+            (0, field_width, field_dim, field),
+            (0, 1, cells_dim, cells),
+        ):
+            parts.append(
+                (
+                    lax.slice_in_dim(array, 0, width, axis=dim),
+                    lax.slice_in_dim(array, array.shape[dim] - width, array.shape[dim], axis=dim),
+                )
+            )
+        channels = field.shape[-1]
+
+        def travel(pieces, pairs):
+            flat = jnp.concatenate([piece.reshape(-1, channels) for piece in pieces], axis=0)
+            moved = lax.ppermute(flat, axis, pairs)
+            split = pieces[0].size // channels
+            return (
+                moved[:split].reshape(pieces[0].shape),
+                moved[split:].reshape(pieces[1].shape),
+            )
+
+        field_top, cells_top = travel(
+            (parts[0][1], parts[1][1]), [(i, (i + 1) % count) for i in range(count)]
+        )
+        field_bottom, cells_bottom = travel(
+            (parts[0][0], parts[1][0]), [((i + 1) % count, i) for i in range(count)]
+        )
+        cells_top = jnp.where(index == 0, jnp.zeros_like(cells_top), cells_top)
+        cells_bottom = jnp.where(index == count - 1, jnp.zeros_like(cells_bottom), cells_bottom)
+        field = jnp.concatenate([field_top, field, field_bottom], axis=field_dim)
+        cells = jnp.concatenate([cells_top, cells, cells_bottom], axis=cells_dim)
+    return field, cells
 
 
 def halving_scatter(value, axes):
@@ -76,7 +115,6 @@
     count = float(height * rows_count * breadth * cols_count * channels)
     field = (("rows", 0), ("cols", 1))
     iterate = probe_init.astype(jnp.bfloat16)
-    padded_probe = extended(iterate, field, 2, True)
 
     def power_step(carry, _):
         padded_probe, iterate = carry
@@ -92,8 +130,11 @@
         padded_probe = (padded_back / scale_now).astype(jnp.bfloat16)
         return (padded_probe, iterate), scale_now
 
-    padded_both = extended(
-        jnp.concatenate([inputs, upstream], axis=0), (("rows", 1), ("cols", 2)), 1, False
+    padded_probe, padded_both = extended_pair(
+        iterate,
+        jnp.concatenate([inputs, upstream], axis=0),
+        (("rows", 0, 1), ("cols", 1, 2)),
+        2,
     )
     padded_in = padded_both[:batch]
     padded_up = padded_both[batch:]

time: 221 us -> 214 us (0.968)
  starting transfers between devices: 102 us -> 82.7 us
  waiting for transfers between devices: 37.8 us -> 46.2 us
  local copies, waits for them, and re-layouts: 24.1 us -> 27.4 us
    ppermute x10 -> x6, starting transfers between devices: 19.8 us -> 5.3 us  [extended(): lax.ppermute(head, axis, [((i + 1) % count, i) for i in range(ends)])]
    ppermute x0 -> x4, waiting for transfers between devices: none -> 14 us  [travel(): moved = lax.ppermute(flat, axis, pairs)]
    ppermute x0 -> x4, starting transfers between devices: none -> 7.77 us  [travel(): moved = lax.ppermute(flat, axis, pairs)]
    ppermute x6, starting transfers between devices: 10.4 us -> 4.55 us  [halving_scatter(): received = lax.ppermute(send, axis, [(i, i ^ step) for i in range(count)])]
    ppermute x10 -> x6, starting transfers between devices: 12.6 us -> 7.25 us  [extended(): lax.ppermute(tail, axis, [(i, (i + 1) % count) for i in range(ends)])]
    ppermute x25, waiting for transfers between devices: 31.8 us -> 27.4 us  [butterfly_sum(): lax.ppermute(value, axis, [(i, i ^ step) for i in range(count)])]
    unnamed x38 -> x52, local copies, waits for them, and re-layouts: 9.89 us -> 9.35 us
  transfers between devices with their start and end apart: 51 -> 47, of which waited for: 23 -> 26; matrix products, arithmetic and copies ran while one was open for 13% -> 12% of each run, Pallas kernels for 0% -> 0%
where the time goes in v10:
time: 214 us; the launch traced here: 212 us
  starting transfers between devices  82.7 us (39%)
  waiting for transfers between devices  46.2 us (22%)
  local copies, waits for them, and re-layouts  27.4 us (13%)
  matrix products  22.1 us (10%)
  other arithmetic  14.8 us (7%)
  loops' own time  14.2 us (7%)
  between operations  4.93 us (2%)
    ppermute x25, starting transfers between devices, butterfly_sum(): lax.ppermute(value, axis, [(i, i ^ step) for i in range(count)])  57.8 us
    ppermute x25, waiting for transfers between devices, butterfly_sum(): lax.ppermute(value, axis, [(i, i ^ step) for i in range(count)])  27.4 us
    conv_general_dilated x10, matrix products, conv(): lax.conv_general_dilated(padded, weights, window_strides=(1, 1), padding=...  15.1 us
    another operation x1, loops' own time, per_device(): lax.scan(power_step, (padded_probe, iterate), None, length=ITERS - 1)  14.2 us
    ppermute x4, waiting for transfers between devices, travel(): moved = lax.ppermute(flat, axis, pairs)  14 us
    unnamed x52, local copies, waits for them, and re-layouts  9.35 us
    ppermute x4, starting transfers between devices, travel(): moved = lax.ppermute(flat, axis, pairs)  7.77 us
    ppermute x6, starting transfers between devices, extended(): lax.ppermute(tail, axis, [(i, (i + 1) % count) for i in range(ends)])  7.25 us
  transfers between devices with their start and end apart: 47, of which 26 were waited for; matrix products, arithmetic and copies ran while one was open for 12% of the time, Pallas kernels for 0%

profile of v10, /device:TPU:0, one launch (start us, length us, event | category | flops | bytes accessed | tf_op | source)
XLA Modules:
  0.0 212.4 jit_solution(8556830713462922048)
XLA Ops:
  0.6 2.2 %copy.25 = bf16[4,16,32,256]{3,0,2,1:T(4,128)(2,1)S(1)} copy(bf16[4,16,32,256]{3,2,1,0:T(8,128)(2,1)} %param.7) | data formatting | bytes 2097152 | tf_op args[1]
  4.3 6.2 %collective-permute-start.11 = (bf16[320,256]{1,0:T(8,128)(2,1)S(1)}, bf16[320,256]{1,0:T(8,128)(2,1)S(1)}, u32[]{:S(2)}, u32[]{:S(2)}) collective-permute-start(bf16[320,256]{1,0:T(8,128)(2,1)S(1)} %pad_maximum_fusion.4), channel_id=1, source_target_pairs={{16,0},{32,16},{48,32},{64,48},{80,64},{96,80},{112,96},{0,112},{1... | collective-permute-start | bytes 491528 | tf_op jit(solution)/shard_map/ppermute | solution.py:57
  11.1 2.9 %collective-permute-done.11 = bf16[320,256]{1,0:T(8,128)(2,1)S(1)} collective-permute-done((bf16[320,256]{1,0:T(8,128)(2,1)S(1)}, bf16[320,256]{1,0:T(8,128)(2,1)S(1)}, u32[]{:S(2)}, u32[]{:S(2)}) %collective-permute-start.11) | collective-permute-done | bytes 163872 | tf_op jit(solution)/shard_map/ppermute | solution.py:57
  14.2 6.0 %collective-permute-done.10 = bf16[320,256]{1,0:T(8,128)(2,1)S(1)} collective-permute-done((bf16[320,256]{1,0:T(8,128)(2,1)S(1)}, bf16[320,256]{1,0:T(8,128)(2,1)S(1)}, u32[]{:S(2)}, u32[]{:S(2)}) %collective-permute-start.10) | collective-permute-done | bytes 163872 | tf_op jit(solution)/shard_map/ppermute | solution.py:57
  22.1 2.0 collective-permute-done.13
  24.2 3.1 %collective-permute-done.12 = bf16[184,256]{1,0:T(8,128)(2,1)S(1)} collective-permute-done((bf16[184,256]{1,0:T(8,128)(2,1)S(1)}, bf16[184,256]{1,0:T(8,128)(2,1)S(1)}, u32[]{:S(2)}, u32[]{:S(2)}) %collective-permute-start.12) | collective-permute-done | bytes 94240 | tf_op jit(solution)/shard_map/ppermute | solution.py:57
  28.6 6.9 %fusion.46 = f32[256,3,3,256]{0,3,2,1:T(8,128)} fusion(bf16[8,18,34,256]{3,0,2,1:T(8,128)(2,1)S(1)} %pad_maximum_fusion.1, bf16[4,16,32,256]{3,2,1,0:T(8,128)(2,1)S(1)} %copy-done.8), kind=kOutput, calls=%fused_computation.63 | convolution fusion | flops 2415919104 | bytes 4661248 | tf_op jit(solution)/shard_map/conv_general_dilated | solution.py:143
  38.6 3.3 %select_convert_fusion = bf16[16,32,5,256]{3,1,2,0:T(8,128)(2,1)S(1)} fusion(bf16[3,3,256,256]{3,2,1,0:T(8,128)(2,1)S(1)} %copy-done.16, bf16[18,4,8,7,256]{4,1,3,2,0:T(4,128)(2,1)S(1)} %fusion.30, pred[32,5]{0,1:T(8,128)(4,1)S(1)} %copy-done.23), kind=kOutput, calls=%fused_computation.38 | convolution fusion | flops 3021209600 | bytes 4554912 | tf_op jit(solution)/shard_map/conv_general_dilated | solution.py:98
  41.8 1.8 copy.43
  45.6 3.2 %select_convert_fusion.1 = bf16[16,32,5,256]{3,1,2,0:T(8,128)(2,1)S(1)} fusion(bf16[3,3,256,256]{3,2,1,0:T(8,128)(2,1)S(1)} %copy-done.16, bf16[18,4,8,7,256]{4,1,3,2,0:T(4,128)(2,1)S(1)} %fusion.29, pred[32,5]{0,1:T(8,128)(4,1)S(1)} %copy-done.23), kind=kOutput, calls=%fused_computation.39 | convolution fusion | flops 3021209600 | bytes 4554912 | tf_op jit(solution)/shard_map/conv_general_dilated | solution.py:98
  50.2 1.5 slice_bitcast_fusion.4
  52.0 3.1 %copy.46 = f32[256,2304]{1,0:T(8,128)} copy(f32[256,2304]{0,1:T(8,128)} %bitcast.130) | data formatting | bytes 4718592 | tf_op jit(solution)/shard_map/optimization_barrier | solution.py:151
  56.5 106.4 %while.14 = (s32[]{:T(128)}, bf16[20,36,256]{2,0,1:T(8,128)(2,1)S(1)}, bf16[16,32,256]{2,0,1:T(8,128)(2,1)}, f32[3]{0:T(128)S(1)}, bf16[3,3,256,256]{3,2,1,0:T(8...) while((s32[]{:T(128)}, bf16[20,36,256]{2,0,1:T(8,128)(2,1)S(1)}, ...), condition=%wide.region_2.3_spmd, body=%wide.region_0.2_spmd.sunk | while | flops 1609732096 | bytes 19315492 | solution.py:154
  61.1 3.0 %collective-permute-start = (f32[]{:T(128)}, f32[]{:T(128)}, u32[]{:S(2)}, u32[]{:S(2)}) collective-permute-start(f32[]{:T(128)} %multiply_reduce_fusion.3), channel_id=1, source_target_pairs={{0,16},{16,0},{32,48},{48,32},{64,80},{80,64},{96,112},{112,96},{1... | collective-permute-start | bytes 20 | tf_op jit(solution)/shard_map/while/body/eval_jaxpr/ppermute | solution.py:33
  64.9 3.0 %collective-permute-start.4 = (f32[2,32,256]{2,0,1:T(2,128)S(1)}, f32[2,32,256]{2,0,1:T(2,128)S(1)}, u32[]{:S(2)}, u32[]{:S(2)}) collective-permute-start(f32[2,32,256]{2,0,1:T(2,128)S(1)} %slice_bitcast_fusion.13), channel_id=1, source_target_pairs={{0,16},{16,32},{32,48},{48,64},{64,80},{80,96},{96,112},{112,0},{1... | collective-permute-start | bytes 196616 | tf_op jit(solution)/shard_map/while/body/eval_jaxpr/ppermute | solution.py:19
  69.2 1.8 collective-permute-start.1
  71.0 1.8 collective-permute-done.1
  73.4 3.0 %collective-permute-start.2 = (f32[]{:T(128)}, f32[]{:T(128)}, u32[]{:S(2)}, u32[]{:S(2)}) collective-permute-start(f32[]{:T(128)} %add.181), channel_id=1, source_target_pairs={{0,64},{16,80},{32,96},{48,112},{64,0},{80,16},{96,32},{112,48},{1... | collective-permute-start | bytes 20 | tf_op jit(solution)/shard_map/while/body/eval_jaxpr/ppermute | solution.py:33
  76.5 2.0 collective-permute-done.2
  82.9 2.2 %collective-permute-done.8 = f32[]{:T(128)} collective-permute-done((f32[]{:T(128)}, f32[]{:T(128)}, u32[]{:S(2)}, u32[]{:S(2)}) %collective-permute-start.8) | collective-permute-done | bytes 36 | tf_op jit(solution)/shard_map/while/body/eval_jaxpr/ppermute | solution.py:33
  85.8 3.4 %collective-permute-start.9 = (f32[]{:T(128)}, f32[]{:T(128)}, u32[]{:S(2)}, u32[]{:S(2)}) collective-permute-start(f32[]{:T(128)} %add.184), channel_id=1, source_target_pairs={{0,8},{2,10},{4,12},{6,14},{8,0},{10,2},{12,4},{14,6},{1,9},{3,11}... | collective-permute-start | bytes 20 | tf_op jit(solution)/shard_map/while/body/eval_jaxpr/ppermute | solution.py:33
  89.2 1.7 collective-permute-done.9
  98.2 2.8 %collective-permute-start.3 = (f32[2,32,256]{2,0,1:T(2,128)S(1)}, f32[2,32,256]{2,0,1:T(2,128)S(1)}, u32[]{:S(2)}, u32[]{:S(2)}) collective-permute-start(f32[2,32,256]{2,0,1:T(2,128)S(1)} %slice_bitcast_fusion.11), channel_id=1, source_target_pairs={{16,0},{32,16},{48,32},{64,48},{80,64},{96,80},{112,96},{0,112},{1... | collective-permute-start | bytes 196616 | tf_op jit(solution)/shard_map/while/body/eval_jaxpr/ppermute | solution.py:21
  103.3 1.7 collective-permute-start.1
  105.0 1.8 collective-permute-done.1
  107.5 4.6 %collective-permute-start.2 = (f32[]{:T(128)}, f32[]{:T(128)}, u32[]{:S(2)}, u32[]{:S(2)}) collective-permute-start(f32[]{:T(128)} %add.181), channel_id=1, source_target_pairs={{0,64},{16,80},{32,96},{48,112},{64,0},{80,16},{96,32},{112,48},{1... | collective-permute-start | bytes 20 | tf_op jit(solution)/shard_map/while/body/eval_jaxpr/ppermute | solution.py:33
  115.6 2.7 %collective-permute-start.8 = (f32[]{:T(128)}, f32[]{:T(128)}, u32[]{:S(2)}, u32[]{:S(2)}) collective-permute-start(f32[]{:T(128)} %add.183), channel_id=1, source_target_pairs={{0,4},{2,6},{4,0},{6,2},{8,12},{10,14},{12,8},{14,10},{1,5},{3,7},... | collective-permute-start | bytes 20 | tf_op jit(solution)/shard_map/while/body/eval_jaxpr/ppermute | solution.py:33
  119.8 4.8 %collective-permute-start.9 = (f32[]{:T(128)}, f32[]{:T(128)}, u32[]{:S(2)}, u32[]{:S(2)}) collective-permute-start(f32[]{:T(128)} %add.184), channel_id=1, source_target_pairs={{0,8},{2,10},{4,12},{6,14},{8,0},{10,2},{12,4},{14,6},{1,9},{3,11}... | collective-permute-start | bytes 20 | tf_op jit(solution)/shard_map/while/body/eval_jaxpr/ppermute | solution.py:33
  130.8 3.0 %collective-permute-start = (f32[]{:T(128)}, f32[]{:T(128)}, u32[]{:S(2)}, u32[]{:S(2)}) collective-permute-start(f32[]{:T(128)} %multiply_reduce_fusion.3), channel_id=1, source_target_pairs={{0,16},{16,0},{32,48},{48,32},{64,80},{80,64},{96,112},{112,96},{1... | collective-permute-start | bytes 20 | tf_op jit(solution)/shard_map/while/body/eval_jaxpr/ppermute | solution.py:33
  133.9 1.8 collective-permute-start.3
  135.8 1.8 collective-permute-start.4
  139.0 1.8 collective-permute-start.1
  140.7 1.8 collective-permute-done.1
  143.2 3.2 %collective-permute-start.2 = (f32[]{:T(128)}, f32[]{:T(128)}, u32[]{:S(2)}, u32[]{:S(2)}) collective-permute-start(f32[]{:T(128)} %add.181), channel_id=1, source_target_pairs={{0,64},{16,80},{32,96},{48,112},{64,0},{80,16},{96,32},{112,48},{1... | collective-permute-start | bytes 20 | tf_op jit(solution)/shard_map/while/body/eval_jaxpr/ppermute | solution.py:33
  146.3 1.9 collective-permute-done.2
  149.6 1.8 collective-permute-start.7
  152.0 3.4 %collective-permute-start.8 = (f32[]{:T(128)}, f32[]{:T(128)}, u32[]{:S(2)}, u32[]{:S(2)}) collective-permute-start(f32[]{:T(128)} %add.183), channel_id=1, source_target_pairs={{0,4},{2,6},{4,0},{6,2},{8,12},{10,14},{12,8},{14,10},{1,5},{3,7},... | collective-permute-start | bytes 20 | tf_op jit(solution)/shard_map/while/body/eval_jaxpr/ppermute | solution.py:33
  156.2 4.1 %collective-permute-start.9 = (f32[]{:T(128)}, f32[]{:T(128)}, u32[]{:S(2)}, u32[]{:S(2)}) collective-permute-start(f32[]{:T(128)} %add.184), channel_id=1, source_target_pairs={{0,8},{2,10},{4,12},{6,14},{8,0},{10,2},{12,4},{14,6},{1,9},{3,11}... | collective-permute-start | bytes 20 | tf_op jit(solution)/shard_map/while/body/eval_jaxpr/ppermute | solution.py:33
  166.5 1.6 select_reduce_fusion
  172.8 2.4 %collective-permute-start.21 = (f32[2]{0:T(128)S(1)}, f32[2]{0:T(128)S(1)}, u32[]{:S(2)}, u32[]{:S(2)}) collective-permute-start(f32[2]{0:T(128)S(1)} %pad_maximum_fusion.16), channel_id=1, source_target_pairs={{0,16},{16,0},{32,48},{48,32},{64,80},{80,64},{96,112},{112,96},{1... | collective-permute-start | bytes 32 | tf_op jit(solution)/shard_map/ppermute | solution.py:33
  179.3 1.7 collective-permute-start.22
  182.1 2.3 %collective-permute-start.17 = (bf16[16,2304]{1,0:T(8,128)(2,1)S(1)}, bf16[16,2304]{1,0:T(8,128)(2,1)S(1)}, u32[]{:S(2)}, u32[]{:S(2)}) collective-permute-start(bf16[16,2304]{1,0:T(8,128)(2,1)S(1)} %dynamic-slice_convert_fusion.3), channel_id=1, source_target_pairs={{0,8},{2,10},{4,12},{6,14},{8,0},{10,2},{12,4},{14,6},{1,9},{3,11}... | collective-permute-start | bytes 221192 | tf_op jit(solution)/shard_map/ppermute | solution.py:89
  185.8 3.7 %collective-permute-start.23 = (f32[2]{0:T(128)S(1)}, f32[2]{0:T(128)S(1)}, u32[]{:S(2)}, u32[]{:S(2)}) collective-permute-start(f32[2]{0:T(128)S(1)} %fusion.81), channel_id=1, source_target_pairs={{0,64},{16,80},{32,96},{48,112},{64,0},{80,16},{96,32},{112,48},{1... | collective-permute-start | bytes 32 | tf_op jit(solution)/shard_map/ppermute | solution.py:33
  189.5 1.5 collective-permute-done.23
  192.4 3.2 %collective-permute-done.25 = f32[2]{0:T(128)S(1)} collective-permute-done((f32[2]{0:T(128)S(1)}, f32[2]{0:T(128)S(1)}, u32[]{:S(2)}, u32[]{:S(2)}) %collective-permute-start.25) | collective-permute-done | bytes 40 | tf_op jit(solution)/shard_map/ppermute | solution.py:33
  197.1 3.6 %collective-permute-done.26 = f32[2]{0:T(128)S(1)} collective-permute-done((f32[2]{0:T(128)S(1)}, f32[2]{0:T(128)S(1)}, u32[]{:S(2)}, u32[]{:S(2)}) %collective-permute-start.26) | collective-permute-done | bytes 40 | tf_op jit(solution)/shard_map/ppermute | solution.py:33
  202.4 2.7 %collective-permute-done.18 = f32[8,2304]{1,0:T(8,128)S(1)} collective-permute-done((f32[8,2304]{1,0:T(8,128)S(1)}, f32[8,2304]{1,0:T(8,128)S(1)}, u32[]{:S(2)}, u32[]{:S(2)}) %collective-permute-start.18) | collective-permute-done | bytes 73760 | tf_op jit(solution)/shard_map/ppermute | solution.py:89
  206.5 1.6 collective-permute-start.20
  (252 shorter events, 61.6 us)
Async XLA Ops:
  4.2 16.3 %copy-start.1 = (bf16[16,32,256]{2,0,1:T(8,128)(2,1)}, bf16[16,32,256]{2,0,1:T(8,128)(2,1)S(1)}, u32[]{:S(2)}) copy-start(bf16[16,32,256]{2,0,1:T(8,128)(2,1)S(1)} %copy.69) | copy-start | bytes 786436
  4.3 9.7 %collective-permute-start.11 = (bf16[320,256]{1,0:T(8,128)(2,1)S(1)}, bf16[320,256]{1,0:T(8,128)(2,1)S(1)}, u32[]{:S(2)}, u32[]{:S(2)}) collective-permute-start(bf16[320,256]{1,0:T(8,128)(2,1)S(1)} %pad_maximum_fusion.4), channel_id=1, source_target_pairs={{16,0},{32,16},{48,32},{64,48},{80,64},{96,80},{112,96},{0,112},{1... | collective-permute-start | bytes 491528 | tf_op jit(solution)/shard_map/ppermute | solution.py:57
  10.6 9.5 %collective-permute-start.10 = (bf16[320,256]{1,0:T(8,128)(2,1)S(1)}, bf16[320,256]{1,0:T(8,128)(2,1)S(1)}, u32[]{:S(2)}, u32[]{:S(2)}) collective-permute-start(bf16[320,256]{1,0:T(8,128)(2,1)S(1)} %pad_maximum_fusion.3), channel_id=1, source_target_pairs={{0,16},{16,32},{32,48},{48,64},{64,80},{80,96},{96,112},{112,0},{1... | collective-permute-start | bytes 491528 | tf_op jit(solution)/shard_map/ppermute | solution.py:57
  20.6 3.5 %collective-permute-start.13 = (bf16[184,256]{1,0:T(8,128)(2,1)S(1)}, bf16[184,256]{1,0:T(8,128)(2,1)S(1)}, u32[]{:S(2)}, u32[]{:S(2)}) collective-permute-start(bf16[184,256]{1,0:T(8,128)(2,1)S(1)} %pad_maximum_fusion.8), channel_id=1, source_target_pairs={{2,0},{4,2},{6,4},{8,6},{10,8},{12,10},{14,12},{0,14},{3,1},{5,3},... | collective-permute-start | bytes 282632 | tf_op jit(solution)/shard_map/ppermute | solution.py:57
  22.0 5.2 %collective-permute-start.12 = (bf16[184,256]{1,0:T(8,128)(2,1)S(1)}, bf16[184,256]{1,0:T(8,128)(2,1)S(1)}, u32[]{:S(2)}, u32[]{:S(2)}) collective-permute-start(bf16[184,256]{1,0:T(8,128)(2,1)S(1)} %pad_maximum_fusion.7), channel_id=1, source_target_pairs={{0,2},{2,4},{4,6},{6,8},{8,10},{10,12},{12,14},{14,0},{1,3},{3,5},... | collective-permute-start | bytes 282632 | tf_op jit(solution)/shard_map/ppermute | solution.py:57
  56.4 108.9 %collective-permute-start.14 = (bf16[128,2304]{1,0:T(8,128)(2,1)S(1)}, bf16[128,2304]{1,0:T(8,128)(2,1)S(1)}, u32[]{:S(2)}, u32[]{:S(2)}) collective-permute-start(bf16[128,2304]{1,0:T(8,128)(2,1)S(1)} %dynamic-slice_convert_fusion), channel_id=1, source_target_pairs={{0,64},{16,80},{32,96},{48,112},{64,0},{80,16},{96,32},{112,48},{1... | collective-permute-start | bytes 1769480 | tf_op jit(solution)/shard_map/ppermute | solution.py:89
  61.1 6.9 %collective-permute-start = (f32[]{:T(128)}, f32[]{:T(128)}, u32[]{:S(2)}, u32[]{:S(2)}) collective-permute-start(f32[]{:T(128)} %multiply_reduce_fusion.3), channel_id=1, source_target_pairs={{0,16},{16,0},{32,48},{48,32},{64,80},{80,64},{96,112},{112,96},{1... | collective-permute-start | bytes 20 | tf_op jit(solution)/shard_map/while/body/eval_jaxpr/ppermute | solution.py:33
  64.2 15.0 %collective-permute-start.3 = (f32[2,32,256]{2,0,1:T(2,128)S(1)}, f32[2,32,256]{2,0,1:T(2,128)S(1)}, u32[]{:S(2)}, u32[]{:S(2)}) collective-permute-start(f32[2,32,256]{2,0,1:T(2,128)S(1)} %slice_bitcast_fusion.11), channel_id=1, source_target_pairs={{16,0},{32,16},{48,32},{64,48},{80,64},{96,80},{112,96},{0,112},{1... | collective-permute-start | bytes 196616 | tf_op jit(solution)/shard_map/while/body/eval_jaxpr/ppermute | solution.py:21
  64.9 14.3 %collective-permute-start.4 = (f32[2,32,256]{2,0,1:T(2,128)S(1)}, f32[2,32,256]{2,0,1:T(2,128)S(1)}, u32[]{:S(2)}, u32[]{:S(2)}) collective-permute-start(f32[2,32,256]{2,0,1:T(2,128)S(1)} %slice_bitcast_fusion.13), channel_id=1, source_target_pairs={{0,16},{16,32},{32,48},{48,64},{64,80},{80,96},{96,112},{112,0},{1... | collective-permute-start | bytes 196616 | tf_op jit(solution)/shard_map/while/body/eval_jaxpr/ppermute | solution.py:19
  69.2 3.6 %collective-permute-start.1 = (f32[]{:T(128)}, f32[]{:T(128)}, u32[]{:S(2)}, u32[]{:S(2)}) collective-permute-start(f32[]{:T(128)} %add.180), channel_id=1, source_target_pairs={{0,32},{16,48},{32,0},{48,16},{64,96},{80,112},{96,64},{112,80},{1... | collective-permute-start | bytes 20 | tf_op jit(solution)/shard_map/while/body/eval_jaxpr/ppermute | solution.py:33
  73.4 5.1 %collective-permute-start.2 = (f32[]{:T(128)}, f32[]{:T(128)}, u32[]{:S(2)}, u32[]{:S(2)}) collective-permute-start(f32[]{:T(128)} %add.181), channel_id=1, source_target_pairs={{0,64},{16,80},{32,96},{48,112},{64,0},{80,16},{96,32},{112,48},{1... | collective-permute-start | bytes 20 | tf_op jit(solution)/shard_map/while/body/eval_jaxpr/ppermute | solution.py:33
  79.3 13.1 %collective-permute-start.5 = (f32[20,2,256]{2,0,1:T(8,128)S(1)}, f32[20,2,256]{2,0,1:T(8,128)S(1)}, u32[]{:S(2)}, u32[]{:S(2)}) collective-permute-start(f32[20,2,256]{2,0,1:T(8,128)S(1)} %get-tuple-element.121), channel_id=1, source_target_pairs={{2,0},{4,2},{6,4},{8,6},{10,8},{12,10},{14,12},{0,14},{3,1},{5,3},... | collective-permute-start | bytes 122888 | tf_op jit(solution)/shard_map/while/body/eval_jaxpr/ppermute | solution.py:21
  79.3 13.0 %collective-permute-start.6 = (f32[20,2,256]{2,0,1:T(8,128)S(1)}, f32[20,2,256]{2,0,1:T(8,128)S(1)}, u32[]{:S(2)}, u32[]{:S(2)}) collective-permute-start(f32[20,2,256]{2,0,1:T(8,128)S(1)} %get-tuple-element.122), channel_id=1, source_target_pairs={{0,2},{2,4},{4,6},{6,8},{8,10},{10,12},{12,14},{14,0},{1,3},{3,5},... | collective-permute-start | bytes 122888 | tf_op jit(solution)/shard_map/while/body/eval_jaxpr/ppermute | solution.py:19
  79.8 1.1 collective-permute-start.7
  81.6 3.6 %collective-permute-start.8 = (f32[]{:T(128)}, f32[]{:T(128)}, u32[]{:S(2)}, u32[]{:S(2)}) collective-permute-start(f32[]{:T(128)} %add.183), channel_id=1, source_target_pairs={{0,4},{2,6},{4,0},{6,2},{8,12},{10,14},{12,8},{14,10},{1,5},{3,7},... | collective-permute-start | bytes 20 | tf_op jit(solution)/shard_map/while/body/eval_jaxpr/ppermute | solution.py:33
  85.8 5.1 %collective-permute-start.9 = (f32[]{:T(128)}, f32[]{:T(128)}, u32[]{:S(2)}, u32[]{:S(2)}) collective-permute-start(f32[]{:T(128)} %add.184), channel_id=1, source_target_pairs={{0,8},{2,10},{4,12},{6,14},{8,0},{10,2},{12,4},{14,6},{1,9},{3,11}... | collective-permute-start | bytes 20 | tf_op jit(solution)/shard_map/while/body/eval_jaxpr/ppermute | solution.py:33
  96.7 5.3 %collective-permute-start = (f32[]{:T(128)}, f32[]{:T(128)}, u32[]{:S(2)}, u32[]{:S(2)}) collective-permute-start(f32[]{:T(128)} %multiply_reduce_fusion.3), channel_id=1, source_target_pairs={{0,16},{16,0},{32,48},{48,32},{64,80},{80,64},{96,112},{112,96},{1... | collective-permute-start | bytes 20 | tf_op jit(solution)/shard_map/while/body/eval_jaxpr/ppermute | solution.py:33
  98.2 15.0 %collective-permute-start.3 = (f32[2,32,256]{2,0,1:T(2,128)S(1)}, f32[2,32,256]{2,0,1:T(2,128)S(1)}, u32[]{:S(2)}, u32[]{:S(2)}) collective-permute-start(f32[2,32,256]{2,0,1:T(2,128)S(1)} %slice_bitcast_fusion.11), channel_id=1, source_target_pairs={{16,0},{32,16},{48,32},{64,48},{80,64},{96,80},{112,96},{0,112},{1... | collective-permute-start | bytes 196616 | tf_op jit(solution)/shard_map/while/body/eval_jaxpr/ppermute | solution.py:21
  101.1 12.2 %collective-permute-start.4 = (f32[2,32,256]{2,0,1:T(2,128)S(1)}, f32[2,32,256]{2,0,1:T(2,128)S(1)}, u32[]{:S(2)}, u32[]{:S(2)}) collective-permute-start(f32[2,32,256]{2,0,1:T(2,128)S(1)} %slice_bitcast_fusion.13), channel_id=1, source_target_pairs={{0,16},{16,32},{32,48},{48,64},{64,80},{80,96},{96,112},{112,0},{1... | collective-permute-start | bytes 196616 | tf_op jit(solution)/shard_map/while/body/eval_jaxpr/ppermute | solution.py:19
  103.3 3.6 %collective-permute-start.1 = (f32[]{:T(128)}, f32[]{:T(128)}, u32[]{:S(2)}, u32[]{:S(2)}) collective-permute-start(f32[]{:T(128)} %add.180), channel_id=1, source_target_pairs={{0,32},{16,48},{32,0},{48,16},{64,96},{80,112},{96,64},{112,80},{1... | collective-permute-start | bytes 20 | tf_op jit(solution)/shard_map/while/body/eval_jaxpr/ppermute | solution.py:33
  107.5 5.1 %collective-permute-start.2 = (f32[]{:T(128)}, f32[]{:T(128)}, u32[]{:S(2)}, u32[]{:S(2)}) collective-permute-start(f32[]{:T(128)} %add.181), channel_id=1, source_target_pairs={{0,64},{16,80},{32,96},{48,112},{64,0},{80,16},{96,32},{112,48},{1... | collective-permute-start | bytes 20 | tf_op jit(solution)/shard_map/while/body/eval_jaxpr/ppermute | solution.py:33
  113.4 13.1 %collective-permute-start.5 = (f32[20,2,256]{2,0,1:T(8,128)S(1)}, f32[20,2,256]{2,0,1:T(8,128)S(1)}, u32[]{:S(2)}, u32[]{:S(2)}) collective-permute-start(f32[20,2,256]{2,0,1:T(8,128)S(1)} %get-tuple-element.121), channel_id=1, source_target_pairs={{2,0},{4,2},{6,4},{8,6},{10,8},{12,10},{14,12},{0,14},{3,1},{5,3},... | collective-permute-start | bytes 122888 | tf_op jit(solution)/shard_map/while/body/eval_jaxpr/ppermute | solution.py:21
  113.4 13.0 %collective-permute-start.6 = (f32[20,2,256]{2,0,1:T(8,128)S(1)}, f32[20,2,256]{2,0,1:T(8,128)S(1)}, u32[]{:S(2)}, u32[]{:S(2)}) collective-permute-start(f32[20,2,256]{2,0,1:T(8,128)S(1)} %get-tuple-element.122), channel_id=1, source_target_pairs={{0,2},{2,4},{4,6},{6,8},{8,10},{10,12},{12,14},{14,0},{1,3},{3,5},... | collective-permute-start | bytes 122888 | tf_op jit(solution)/shard_map/while/body/eval_jaxpr/ppermute | solution.py:19
  113.9 1.1 collective-permute-start.7
  115.6 3.6 %collective-permute-start.8 = (f32[]{:T(128)}, f32[]{:T(128)}, u32[]{:S(2)}, u32[]{:S(2)}) collective-permute-start(f32[]{:T(128)} %add.183), channel_id=1, source_target_pairs={{0,4},{2,6},{4,0},{6,2},{8,12},{10,14},{12,8},{14,10},{1,5},{3,7},... | collective-permute-start | bytes 20 | tf_op jit(solution)/shard_map/while/body/eval_jaxpr/ppermute | solution.py:33
  119.8 5.1 %collective-permute-start.9 = (f32[]{:T(128)}, f32[]{:T(128)}, u32[]{:S(2)}, u32[]{:S(2)}) collective-permute-start(f32[]{:T(128)} %add.184), channel_id=1, source_target_pairs={{0,8},{2,10},{4,12},{6,14},{8,0},{10,2},{12,4},{14,6},{1,9},{3,11}... | collective-permute-start | bytes 20 | tf_op jit(solution)/shard_map/while/body/eval_jaxpr/ppermute | solution.py:33
  130.8 6.9 %collective-permute-start = (f32[]{:T(128)}, f32[]{:T(128)}, u32[]{:S(2)}, u32[]{:S(2)}) collective-permute-start(f32[]{:T(128)} %multiply_reduce_fusion.3), channel_id=1, source_target_pairs={{0,16},{16,0},{32,48},{48,32},{64,80},{80,64},{96,112},{112,96},{1... | collective-permute-start | bytes 20 | tf_op jit(solution)/shard_map/while/body/eval_jaxpr/ppermute | solution.py:33
  133.9 15.0 %collective-permute-start.3 = (f32[2,32,256]{2,0,1:T(2,128)S(1)}, f32[2,32,256]{2,0,1:T(2,128)S(1)}, u32[]{:S(2)}, u32[]{:S(2)}) collective-permute-start(f32[2,32,256]{2,0,1:T(2,128)S(1)} %slice_bitcast_fusion.11), channel_id=1, source_target_pairs={{16,0},{32,16},{48,32},{64,48},{80,64},{96,80},{112,96},{0,112},{1... | collective-permute-start | bytes 196616 | tf_op jit(solution)/shard_map/while/body/eval_jaxpr/ppermute | solution.py:21
  135.8 13.1 %collective-permute-start.4 = (f32[2,32,256]{2,0,1:T(2,128)S(1)}, f32[2,32,256]{2,0,1:T(2,128)S(1)}, u32[]{:S(2)}, u32[]{:S(2)}) collective-permute-start(f32[2,32,256]{2,0,1:T(2,128)S(1)} %slice_bitcast_fusion.13), channel_id=1, source_target_pairs={{0,16},{16,32},{32,48},{48,64},{64,80},{80,96},{96,112},{112,0},{1... | collective-permute-start | bytes 196616 | tf_op jit(solution)/shard_map/while/body/eval_jaxpr/ppermute | solution.py:19
  139.0 3.6 %collective-permute-start.1 = (f32[]{:T(128)}, f32[]{:T(128)}, u32[]{:S(2)}, u32[]{:S(2)}) collective-permute-start(f32[]{:T(128)} %add.180), channel_id=1, source_target_pairs={{0,32},{16,48},{32,0},{48,16},{64,96},{80,112},{96,64},{112,80},{1... | collective-permute-start | bytes 20 | tf_op jit(solution)/shard_map/while/body/eval_jaxpr/ppermute | solution.py:33
  143.2 5.1 %collective-permute-start.2 = (f32[]{:T(128)}, f32[]{:T(128)}, u32[]{:S(2)}, u32[]{:S(2)}) collective-permute-start(f32[]{:T(128)} %add.181), channel_id=1, source_target_pairs={{0,64},{16,80},{32,96},{48,112},{64,0},{80,16},{96,32},{112,48},{1... | collective-permute-start | bytes 20 | tf_op jit(solution)/shard_map/while/body/eval_jaxpr/ppermute | solution.py:33
  149.0 13.8 %collective-permute-start.5 = (f32[20,2,256]{2,0,1:T(8,128)S(1)}, f32[20,2,256]{2,0,1:T(8,128)S(1)}, u32[]{:S(2)}, u32[]{:S(2)}) collective-permute-start(f32[20,2,256]{2,0,1:T(8,128)S(1)} %get-tuple-element.121), channel_id=1, source_target_pairs={{2,0},{4,2},{6,4},{8,6},{10,8},{12,10},{14,12},{0,14},{3,1},{5,3},... | collective-permute-start | bytes 122888 | tf_op jit(solution)/shard_map/while/body/eval_jaxpr/ppermute | solution.py:21
  149.1 13.7 %collective-permute-start.6 = (f32[20,2,256]{2,0,1:T(8,128)S(1)}, f32[20,2,256]{2,0,1:T(8,128)S(1)}, u32[]{:S(2)}, u32[]{:S(2)}) collective-permute-start(f32[20,2,256]{2,0,1:T(8,128)S(1)} %get-tuple-element.122), channel_id=1, source_target_pairs={{0,2},{2,4},{4,6},{6,8},{8,10},{10,12},{12,14},{14,0},{1,3},{3,5},... | collective-permute-start | bytes 122888 | tf_op jit(solution)/shard_map/while/body/eval_jaxpr/ppermute | solution.py:19
  149.6 1.8 collective-permute-start.7
  152.0 3.6 %collective-permute-start.8 = (f32[]{:T(128)}, f32[]{:T(128)}, u32[]{:S(2)}, u32[]{:S(2)}) collective-permute-start(f32[]{:T(128)} %add.183), channel_id=1, source_target_pairs={{0,4},{2,6},{4,0},{6,2},{8,12},{10,14},{12,8},{14,10},{1,5},{3,7},... | collective-permute-start | bytes 20 | tf_op jit(solution)/shard_map/while/body/eval_jaxpr/ppermute | solution.py:33
  156.2 5.1 %collective-permute-start.9 = (f32[]{:T(128)}, f32[]{:T(128)}, u32[]{:S(2)}, u32[]{:S(2)}) collective-permute-start(f32[]{:T(128)} %add.184), channel_id=1, source_target_pairs={{0,8},{2,10},{4,12},{6,14},{8,0},{10,2},{12,4},{14,6},{1,9},{3,11}... | collective-permute-start | bytes 20 | tf_op jit(solution)/shard_map/while/body/eval_jaxpr/ppermute | solution.py:33
  166.0 9.2 %collective-permute-start.15 = (bf16[64,2304]{1,0:T(8,128)(2,1)S(1)}, bf16[64,2304]{1,0:T(8,128)(2,1)S(1)}, u32[]{:S(2)}, u32[]{:S(2)}) collective-permute-start(bf16[64,2304]{1,0:T(8,128)(2,1)S(1)} %dynamic-slice_convert_fusion.1), channel_id=1, source_target_pairs={{0,32},{16,48},{32,0},{48,16},{64,96},{80,112},{96,64},{112,80},{1... | collective-permute-start | bytes 884744 | tf_op jit(solution)/shard_map/ppermute | solution.py:89
  172.8 5.1 %collective-permute-start.21 = (f32[2]{0:T(128)S(1)}, f32[2]{0:T(128)S(1)}, u32[]{:S(2)}, u32[]{:S(2)}) collective-permute-start(f32[2]{0:T(128)S(1)} %pad_maximum_fusion.16), channel_id=1, source_target_pairs={{0,16},{16,0},{32,48},{48,32},{64,80},{80,64},{96,112},{112,96},{1... | collective-permute-start | bytes 32 | tf_op jit(solution)/shard_map/ppermute | solution.py:33
  175.3 6.7 %collective-permute-start.16 = (bf16[32,2304]{1,0:T(8,128)(2,1)S(1)}, bf16[32,2304]{1,0:T(8,128)(2,1)S(1)}, u32[]{:S(2)}, u32[]{:S(2)}) collective-permute-start(bf16[32,2304]{1,0:T(8,128)(2,1)S(1)} %dynamic-slice_convert_fusion.2), channel_id=1, source_target_pairs={{0,16},{16,0},{32,48},{48,32},{64,80},{80,64},{96,112},{112,96},{1... | collective-permute-start | bytes 442376 | tf_op jit(solution)/shard_map/ppermute | solution.py:89
  179.3 5.1 %collective-permute-start.22 = (f32[2]{0:T(128)S(1)}, f32[2]{0:T(128)S(1)}, u32[]{:S(2)}, u32[]{:S(2)}) collective-permute-start(f32[2]{0:T(128)S(1)} %fusion.80), channel_id=1, source_target_pairs={{0,32},{16,48},{32,0},{48,16},{64,96},{80,112},{96,64},{112,80},{1... | collective-permute-start | bytes 32 | tf_op jit(solution)/shard_map/ppermute | solution.py:33
  182.1 18.6 %collective-permute-start.17 = (bf16[16,2304]{1,0:T(8,128)(2,1)S(1)}, bf16[16,2304]{1,0:T(8,128)(2,1)S(1)}, u32[]{:S(2)}, u32[]{:S(2)}) collective-permute-start(bf16[16,2304]{1,0:T(8,128)(2,1)S(1)} %dynamic-slice_convert_fusion.3), channel_id=1, source_target_pairs={{0,8},{2,10},{4,12},{6,14},{8,0},{10,2},{12,4},{14,6},{1,9},{3,11}... | collective-permute-start | bytes 221192 | tf_op jit(solution)/shard_map/ppermute | solution.py:89
  185.8 5.2 %collective-permute-start.23 = (f32[2]{0:T(128)S(1)}, f32[2]{0:T(128)S(1)}, u32[]{:S(2)}, u32[]{:S(2)}) collective-permute-start(f32[2]{0:T(128)S(1)} %fusion.81), channel_id=1, source_target_pairs={{0,64},{16,80},{32,96},{48,112},{64,0},{80,16},{96,32},{112,48},{1... | collective-permute-start | bytes 32 | tf_op jit(solution)/shard_map/ppermute | solution.py:33
  191.0 1.1 collective-permute-start.24
  192.1 3.5 %collective-permute-start.25 = (f32[2]{0:T(128)S(1)}, f32[2]{0:T(128)S(1)}, u32[]{:S(2)}, u32[]{:S(2)}) collective-permute-start(f32[2]{0:T(128)S(1)} %add.156), channel_id=1, source_target_pairs={{0,4},{2,6},{4,0},{6,2},{8,12},{10,14},{12,8},{14,10},{1,5},{3,7},... | collective-permute-start | bytes 32 | tf_op jit(solution)/shard_map/ppermute | solution.py:33
  195.6 5.0 %collective-permute-start.26 = (f32[2]{0:T(128)S(1)}, f32[2]{0:T(128)S(1)}, u32[]{:S(2)}, u32[]{:S(2)}) collective-permute-start(f32[2]{0:T(128)S(1)} %add.157), channel_id=1, source_target_pairs={{0,8},{2,10},{4,12},{6,14},{8,0},{10,2},{12,4},{14,6},{1,9},{3,11}... | collective-permute-start | bytes 32 | tf_op jit(solution)/shard_map/ppermute | solution.py:33
  200.7 4.4 %collective-permute-start.18 = (f32[8,2304]{1,0:T(8,128)S(1)}, f32[8,2304]{1,0:T(8,128)S(1)}, u32[]{:S(2)}, u32[]{:S(2)}) collective-permute-start(f32[8,2304]{1,0:T(8,128)S(1)} %constant_dynamic-slice_fusion.1), channel_id=1, source_target_pairs={{0,4},{2,6},{4,0},{6,2},{8,12},{10,14},{12,8},{14,10},{1,5},{3,7},... | collective-permute-start | bytes 221192 | tf_op jit(solution)/shard_map/ppermute | solution.py:89
  205.2 1.3 collective-permute-start.19
  206.5 4.1 %collective-permute-start.20 = (f32[4,2304]{1,0:T(4,128)S(1)}, f32[4,2304]{1,0:T(4,128)S(1)}, u32[]{:S(2)}, u32[]{:S(2)}) collective-permute-start(f32[4,2304]{1,0:T(4,128)S(1)} %dynamic-slice_add_fusion.1), channel_id=1, source_target_pairs={{0,1},{1,0},{2,3},{3,2},{4,5},{5,4},{6,7},{7,6},{8,9},{9,8},{10,11... | collective-permute-start | bytes 110600 | tf_op jit(solution)/shard_map/ppermute | solution.py:33
  (27 other events, 61.9 us)

commit v11 on v10

--- a/solution.py
+++ b/solution.py
@@ -84,8 +84,7 @@
             upper = (index // step) % 2
             keep = lax.dynamic_slice_in_dim(value, upper * half, half, axis=0)
             send = lax.dynamic_slice_in_dim(value, (1 - upper) * half, half, axis=0)
-            if send.size * 32 > 256 * 2304:
-                send = send.astype(jnp.bfloat16)
+            send = send.astype(jnp.bfloat16)
             received = lax.ppermute(send, axis, [(i, i ^ step) for i in range(count)])
             value = keep + received.astype(jnp.float32)
             step //= 2

time: 214 us -> 214 us (level)
  no operation moved by 1% of the time
where the time goes in v11:
time: 214 us; the launch traced here: 212 us
  starting transfers between devices  82.7 us (39%)
  waiting for transfers between devices  45.8 us (21%)
  local copies, waits for them, and re-layouts  27.4 us (13%)
  matrix products  22.1 us (10%)
  other arithmetic  14.8 us (7%)
  loops' own time  14.2 us (7%)
  between operations  4.93 us (2%)
    ppermute x25, starting transfers between devices, butterfly_sum(): lax.ppermute(value, axis, [(i, i ^ step) for i in range(count)])  57.8 us
    ppermute x25, waiting for transfers between devices, butterfly_sum(): lax.ppermute(value, axis, [(i, i ^ step) for i in range(count)])  27.4 us
    conv_general_dilated x10, matrix products, conv(): lax.conv_general_dilated(padded, weights, window_strides=(1, 1), padding=...  15.1 us
    another operation x1, loops' own time, per_device(): lax.scan(power_step, (padded_probe, iterate), None, length=ITERS - 1)  14.2 us
    ppermute x4, waiting for transfers between devices, travel(): moved = lax.ppermute(flat, axis, pairs)  14 us
    unnamed x52, local copies, waits for them, and re-layouts  9.35 us
    ppermute x4, starting transfers between devices, travel(): moved = lax.ppermute(flat, axis, pairs)  7.77 us
    ppermute x6, starting transfers between devices, extended(): lax.ppermute(tail, axis, [(i, (i + 1) % count) for i in range(ends)])  7.25 us
  transfers between devices with their start and end apart: 47, of which 26 were waited for; matrix products, arithmetic and copies ran while one was open for 12% of the time, Pallas kernels for 0%

profile of v11, /device:TPU:0, one launch (start us, length us, event | category | flops | bytes accessed | tf_op | source)
XLA Modules:
  0.0 212.0 jit_solution(11802882819162344739)
XLA Ops:
  0.6 2.2 %copy.25 = bf16[4,16,32,256]{3,0,2,1:T(4,128)(2,1)S(1)} copy(bf16[4,16,32,256]{3,2,1,0:T(8,128)(2,1)} %param.7) | data formatting | bytes 2097152 | tf_op args[1]
  4.3 6.2 %collective-permute-start.11 = (bf16[320,256]{1,0:T(8,128)(2,1)S(1)}, bf16[320,256]{1,0:T(8,128)(2,1)S(1)}, u32[]{:S(2)}, u32[]{:S(2)}) collective-permute-start(bf16[320,256]{1,0:T(8,128)(2,1)S(1)} %pad_maximum_fusion.4), channel_id=1, source_target_pairs={{16,0},{32,16},{48,32},{64,48},{80,64},{96,80},{112,96},{0,112},{1... | collective-permute-start | bytes 491528 | tf_op jit(solution)/shard_map/ppermute | solution.py:57
  11.1 2.9 %collective-permute-done.11 = bf16[320,256]{1,0:T(8,128)(2,1)S(1)} collective-permute-done((bf16[320,256]{1,0:T(8,128)(2,1)S(1)}, bf16[320,256]{1,0:T(8,128)(2,1)S(1)}, u32[]{:S(2)}, u32[]{:S(2)}) %collective-permute-start.11) | collective-permute-done | bytes 163872 | tf_op jit(solution)/shard_map/ppermute | solution.py:57
  14.2 6.0 %collective-permute-done.10 = bf16[320,256]{1,0:T(8,128)(2,1)S(1)} collective-permute-done((bf16[320,256]{1,0:T(8,128)(2,1)S(1)}, bf16[320,256]{1,0:T(8,128)(2,1)S(1)}, u32[]{:S(2)}, u32[]{:S(2)}) %collective-permute-start.10) | collective-permute-done | bytes 163872 | tf_op jit(solution)/shard_map/ppermute | solution.py:57
  22.1 2.0 collective-permute-done.13
  24.2 3.1 %collective-permute-done.12 = bf16[184,256]{1,0:T(8,128)(2,1)S(1)} collective-permute-done((bf16[184,256]{1,0:T(8,128)(2,1)S(1)}, bf16[184,256]{1,0:T(8,128)(2,1)S(1)}, u32[]{:S(2)}, u32[]{:S(2)}) %collective-permute-start.12) | collective-permute-done | bytes 94240 | tf_op jit(solution)/shard_map/ppermute | solution.py:57
  28.6 6.9 %fusion.46 = f32[256,3,3,256]{0,3,2,1:T(8,128)} fusion(bf16[8,18,34,256]{3,0,2,1:T(8,128)(2,1)S(1)} %pad_maximum_fusion.1, bf16[4,16,32,256]{3,2,1,0:T(8,128)(2,1)S(1)} %copy-done.8), kind=kOutput, calls=%fused_computation.63 | convolution fusion | flops 2415919104 | bytes 4661248 | tf_op jit(solution)/shard_map/conv_general_dilated | solution.py:142
  38.6 3.3 %select_convert_fusion = bf16[16,32,5,256]{3,1,2,0:T(8,128)(2,1)S(1)} fusion(bf16[3,3,256,256]{3,2,1,0:T(8,128)(2,1)S(1)} %copy-done.16, bf16[18,4,8,7,256]{4,1,3,2,0:T(4,128)(2,1)S(1)} %fusion.30, pred[32,5]{0,1:T(8,128)(4,1)S(1)} %copy-done.23), kind=kOutput, calls=%fused_computation.38 | convolution fusion | flops 3021209600 | bytes 4554912 | tf_op jit(solution)/shard_map/conv_general_dilated | solution.py:97
  41.8 1.8 copy.43
  45.6 3.2 %select_convert_fusion.1 = bf16[16,32,5,256]{3,1,2,0:T(8,128)(2,1)S(1)} fusion(bf16[3,3,256,256]{3,2,1,0:T(8,128)(2,1)S(1)} %copy-done.16, bf16[18,4,8,7,256]{4,1,3,2,0:T(4,128)(2,1)S(1)} %fusion.29, pred[32,5]{0,1:T(8,128)(4,1)S(1)} %copy-done.23), kind=kOutput, calls=%fused_computation.39 | convolution fusion | flops 3021209600 | bytes 4554912 | tf_op jit(solution)/shard_map/conv_general_dilated | solution.py:97
  50.2 1.5 slice_bitcast_fusion.4
  52.0 3.1 %copy.46 = f32[256,2304]{1,0:T(8,128)} copy(f32[256,2304]{0,1:T(8,128)} %bitcast.130) | data formatting | bytes 4718592 | tf_op jit(solution)/shard_map/optimization_barrier | solution.py:150
  56.5 106.4 %while.14 = (s32[]{:T(128)}, bf16[20,36,256]{2,0,1:T(8,128)(2,1)S(1)}, bf16[16,32,256]{2,0,1:T(8,128)(2,1)}, f32[3]{0:T(128)S(1)}, bf16[3,3,256,256]{3,2,1,0:T(8...) while((s32[]{:T(128)}, bf16[20,36,256]{2,0,1:T(8,128)(2,1)S(1)}, ...), condition=%wide.region_2.3_spmd, body=%wide.region_0.2_spmd.sunk | while | flops 1609732096 | bytes 19315492 | solution.py:153
  61.1 3.0 %collective-permute-start = (f32[]{:T(128)}, f32[]{:T(128)}, u32[]{:S(2)}, u32[]{:S(2)}) collective-permute-start(f32[]{:T(128)} %multiply_reduce_fusion.3), channel_id=1, source_target_pairs={{0,16},{16,0},{32,48},{48,32},{64,80},{80,64},{96,112},{112,96},{1... | collective-permute-start | bytes 20 | tf_op jit(solution)/shard_map/while/body/eval_jaxpr/ppermute | solution.py:33
  64.9 3.0 %collective-permute-start.4 = (f32[2,32,256]{2,0,1:T(2,128)S(1)}, f32[2,32,256]{2,0,1:T(2,128)S(1)}, u32[]{:S(2)}, u32[]{:S(2)}) collective-permute-start(f32[2,32,256]{2,0,1:T(2,128)S(1)} %slice_bitcast_fusion.13), channel_id=1, source_target_pairs={{0,16},{16,32},{32,48},{48,64},{64,80},{80,96},{96,112},{112,0},{1... | collective-permute-start | bytes 196616 | tf_op jit(solution)/shard_map/while/body/eval_jaxpr/ppermute | solution.py:19
  69.2 1.8 collective-permute-start.1
  71.0 1.8 collective-permute-done.1
  73.4 3.0 %collective-permute-start.2 = (f32[]{:T(128)}, f32[]{:T(128)}, u32[]{:S(2)}, u32[]{:S(2)}) collective-permute-start(f32[]{:T(128)} %add.181), channel_id=1, source_target_pairs={{0,64},{16,80},{32,96},{48,112},{64,0},{80,16},{96,32},{112,48},{1... | collective-permute-start | bytes 20 | tf_op jit(solution)/shard_map/while/body/eval_jaxpr/ppermute | solution.py:33
  76.5 2.0 collective-permute-done.2
  82.9 2.2 %collective-permute-done.8 = f32[]{:T(128)} collective-permute-done((f32[]{:T(128)}, f32[]{:T(128)}, u32[]{:S(2)}, u32[]{:S(2)}) %collective-permute-start.8) | collective-permute-done | bytes 36 | tf_op jit(solution)/shard_map/while/body/eval_jaxpr/ppermute | solution.py:33
  85.8 3.4 %collective-permute-start.9 = (f32[]{:T(128)}, f32[]{:T(128)}, u32[]{:S(2)}, u32[]{:S(2)}) collective-permute-start(f32[]{:T(128)} %add.184), channel_id=1, source_target_pairs={{0,8},{2,10},{4,12},{6,14},{8,0},{10,2},{12,4},{14,6},{1,9},{3,11}... | collective-permute-start | bytes 20 | tf_op jit(solution)/shard_map/while/body/eval_jaxpr/ppermute | solution.py:33
  89.2 1.7 collective-permute-done.9
  98.2 2.8 %collective-permute-start.3 = (f32[2,32,256]{2,0,1:T(2,128)S(1)}, f32[2,32,256]{2,0,1:T(2,128)S(1)}, u32[]{:S(2)}, u32[]{:S(2)}) collective-permute-start(f32[2,32,256]{2,0,1:T(2,128)S(1)} %slice_bitcast_fusion.11), channel_id=1, source_target_pairs={{16,0},{32,16},{48,32},{64,48},{80,64},{96,80},{112,96},{0,112},{1... | collective-permute-start | bytes 196616 | tf_op jit(solution)/shard_map/while/body/eval_jaxpr/ppermute | solution.py:21
  103.3 1.7 collective-permute-start.1
  105.0 1.8 collective-permute-done.1
  107.5 4.6 %collective-permute-start.2 = (f32[]{:T(128)}, f32[]{:T(128)}, u32[]{:S(2)}, u32[]{:S(2)}) collective-permute-start(f32[]{:T(128)} %add.181), channel_id=1, source_target_pairs={{0,64},{16,80},{32,96},{48,112},{64,0},{80,16},{96,32},{112,48},{1... | collective-permute-start | bytes 20 | tf_op jit(solution)/shard_map/while/body/eval_jaxpr/ppermute | solution.py:33
  115.6 2.7 %collective-permute-start.8 = (f32[]{:T(128)}, f32[]{:T(128)}, u32[]{:S(2)}, u32[]{:S(2)}) collective-permute-start(f32[]{:T(128)} %add.183), channel_id=1, source_target_pairs={{0,4},{2,6},{4,0},{6,2},{8,12},{10,14},{12,8},{14,10},{1,5},{3,7},... | collective-permute-start | bytes 20 | tf_op jit(solution)/shard_map/while/body/eval_jaxpr/ppermute | solution.py:33
  119.8 4.8 %collective-permute-start.9 = (f32[]{:T(128)}, f32[]{:T(128)}, u32[]{:S(2)}, u32[]{:S(2)}) collective-permute-start(f32[]{:T(128)} %add.184), channel_id=1, source_target_pairs={{0,8},{2,10},{4,12},{6,14},{8,0},{10,2},{12,4},{14,6},{1,9},{3,11}... | collective-permute-start | bytes 20 | tf_op jit(solution)/shard_map/while/body/eval_jaxpr/ppermute | solution.py:33
  130.8 3.0 %collective-permute-start = (f32[]{:T(128)}, f32[]{:T(128)}, u32[]{:S(2)}, u32[]{:S(2)}) collective-permute-start(f32[]{:T(128)} %multiply_reduce_fusion.3), channel_id=1, source_target_pairs={{0,16},{16,0},{32,48},{48,32},{64,80},{80,64},{96,112},{112,96},{1... | collective-permute-start | bytes 20 | tf_op jit(solution)/shard_map/while/body/eval_jaxpr/ppermute | solution.py:33
  133.9 1.8 collective-permute-start.3
  135.8 1.8 collective-permute-start.4
  139.0 1.8 collective-permute-start.1
  140.7 1.8 collective-permute-done.1
  143.2 3.2 %collective-permute-start.2 = (f32[]{:T(128)}, f32[]{:T(128)}, u32[]{:S(2)}, u32[]{:S(2)}) collective-permute-start(f32[]{:T(128)} %add.181), channel_id=1, source_target_pairs={{0,64},{16,80},{32,96},{48,112},{64,0},{80,16},{96,32},{112,48},{1... | collective-permute-start | bytes 20 | tf_op jit(solution)/shard_map/while/body/eval_jaxpr/ppermute | solution.py:33
  146.3 1.9 collective-permute-done.2
  149.6 1.8 collective-permute-start.7
  152.0 3.4 %collective-permute-start.8 = (f32[]{:T(128)}, f32[]{:T(128)}, u32[]{:S(2)}, u32[]{:S(2)}) collective-permute-start(f32[]{:T(128)} %add.183), channel_id=1, source_target_pairs={{0,4},{2,6},{4,0},{6,2},{8,12},{10,14},{12,8},{14,10},{1,5},{3,7},... | collective-permute-start | bytes 20 | tf_op jit(solution)/shard_map/while/body/eval_jaxpr/ppermute | solution.py:33
  156.2 4.1 %collective-permute-start.9 = (f32[]{:T(128)}, f32[]{:T(128)}, u32[]{:S(2)}, u32[]{:S(2)}) collective-permute-start(f32[]{:T(128)} %add.184), channel_id=1, source_target_pairs={{0,8},{2,10},{4,12},{6,14},{8,0},{10,2},{12,4},{14,6},{1,9},{3,11}... | collective-permute-start | bytes 20 | tf_op jit(solution)/shard_map/while/body/eval_jaxpr/ppermute | solution.py:33
  166.5 1.6 select_reduce_fusion
  172.8 2.4 %collective-permute-start.21 = (f32[2]{0:T(128)S(1)}, f32[2]{0:T(128)S(1)}, u32[]{:S(2)}, u32[]{:S(2)}) collective-permute-start(f32[2]{0:T(128)S(1)} %pad_maximum_fusion.16), channel_id=1, source_target_pairs={{0,16},{16,0},{32,48},{48,32},{64,80},{80,64},{96,112},{112,96},{1... | collective-permute-start | bytes 32 | tf_op jit(solution)/shard_map/ppermute | solution.py:33
  179.3 1.7 collective-permute-start.22
  182.1 2.3 %collective-permute-start.17 = (bf16[16,2304]{1,0:T(8,128)(2,1)S(1)}, bf16[16,2304]{1,0:T(8,128)(2,1)S(1)}, u32[]{:S(2)}, u32[]{:S(2)}) collective-permute-start(bf16[16,2304]{1,0:T(8,128)(2,1)S(1)} %dynamic-slice_convert_fusion.3), channel_id=1, source_target_pairs={{0,8},{2,10},{4,12},{6,14},{8,0},{10,2},{12,4},{14,6},{1,9},{3,11}... | collective-permute-start | bytes 221192 | tf_op jit(solution)/shard_map/ppermute | solution.py:88
  185.8 3.7 %collective-permute-start.23 = (f32[2]{0:T(128)S(1)}, f32[2]{0:T(128)S(1)}, u32[]{:S(2)}, u32[]{:S(2)}) collective-permute-start(f32[2]{0:T(128)S(1)} %fusion.81), channel_id=1, source_target_pairs={{0,64},{16,80},{32,96},{48,112},{64,0},{80,16},{96,32},{112,48},{1... | collective-permute-start | bytes 32 | tf_op jit(solution)/shard_map/ppermute | solution.py:33
  189.5 1.5 collective-permute-done.23
  192.4 3.2 %collective-permute-done.25 = f32[2]{0:T(128)S(1)} collective-permute-done((f32[2]{0:T(128)S(1)}, f32[2]{0:T(128)S(1)}, u32[]{:S(2)}, u32[]{:S(2)}) %collective-permute-start.25) | collective-permute-done | bytes 40 | tf_op jit(solution)/shard_map/ppermute | solution.py:33
  197.1 3.6 %collective-permute-done.26 = f32[2]{0:T(128)S(1)} collective-permute-done((f32[2]{0:T(128)S(1)}, f32[2]{0:T(128)S(1)}, u32[]{:S(2)}, u32[]{:S(2)}) %collective-permute-start.26) | collective-permute-done | bytes 40 | tf_op jit(solution)/shard_map/ppermute | solution.py:33
  202.4 2.4 %collective-permute-done.18 = bf16[8,2304]{1,0:T(8,128)(2,1)S(1)} collective-permute-done((bf16[8,2304]{1,0:T(8,128)(2,1)S(1)}, bf16[8,2304]{1,0:T(8,128)(2,1)S(1)}, u32[]{:S(2)}, u32[]{:S(2)}) %collective-permute-start.18) | collective-permute-done | bytes 36896 | tf_op jit(solution)/shard_map/ppermute | solution.py:88
  206.1 1.6 collective-permute-start.20
  (252 shorter events, 61.6 us)
Async XLA Ops:
  4.2 16.3 %copy-start.1 = (bf16[16,32,256]{2,0,1:T(8,128)(2,1)}, bf16[16,32,256]{2,0,1:T(8,128)(2,1)S(1)}, u32[]{:S(2)}) copy-start(bf16[16,32,256]{2,0,1:T(8,128)(2,1)S(1)} %copy.69) | copy-start | bytes 786436
  4.3 9.7 %collective-permute-start.11 = (bf16[320,256]{1,0:T(8,128)(2,1)S(1)}, bf16[320,256]{1,0:T(8,128)(2,1)S(1)}, u32[]{:S(2)}, u32[]{:S(2)}) collective-permute-start(bf16[320,256]{1,0:T(8,128)(2,1)S(1)} %pad_maximum_fusion.4), channel_id=1, source_target_pairs={{16,0},{32,16},{48,32},{64,48},{80,64},{96,80},{112,96},{0,112},{1... | collective-permute-start | bytes 491528 | tf_op jit(solution)/shard_map/ppermute | solution.py:57
  10.6 9.5 %collective-permute-start.10 = (bf16[320,256]{1,0:T(8,128)(2,1)S(1)}, bf16[320,256]{1,0:T(8,128)(2,1)S(1)}, u32[]{:S(2)}, u32[]{:S(2)}) collective-permute-start(bf16[320,256]{1,0:T(8,128)(2,1)S(1)} %pad_maximum_fusion.3), channel_id=1, source_target_pairs={{0,16},{16,32},{32,48},{48,64},{64,80},{80,96},{96,112},{112,0},{1... | collective-permute-start | bytes 491528 | tf_op jit(solution)/shard_map/ppermute | solution.py:57
  20.6 3.5 %collective-permute-start.13 = (bf16[184,256]{1,0:T(8,128)(2,1)S(1)}, bf16[184,256]{1,0:T(8,128)(2,1)S(1)}, u32[]{:S(2)}, u32[]{:S(2)}) collective-permute-start(bf16[184,256]{1,0:T(8,128)(2,1)S(1)} %pad_maximum_fusion.8), channel_id=1, source_target_pairs={{2,0},{4,2},{6,4},{8,6},{10,8},{12,10},{14,12},{0,14},{3,1},{5,3},... | collective-permute-start | bytes 282632 | tf_op jit(solution)/shard_map/ppermute | solution.py:57
  22.0 5.2 %collective-permute-start.12 = (bf16[184,256]{1,0:T(8,128)(2,1)S(1)}, bf16[184,256]{1,0:T(8,128)(2,1)S(1)}, u32[]{:S(2)}, u32[]{:S(2)}) collective-permute-start(bf16[184,256]{1,0:T(8,128)(2,1)S(1)} %pad_maximum_fusion.7), channel_id=1, source_target_pairs={{0,2},{2,4},{4,6},{6,8},{8,10},{10,12},{12,14},{14,0},{1,3},{3,5},... | collective-permute-start | bytes 282632 | tf_op jit(solution)/shard_map/ppermute | solution.py:57
  56.4 108.9 %collective-permute-start.14 = (bf16[128,2304]{1,0:T(8,128)(2,1)S(1)}, bf16[128,2304]{1,0:T(8,128)(2,1)S(1)}, u32[]{:S(2)}, u32[]{:S(2)}) collective-permute-start(bf16[128,2304]{1,0:T(8,128)(2,1)S(1)} %dynamic-slice_convert_fusion), channel_id=1, source_target_pairs={{0,64},{16,80},{32,96},{48,112},{64,0},{80,16},{96,32},{112,48},{1... | collective-permute-start | bytes 1769480 | tf_op jit(solution)/shard_map/ppermute | solution.py:88
  61.1 6.9 %collective-permute-start = (f32[]{:T(128)}, f32[]{:T(128)}, u32[]{:S(2)}, u32[]{:S(2)}) collective-permute-start(f32[]{:T(128)} %multiply_reduce_fusion.3), channel_id=1, source_target_pairs={{0,16},{16,0},{32,48},{48,32},{64,80},{80,64},{96,112},{112,96},{1... | collective-permute-start | bytes 20 | tf_op jit(solution)/shard_map/while/body/eval_jaxpr/ppermute | solution.py:33
  64.2 15.0 %collective-permute-start.3 = (f32[2,32,256]{2,0,1:T(2,128)S(1)}, f32[2,32,256]{2,0,1:T(2,128)S(1)}, u32[]{:S(2)}, u32[]{:S(2)}) collective-permute-start(f32[2,32,256]{2,0,1:T(2,128)S(1)} %slice_bitcast_fusion.11), channel_id=1, source_target_pairs={{16,0},{32,16},{48,32},{64,48},{80,64},{96,80},{112,96},{0,112},{1... | collective-permute-start | bytes 196616 | tf_op jit(solution)/shard_map/while/body/eval_jaxpr/ppermute | solution.py:21
  64.9 14.3 %collective-permute-start.4 = (f32[2,32,256]{2,0,1:T(2,128)S(1)}, f32[2,32,256]{2,0,1:T(2,128)S(1)}, u32[]{:S(2)}, u32[]{:S(2)}) collective-permute-start(f32[2,32,256]{2,0,1:T(2,128)S(1)} %slice_bitcast_fusion.13), channel_id=1, source_target_pairs={{0,16},{16,32},{32,48},{48,64},{64,80},{80,96},{96,112},{112,0},{1... | collective-permute-start | bytes 196616 | tf_op jit(solution)/shard_map/while/body/eval_jaxpr/ppermute | solution.py:19
  69.2 3.6 %collective-permute-start.1 = (f32[]{:T(128)}, f32[]{:T(128)}, u32[]{:S(2)}, u32[]{:S(2)}) collective-permute-start(f32[]{:T(128)} %add.180), channel_id=1, source_target_pairs={{0,32},{16,48},{32,0},{48,16},{64,96},{80,112},{96,64},{112,80},{1... | collective-permute-start | bytes 20 | tf_op jit(solution)/shard_map/while/body/eval_jaxpr/ppermute | solution.py:33
  73.4 5.1 %collective-permute-start.2 = (f32[]{:T(128)}, f32[]{:T(128)}, u32[]{:S(2)}, u32[]{:S(2)}) collective-permute-start(f32[]{:T(128)} %add.181), channel_id=1, source_target_pairs={{0,64},{16,80},{32,96},{48,112},{64,0},{80,16},{96,32},{112,48},{1... | collective-permute-start | bytes 20 | tf_op jit(solution)/shard_map/while/body/eval_jaxpr/ppermute | solution.py:33
  79.3 13.1 %collective-permute-start.5 = (f32[20,2,256]{2,0,1:T(8,128)S(1)}, f32[20,2,256]{2,0,1:T(8,128)S(1)}, u32[]{:S(2)}, u32[]{:S(2)}) collective-permute-start(f32[20,2,256]{2,0,1:T(8,128)S(1)} %get-tuple-element.121), channel_id=1, source_target_pairs={{2,0},{4,2},{6,4},{8,6},{10,8},{12,10},{14,12},{0,14},{3,1},{5,3},... | collective-permute-start | bytes 122888 | tf_op jit(solution)/shard_map/while/body/eval_jaxpr/ppermute | solution.py:21
  79.3 13.0 %collective-permute-start.6 = (f32[20,2,256]{2,0,1:T(8,128)S(1)}, f32[20,2,256]{2,0,1:T(8,128)S(1)}, u32[]{:S(2)}, u32[]{:S(2)}) collective-permute-start(f32[20,2,256]{2,0,1:T(8,128)S(1)} %get-tuple-element.122), channel_id=1, source_target_pairs={{0,2},{2,4},{4,6},{6,8},{8,10},{10,12},{12,14},{14,0},{1,3},{3,5},... | collective-permute-start | bytes 122888 | tf_op jit(solution)/shard_map/while/body/eval_jaxpr/ppermute | solution.py:19
  79.8 1.1 collective-permute-start.7
  81.6 3.6 %collective-permute-start.8 = (f32[]{:T(128)}, f32[]{:T(128)}, u32[]{:S(2)}, u32[]{:S(2)}) collective-permute-start(f32[]{:T(128)} %add.183), channel_id=1, source_target_pairs={{0,4},{2,6},{4,0},{6,2},{8,12},{10,14},{12,8},{14,10},{1,5},{3,7},... | collective-permute-start | bytes 20 | tf_op jit(solution)/shard_map/while/body/eval_jaxpr/ppermute | solution.py:33
  85.8 5.1 %collective-permute-start.9 = (f32[]{:T(128)}, f32[]{:T(128)}, u32[]{:S(2)}, u32[]{:S(2)}) collective-permute-start(f32[]{:T(128)} %add.184), channel_id=1, source_target_pairs={{0,8},{2,10},{4,12},{6,14},{8,0},{10,2},{12,4},{14,6},{1,9},{3,11}... | collective-permute-start | bytes 20 | tf_op jit(solution)/shard_map/while/body/eval_jaxpr/ppermute | solution.py:33
  96.7 5.3 %collective-permute-start = (f32[]{:T(128)}, f32[]{:T(128)}, u32[]{:S(2)}, u32[]{:S(2)}) collective-permute-start(f32[]{:T(128)} %multiply_reduce_fusion.3), channel_id=1, source_target_pairs={{0,16},{16,0},{32,48},{48,32},{64,80},{80,64},{96,112},{112,96},{1... | collective-permute-start | bytes 20 | tf_op jit(solution)/shard_map/while/body/eval_jaxpr/ppermute | solution.py:33
  98.2 15.0 %collective-permute-start.3 = (f32[2,32,256]{2,0,1:T(2,128)S(1)}, f32[2,32,256]{2,0,1:T(2,128)S(1)}, u32[]{:S(2)}, u32[]{:S(2)}) collective-permute-start(f32[2,32,256]{2,0,1:T(2,128)S(1)} %slice_bitcast_fusion.11), channel_id=1, source_target_pairs={{16,0},{32,16},{48,32},{64,48},{80,64},{96,80},{112,96},{0,112},{1... | collective-permute-start | bytes 196616 | tf_op jit(solution)/shard_map/while/body/eval_jaxpr/ppermute | solution.py:21
  101.1 12.2 %collective-permute-start.4 = (f32[2,32,256]{2,0,1:T(2,128)S(1)}, f32[2,32,256]{2,0,1:T(2,128)S(1)}, u32[]{:S(2)}, u32[]{:S(2)}) collective-permute-start(f32[2,32,256]{2,0,1:T(2,128)S(1)} %slice_bitcast_fusion.13), channel_id=1, source_target_pairs={{0,16},{16,32},{32,48},{48,64},{64,80},{80,96},{96,112},{112,0},{1... | collective-permute-start | bytes 196616 | tf_op jit(solution)/shard_map/while/body/eval_jaxpr/ppermute | solution.py:19
  103.3 3.6 %collective-permute-start.1 = (f32[]{:T(128)}, f32[]{:T(128)}, u32[]{:S(2)}, u32[]{:S(2)}) collective-permute-start(f32[]{:T(128)} %add.180), channel_id=1, source_target_pairs={{0,32},{16,48},{32,0},{48,16},{64,96},{80,112},{96,64},{112,80},{1... | collective-permute-start | bytes 20 | tf_op jit(solution)/shard_map/while/body/eval_jaxpr/ppermute | solution.py:33
  107.5 5.1 %collective-permute-start.2 = (f32[]{:T(128)}, f32[]{:T(128)}, u32[]{:S(2)}, u32[]{:S(2)}) collective-permute-start(f32[]{:T(128)} %add.181), channel_id=1, source_target_pairs={{0,64},{16,80},{32,96},{48,112},{64,0},{80,16},{96,32},{112,48},{1... | collective-permute-start | bytes 20 | tf_op jit(solution)/shard_map/while/body/eval_jaxpr/ppermute | solution.py:33
  113.4 13.1 %collective-permute-start.5 = (f32[20,2,256]{2,0,1:T(8,128)S(1)}, f32[20,2,256]{2,0,1:T(8,128)S(1)}, u32[]{:S(2)}, u32[]{:S(2)}) collective-permute-start(f32[20,2,256]{2,0,1:T(8,128)S(1)} %get-tuple-element.121), channel_id=1, source_target_pairs={{2,0},{4,2},{6,4},{8,6},{10,8},{12,10},{14,12},{0,14},{3,1},{5,3},... | collective-permute-start | bytes 122888 | tf_op jit(solution)/shard_map/while/body/eval_jaxpr/ppermute | solution.py:21
  113.4 13.0 %collective-permute-start.6 = (f32[20,2,256]{2,0,1:T(8,128)S(1)}, f32[20,2,256]{2,0,1:T(8,128)S(1)}, u32[]{:S(2)}, u32[]{:S(2)}) collective-permute-start(f32[20,2,256]{2,0,1:T(8,128)S(1)} %get-tuple-element.122), channel_id=1, source_target_pairs={{0,2},{2,4},{4,6},{6,8},{8,10},{10,12},{12,14},{14,0},{1,3},{3,5},... | collective-permute-start | bytes 122888 | tf_op jit(solution)/shard_map/while/body/eval_jaxpr/ppermute | solution.py:19
  113.9 1.1 collective-permute-start.7
  115.6 3.6 %collective-permute-start.8 = (f32[]{:T(128)}, f32[]{:T(128)}, u32[]{:S(2)}, u32[]{:S(2)}) collective-permute-start(f32[]{:T(128)} %add.183), channel_id=1, source_target_pairs={{0,4},{2,6},{4,0},{6,2},{8,12},{10,14},{12,8},{14,10},{1,5},{3,7},... | collective-permute-start | bytes 20 | tf_op jit(solution)/shard_map/while/body/eval_jaxpr/ppermute | solution.py:33
  119.8 5.1 %collective-permute-start.9 = (f32[]{:T(128)}, f32[]{:T(128)}, u32[]{:S(2)}, u32[]{:S(2)}) collective-permute-start(f32[]{:T(128)} %add.184), channel_id=1, source_target_pairs={{0,8},{2,10},{4,12},{6,14},{8,0},{10,2},{12,4},{14,6},{1,9},{3,11}... | collective-permute-start | bytes 20 | tf_op jit(solution)/shard_map/while/body/eval_jaxpr/ppermute | solution.py:33
  130.8 6.9 %collective-permute-start = (f32[]{:T(128)}, f32[]{:T(128)}, u32[]{:S(2)}, u32[]{:S(2)}) collective-permute-start(f32[]{:T(128)} %multiply_reduce_fusion.3), channel_id=1, source_target_pairs={{0,16},{16,0},{32,48},{48,32},{64,80},{80,64},{96,112},{112,96},{1... | collective-permute-start | bytes 20 | tf_op jit(solution)/shard_map/while/body/eval_jaxpr/ppermute | solution.py:33
  133.9 15.0 %collective-permute-start.3 = (f32[2,32,256]{2,0,1:T(2,128)S(1)}, f32[2,32,256]{2,0,1:T(2,128)S(1)}, u32[]{:S(2)}, u32[]{:S(2)}) collective-permute-start(f32[2,32,256]{2,0,1:T(2,128)S(1)} %slice_bitcast_fusion.11), channel_id=1, source_target_pairs={{16,0},{32,16},{48,32},{64,48},{80,64},{96,80},{112,96},{0,112},{1... | collective-permute-start | bytes 196616 | tf_op jit(solution)/shard_map/while/body/eval_jaxpr/ppermute | solution.py:21
  135.8 13.1 %collective-permute-start.4 = (f32[2,32,256]{2,0,1:T(2,128)S(1)}, f32[2,32,256]{2,0,1:T(2,128)S(1)}, u32[]{:S(2)}, u32[]{:S(2)}) collective-permute-start(f32[2,32,256]{2,0,1:T(2,128)S(1)} %slice_bitcast_fusion.13), channel_id=1, source_target_pairs={{0,16},{16,32},{32,48},{48,64},{64,80},{80,96},{96,112},{112,0},{1... | collective-permute-start | bytes 196616 | tf_op jit(solution)/shard_map/while/body/eval_jaxpr/ppermute | solution.py:19
  139.0 3.6 %collective-permute-start.1 = (f32[]{:T(128)}, f32[]{:T(128)}, u32[]{:S(2)}, u32[]{:S(2)}) collective-permute-start(f32[]{:T(128)} %add.180), channel_id=1, source_target_pairs={{0,32},{16,48},{32,0},{48,16},{64,96},{80,112},{96,64},{112,80},{1... | collective-permute-start | bytes 20 | tf_op jit(solution)/shard_map/while/body/eval_jaxpr/ppermute | solution.py:33
  143.2 5.1 %collective-permute-start.2 = (f32[]{:T(128)}, f32[]{:T(128)}, u32[]{:S(2)}, u32[]{:S(2)}) collective-permute-start(f32[]{:T(128)} %add.181), channel_id=1, source_target_pairs={{0,64},{16,80},{32,96},{48,112},{64,0},{80,16},{96,32},{112,48},{1... | collective-permute-start | bytes 20 | tf_op jit(solution)/shard_map/while/body/eval_jaxpr/ppermute | solution.py:33
  149.0 13.8 %collective-permute-start.5 = (f32[20,2,256]{2,0,1:T(8,128)S(1)}, f32[20,2,256]{2,0,1:T(8,128)S(1)}, u32[]{:S(2)}, u32[]{:S(2)}) collective-permute-start(f32[20,2,256]{2,0,1:T(8,128)S(1)} %get-tuple-element.121), channel_id=1, source_target_pairs={{2,0},{4,2},{6,4},{8,6},{10,8},{12,10},{14,12},{0,14},{3,1},{5,3},... | collective-permute-start | bytes 122888 | tf_op jit(solution)/shard_map/while/body/eval_jaxpr/ppermute | solution.py:21
  149.1 13.7 %collective-permute-start.6 = (f32[20,2,256]{2,0,1:T(8,128)S(1)}, f32[20,2,256]{2,0,1:T(8,128)S(1)}, u32[]{:S(2)}, u32[]{:S(2)}) collective-permute-start(f32[20,2,256]{2,0,1:T(8,128)S(1)} %get-tuple-element.122), channel_id=1, source_target_pairs={{0,2},{2,4},{4,6},{6,8},{8,10},{10,12},{12,14},{14,0},{1,3},{3,5},... | collective-permute-start | bytes 122888 | tf_op jit(solution)/shard_map/while/body/eval_jaxpr/ppermute | solution.py:19
  149.6 1.8 collective-permute-start.7
  152.0 3.6 %collective-permute-start.8 = (f32[]{:T(128)}, f32[]{:T(128)}, u32[]{:S(2)}, u32[]{:S(2)}) collective-permute-start(f32[]{:T(128)} %add.183), channel_id=1, source_target_pairs={{0,4},{2,6},{4,0},{6,2},{8,12},{10,14},{12,8},{14,10},{1,5},{3,7},... | collective-permute-start | bytes 20 | tf_op jit(solution)/shard_map/while/body/eval_jaxpr/ppermute | solution.py:33
  156.2 5.1 %collective-permute-start.9 = (f32[]{:T(128)}, f32[]{:T(128)}, u32[]{:S(2)}, u32[]{:S(2)}) collective-permute-start(f32[]{:T(128)} %add.184), channel_id=1, source_target_pairs={{0,8},{2,10},{4,12},{6,14},{8,0},{10,2},{12,4},{14,6},{1,9},{3,11}... | collective-permute-start | bytes 20 | tf_op jit(solution)/shard_map/while/body/eval_jaxpr/ppermute | solution.py:33
  166.0 9.2 %collective-permute-start.15 = (bf16[64,2304]{1,0:T(8,128)(2,1)S(1)}, bf16[64,2304]{1,0:T(8,128)(2,1)S(1)}, u32[]{:S(2)}, u32[]{:S(2)}) collective-permute-start(bf16[64,2304]{1,0:T(8,128)(2,1)S(1)} %dynamic-slice_convert_fusion.1), channel_id=1, source_target_pairs={{0,32},{16,48},{32,0},{48,16},{64,96},{80,112},{96,64},{112,80},{1... | collective-permute-start | bytes 884744 | tf_op jit(solution)/shard_map/ppermute | solution.py:88
  172.8 5.1 %collective-permute-start.21 = (f32[2]{0:T(128)S(1)}, f32[2]{0:T(128)S(1)}, u32[]{:S(2)}, u32[]{:S(2)}) collective-permute-start(f32[2]{0:T(128)S(1)} %pad_maximum_fusion.16), channel_id=1, source_target_pairs={{0,16},{16,0},{32,48},{48,32},{64,80},{80,64},{96,112},{112,96},{1... | collective-permute-start | bytes 32 | tf_op jit(solution)/shard_map/ppermute | solution.py:33
  175.3 6.7 %collective-permute-start.16 = (bf16[32,2304]{1,0:T(8,128)(2,1)S(1)}, bf16[32,2304]{1,0:T(8,128)(2,1)S(1)}, u32[]{:S(2)}, u32[]{:S(2)}) collective-permute-start(bf16[32,2304]{1,0:T(8,128)(2,1)S(1)} %dynamic-slice_convert_fusion.2), channel_id=1, source_target_pairs={{0,16},{16,0},{32,48},{48,32},{64,80},{80,64},{96,112},{112,96},{1... | collective-permute-start | bytes 442376 | tf_op jit(solution)/shard_map/ppermute | solution.py:88
  179.3 5.1 %collective-permute-start.22 = (f32[2]{0:T(128)S(1)}, f32[2]{0:T(128)S(1)}, u32[]{:S(2)}, u32[]{:S(2)}) collective-permute-start(f32[2]{0:T(128)S(1)} %fusion.80), channel_id=1, source_target_pairs={{0,32},{16,48},{32,0},{48,16},{64,96},{80,112},{96,64},{112,80},{1... | collective-permute-start | bytes 32 | tf_op jit(solution)/shard_map/ppermute | solution.py:33
  182.1 18.6 %collective-permute-start.17 = (bf16[16,2304]{1,0:T(8,128)(2,1)S(1)}, bf16[16,2304]{1,0:T(8,128)(2,1)S(1)}, u32[]{:S(2)}, u32[]{:S(2)}) collective-permute-start(bf16[16,2304]{1,0:T(8,128)(2,1)S(1)} %dynamic-slice_convert_fusion.3), channel_id=1, source_target_pairs={{0,8},{2,10},{4,12},{6,14},{8,0},{10,2},{12,4},{14,6},{1,9},{3,11}... | collective-permute-start | bytes 221192 | tf_op jit(solution)/shard_map/ppermute | solution.py:88
  185.8 5.2 %collective-permute-start.23 = (f32[2]{0:T(128)S(1)}, f32[2]{0:T(128)S(1)}, u32[]{:S(2)}, u32[]{:S(2)}) collective-permute-start(f32[2]{0:T(128)S(1)} %fusion.81), channel_id=1, source_target_pairs={{0,64},{16,80},{32,96},{48,112},{64,0},{80,16},{96,32},{112,48},{1... | collective-permute-start | bytes 32 | tf_op jit(solution)/shard_map/ppermute | solution.py:33
  191.0 1.1 collective-permute-start.24
  192.1 3.5 %collective-permute-start.25 = (f32[2]{0:T(128)S(1)}, f32[2]{0:T(128)S(1)}, u32[]{:S(2)}, u32[]{:S(2)}) collective-permute-start(f32[2]{0:T(128)S(1)} %add.156), channel_id=1, source_target_pairs={{0,4},{2,6},{4,0},{6,2},{8,12},{10,14},{12,8},{14,10},{1,5},{3,7},... | collective-permute-start | bytes 32 | tf_op jit(solution)/shard_map/ppermute | solution.py:33
  195.6 5.0 %collective-permute-start.26 = (f32[2]{0:T(128)S(1)}, f32[2]{0:T(128)S(1)}, u32[]{:S(2)}, u32[]{:S(2)}) collective-permute-start(f32[2]{0:T(128)S(1)} %add.157), channel_id=1, source_target_pairs={{0,8},{2,10},{4,12},{6,14},{8,0},{10,2},{12,4},{14,6},{1,9},{3,11}... | collective-permute-start | bytes 32 | tf_op jit(solution)/shard_map/ppermute | solution.py:33
  200.7 4.0 %collective-permute-start.18 = (bf16[8,2304]{1,0:T(8,128)(2,1)S(1)}, bf16[8,2304]{1,0:T(8,128)(2,1)S(1)}, u32[]{:S(2)}, u32[]{:S(2)}) collective-permute-start(bf16[8,2304]{1,0:T(8,128)(2,1)S(1)} %dynamic-slice_convert_fusion.4), channel_id=1, source_target_pairs={{0,4},{2,6},{4,0},{6,2},{8,12},{10,14},{12,8},{14,10},{1,5},{3,7},... | collective-permute-start | bytes 110600 | tf_op jit(solution)/shard_map/ppermute | solution.py:88
  204.8 1.3 collective-permute-start.19
  206.1 4.1 %collective-permute-start.20 = (f32[4,2304]{1,0:T(4,128)S(1)}, f32[4,2304]{1,0:T(4,128)S(1)}, u32[]{:S(2)}, u32[]{:S(2)}) collective-permute-start(f32[4,2304]{1,0:T(4,128)S(1)} %convert_add_fusion.5), channel_id=1, source_target_pairs={{0,1},{1,0},{2,3},{3,2},{4,5},{5,4},{6,7},{7,6},{8,9},{9,8},{10,11... | collective-permute-start | bytes 110600 | tf_op jit(solution)/shard_map/ppermute | solution.py:33
  (27 other events, 61.9 us)

commit v12 on v10

--- a/solution.py
+++ b/solution.py
@@ -126,7 +126,6 @@
         padded_back = extended(row_padded, field[1:], 2, True)
         squared = butterfly_sum(squared, ("cols",))
         scale_now = jnp.sqrt(squared / count + 1e-06)
-        iterate = (back / scale_now).astype(jnp.bfloat16)
         padded_probe = (padded_back / scale_now).astype(jnp.bfloat16)
         return (padded_probe, iterate), scale_now
 
@@ -156,7 +155,7 @@
     )
     image = conv(padded_probe[None], kernel, False).astype(jnp.bfloat16)
     back = conv(image, kernel, True)[0]
-    wide_iter = iterate.astype(jnp.float32)
+    wide_iter = padded_probe[2:-2, 2:-2].astype(jnp.float32)
     totals = butterfly_sum(
         jnp.stack([jnp.sum(back * back), jnp.sum(wide_iter * wide_iter)]),
         ("rows", "cols"),

time: 214 us -> 223 us (1.042)
  matrix products: 22.1 us -> 34.8 us
  local copies, waits for them, and re-layouts: 27.4 us -> 24 us
    conv_general_dilated x10, matrix products: 15.1 us -> 28 us  [conv(): lax.conv_general_dilated(padded, weights, window_strides=(1, 1), padding=...]
    while x6 -> x0, local copies, waits for them, and re-layouts: 3.25 us -> none
    convert_element_type x3 -> x0, other arithmetic: 2.24 us -> none  [power_step(): iterate = (back / scale_now).astype(jnp.bfloat16)]
    unnamed x52 -> x40, local copies, waits for them, and re-layouts: 9.35 us -> 9.66 us
  transfers between devices with their start and end apart: 47 -> 47, of which waited for: 26 -> 25; matrix products, arithmetic and copies ran while one was open for 12% -> 15% of each run, Pallas kernels for 0% -> 0%
where the time goes in v12:
time: 223 us; the launch traced here: 221 us
  starting transfers between devices  83.1 us (37%)
  waiting for transfers between devices  47.3 us (21%)
  matrix products  34.8 us (16%)
  local copies, waits for them, and re-layouts  24 us (11%)
  other arithmetic  13.6 us (6%)
  loops' own time  13.2 us (6%)
  between operations  4.82 us (2%)
    ppermute x25, starting transfers between devices, butterfly_sum(): lax.ppermute(value, axis, [(i, i ^ step) for i in range(count)])  57.2 us
    ppermute x25, waiting for transfers between devices, butterfly_sum(): lax.ppermute(value, axis, [(i, i ^ step) for i in range(count)])  28.5 us
    conv_general_dilated x10, matrix products, conv(): lax.conv_general_dilated(padded, weights, window_strides=(1, 1), padding=...  28 us
    ppermute x4, waiting for transfers between devices, travel(): moved = lax.ppermute(flat, axis, pairs)  13.3 us
    another operation x1, loops' own time, per_device(): lax.scan(power_step, (padded_probe, iterate), None, length=ITERS - 1)  13.2 us
    unnamed x40, local copies, waits for them, and re-layouts  9.66 us
    ppermute x4, starting transfers between devices, travel(): moved = lax.ppermute(flat, axis, pairs)  7.77 us
    ppermute x6, starting transfers between devices, extended(): lax.ppermute(tail, axis, [(i, (i + 1) % count) for i in range(ends)])  7.29 us
  transfers between devices with their start and end apart: 47, of which 25 were waited for; matrix products, arithmetic and copies ran while one was open for 15% of the time, Pallas kernels for 0%

profile of v12, /device:TPU:0, one launch (start us, length us, event | category | flops | bytes accessed | tf_op | source)
XLA Modules:
  0.0 220.9 jit_solution(10367206784362064997)
XLA Ops:
  2.1 2.1 copy.24
  5.4 6.2 %collective-permute-start.11 = (bf16[320,256]{1,0:T(8,128)(2,1)S(1)}, bf16[320,256]{1,0:T(8,128)(2,1)S(1)}, u32[]{:S(2)}, u32[]{:S(2)}) collective-permute-start(bf16[320,256]{1,0:T(8,128)(2,1)S(1)} %pad_maximum_fusion.4), channel_id=1, source_target_pairs={{16,0},{32,16},{48,32},{64,48},{80,64},{96,80},{112,96},{0,112},{1... | collective-permute-start | bytes 491528 | tf_op jit(solution)/shard_map/ppermute | solution.py:57
  12.2 2.9 %collective-permute-done.11 = bf16[320,256]{1,0:T(8,128)(2,1)S(1)} collective-permute-done((bf16[320,256]{1,0:T(8,128)(2,1)S(1)}, bf16[320,256]{1,0:T(8,128)(2,1)S(1)}, u32[]{:S(2)}, u32[]{:S(2)}) %collective-permute-start.11) | collective-permute-done | bytes 163872 | tf_op jit(solution)/shard_map/ppermute | solution.py:57
  15.3 5.9 %collective-permute-done.10 = bf16[320,256]{1,0:T(8,128)(2,1)S(1)} collective-permute-done((bf16[320,256]{1,0:T(8,128)(2,1)S(1)}, bf16[320,256]{1,0:T(8,128)(2,1)S(1)}, u32[]{:S(2)}, u32[]{:S(2)}) %collective-permute-start.10) | collective-permute-done | bytes 163872 | tf_op jit(solution)/shard_map/ppermute | solution.py:57
  23.6 2.1 collective-permute-done.13
  26.4 2.3 %collective-permute-done.12 = bf16[184,256]{1,0:T(8,128)(2,1)S(1)} collective-permute-done((bf16[184,256]{1,0:T(8,128)(2,1)S(1)}, bf16[184,256]{1,0:T(8,128)(2,1)S(1)}, u32[]{:S(2)}, u32[]{:S(2)}) %collective-permute-start.12) | collective-permute-done | bytes 94240 | tf_op jit(solution)/shard_map/ppermute | solution.py:57
  30.1 6.9 %fusion.46 = f32[256,3,3,256]{0,3,2,1:T(8,128)} fusion(bf16[8,18,34,256]{3,0,2,1:T(8,128)(2,1)S(1)} %pad_maximum_fusion.1, bf16[4,16,32,256]{3,2,1,0:T(8,128)(2,1)S(1)} %copy-done.5), kind=kOutput, calls=%fused_computation.62 | convolution fusion | flops 2415919104 | bytes 4661248 | tf_op jit(solution)/shard_map/conv_general_dilated | solution.py:142
  40.1 4.5 %select_convert_fusion = bf16[16,32,5,256]{3,1,2,0:T(8,128)(2,1)S(1)} fusion(bf16[3,3,256,256]{3,2,1,0:T(8,128)(2,1)} %param.8, bf16[18,4,8,7,256]{4,1,3,2,0:T(4,128)(2,1)S(1)} %fusion.30, pred[32,5]{0,1:T(8,128)(4,1)S(1)} %copy-done.16), kind=kOutput, calls=%fused_computation.37 | convolution fusion | flops 3021209600 | bytes 4554912 | tf_op jit(solution)/shard_map/conv_general_dilated | solution.py:98
  47.3 4.5 %select_convert_fusion.1 = bf16[16,32,5,256]{3,1,2,0:T(8,128)(2,1)S(1)} fusion(bf16[3,3,256,256]{3,2,1,0:T(8,128)(2,1)} %param.8, bf16[18,4,8,7,256]{4,1,3,2,0:T(4,128)(2,1)S(1)} %fusion.29, pred[32,5]{0,1:T(8,128)(4,1)S(1)} %copy-done.16), kind=kOutput, calls=%fused_computation.38 | convolution fusion | flops 3021209600 | bytes 4554912 | tf_op jit(solution)/shard_map/conv_general_dilated | solution.py:98
  54.2 3.1 %copy.46 = f32[256,2304]{1,0:T(8,128)} copy(f32[256,2304]{0,1:T(8,128)} %bitcast.125) | data formatting | bytes 4718592 | tf_op jit(solution)/shard_map/optimization_barrier | solution.py:150
  57.3 2.1 dynamic-slice_convert_fusion
  59.4 109.8 %while.12 = (s32[]{:T(128)}, bf16[20,36,256]{2,0,1:T(8,128)(2,1)S(1)}, f32[3]{0:T(128)S(1)}, bf16[3,3,256,256]{3,2,1,0:T(8,128)(2,1)}, s32[]{:T(128)}, /*index=5...) while((s32[]{:T(128)}, bf16[20,36,256]{2,0,1:T(8,128)(2,1)S(1)}, f32[3]{0:T(128)S(1)}, ...), condition=%wide.region_2.3_spmd, body=%wide.region_0.2_spmd.sunk | while | flops 1609469952 | bytes 13810427 | solution.py:153
  59.9 2.3 %fusion.95 = bf16[18,1,8,5,256]{4,2,3,0,1:T(8,128)(2,1)S(1)} fusion(bf16[3,3,256,256]{3,2,1,0:T(8,128)(2,1)} %get-tuple-element.133, bf16[20,1,7,2,256]{4,2,3,0,1:T(8,128)(2,1)S(1)} %slice.185, bf16[20,1,8,5,256]{4,2,3,0,1:T(8,128)(2,1)S(1)} %copy.74, pred[8,5]{0,1:T(8,128)(4,1)S(1)} %get-tuple-element.136), kind=kOutput, calls=%fused_computation.3.clone.1 | convolution fusion | flops 851619840 | bytes 2101288 | tf_op jit(solution)/shard_map/while/body/eval_jaxpr/conv_general_dilated | solution.py:98
  62.3 2.2 %fusion.96 = f32[16,8,5,256]{3,1,2,0:T(8,128)S(1)} fusion(bf16[3,3,256,256]{3,2,1,0:T(8,128)(2,1)} %get-tuple-element.133, bf16[18,1,7,2,256]{4,2,3,0,1:T(8,128)(2,1)S(1)} %slice.186, bf16[18,1,8,5,256]{4,2,3,0,1:T(8,128)(2,1)S(1)} %fusion.95), kind=kOutput, calls=%fused_computation.20.clone.1 | convolution fusion | flops 756523008 | bytes 2332672 | tf_op jit(solution)/shard_map/while/body/eval_jaxpr/conv_general_dilated | solution.py:98
  65.5 3.1 %collective-permute-start = (f32[]{:T(128)}, f32[]{:T(128)}, u32[]{:S(2)}, u32[]{:S(2)}) collective-permute-start(f32[]{:T(128)} %multiply_reduce_fusion.3), channel_id=1, source_target_pairs={{0,16},{16,0},{32,48},{48,32},{64,80},{80,64},{96,112},{112,96},{1... | collective-permute-start | bytes 20 | tf_op jit(solution)/shard_map/while/body/eval_jaxpr/ppermute | solution.py:33
  69.3 3.0 %collective-permute-start.4 = (f32[2,32,256]{2,0,1:T(2,128)S(1)}, f32[2,32,256]{2,0,1:T(2,128)S(1)}, u32[]{:S(2)}, u32[]{:S(2)}) collective-permute-start(f32[2,32,256]{2,0,1:T(2,128)S(1)} %slice_bitcast_fusion.13), channel_id=1, source_target_pairs={{0,16},{16,32},{32,48},{48,64},{64,80},{80,96},{96,112},{112,0},{1... | collective-permute-start | bytes 196616 | tf_op jit(solution)/shard_map/while/body/eval_jaxpr/ppermute | solution.py:19
  75.3 2.0 collective-permute-done.1
  77.9 3.0 %collective-permute-start.2 = (f32[]{:T(128)}, f32[]{:T(128)}, u32[]{:S(2)}, u32[]{:S(2)}) collective-permute-start(f32[]{:T(128)} %add.181), channel_id=1, source_target_pairs={{0,64},{16,80},{32,96},{48,112},{64,0},{80,16},{96,32},{112,48},{1... | collective-permute-start | bytes 20 | tf_op jit(solution)/shard_map/while/body/eval_jaxpr/ppermute | solution.py:33
  80.9 2.2 %collective-permute-done.2 = f32[]{:T(128)} collective-permute-done((f32[]{:T(128)}, f32[]{:T(128)}, u32[]{:S(2)}, u32[]{:S(2)}) %collective-permute-start.2) | collective-permute-done | bytes 36 | tf_op jit(solution)/shard_map/while/body/eval_jaxpr/ppermute | solution.py:33
  87.6 2.3 %collective-permute-done.8 = f32[]{:T(128)} collective-permute-done((f32[]{:T(128)}, f32[]{:T(128)}, u32[]{:S(2)}, u32[]{:S(2)}) %collective-permute-start.8) | collective-permute-done | bytes 36 | tf_op jit(solution)/shard_map/while/body/eval_jaxpr/ppermute | solution.py:33
  90.5 3.4 %collective-permute-start.9 = (f32[]{:T(128)}, f32[]{:T(128)}, u32[]{:S(2)}, u32[]{:S(2)}) collective-permute-start(f32[]{:T(128)} %add.184), channel_id=1, source_target_pairs={{0,8},{2,10},{4,12},{6,14},{8,0},{10,2},{12,4},{14,6},{1,9},{3,11}... | collective-permute-start | bytes 20 | tf_op jit(solution)/shard_map/while/body/eval_jaxpr/ppermute | solution.py:33
  93.9 1.8 collective-permute-done.9
  96.8 2.3 %fusion.95 = bf16[18,1,8,5,256]{4,2,3,0,1:T(8,128)(2,1)S(1)} fusion(bf16[3,3,256,256]{3,2,1,0:T(8,128)(2,1)} %get-tuple-element.133, bf16[20,1,7,2,256]{4,2,3,0,1:T(8,128)(2,1)S(1)} %slice.185, bf16[20,1,8,5,256]{4,2,3,0,1:T(8,128)(2,1)S(1)} %copy.74, pred[8,5]{0,1:T(8,128)(4,1)S(1)} %get-tuple-element.136), kind=kOutput, calls=%fused_computation.3.clone.1 | convolution fusion | flops 851619840 | bytes 2101288 | tf_op jit(solution)/shard_map/while/body/eval_jaxpr/conv_general_dilated | solution.py:98
  99.1 2.2 %fusion.96 = f32[16,8,5,256]{3,1,2,0:T(8,128)S(1)} fusion(bf16[3,3,256,256]{3,2,1,0:T(8,128)(2,1)} %get-tuple-element.133, bf16[18,1,7,2,256]{4,2,3,0,1:T(8,128)(2,1)S(1)} %slice.186, bf16[18,1,8,5,256]{4,2,3,0,1:T(8,128)(2,1)S(1)} %fusion.95), kind=kOutput, calls=%fused_computation.20.clone.1 | convolution fusion | flops 756523008 | bytes 2332672 | tf_op jit(solution)/shard_map/while/body/eval_jaxpr/conv_general_dilated | solution.py:98
  103.8 2.7 %collective-permute-start.3 = (f32[2,32,256]{2,0,1:T(2,128)S(1)}, f32[2,32,256]{2,0,1:T(2,128)S(1)}, u32[]{:S(2)}, u32[]{:S(2)}) collective-permute-start(f32[2,32,256]{2,0,1:T(2,128)S(1)} %slice_bitcast_fusion.11), channel_id=1, source_target_pairs={{16,0},{32,16},{48,32},{64,48},{80,64},{96,80},{112,96},{0,112},{1... | collective-permute-start | bytes 196616 | tf_op jit(solution)/shard_map/while/body/eval_jaxpr/ppermute | solution.py:21
  110.6 2.0 collective-permute-done.1
  113.1 4.5 %collective-permute-start.2 = (f32[]{:T(128)}, f32[]{:T(128)}, u32[]{:S(2)}, u32[]{:S(2)}) collective-permute-start(f32[]{:T(128)} %add.181), channel_id=1, source_target_pairs={{0,64},{16,80},{32,96},{48,112},{64,0},{80,16},{96,32},{112,48},{1... | collective-permute-start | bytes 20 | tf_op jit(solution)/shard_map/while/body/eval_jaxpr/ppermute | solution.py:33
  121.5 2.7 %collective-permute-start.8 = (f32[]{:T(128)}, f32[]{:T(128)}, u32[]{:S(2)}, u32[]{:S(2)}) collective-permute-start(f32[]{:T(128)} %add.183), channel_id=1, source_target_pairs={{0,4},{2,6},{4,0},{6,2},{8,12},{10,14},{12,8},{14,10},{1,5},{3,7},... | collective-permute-start | bytes 20 | tf_op jit(solution)/shard_map/while/body/eval_jaxpr/ppermute | solution.py:33
  125.8 4.7 %collective-permute-start.9 = (f32[]{:T(128)}, f32[]{:T(128)}, u32[]{:S(2)}, u32[]{:S(2)}) collective-permute-start(f32[]{:T(128)} %add.184), channel_id=1, source_target_pairs={{0,8},{2,10},{4,12},{6,14},{8,0},{10,2},{12,4},{14,6},{1,9},{3,11}... | collective-permute-start | bytes 20 | tf_op jit(solution)/shard_map/while/body/eval_jaxpr/ppermute | solution.py:33
  132.0 2.3 %fusion.95 = bf16[18,1,8,5,256]{4,2,3,0,1:T(8,128)(2,1)S(1)} fusion(bf16[3,3,256,256]{3,2,1,0:T(8,128)(2,1)} %get-tuple-element.133, bf16[20,1,7,2,256]{4,2,3,0,1:T(8,128)(2,1)S(1)} %slice.185, bf16[20,1,8,5,256]{4,2,3,0,1:T(8,128)(2,1)S(1)} %copy.74, pred[8,5]{0,1:T(8,128)(4,1)S(1)} %get-tuple-element.136), kind=kOutput, calls=%fused_computation.3.clone.1 | convolution fusion | flops 851619840 | bytes 2101288 | tf_op jit(solution)/shard_map/while/body/eval_jaxpr/conv_general_dilated | solution.py:98
  134.4 2.2 %fusion.96 = f32[16,8,5,256]{3,1,2,0:T(8,128)S(1)} fusion(bf16[3,3,256,256]{3,2,1,0:T(8,128)(2,1)} %get-tuple-element.133, bf16[18,1,7,2,256]{4,2,3,0,1:T(8,128)(2,1)S(1)} %slice.186, bf16[18,1,8,5,256]{4,2,3,0,1:T(8,128)(2,1)S(1)} %fusion.95), kind=kOutput, calls=%fused_computation.20.clone.1 | convolution fusion | flops 756523008 | bytes 2332672 | tf_op jit(solution)/shard_map/while/body/eval_jaxpr/conv_general_dilated | solution.py:98
  137.6 3.0 %collective-permute-start = (f32[]{:T(128)}, f32[]{:T(128)}, u32[]{:S(2)}, u32[]{:S(2)}) collective-permute-start(f32[]{:T(128)} %multiply_reduce_fusion.3), channel_id=1, source_target_pairs={{0,16},{16,0},{32,48},{48,32},{64,80},{80,64},{96,112},{112,96},{1... | collective-permute-start | bytes 20 | tf_op jit(solution)/shard_map/while/body/eval_jaxpr/ppermute | solution.py:33
  140.6 1.9 collective-permute-start.3
  142.5 1.8 collective-permute-start.4
  147.3 2.0 collective-permute-done.1
  149.9 3.2 %collective-permute-start.2 = (f32[]{:T(128)}, f32[]{:T(128)}, u32[]{:S(2)}, u32[]{:S(2)}) collective-permute-start(f32[]{:T(128)} %add.181), channel_id=1, source_target_pairs={{0,64},{16,80},{32,96},{48,112},{64,0},{80,16},{96,32},{112,48},{1... | collective-permute-start | bytes 20 | tf_op jit(solution)/shard_map/while/body/eval_jaxpr/ppermute | solution.py:33
  153.1 2.1 collective-permute-done.2
  156.4 1.9 collective-permute-start.7
  158.9 3.4 %collective-permute-start.8 = (f32[]{:T(128)}, f32[]{:T(128)}, u32[]{:S(2)}, u32[]{:S(2)}) collective-permute-start(f32[]{:T(128)} %add.183), channel_id=1, source_target_pairs={{0,4},{2,6},{4,0},{6,2},{8,12},{10,14},{12,8},{14,10},{1,5},{3,7},... | collective-permute-start | bytes 20 | tf_op jit(solution)/shard_map/while/body/eval_jaxpr/ppermute | solution.py:33
  163.2 4.1 %collective-permute-start.9 = (f32[]{:T(128)}, f32[]{:T(128)}, u32[]{:S(2)}, u32[]{:S(2)}) collective-permute-start(f32[]{:T(128)} %add.184), channel_id=1, source_target_pairs={{0,8},{2,10},{4,12},{6,14},{8,0},{10,2},{12,4},{14,6},{1,9},{3,11}... | collective-permute-start | bytes 20 | tf_op jit(solution)/shard_map/while/body/eval_jaxpr/ppermute | solution.py:33
  169.5 2.5 %fusion.43 = bf16[18,1,8,5,256]{4,2,3,0,1:T(8,128)(2,1)S(1)} fusion(bf16[3,3,256,256]{3,2,1,0:T(8,128)(2,1)} %param.8, bf16[20,1,7,2,256]{4,2,3,0,1:T(8,128)(2,1)S(1)} %slice.139, bf16[20,1,8,5,256]{4,2,3,0,1:T(8,128)(2,1)S(1)} %copy.49, pred[8,5]{0,1:T(8,128)(4,1)S(1)} %get-tuple-element.179), kind=kOutput, calls=%fused_computation.52 | convolution fusion | flops 851619840 | bytes 2101288 | tf_op jit(solution)/shard_map/conv_general_dilated | solution.py:98
  173.7 2.8 %select_reduce_fusion = (f32[]{:T(128)}, f32[16,8,5,256]{3,1,2,0:T(8,128)S(1)}) fusion(pred[8,5]{0,1:T(8,128)(4,1)S(1)} %copy-done.14, bf16[3,3,256,256]{3,2,1,0:T(8,128)(2,1)} %param.8, bf16[18,1,7,2,256]{4,2,3,0,1:T(8,128)(2,1)S(1)} %slice.140, bf16[18,1,8,5,256]{4,2,3,0,1:T(8,128)(2,1)S(1)} %fusion.43), kind=kOutput, calls=%fused_computation.64 | convolution fusion | flops 757014528 | bytes 2332716 | tf_op jit(solution)/shard_map/conv_general_dilated | solution.py:98
  182.8 2.2 collective-permute-start.16
  189.6 2.8 %collective-permute-start.17 = (bf16[16,2304]{1,0:T(8,128)(2,1)S(1)}, bf16[16,2304]{1,0:T(8,128)(2,1)S(1)}, u32[]{:S(2)}, u32[]{:S(2)}) collective-permute-start(bf16[16,2304]{1,0:T(8,128)(2,1)S(1)} %dynamic-slice_convert_fusion.3), channel_id=1, source_target_pairs={{0,8},{2,10},{4,12},{6,14},{8,0},{10,2},{12,4},{14,6},{1,9},{3,11}... | collective-permute-start | bytes 221192 | tf_op jit(solution)/shard_map/ppermute | solution.py:89
  193.8 4.1 %collective-permute-start.23 = (f32[2]{0:T(128)S(1)}, f32[2]{0:T(128)S(1)}, u32[]{:S(2)}, u32[]{:S(2)}) collective-permute-start(f32[2]{0:T(128)S(1)} %fusion.81), channel_id=1, source_target_pairs={{0,64},{16,80},{32,96},{48,112},{64,0},{80,16},{96,32},{112,48},{1... | collective-permute-start | bytes 32 | tf_op jit(solution)/shard_map/ppermute | solution.py:33
  200.7 3.5 %collective-permute-done.25 = f32[2]{0:T(128)S(1)} collective-permute-done((f32[2]{0:T(128)S(1)}, f32[2]{0:T(128)S(1)}, u32[]{:S(2)}, u32[]{:S(2)}) %collective-permute-start.25) | collective-permute-done | bytes 40 | tf_op jit(solution)/shard_map/ppermute | solution.py:33
  205.5 3.6 %collective-permute-done.26 = f32[2]{0:T(128)S(1)} collective-permute-done((f32[2]{0:T(128)S(1)}, f32[2]{0:T(128)S(1)}, u32[]{:S(2)}, u32[]{:S(2)}) %collective-permute-start.26) | collective-permute-done | bytes 40 | tf_op jit(solution)/shard_map/ppermute | solution.py:33
  210.7 3.0 %collective-permute-done.18 = f32[8,2304]{1,0:T(8,128)S(1)} collective-permute-done((f32[8,2304]{1,0:T(8,128)S(1)}, f32[8,2304]{1,0:T(8,128)S(1)}, u32[]{:S(2)}, u32[]{:S(2)}) %collective-permute-start.18) | collective-permute-done | bytes 73760 | tf_op jit(solution)/shard_map/ppermute | solution.py:89
  (231 shorter events, 60.9 us)
Async XLA Ops:
  2.1 19.3 %copy-start.2 = (bf16[16,32,256]{2,0,1:T(8,128)(2,1)}, bf16[16,32,256]{2,0,1:T(8,128)(2,1)S(1)}, u32[]{:S(2)}) copy-start(bf16[16,32,256]{2,0,1:T(8,128)(2,1)S(1)} %copy.69) | copy-start | bytes 786436
  5.4 9.7 %collective-permute-start.11 = (bf16[320,256]{1,0:T(8,128)(2,1)S(1)}, bf16[320,256]{1,0:T(8,128)(2,1)S(1)}, u32[]{:S(2)}, u32[]{:S(2)}) collective-permute-start(bf16[320,256]{1,0:T(8,128)(2,1)S(1)} %pad_maximum_fusion.4), channel_id=1, source_target_pairs={{16,0},{32,16},{48,32},{64,48},{80,64},{96,80},{112,96},{0,112},{1... | collective-permute-start | bytes 491528 | tf_op jit(solution)/shard_map/ppermute | solution.py:57
  11.7 9.5 %collective-permute-start.10 = (bf16[320,256]{1,0:T(8,128)(2,1)S(1)}, bf16[320,256]{1,0:T(8,128)(2,1)S(1)}, u32[]{:S(2)}, u32[]{:S(2)}) collective-permute-start(bf16[320,256]{1,0:T(8,128)(2,1)S(1)} %pad_maximum_fusion.3), channel_id=1, source_target_pairs={{0,16},{16,32},{32,48},{48,64},{64,80},{80,96},{96,112},{112,0},{1... | collective-permute-start | bytes 491528 | tf_op jit(solution)/shard_map/ppermute | solution.py:57
  22.3 3.5 %collective-permute-start.13 = (bf16[184,256]{1,0:T(8,128)(2,1)S(1)}, bf16[184,256]{1,0:T(8,128)(2,1)S(1)}, u32[]{:S(2)}, u32[]{:S(2)}) collective-permute-start(bf16[184,256]{1,0:T(8,128)(2,1)S(1)} %pad_maximum_fusion.8), channel_id=1, source_target_pairs={{2,0},{4,2},{6,4},{8,6},{10,8},{12,10},{14,12},{0,14},{3,1},{5,3},... | collective-permute-start | bytes 282632 | tf_op jit(solution)/shard_map/ppermute | solution.py:57
  23.6 5.2 %collective-permute-start.12 = (bf16[184,256]{1,0:T(8,128)(2,1)S(1)}, bf16[184,256]{1,0:T(8,128)(2,1)S(1)}, u32[]{:S(2)}, u32[]{:S(2)}) collective-permute-start(bf16[184,256]{1,0:T(8,128)(2,1)S(1)} %pad_maximum_fusion.7), channel_id=1, source_target_pairs={{0,2},{2,4},{4,6},{6,8},{8,10},{10,12},{12,14},{14,0},{1,3},{3,5},... | collective-permute-start | bytes 282632 | tf_op jit(solution)/shard_map/ppermute | solution.py:57
  59.4 112.6 %collective-permute-start.14 = (bf16[128,2304]{1,0:T(8,128)(2,1)}, bf16[128,2304]{1,0:T(8,128)(2,1)}, u32[]{:S(2)}, u32[]{:S(2)}) collective-permute-start(bf16[128,2304]{1,0:T(8,128)(2,1)} %dynamic-slice_convert_fusion), channel_id=1, source_target_pairs={{0,64},{16,80},{32,96},{48,112},{64,0},{80,16},{96,32},{112,48},{1... | collective-permute-start | bytes 1769480 | tf_op jit(solution)/shard_map/ppermute | solution.py:89
  65.5 6.9 %collective-permute-start = (f32[]{:T(128)}, f32[]{:T(128)}, u32[]{:S(2)}, u32[]{:S(2)}) collective-permute-start(f32[]{:T(128)} %multiply_reduce_fusion.3), channel_id=1, source_target_pairs={{0,16},{16,0},{32,48},{48,32},{64,80},{80,64},{96,112},{112,96},{1... | collective-permute-start | bytes 20 | tf_op jit(solution)/shard_map/while/body/eval_jaxpr/ppermute | solution.py:33
  68.6 15.1 %collective-permute-start.3 = (f32[2,32,256]{2,0,1:T(2,128)S(1)}, f32[2,32,256]{2,0,1:T(2,128)S(1)}, u32[]{:S(2)}, u32[]{:S(2)}) collective-permute-start(f32[2,32,256]{2,0,1:T(2,128)S(1)} %slice_bitcast_fusion.11), channel_id=1, source_target_pairs={{16,0},{32,16},{48,32},{64,48},{80,64},{96,80},{112,96},{0,112},{1... | collective-permute-start | bytes 196616 | tf_op jit(solution)/shard_map/while/body/eval_jaxpr/ppermute | solution.py:21
  69.3 14.4 %collective-permute-start.4 = (f32[2,32,256]{2,0,1:T(2,128)S(1)}, f32[2,32,256]{2,0,1:T(2,128)S(1)}, u32[]{:S(2)}, u32[]{:S(2)}) collective-permute-start(f32[2,32,256]{2,0,1:T(2,128)S(1)} %slice_bitcast_fusion.13), channel_id=1, source_target_pairs={{0,16},{16,32},{32,48},{48,64},{64,80},{80,96},{96,112},{112,0},{1... | collective-permute-start | bytes 196616 | tf_op jit(solution)/shard_map/while/body/eval_jaxpr/ppermute | solution.py:19
  73.6 3.7 %collective-permute-start.1 = (f32[]{:T(128)}, f32[]{:T(128)}, u32[]{:S(2)}, u32[]{:S(2)}) collective-permute-start(f32[]{:T(128)} %add.180), channel_id=1, source_target_pairs={{0,32},{16,48},{32,0},{48,16},{64,96},{80,112},{96,64},{112,80},{1... | collective-permute-start | bytes 20 | tf_op jit(solution)/shard_map/while/body/eval_jaxpr/ppermute | solution.py:33
  77.9 5.2 %collective-permute-start.2 = (f32[]{:T(128)}, f32[]{:T(128)}, u32[]{:S(2)}, u32[]{:S(2)}) collective-permute-start(f32[]{:T(128)} %add.181), channel_id=1, source_target_pairs={{0,64},{16,80},{32,96},{48,112},{64,0},{80,16},{96,32},{112,48},{1... | collective-permute-start | bytes 20 | tf_op jit(solution)/shard_map/while/body/eval_jaxpr/ppermute | solution.py:33
  83.9 12.6 %collective-permute-start.5 = (f32[20,2,256]{2,0,1:T(8,128)S(1)}, f32[20,2,256]{2,0,1:T(8,128)S(1)}, u32[]{:S(2)}, u32[]{:S(2)}) collective-permute-start(f32[20,2,256]{2,0,1:T(8,128)S(1)} %get-tuple-element.109), channel_id=1, source_target_pairs={{2,0},{4,2},{6,4},{8,6},{10,8},{12,10},{14,12},{0,14},{3,1},{5,3},... | collective-permute-start | bytes 122888 | tf_op jit(solution)/shard_map/while/body/eval_jaxpr/ppermute | solution.py:21
  83.9 12.6 %collective-permute-start.6 = (f32[20,2,256]{2,0,1:T(8,128)S(1)}, f32[20,2,256]{2,0,1:T(8,128)S(1)}, u32[]{:S(2)}, u32[]{:S(2)}) collective-permute-start(f32[20,2,256]{2,0,1:T(8,128)S(1)} %get-tuple-element.110), channel_id=1, source_target_pairs={{0,2},{2,4},{4,6},{6,8},{8,10},{10,12},{12,14},{14,0},{1,3},{3,5},... | collective-permute-start | bytes 122888 | tf_op jit(solution)/shard_map/while/body/eval_jaxpr/ppermute | solution.py:19
  84.4 1.3 collective-permute-start.7
  86.2 3.7 %collective-permute-start.8 = (f32[]{:T(128)}, f32[]{:T(128)}, u32[]{:S(2)}, u32[]{:S(2)}) collective-permute-start(f32[]{:T(128)} %add.183), channel_id=1, source_target_pairs={{0,4},{2,6},{4,0},{6,2},{8,12},{10,14},{12,8},{14,10},{1,5},{3,7},... | collective-permute-start | bytes 20 | tf_op jit(solution)/shard_map/while/body/eval_jaxpr/ppermute | solution.py:33
  90.5 5.2 %collective-permute-start.9 = (f32[]{:T(128)}, f32[]{:T(128)}, u32[]{:S(2)}, u32[]{:S(2)}) collective-permute-start(f32[]{:T(128)} %add.184), channel_id=1, source_target_pairs={{0,8},{2,10},{4,12},{6,14},{8,0},{10,2},{12,4},{14,6},{1,9},{3,11}... | collective-permute-start | bytes 20 | tf_op jit(solution)/shard_map/while/body/eval_jaxpr/ppermute | solution.py:33
  102.3 5.3 %collective-permute-start = (f32[]{:T(128)}, f32[]{:T(128)}, u32[]{:S(2)}, u32[]{:S(2)}) collective-permute-start(f32[]{:T(128)} %multiply_reduce_fusion.3), channel_id=1, source_target_pairs={{0,16},{16,0},{32,48},{48,32},{64,80},{80,64},{96,112},{112,96},{1... | collective-permute-start | bytes 20 | tf_op jit(solution)/shard_map/while/body/eval_jaxpr/ppermute | solution.py:33
  103.8 15.1 %collective-permute-start.3 = (f32[2,32,256]{2,0,1:T(2,128)S(1)}, f32[2,32,256]{2,0,1:T(2,128)S(1)}, u32[]{:S(2)}, u32[]{:S(2)}) collective-permute-start(f32[2,32,256]{2,0,1:T(2,128)S(1)} %slice_bitcast_fusion.11), channel_id=1, source_target_pairs={{16,0},{32,16},{48,32},{64,48},{80,64},{96,80},{112,96},{0,112},{1... | collective-permute-start | bytes 196616 | tf_op jit(solution)/shard_map/while/body/eval_jaxpr/ppermute | solution.py:21
  106.6 12.3 %collective-permute-start.4 = (f32[2,32,256]{2,0,1:T(2,128)S(1)}, f32[2,32,256]{2,0,1:T(2,128)S(1)}, u32[]{:S(2)}, u32[]{:S(2)}) collective-permute-start(f32[2,32,256]{2,0,1:T(2,128)S(1)} %slice_bitcast_fusion.13), channel_id=1, source_target_pairs={{0,16},{16,32},{32,48},{48,64},{64,80},{80,96},{96,112},{112,0},{1... | collective-permute-start | bytes 196616 | tf_op jit(solution)/shard_map/while/body/eval_jaxpr/ppermute | solution.py:19
  108.8 3.7 %collective-permute-start.1 = (f32[]{:T(128)}, f32[]{:T(128)}, u32[]{:S(2)}, u32[]{:S(2)}) collective-permute-start(f32[]{:T(128)} %add.180), channel_id=1, source_target_pairs={{0,32},{16,48},{32,0},{48,16},{64,96},{80,112},{96,64},{112,80},{1... | collective-permute-start | bytes 20 | tf_op jit(solution)/shard_map/while/body/eval_jaxpr/ppermute | solution.py:33
  113.1 5.2 %collective-permute-start.2 = (f32[]{:T(128)}, f32[]{:T(128)}, u32[]{:S(2)}, u32[]{:S(2)}) collective-permute-start(f32[]{:T(128)} %add.181), channel_id=1, source_target_pairs={{0,64},{16,80},{32,96},{48,112},{64,0},{80,16},{96,32},{112,48},{1... | collective-permute-start | bytes 20 | tf_op jit(solution)/shard_map/while/body/eval_jaxpr/ppermute | solution.py:33
  119.1 12.6 %collective-permute-start.5 = (f32[20,2,256]{2,0,1:T(8,128)S(1)}, f32[20,2,256]{2,0,1:T(8,128)S(1)}, u32[]{:S(2)}, u32[]{:S(2)}) collective-permute-start(f32[20,2,256]{2,0,1:T(8,128)S(1)} %get-tuple-element.109), channel_id=1, source_target_pairs={{2,0},{4,2},{6,4},{8,6},{10,8},{12,10},{14,12},{0,14},{3,1},{5,3},... | collective-permute-start | bytes 122888 | tf_op jit(solution)/shard_map/while/body/eval_jaxpr/ppermute | solution.py:21
  119.1 12.6 %collective-permute-start.6 = (f32[20,2,256]{2,0,1:T(8,128)S(1)}, f32[20,2,256]{2,0,1:T(8,128)S(1)}, u32[]{:S(2)}, u32[]{:S(2)}) collective-permute-start(f32[20,2,256]{2,0,1:T(8,128)S(1)} %get-tuple-element.110), channel_id=1, source_target_pairs={{0,2},{2,4},{4,6},{6,8},{8,10},{10,12},{12,14},{14,0},{1,3},{3,5},... | collective-permute-start | bytes 122888 | tf_op jit(solution)/shard_map/while/body/eval_jaxpr/ppermute | solution.py:19
  119.6 1.3 collective-permute-start.7
  121.5 3.7 %collective-permute-start.8 = (f32[]{:T(128)}, f32[]{:T(128)}, u32[]{:S(2)}, u32[]{:S(2)}) collective-permute-start(f32[]{:T(128)} %add.183), channel_id=1, source_target_pairs={{0,4},{2,6},{4,0},{6,2},{8,12},{10,14},{12,8},{14,10},{1,5},{3,7},... | collective-permute-start | bytes 20 | tf_op jit(solution)/shard_map/while/body/eval_jaxpr/ppermute | solution.py:33
  125.8 5.2 %collective-permute-start.9 = (f32[]{:T(128)}, f32[]{:T(128)}, u32[]{:S(2)}, u32[]{:S(2)}) collective-permute-start(f32[]{:T(128)} %add.184), channel_id=1, source_target_pairs={{0,8},{2,10},{4,12},{6,14},{8,0},{10,2},{12,4},{14,6},{1,9},{3,11}... | collective-permute-start | bytes 20 | tf_op jit(solution)/shard_map/while/body/eval_jaxpr/ppermute | solution.py:33
  137.6 6.8 %collective-permute-start = (f32[]{:T(128)}, f32[]{:T(128)}, u32[]{:S(2)}, u32[]{:S(2)}) collective-permute-start(f32[]{:T(128)} %multiply_reduce_fusion.3), channel_id=1, source_target_pairs={{0,16},{16,0},{32,48},{48,32},{64,80},{80,64},{96,112},{112,96},{1... | collective-permute-start | bytes 20 | tf_op jit(solution)/shard_map/while/body/eval_jaxpr/ppermute | solution.py:33
  140.6 15.1 %collective-permute-start.3 = (f32[2,32,256]{2,0,1:T(2,128)S(1)}, f32[2,32,256]{2,0,1:T(2,128)S(1)}, u32[]{:S(2)}, u32[]{:S(2)}) collective-permute-start(f32[2,32,256]{2,0,1:T(2,128)S(1)} %slice_bitcast_fusion.11), channel_id=1, source_target_pairs={{16,0},{32,16},{48,32},{64,48},{80,64},{96,80},{112,96},{0,112},{1... | collective-permute-start | bytes 196616 | tf_op jit(solution)/shard_map/while/body/eval_jaxpr/ppermute | solution.py:21
  142.5 13.2 %collective-permute-start.4 = (f32[2,32,256]{2,0,1:T(2,128)S(1)}, f32[2,32,256]{2,0,1:T(2,128)S(1)}, u32[]{:S(2)}, u32[]{:S(2)}) collective-permute-start(f32[2,32,256]{2,0,1:T(2,128)S(1)} %slice_bitcast_fusion.13), channel_id=1, source_target_pairs={{0,16},{16,32},{32,48},{48,64},{64,80},{80,96},{96,112},{112,0},{1... | collective-permute-start | bytes 196616 | tf_op jit(solution)/shard_map/while/body/eval_jaxpr/ppermute | solution.py:19
  145.6 3.7 %collective-permute-start.1 = (f32[]{:T(128)}, f32[]{:T(128)}, u32[]{:S(2)}, u32[]{:S(2)}) collective-permute-start(f32[]{:T(128)} %add.180), channel_id=1, source_target_pairs={{0,32},{16,48},{32,0},{48,16},{64,96},{80,112},{96,64},{112,80},{1... | collective-permute-start | bytes 20 | tf_op jit(solution)/shard_map/while/body/eval_jaxpr/ppermute | solution.py:33
  149.9 5.2 %collective-permute-start.2 = (f32[]{:T(128)}, f32[]{:T(128)}, u32[]{:S(2)}, u32[]{:S(2)}) collective-permute-start(f32[]{:T(128)} %add.181), channel_id=1, source_target_pairs={{0,64},{16,80},{32,96},{48,112},{64,0},{80,16},{96,32},{112,48},{1... | collective-permute-start | bytes 20 | tf_op jit(solution)/shard_map/while/body/eval_jaxpr/ppermute | solution.py:33
  155.9 13.3 %collective-permute-start.5 = (f32[20,2,256]{2,0,1:T(8,128)S(1)}, f32[20,2,256]{2,0,1:T(8,128)S(1)}, u32[]{:S(2)}, u32[]{:S(2)}) collective-permute-start(f32[20,2,256]{2,0,1:T(8,128)S(1)} %get-tuple-element.109), channel_id=1, source_target_pairs={{2,0},{4,2},{6,4},{8,6},{10,8},{12,10},{14,12},{0,14},{3,1},{5,3},... | collective-permute-start | bytes 122888 | tf_op jit(solution)/shard_map/while/body/eval_jaxpr/ppermute | solution.py:21
  155.9 13.3 %collective-permute-start.6 = (f32[20,2,256]{2,0,1:T(8,128)S(1)}, f32[20,2,256]{2,0,1:T(8,128)S(1)}, u32[]{:S(2)}, u32[]{:S(2)}) collective-permute-start(f32[20,2,256]{2,0,1:T(8,128)S(1)} %get-tuple-element.110), channel_id=1, source_target_pairs={{0,2},{2,4},{4,6},{6,8},{8,10},{10,12},{12,14},{14,0},{1,3},{3,5},... | collective-permute-start | bytes 122888 | tf_op jit(solution)/shard_map/while/body/eval_jaxpr/ppermute | solution.py:19
  156.4 1.9 collective-permute-start.7
  158.9 3.7 %collective-permute-start.8 = (f32[]{:T(128)}, f32[]{:T(128)}, u32[]{:S(2)}, u32[]{:S(2)}) collective-permute-start(f32[]{:T(128)} %add.183), channel_id=1, source_target_pairs={{0,4},{2,6},{4,0},{6,2},{8,12},{10,14},{12,8},{14,10},{1,5},{3,7},... | collective-permute-start | bytes 20 | tf_op jit(solution)/shard_map/while/body/eval_jaxpr/ppermute | solution.py:33
  163.2 5.2 %collective-permute-start.9 = (f32[]{:T(128)}, f32[]{:T(128)}, u32[]{:S(2)}, u32[]{:S(2)}) collective-permute-start(f32[]{:T(128)} %add.184), channel_id=1, source_target_pairs={{0,8},{2,10},{4,12},{6,14},{8,0},{10,2},{12,4},{14,6},{1,9},{3,11}... | collective-permute-start | bytes 20 | tf_op jit(solution)/shard_map/while/body/eval_jaxpr/ppermute | solution.py:33
  173.3 9.5 %collective-permute-start.15 = (bf16[64,2304]{1,0:T(8,128)(2,1)S(1)}, bf16[64,2304]{1,0:T(8,128)(2,1)S(1)}, u32[]{:S(2)}, u32[]{:S(2)}) collective-permute-start(bf16[64,2304]{1,0:T(8,128)(2,1)S(1)} %dynamic-slice_convert_fusion.1), channel_id=1, source_target_pairs={{0,32},{16,48},{32,0},{48,16},{64,96},{80,112},{96,64},{112,80},{1... | collective-permute-start | bytes 884744 | tf_op jit(solution)/shard_map/ppermute | solution.py:89
  179.9 5.1 %collective-permute-start.21 = (f32[2]{0:T(128)S(1)}, f32[2]{0:T(128)S(1)}, u32[]{:S(2)}, u32[]{:S(2)}) collective-permute-start(f32[2]{0:T(128)S(1)} %pad_maximum_fusion.16), channel_id=1, source_target_pairs={{0,16},{16,0},{32,48},{48,32},{64,80},{80,64},{96,112},{112,96},{1... | collective-permute-start | bytes 32 | tf_op jit(solution)/shard_map/ppermute | solution.py:33
  182.8 6.7 %collective-permute-start.16 = (bf16[32,2304]{1,0:T(8,128)(2,1)S(1)}, bf16[32,2304]{1,0:T(8,128)(2,1)S(1)}, u32[]{:S(2)}, u32[]{:S(2)}) collective-permute-start(bf16[32,2304]{1,0:T(8,128)(2,1)S(1)} %dynamic-slice_convert_fusion.2), channel_id=1, source_target_pairs={{0,16},{16,0},{32,48},{48,32},{64,80},{80,64},{96,112},{112,96},{1... | collective-permute-start | bytes 442376 | tf_op jit(solution)/shard_map/ppermute | solution.py:89
  186.4 6.1 %collective-permute-start.22 = (f32[2]{0:T(128)S(1)}, f32[2]{0:T(128)S(1)}, u32[]{:S(2)}, u32[]{:S(2)}) collective-permute-start(f32[2]{0:T(128)S(1)} %fusion.80), channel_id=1, source_target_pairs={{0,32},{16,48},{32,0},{48,16},{64,96},{80,112},{96,64},{112,80},{1... | collective-permute-start | bytes 32 | tf_op jit(solution)/shard_map/ppermute | solution.py:33
  189.6 19.6 %collective-permute-start.17 = (bf16[16,2304]{1,0:T(8,128)(2,1)S(1)}, bf16[16,2304]{1,0:T(8,128)(2,1)S(1)}, u32[]{:S(2)}, u32[]{:S(2)}) collective-permute-start(bf16[16,2304]{1,0:T(8,128)(2,1)S(1)} %dynamic-slice_convert_fusion.3), channel_id=1, source_target_pairs={{0,8},{2,10},{4,12},{6,14},{8,0},{10,2},{12,4},{14,6},{1,9},{3,11}... | collective-permute-start | bytes 221192 | tf_op jit(solution)/shard_map/ppermute | solution.py:89
  193.8 5.7 %collective-permute-start.23 = (f32[2]{0:T(128)S(1)}, f32[2]{0:T(128)S(1)}, u32[]{:S(2)}, u32[]{:S(2)}) collective-permute-start(f32[2]{0:T(128)S(1)} %fusion.81), channel_id=1, source_target_pairs={{0,64},{16,80},{32,96},{48,112},{64,0},{80,16},{96,32},{112,48},{1... | collective-permute-start | bytes 32 | tf_op jit(solution)/shard_map/ppermute | solution.py:33
  199.5 1.1 collective-permute-start.24
  200.6 3.5 %collective-permute-start.25 = (f32[2]{0:T(128)S(1)}, f32[2]{0:T(128)S(1)}, u32[]{:S(2)}, u32[]{:S(2)}) collective-permute-start(f32[2]{0:T(128)S(1)} %add.156), channel_id=1, source_target_pairs={{0,4},{2,6},{4,0},{6,2},{8,12},{10,14},{12,8},{14,10},{1,5},{3,7},... | collective-permute-start | bytes 32 | tf_op jit(solution)/shard_map/ppermute | solution.py:33
  204.1 5.0 %collective-permute-start.26 = (f32[2]{0:T(128)S(1)}, f32[2]{0:T(128)S(1)}, u32[]{:S(2)}, u32[]{:S(2)}) collective-permute-start(f32[2]{0:T(128)S(1)} %add.157), channel_id=1, source_target_pairs={{0,8},{2,10},{4,12},{6,14},{8,0},{10,2},{12,4},{14,6},{1,9},{3,11}... | collective-permute-start | bytes 32 | tf_op jit(solution)/shard_map/ppermute | solution.py:33
  209.2 4.4 %collective-permute-start.18 = (f32[8,2304]{1,0:T(8,128)S(1)}, f32[8,2304]{1,0:T(8,128)S(1)}, u32[]{:S(2)}, u32[]{:S(2)}) collective-permute-start(f32[8,2304]{1,0:T(8,128)S(1)} %constant_dynamic-slice_fusion.1), channel_id=1, source_target_pairs={{0,4},{2,6},{4,0},{6,2},{8,12},{10,14},{12,8},{14,10},{1,5},{3,7},... | collective-permute-start | bytes 221192 | tf_op jit(solution)/shard_map/ppermute | solution.py:89
  213.7 1.3 collective-permute-start.19
  215.0 4.1 %collective-permute-start.20 = (f32[4,2304]{1,0:T(4,128)S(1)}, f32[4,2304]{1,0:T(4,128)S(1)}, u32[]{:S(2)}, u32[]{:S(2)}) collective-permute-start(f32[4,2304]{1,0:T(4,128)S(1)} %dynamic-slice_add_fusion.1), channel_id=1, source_target_pairs={{0,1},{1,0},{2,3},{3,2},{4,5},{5,4},{6,7},{7,6},{8,9},{9,8},{10,11... | collective-permute-start | bytes 110600 | tf_op jit(solution)/shard_map/ppermute | solution.py:33
  (18 other events, 40.1 us)
